TPU v7x, 128 devices: a whole 4x4x4 slice. The times are simulated.
128 devices in a mesh: chaos: 8 (over x, y_hi), space: 16 (over y_lo, z, core).
Axes of the slice: x: 4, y: 4 (y_hi: 2, y_lo: 2; y = y_hi * 2 + y_lo), z: 4, core: 2. Of those that a mesh axis runs over, the one named last changes fastest.
Arguments:
- modes: float32 [120, 128, 2048], P('chaos', 'space'), may hold values from -2 to 2
- kl_fields: float32 [8, 128, 2048], P(None, 'space'), may hold values from 0.1 to 1
- triples: int32 [624, 3], replicated, may hold values from 0 to 119, as said below
- ratios: int32 [624, 2], replicated, may hold values from 1 to 12, as said below
- mode_of_slot: int32 [120], replicated, may hold values from 0 to 119, each once
Outputs:
- applied: float32 [120, 128, 2048], P('chaos', 'space')
Inputs may be any that keep to these rules, and one draw needn't show every extreme that they name: `triples`: rows are distinct. Modes are the multi-indices of total degree at most 3 in 7 variables. Every mode i has the row (i, i, 0); every other row (i, j, k) has k of 1 or more, and the multi-indices of i and j differ by one in variable k and agree elsewhere; each such pair appears in both orders. `ratios`: column 0 is a positive numerator, column 1 a denominator of 1 to 4. `mode_of_slot`: A permutation.
All inputs are finite; a program needn't handle non-finite values.
Results may differ from a plain program's by a relative error of at most 0.000082.
Values sent between devices are 32-bit elements; how exact they have to be, the bound alone decides.
No kernel may reach another device: no remote copies, remote signals or barrier semaphores. Data moves between devices by JAX's collectives and lax.ppermute only.
A program may use at most 128 MiB of HBM per device.

v0:
```python
import jax
import jax.numpy as jnp
from jax import lax
from jax.sharding import PartitionSpec as P

HIGHEST_PRECISION = lax.Precision.HIGHEST


def extended_2(x, sides, width):
    for axis, dim in sides:
        count, length = (lax.axis_size(axis), x.shape[dim])
        up = [(i, (i + 1) % count) for i in range(count - 1)]
        down = [(j, i) for i, j in up]
        last = lax.slice_in_dim(x, length - width, length, axis=dim)
        first = lax.slice_in_dim(x, 0, width, axis=dim)
        before = lax.ppermute(last, axis, up)
        after = lax.ppermute(first, axis, down)
        x = jnp.concatenate([before, x, after], axis=dim)
    return x


def from_root(block, axis, owner):
    block = jnp.where(lax.axis_index(axis) == owner, block, jnp.zeros_like(block))
    return lax.psum(block, axis)


def diffuse(values, factor):
    center = values[:, 1:-1, :]
    coef_mid = factor[1:-1, :]
    result = (coef_mid + factor[:-2, :]) * (center - values[:, :-2, :])
    result = result + (coef_mid + factor[2:, :]) * (center - values[:, 2:, :])
    zero_col = jnp.zeros_like(center[:, :, :1])
    left_cell = jnp.concatenate([zero_col, center[:, :, :-1]], axis=2)
    right_cell = jnp.concatenate([center[:, :, 1:], zero_col], axis=2)
    coef_zero = jnp.zeros_like(coef_mid[:, :1])
    coef_left = jnp.concatenate([coef_zero, coef_mid[:, :-1]], axis=1)
    coef_right = jnp.concatenate([coef_mid[:, 1:], coef_zero], axis=1)
    result = result + (coef_mid + coef_left) * (center - left_cell)
    result = result + (coef_mid + coef_right) * (center - right_cell)
    return 0.5 * result


def coupling_table(triples, ratios, mode_of_slot, kl_terms, mode_count):
    matches = triples[:, :2, None] == mode_of_slot[None, None, :]
    slot_pairs = jnp.sum(jnp.where(matches, jnp.arange(mode_count, dtype=jnp.int32), 0), axis=2)
    weights = ratios[:, 0].astype(jnp.float32) / ratios[:, 1].astype(jnp.float32)
    flat_index = (triples[:, 2] * mode_count + slot_pairs[:, 0]) * mode_count + slot_pairs[:, 1]
    coupling = (
        jnp.zeros((kl_terms * mode_count * mode_count,), jnp.float32).at[flat_index].add(weights)
    )
    return coupling.reshape(kl_terms, mode_count, mode_count)


def local(modes, kl_fields, triples, ratios, mode_of_slot):
    groups = lax.axis_size("chaos")
    own_modes = modes.shape[0]
    mode_count = own_modes * groups
    kl_terms = kl_fields.shape[0]
    slab_rows = modes.shape[1]
    raster_cols = modes.shape[2]
    first_slot = lax.axis_index("chaos") * own_modes
    coupling = coupling_table(triples, ratios, mode_of_slot, kl_terms, mode_count)
    local_rows = lax.dynamic_slice_in_dim(coupling, first_slot, own_modes, 1).reshape(
        kl_terms * own_modes, mode_count
    )
    joined = jnp.concatenate([modes, kl_fields], axis=0)
    padded = extended_2(joined, (("space", 1),), 1)
    source = padded[:own_modes]
    coefficients = padded[own_modes:]
    rim_depth = source.shape[1]
    flat_source = source.reshape(own_modes, rim_depth * raster_cols)
    zero_sum = jnp.zeros((kl_terms * own_modes, rim_depth * raster_cols), jnp.float32)
    mixed_fields = zero_sum
    for owner in range(groups):
        received = from_root(flat_source, "chaos", owner)
        mode_block = lax.dynamic_slice_in_dim(local_rows, owner * own_modes, received.shape[0], 1)
        mixed_fields = mixed_fields + jnp.dot(
            mode_block, received, precision=HIGHEST_PRECISION, preferred_element_type=jnp.float32
        )
    extended = mixed_fields.reshape(kl_terms, own_modes, rim_depth, raster_cols)
    applied = jnp.zeros((own_modes, slab_rows, raster_cols), jnp.float32)
    for kl_index in range(kl_terms):
        applied = applied + diffuse(extended[kl_index], coefficients[kl_index])
    return applied


def solution(mesh):
    return jax.shard_map(
        local,
        mesh=mesh,
        in_specs=(P("chaos", "space", None), P(None, "space", None), P(), P(), P()),
        out_specs=P("chaos", "space", None),
        check_vma=False,
    )
```

profile of v0, /device:TPU:5, one launch (start us, length us, event | category | flops | bytes accessed | tf_op | source)
XLA Modules:
  0.0 603.4 jit_solution(7292626513668426113)
XLA Ops:
  8.2 2.6 collective-permute-start.1
  10.9 3.4 collective-permute-start
  36.8 4.9 scatter_custom_fusion
  46.8 419.7 %all-reduce.35.cloned.1.call-done = (f32[15,20480]{1,0:T(8,128)}, f32[15,20480]{1,0:T(8,128)}, f32[15,20480]{1,0:T(8,128)}, f32[15,20480]{1,0:T(8,128)}, f32[15,...) async-done(((f32[15,20480]{1,0:T(8,128)}, f32[15,20480]{1,0:T(8,128)}, f32[15,20480]{1,0:T(8,128)}, f32[15,20480]{1,0:T(8,128)}, ...) | async-done | bytes 9830416 | tf_op jit(solution)/shard_map/psum | solution.py:24
  466.5 9.2 %fusion.75 = f32[120,20480]{1,0:T(8,128)S(1)} fusion(f32[15,20480]{1,0:T(8,128)} %get-tuple-element.5, f32[120,120]{1,0:T(8,128)S(1)} %reshape.94), kind=kOutput, calls=%fused_computation.142 | convolution fusion | flops 442368000 | bytes 11116800 | tf_op jit(solution)/shard_map/dot_general | solution.py:77
  475.8 8.2 %convolution_add_fusion.6 = f32[120,20480]{1,0:T(8,128)S(1)} fusion(f32[120,20480]{1,0:T(8,128)S(1)} %fusion.75, f32[15,20480]{1,0:T(8,128)S(1)} %copy-done.13, f32[120,120]{1,0:T(8,128)S(1)} %reshape.94), kind=kOutput, calls=%fused_computation.7 | convolution fusion | flops 444825600 | bytes 20947200 | tf_op jit(solution)/shard_map/dot_general | solution.py:77
  484.0 8.3 %convolution_add_fusion.5 = f32[120,20480]{1,0:T(8,128)S(1)} fusion(f32[120,20480]{1,0:T(8,128)S(1)} %convolution_add_fusion.6, f32[15,20480]{1,0:T(8,128)S(1)} %copy-done.12, f32[120,120]{1,0:T(8,128)S(1)} %reshape.94), kind=kOutput, calls=%fused_computation.6 | convolution fusion | flops 444825600 | bytes 20947200 | tf_op jit(solution)/shard_map/dot_general | solution.py:77
  492.3 7.9 %convolution_add_fusion.4 = f32[120,20480]{1,0:T(8,128)S(1)} fusion(f32[120,20480]{1,0:T(8,128)S(1)} %convolution_add_fusion.5, f32[15,20480]{1,0:T(8,128)S(1)} %copy-done.11, f32[120,120]{1,0:T(8,128)S(1)} %reshape.94), kind=kOutput, calls=%fused_computation.5 | convolution fusion | flops 444825600 | bytes 20947200 | tf_op jit(solution)/shard_map/dot_general | solution.py:77
  500.3 8.1 %convolution_add_fusion.3 = f32[120,20480]{1,0:T(8,128)S(1)} fusion(f32[120,20480]{1,0:T(8,128)S(1)} %convolution_add_fusion.4, f32[15,20480]{1,0:T(8,128)S(1)} %copy-done.10, f32[120,120]{1,0:T(8,128)S(1)} %reshape.94), kind=kOutput, calls=%fused_computation.4 | convolution fusion | flops 444825600 | bytes 20947200 | tf_op jit(solution)/shard_map/dot_general | solution.py:77
  508.4 7.9 %convolution_add_fusion.2 = f32[120,20480]{1,0:T(8,128)S(1)} fusion(f32[120,20480]{1,0:T(8,128)S(1)} %convolution_add_fusion.3, f32[15,20480]{1,0:T(8,128)S(1)} %copy-done.9, f32[120,120]{1,0:T(8,128)S(1)} %reshape.94), kind=kOutput, calls=%fused_computation.3 | convolution fusion | flops 444825600 | bytes 20947200 | tf_op jit(solution)/shard_map/dot_general | solution.py:77
  516.4 10.0 %convolution_add_fusion.1 = f32[120,20480]{1,0:T(8,128)S(1)} fusion(f32[120,20480]{1,0:T(8,128)S(1)} %convolution_add_fusion.2, f32[15,20480]{1,0:T(8,128)S(1)} %copy-done.8, f32[120,120]{1,0:T(8,128)S(1)} %reshape.94), kind=kOutput, calls=%fused_computation.2 | convolution fusion | flops 444825600 | bytes 20947200 | tf_op jit(solution)/shard_map/dot_general | solution.py:77
  526.4 10.8 %convolution_add_fusion = f32[120,20480]{1,0:T(8,128)} fusion(f32[120,20480]{1,0:T(8,128)S(1)} %convolution_add_fusion.1, f32[15,20480]{1,0:T(8,128)S(1)} %copy-done.7, f32[120,120]{1,0:T(8,128)S(1)} %reshape.94), kind=kOutput, calls=%fused_computation.1 | convolution fusion | flops 444825600 | bytes 20947200 | tf_op jit(solution)/shard_map/dot_general | solution.py:77
  537.1 8.7 %fusion.80 = (f32[15,20480]{1,0:T(8,128)}, f32[15,20480]{1,0:T(8,128)}, f32[15,20480]{1,0:T(8,128)}, f32[15,20480]{1,0:T(8,128)}, f32[15,20480]{1,0:T(8,128)}, /...) fusion(f32[120,20480]{1,0:T(8,128)} %convolution_add_fusion), kind=kLoop, calls=%fused_computation.162 | loop fusion | bytes 19660800 | tf_op jit(solution)/shard_map/slice | solution.py:83
  547.6 3.1 squeeze.44
  550.7 3.1 squeeze.43
  553.8 3.0 squeeze.42
  556.8 3.1 squeeze.20
  559.9 3.1 squeeze.19
  563.0 3.0 squeeze.18
  567.8 4.2 fusion.81
  572.0 2.6 fusion.83
  575.4 2.6 fusion.85
  579.0 2.6 fusion.87
  581.7 14.4 %fusion.5 = f32[15,8,2048]{2,1,0:T(8,128)} fusion(f32[15,10,2048]{2,1,0:T(8,128)S(1)} %copy-done, f32[15,10,2048]{2,1,0:T(8,128)S(1)} %copy-done.1, f32[15,10,2048]{2,1,0:T(8,128)S(1)} %copy-done.2, f32[15,10,2048]{2,1,0:T(8,128)S(1)} %copy-done.3, f32[15,10,2048]{2,1,0:T(8,128)} %squeeze.19, f32[15,10,2048]{2,1,0:T(8,128)} %squeeze.18, ...), kind=kLoop, calls=%fused_computation.16 | loop fusion | flops 23592960 | bytes 42394112 | tf_op jit(solution)/shard_map/add | solution.py:83
  (112 shorter events, 34.5 us)
Async XLA Ops:
  6.5 460.0 %all-reduce.35.cloned.1.call-start = ((), (), s32[]{:S(2)}) async-start(), calls=%async_computation | async-start | bytes 20971520 | tf_op jit(solution)/shard_map/psum | solution.py:24
  8.2 7.5 %collective-permute-start.1 = (f32[23,1,2048]{2,0,1:T(8,128)S(1)}, f32[23,1,2048]{2,0,1:T(8,128)S(1)}, u32[]{:S(2)}, u32[]{:S(2)}) collective-permute-start(f32[23,1,2048]{2,0,1:T(8,128)S(1)} %copy.36), channel_id=1, source_target_pairs={{1,0},{2,1},{3,2},{4,3},{5,4},{6,5},{7,6},{8,7},{9,8},{10,9},{11,1... | collective-permute-start | bytes 565256 | tf_op jit(solution)/shard_map/ppermute | solution.py:17
  10.9 6.0 %collective-permute-start = (f32[23,1,2048]{2,0,1:T(8,128)S(1)}, f32[23,1,2048]{2,0,1:T(8,128)S(1)}, u32[]{:S(2)}, u32[]{:S(2)}) collective-permute-start(f32[23,1,2048]{2,0,1:T(8,128)S(1)} %copy.34), channel_id=1, source_target_pairs={{0,1},{1,2},{2,3},{3,4},{4,5},{5,6},{6,7},{7,8},{8,9},{9,10},{10,1... | collective-permute-start | bytes 565256 | tf_op jit(solution)/shard_map/ppermute | solution.py:16
  466.5 9.3 %copy-start.13 = (f32[15,20480]{1,0:T(8,128)S(1)}, f32[15,20480]{1,0:T(8,128)}, u32[]{:S(2)}) copy-start(f32[15,20480]{1,0:T(8,128)} %get-tuple-element.6) | copy-start | bytes 3686404
  475.8 8.2 %copy-start.12 = (f32[15,20480]{1,0:T(8,128)S(1)}, f32[15,20480]{1,0:T(8,128)}, u32[]{:S(2)}) copy-start(f32[15,20480]{1,0:T(8,128)} %get-tuple-element.7) | copy-start | bytes 3686404
  483.9 8.4 %copy-start.11 = (f32[15,20480]{1,0:T(8,128)S(1)}, f32[15,20480]{1,0:T(8,128)}, u32[]{:S(2)}) copy-start(f32[15,20480]{1,0:T(8,128)} %get-tuple-element.8) | copy-start | bytes 3686404
  492.3 7.9 %copy-start.10 = (f32[15,20480]{1,0:T(8,128)S(1)}, f32[15,20480]{1,0:T(8,128)}, u32[]{:S(2)}) copy-start(f32[15,20480]{1,0:T(8,128)} %get-tuple-element.9) | copy-start | bytes 3686404
  500.3 8.1 %copy-start.9 = (f32[15,20480]{1,0:T(8,128)S(1)}, f32[15,20480]{1,0:T(8,128)}, u32[]{:S(2)}) copy-start(f32[15,20480]{1,0:T(8,128)} %get-tuple-element.10) | copy-start | bytes 3686404
  508.4 7.9 %copy-start.8 = (f32[15,20480]{1,0:T(8,128)S(1)}, f32[15,20480]{1,0:T(8,128)}, u32[]{:S(2)}) copy-start(f32[15,20480]{1,0:T(8,128)} %get-tuple-element.11) | copy-start | bytes 3686404
  516.4 10.0 %copy-start.7 = (f32[15,20480]{1,0:T(8,128)S(1)}, f32[15,20480]{1,0:T(8,128)}, u32[]{:S(2)}) copy-start(f32[15,20480]{1,0:T(8,128)} %get-tuple-element.12) | copy-start | bytes 3686404
  567.8 4.2 copy-start.4
  567.8 4.2 copy-start.5
  572.0 3.5 copy-start.3
  575.4 3.5 copy-start.1
  578.9 2.7 copy-start.18
  578.9 2.7 copy-start.19
  578.9 2.7 copy-start.20
  579.0 2.7 copy-start.21
  579.0 2.7 copy-start.22
  579.0 2.7 copy-start.23
  579.0 2.7 copy-start.24
  579.0 2.7 copy-start.25
  579.0 2.7 copy-start.26
  579.0 2.7 copy-start.27
  (12 other events, 23.0 us)
Sparse Core Ops, SparseCore 0:
  36.0 430.4 all-reduce.34
where the time goes:
time: 612 us; the launch traced here: 603 us
  waiting for transfers between devices  422 us (69%)
  matrix products  70.4 us (12%)
  local copies, waits for them, and re-layouts  64.6 us (11%)
  other arithmetic  25.7 us (4%)
  between operations  14.4 us (2%)
    psum x1, waiting for transfers between devices, from_root(): return lax.psum(block, axis)  420 us
    dot_general x8, matrix products, local(): jnp.dot(mode_block, received, precision=HIGHEST_PRECISION, preferred_elem...  70.4 us
    squeeze x8, local copies, waits for them, and re-layouts, local(): applied = applied + diffuse(extended[kl_index], coefficients[kl_index])  21.9 us
    unnamed x81, local copies, waits for them, and re-layouts  19.7 us
    add x1, other arithmetic, local(): applied = applied + diffuse(extended[kl_index], coefficients[kl_index])  14.4 us
  transfers between devices with their start and end apart: 3, of which 3 were waited for; matrix products, arithmetic and copies ran while one was open for 2% of the time, Pallas kernels for 0%

commit v1 on v0

v1 whole, which is shorter than its diff:
```python
import jax
import jax.numpy as jnp
from jax import lax
from jax.sharding import PartitionSpec as P


def extended_2(x, sides, width):
    for axis, dim in sides:
        count, length = (lax.axis_size(axis), x.shape[dim])
        up = [(i, (i + 1) % count) for i in range(count - 1)]
        down = [(j, i) for i, j in up]
        last = lax.slice_in_dim(x, length - width, length, axis=dim)
        first = lax.slice_in_dim(x, 0, width, axis=dim)
        before = lax.ppermute(last, axis, up)
        after = lax.ppermute(first, axis, down)
        x = jnp.concatenate([before, x, after], axis=dim)
    return x


def shift_cols(x, direction):
    zero = jnp.zeros_like(x[..., :1])
    if direction > 0:
        return jnp.concatenate([zero, x[..., :-1]], axis=-1)
    return jnp.concatenate([x[..., 1:], zero], axis=-1)


def coupling_table(triples, ratios, mode_of_slot, kl_terms, mode_count):
    matches = triples[:, :2, None] == mode_of_slot[None, None, :]
    slot_pairs = jnp.sum(jnp.where(matches, jnp.arange(mode_count, dtype=jnp.int32), 0), axis=2)
    weights = ratios[:, 0].astype(jnp.float32) / ratios[:, 1].astype(jnp.float32)
    flat_index = (triples[:, 2] * mode_count + slot_pairs[:, 0]) * mode_count + slot_pairs[:, 1]
    coupling = (
        jnp.zeros((kl_terms * mode_count * mode_count,), jnp.float32).at[flat_index].add(weights)
    )
    return coupling.reshape(kl_terms, mode_count, mode_count)


def neighbour_table(local_rows):
    mode_count = local_rows.shape[-1]
    present = local_rows > 0
    first = jnp.argmax(present, axis=-1).astype(jnp.int32)
    last = (mode_count - 1 - jnp.argmax(present[..., ::-1], axis=-1)).astype(jnp.int32)
    w_first = jnp.take_along_axis(local_rows, first[..., None], axis=-1)[..., 0]
    w_last = jnp.take_along_axis(local_rows, last[..., None], axis=-1)[..., 0]
    w_last = jnp.where(last == first, jnp.zeros_like(w_last), w_last)
    return first, last, w_first, w_last


def local(modes, kl_fields, triples, ratios, mode_of_slot):
    groups = lax.axis_size("chaos")
    own_modes = modes.shape[0]
    mode_count = own_modes * groups
    kl_terms = kl_fields.shape[0]
    first_slot = lax.axis_index("chaos") * own_modes
    coupling = coupling_table(triples, ratios, mode_of_slot, kl_terms, mode_count)
    local_rows = lax.dynamic_slice_in_dim(coupling, first_slot, own_modes, 1)
    first, last, w_first, w_last = neighbour_table(local_rows)

    joined = jnp.concatenate([modes, kl_fields], axis=0)
    padded = extended_2(joined, (("space", 1),), 1)
    source = padded[:own_modes]
    coef = padded[own_modes:]
    every = lax.all_gather(source, "chaos", axis=0, tiled=True)

    a_c = coef[:, 1:-1]
    c_up = (a_c + coef[:, :-2])[:, None]
    c_dn = (a_c + coef[:, 2:])[:, None]
    c_lf = (a_c + shift_cols(a_c, 1))[:, None]
    c_rt = (a_c + shift_cols(a_c, -1))[:, None]

    g_first = jnp.take(every, first.reshape(-1), axis=0).reshape((kl_terms, own_modes) + every.shape[1:])
    g_last = jnp.take(every, last.reshape(-1), axis=0).reshape((kl_terms, own_modes) + every.shape[1:])
    mixed = w_first[:, :, None, None] * g_first + w_last[:, :, None, None] * g_last
    center = mixed[:, :, 1:-1]
    result = c_up * (center - mixed[:, :, :-2])
    result = result + c_dn * (center - mixed[:, :, 2:])
    result = result + c_lf * (center - shift_cols(center, 1))
    result = result + c_rt * (center - shift_cols(center, -1))
    return 0.5 * jnp.sum(result, axis=0)


def solution(mesh):
    return jax.shard_map(
        local,
        mesh=mesh,
        in_specs=(P("chaos", "space", None), P(None, "space", None), P(), P(), P()),
        out_specs=P("chaos", "space", None),
        check_vma=False,
    )
```

time: 612 us -> 302 us (0.49)
  the two profiles are of different devices: /device:TPU:5 before, /device:TPU:1 now
where the time goes in v1:
time: 302 us
  waiting for transfers between devices  166 us (55%)
  local copies, waits for them, and re-layouts  61.8 us (20%)
  other arithmetic  53.2 us (18%)
  between operations  13.7 us (5%)
  starting transfers between devices  6.88 us (2%)
    all_gather x1, waiting for transfers between devices, local(): every = lax.all_gather(source, 'chaos', axis=0, tiled=True)  161 us
    reduce_sum x1, other arithmetic, local(): return 0.5 * jnp.sum(result, axis=0)  18.3 us
    slice x2, local copies, waits for them, and re-layouts, shift_cols(): return jnp.concatenate([zero, x[..., :-1]], axis=-1)  15.9 us
    gather x1, local copies, waits for them, and re-layouts, local(): jnp.take(every, first.reshape(-1), axis=0)  15.1 us
    gather x1, local copies, waits for them, and re-layouts, local(): jnp.take(every, last.reshape(-1), axis=0)  15.1 us
    select_n x2, other arithmetic, local(): jnp.take(every, first.reshape(-1), axis=0)  11.6 us
    add x1, other arithmetic, local(): w_first[:, :, None, None] * g_first + w_last[:, :, None, None] * g_last  7.05 us
    select_n x2, other arithmetic, local(): jnp.take(every, last.reshape(-1), axis=0)  6.84 us
  transfers between devices with their start and end apart: 3, of which 3 were waited for; matrix products, arithmetic and copies ran while one was open for 5% of the time, Pallas kernels for 0%

profile of v1, /device:TPU:1, one launch (start us, length us, event | category | flops | bytes accessed | tf_op | source)
XLA Modules:
  0.0 301.8 jit_solution(17905389642816986577)
XLA Ops:
  6.6 1.8 copy.16
  8.4 1.4 copy.18
  9.8 4.9 %collective-permute-start = (f32[23,1,2048]{2,0,1:T(8,128)S(1)}, f32[23,1,2048]{2,0,1:T(8,128)S(1)}, u32[]{:S(2)}, u32[]{:S(2)}) collective-permute-start(f32[23,1,2048]{2,0,1:T(8,128)S(1)} %get-tuple-element.17), channel_id=1, source_target_pairs={{0,1},{1,2},{2,3},{3,4},{4,5},{5,6},{6,7},{7,8},{8,9},{9,10},{10,1... | collective-permute-start | bytes 565256 | tf_op jit(solution)/shard_map/ppermute | solution.py:14
  14.7 1.9 collective-permute-start.1
  17.3 4.4 %collective-permute-done.1 = f32[23,1,2048]{2,0,1:T(8,128)S(1)} collective-permute-done((f32[23,1,2048]{2,0,1:T(8,128)S(1)}, f32[23,1,2048]{2,0,1:T(8,128)S(1)}, u32[]{:S(2)}, u32[]{:S(2)}) %collective-permute-start.1) | collective-permute-done | bytes 188448 | tf_op jit(solution)/shard_map/ppermute | solution.py:15
  21.8 2.0 copy.20
  24.1 4.7 %scatter_custom_fusion = f32[115200]{0:T(1024)S(1)} fusion(s32[624]{0:T(1024)S(1)} %fusion.22, f32[624]{0:T(1024)S(1)} %fusion.24, f32[]{:T(128)} %constant.6.clone.1), kind=kCustom, calls=%fused_computation.29 | custom fusion | flops 624 | bytes 460804 | tf_op jit(solution)/shard_map/scatter-add | solution.py:33
  29.5 1.1 iota_reduce_fusion.1
  30.7 0.9 iota_reduce_fusion
  31.7 2.1 gather_fusion.2
  34.0 2.1 gather_fusion
  36.5 1.0 pad_add_fusion.1
  37.6 1.1 copy.19
  38.7 1.1 copy.22
  39.8 161.2 %all-gather.2.cloned.1.call-done = f32[120,10,2048]{2,1,0:T(8,128)} async-done(((f32[15,10,2048]{2,1,0:T(8,128)}), f32[120,10,2048]{2,1,0:T(8,128)}) %all-gather.2.cloned.1.call-update) | async-done | bytes 9830416 | tf_op jit(solution)/shard_map/all_gather | solution.py:63
  201.0 15.1 %gather_fusion.1 = f32[120,10,2048]{2,1,0:T(8,128)} fusion(f32[120,10,2048]{2,1,0:T(8,128)} %all-gather.2.cloned.1.call-done, s32[1024]{0:T(1024)S(1)} %pad_clamp_fusion.1), kind=kCustom, calls=%fused_computation.1.clone | custom fusion | bytes 19661280 | tf_op jit(solution)/shard_map/jit(_take)/gather | solution.py:71
  216.1 11.6 %broadcast_select_fusion.1 = f32[120,10,2048]{2,1,0:T(8,128)} fusion(f32[120,10,2048]{2,1,0:T(8,128)} %gather_fusion.1, pred[120]{0:T(512)(128)(4,1)S(1)} %compare_and_fusion.1), kind=kLoop, calls=%fused_computation.15 | loop fusion | flops 2457600 | bytes 19660920 | tf_op jit(solution)/shard_map/jit(_take)/select_n | solution.py:71
  227.7 15.1 %gather_fusion.3 = f32[120,10,2048]{2,1,0:T(8,128)} fusion(f32[120,10,2048]{2,1,0:T(8,128)} %all-gather.2.cloned.1.call-done, s32[1024]{0:T(1024)S(1)} %pad_clamp_fusion), kind=kCustom, calls=%fused_computation.3.clone | custom fusion | bytes 19661280 | tf_op jit(solution)/shard_map/jit(_take)/gather | solution.py:72
  242.8 6.8 %broadcast_select_fusion = f32[120,10,2048]{2,1,0:T(8,128)S(1)} fusion(f32[120,10,2048]{2,1,0:T(8,128)} %gather_fusion.3, pred[120]{0:T(512)(128)(4,1)S(1)} %compare_and_fusion), kind=kLoop, calls=%fused_computation.14 | loop fusion | flops 2457600 | bytes 19660920 | tf_op jit(solution)/shard_map/jit(_take)/select_n | solution.py:72
  249.6 3.2 %copy-done = f32[120,10,2048]{2,1,0:T(8,128)S(1)} copy-done((f32[120,10,2048]{2,1,0:T(8,128)S(1)}, f32[120,10,2048]{2,1,0:T(8,128)}, u32[]{:S(2)}) %copy-start) | copy-done | bytes 9830424
  252.8 7.1 %multiply_add_fusion = f32[8,15,10,2048]{3,2,1,0:T(8,128)} fusion(f32[8,15,10,2048]{3,2,1,0:T(8,128)S(1)} %bitcast.31, f32[8,15,10,2048]{3,2,1,0:T(8,128)S(1)} %bitcast.30, f32[8,15]{1,0:T(8,128)S(1)} %bitcast_select_fusion, f32[8,15]{1,0:T(8,128)S(1)} %select_bitcast_fusion), kind=kLoop, calls=%fused_computation.5 | loop fusion | flops 7372800 | bytes 29492160 | tf_op jit(solution)/shard_map/add | solution.py:73
  259.8 15.7 %fusion.25 = (f32[8,15,8,2047]{3,2,1,0:T(8,128)S(1)}, f32[8,15,8,2047]{3,2,1,0:T(8,128)}) fusion(f32[8,15,10,2048]{3,2,1,0:T(8,128)} %multiply_add_fusion), kind=kLoop, calls=%fused_computation.76 | loop fusion | bytes 31441920 | tf_op jit(solution)/shard_map/slice | solution.py:23
  275.5 18.3 %fusion.4 = f32[15,8,2048]{2,1,0:T(8,128)S(1)} fusion(f32[8,15,10,2048]{3,2,1,0:T(8,128)} %multiply_add_fusion, f32[8,15,8,2047]{3,2,1,0:T(8,128)} %get-tuple-element.14, f32[8,15,8,2047]{3,2,1,0:T(8,128)S(1)} %get-tuple-element.13, f32[8,8,2048]{2,1,0:T(8,128)} %get-tuple-element.20, f32[8,8,2048]{2,1,0:T(8,128)S(1)} %get-tuple-element.19, ...), kind=kLoop, calls=%fused_computation.11 | loop fusion | flops 23347200 | bytes 42394112 | tf_op jit(solution)/shard_map/reduce_sum | solution.py:79
  293.9 1.1 broadcast_multiply_fusion
  (49 shorter events, 2.6 us)
Async XLA Ops:
  6.5 17.3 %slice-start = ((s32[624,3]{0,1:T(4,128)}), s32[624,2]{0,1:T(2,128)S(1)}, s32[]{:S(2)}) async-start(s32[624,3]{0,1:T(4,128)} %param.11), calls=%async_computation.1 | async-start | bytes 10240 | tf_op jit(solution)/shard_map/slice | solution.py:28
  6.5 17.5 %copy-start.4 = (s32[624,3]{0,1:T(4,128)S(1)}, s32[624,3]{0,1:T(4,128)}, u32[]{:S(2)}) copy-start(s32[624,3]{0,1:T(4,128)} %param.11) | copy-start | bytes 22468
  6.5 17.3 %copy-start.6 = (s32[120]{0:T(128)S(1)}, s32[120]{0:T(128)}, u32[]{:S(2)}) copy-start(s32[120]{0:T(128)} %param.13) | copy-start | bytes 1444
  6.5 17.5 %copy-start.5 = (s32[624,2]{0,1:T(2,128)S(1)}, s32[624,2]{0,1:T(2,128)}, u32[]{:S(2)}) copy-start(s32[624,2]{0,1:T(2,128)} %param.12) | copy-start | bytes 14980
  6.5 194.5 %all-gather.2.cloned.1.call-start = ((), (), s32[]{:S(2)}) async-start(), calls=%async_computation | async-start | bytes 17694720 | tf_op jit(solution)/shard_map/all_gather | solution.py:63
  9.8 7.5 %collective-permute-start = (f32[23,1,2048]{2,0,1:T(8,128)S(1)}, f32[23,1,2048]{2,0,1:T(8,128)S(1)}, u32[]{:S(2)}, u32[]{:S(2)}) collective-permute-start(f32[23,1,2048]{2,0,1:T(8,128)S(1)} %get-tuple-element.17), channel_id=1, source_target_pairs={{0,1},{1,2},{2,3},{3,4},{4,5},{5,6},{6,7},{7,8},{8,9},{9,10},{10,1... | collective-permute-start | bytes 565256 | tf_op jit(solution)/shard_map/ppermute | solution.py:14
  14.7 7.0 %collective-permute-start.1 = (f32[23,1,2048]{2,0,1:T(8,128)S(1)}, f32[23,1,2048]{2,0,1:T(8,128)S(1)}, u32[]{:S(2)}, u32[]{:S(2)}) collective-permute-start(f32[23,1,2048]{2,0,1:T(8,128)S(1)} %get-tuple-element.18), channel_id=1, source_target_pairs={{1,0},{2,1},{3,2},{4,3},{5,4},{6,5},{7,6},{8,7},{9,8},{10,9},{11,1... | collective-permute-start | bytes 565256 | tf_op jit(solution)/shard_map/ppermute | solution.py:15
  21.7 2.4 copy-start.2
  21.8 14.5 %copy-start.1 = (f32[8,8,2048]{2,1,0:T(8,128)S(1)}, f32[8,8,2048]{2,1,0:T(8,128)}, u32[]{:S(2)}) copy-start(f32[8,8,2048]{2,1,0:T(8,128)} %param.10) | copy-start | bytes 1572868
  29.4 8.1 %copy-start.3 = (f32[23,1,2048]{2,0,1:T(8,128)S(1)}, f32[23,1,2048]{2,0,1:T(8,128)}, u32[]{:S(2)}) copy-start(f32[23,1,2048]{2,0,1:T(8,128)} %copy-done.2) | copy-start | bytes 565252
  242.8 10.0 %copy-start = (f32[120,10,2048]{2,1,0:T(8,128)S(1)}, f32[120,10,2048]{2,1,0:T(8,128)}, u32[]{:S(2)}) copy-start(f32[120,10,2048]{2,1,0:T(8,128)} %broadcast_select_fusion.1) | copy-start | bytes 29491204
Sparse Core Ops, SparseCore 0:
  24.0 176.9 all-gather.1

commit v2 on v1

--- a/solution.py
+++ b/solution.py
@@ -46,6 +46,29 @@
     return first, last, w_first, w_last
 
 
+def shifted(x, step):
+    count = lax.axis_size("chaos")
+    return lax.ppermute(x, "chaos", [(c, (c + step) % count) for c in range(count)])
+
+
+def ring_gather(block):
+    count = lax.axis_size("chaos")
+    me = lax.axis_index("chaos")
+    half = block.shape[-1] // 2
+    partner = lax.ppermute(block, "chaos", [(c, c ^ 1) for c in range(count)])
+    pieces = []
+    owners = []
+    for base, origin in ((block, me), (partner, me ^ 1)):
+        from_left = shifted(base, 2)
+        from_right = shifted(base, -2)
+        far = jnp.concatenate(
+            [shifted(from_left[..., :half], 2), shifted(from_right[..., half:], -2)], axis=-1
+        )
+        pieces += [base, from_left, from_right, far]
+        owners += [origin, (origin - 2) % count, (origin + 2) % count, (origin + 4) % count]
+    return jnp.concatenate(pieces, axis=0), jnp.stack(owners).astype(jnp.int32)
+
+
 def local(modes, kl_fields, triples, ratios, mode_of_slot):
     groups = lax.axis_size("chaos")
     own_modes = modes.shape[0]
@@ -60,7 +83,12 @@
     padded = extended_2(joined, (("space", 1),), 1)
     source = padded[:own_modes]
     coef = padded[own_modes:]
-    every = lax.all_gather(source, "chaos", axis=0, tiled=True)
+    every, order = ring_gather(source)
+    owner = jnp.arange(mode_count, dtype=jnp.int32) // own_modes
+    position = jnp.argmax(order[None, :] == owner[:, None], axis=1).astype(jnp.int32)
+    place = position * own_modes + jnp.arange(mode_count, dtype=jnp.int32) % own_modes
+    first = place[first]
+    last = place[last]
 
     a_c = coef[:, 1:-1]
     c_up = (a_c + coef[:, :-2])[:, None]

time: 302 us -> 216 us (0.72)
  waiting for transfers between devices: 166 us -> 62.1 us
  starting transfers between devices: 6.88 us -> 20.3 us
  between operations: 13.7 us -> 0.49 us
  other arithmetic: 53.2 us -> 63.5 us
  local copies, waits for them, and re-layouts: 61.8 us -> 68.9 us
    all_gather x1 -> x0, waiting for transfers between devices: 161 us -> none  [local(): every = lax.all_gather(source, 'chaos', axis=0, tiled=True)]
    ppermute x0 -> x9, waiting for transfers between devices: none -> 62.1 us  [the longest x8 62.1 us: shifted(): lax.ppermute(x, 'chaos', [(c, (c + step) % count) for c in range(count)])]
    ppermute x0 -> x9, starting transfers between devices: none -> 13.5 us  [the longest x8 10.6 us: shifted(): lax.ppermute(x, 'chaos', [(c, (c + step) % count) for c in range(count)])]
    add x1, other arithmetic: 7.05 us -> 19 us  [local(): w_first[:, :, None, None] * g_first + w_last[:, :, None, None] * g_last]
    unnamed x16 -> x14, local copies, waits for them, and re-layouts: 6.33 us -> 17.1 us
    slice x2, local copies, waits for them, and re-layouts: 15.9 us -> 5.68 us  [shift_cols(): return jnp.concatenate([zero, x[..., :-1]], axis=-1)]
    reduce_sum x1, other arithmetic: 18.3 us -> 8.7 us  [local(): return 0.5 * jnp.sum(result, axis=0)]
    ppermute x1, waiting for transfers between devices: 4.4 us -> 0.01 us  [extended_2(): after = lax.ppermute(first, axis, down)]
  transfers between devices with their start and end apart: 3 -> 11, of which waited for: 3 -> 5; matrix products, arithmetic and copies ran while one was open for 5% -> 18% of each run, Pallas kernels for 0% -> 0%
where the time goes in v2:
time: 216 us; the launch traced here: 215 us
  local copies, waits for them, and re-layouts  68.9 us (32%)
  other arithmetic  63.5 us (29%)
  waiting for transfers between devices  62.1 us (29%)
  starting transfers between devices  20.3 us (9%)
    ppermute x8, waiting for transfers between devices, shifted(): lax.ppermute(x, 'chaos', [(c, (c + step) % count) for c in range(count)])  62.1 us
    add x1, other arithmetic, local(): w_first[:, :, None, None] * g_first + w_last[:, :, None, None] * g_last  19 us
    unnamed x14, local copies, waits for them, and re-layouts  17.1 us
    gather x1, local copies, waits for them, and re-layouts, local(): jnp.take(every, last.reshape(-1), axis=0)  15 us
    gather x1, local copies, waits for them, and re-layouts, local(): jnp.take(every, first.reshape(-1), axis=0)  15 us
    select_n x2, other arithmetic, local(): jnp.take(every, first.reshape(-1), axis=0)  12.8 us
    ppermute x8, starting transfers between devices, shifted(): lax.ppermute(x, 'chaos', [(c, (c + step) % count) for c in range(count)])  10.6 us
    reduce_sum x1, other arithmetic, local(): return 0.5 * jnp.sum(result, axis=0)  8.7 us
  transfers between devices with their start and end apart: 11, of which 5 were waited for; matrix products, arithmetic and copies ran while one was open for 18% of the time, Pallas kernels for 0%

profile of v2, /device:TPU:1, one launch (start us, length us, event | category | flops | bytes accessed | tf_op | source)
XLA Modules:
  0.0 215.3 jit_solution(14996524447965301485)
XLA Ops:
  2.7 4.9 %collective-permute-start = (f32[23,1,2048]{2,0,1:T(8,128)S(1)}, f32[23,1,2048]{2,0,1:T(8,128)S(1)}, u32[]{:S(2)}, u32[]{:S(2)}) collective-permute-start(f32[23,1,2048]{2,0,1:T(8,128)S(1)} %copy.91), channel_id=1, source_target_pairs={{0,1},{1,2},{2,3},{3,4},{4,5},{5,6},{6,7},{7,8},{8,9},{9,10},{10,1... | collective-permute-start | bytes 565256 | tf_op jit(solution)/shard_map/ppermute | solution.py:14
  12.7 4.7 %scatter_custom_fusion = f32[115200]{0:T(1024)S(1)} fusion(s32[624]{0:T(1024)S(1)} %fusion.23, f32[624]{0:T(1024)S(1)} %fusion.25, f32[]{:T(128)} %constant.102.clone.1), kind=kCustom, calls=%fused_computation.37 | custom fusion | flops 624 | bytes 460804 | tf_op jit(solution)/shard_map/scatter-add | solution.py:33
  23.5 2.1 gather_fusion.2
  32.2 2.9 %collective-permute-start.6 = (f32[15,10,2048]{2,0,1:T(8,128)}, f32[15,10,2048]{2,0,1:T(8,128)}, u32[]{:S(2)}, u32[]{:S(2)}) collective-permute-start(f32[15,10,2048]{2,0,1:T(8,128)} %copy.97), channel_id=1, source_target_pairs={{0,16},{16,0},{32,48},{48,32},{64,80},{80,64},{96,112},{112,96},{1... | collective-permute-start | bytes 3686408 | tf_op jit(solution)/shard_map/ppermute | solution.py:58
  35.3 2.1 gather_fusion.4
  40.1 20.2 %collective-permute-done.3 = f32[15,10,2048]{2,0,1:T(8,128)} collective-permute-done((f32[15,10,2048]{2,0,1:T(8,128)}, f32[15,10,2048]{2,0,1:T(8,128)}, u32[]{:S(2)}, u32[]{:S(2)}) %collective-permute-start.3) | collective-permute-done | bytes 1228832 | tf_op jit(solution)/shard_map/ppermute | solution.py:51
  61.5 2.3 %collective-permute-start.5 = (f32[15,10,1024]{2,0,1:T(8,128)S(1)}, f32[15,10,1024]{2,0,1:T(8,128)S(1)}, u32[]{:S(2)}, u32[]{:S(2)}) collective-permute-start(f32[15,10,1024]{2,0,1:T(8,128)S(1)} %slice.126), channel_id=1, source_target_pairs={{0,96},{16,112},{32,0},{48,16},{64,32},{80,48},{96,64},{112,80},{1... | collective-permute-start | bytes 1843208 | tf_op jit(solution)/shard_map/ppermute | solution.py:51
  64.3 2.3 %collective-permute-start.8 = (f32[15,10,2048]{2,0,1:T(8,128)}, f32[15,10,2048]{2,0,1:T(8,128)S(1)}, u32[]{:S(2)}, u32[]{:S(2)}) collective-permute-start(f32[15,10,2048]{2,0,1:T(8,128)} %collective-permute-done.6), channel_id=1, source_target_pairs={{0,96},{16,112},{32,0},{48,16},{64,32},{80,48},{96,64},{112,80},{1... | collective-permute-start | bytes 3686408 | tf_op jit(solution)/shard_map/ppermute | solution.py:51
  68.7 3.4 %copy_dynamic-update-slice_fusion.3 = f32[120,10,2048]{2,1,0:T(8,128)} fusion(f32[120,10,2048]{2,1,0:T(8,128)} %copy_dynamic-update-slice_fusion.4, f32[15,10,2048]{2,0,1:T(8,128)} %collective-permute-done.3), kind=kLoop, calls=%fused_computation.27 | loop fusion | bytes 3276800
  72.0 6.3 %collective-permute-done.5 = f32[15,10,1024]{2,0,1:T(8,128)S(1)} collective-permute-done((f32[15,10,1024]{2,0,1:T(8,128)S(1)}, f32[15,10,1024]{2,0,1:T(8,128)S(1)}, u32[]{:S(2)}, u32[]{:S(2)}) %collective-permute-start.5) | collective-permute-done | bytes 614432 | tf_op jit(solution)/shard_map/ppermute | solution.py:51
  78.7 3.1 %collective-permute-done.4 = f32[15,10,1024]{2,0,1:T(8,128)S(1)} collective-permute-done((f32[15,10,1024]{2,0,1:T(8,128)S(1)}, f32[15,10,1024]{2,0,1:T(8,128)S(1)}, u32[]{:S(2)}, u32[]{:S(2)}) %collective-permute-start.4) | collective-permute-done | bytes 614432 | tf_op jit(solution)/shard_map/ppermute | solution.py:51
  83.6 3.4 %copy_dynamic-update-slice_fusion.2 = f32[120,10,2048]{2,1,0:T(8,128)} fusion(f32[120,10,2048]{2,1,0:T(8,128)} %maximum_dynamic-update-slice_fusion.1, f32[15,10,2048]{2,0,1:T(8,128)} %collective-permute-done.6), kind=kLoop, calls=%fused_computation.26 | loop fusion | bytes 3276800
  87.1 21.6 %collective-permute-done.7 = f32[15,10,2048]{2,0,1:T(8,128)S(1)} collective-permute-done((f32[15,10,2048]{2,0,1:T(8,128)}, f32[15,10,2048]{2,0,1:T(8,128)S(1)}, u32[]{:S(2)}, u32[]{:S(2)}) %collective-permute-start.7) | collective-permute-done | bytes 1228832 | tf_op jit(solution)/shard_map/ppermute | solution.py:51
  108.9 2.7 %collective-permute-start.10 = (f32[15,10,1024]{2,0,1:T(8,128)S(1)}, f32[15,10,1024]{2,0,1:T(8,128)S(1)}, u32[]{:S(2)}, u32[]{:S(2)}) collective-permute-start(f32[15,10,1024]{2,0,1:T(8,128)S(1)} %slice.128), channel_id=1, source_target_pairs={{0,96},{16,112},{32,0},{48,16},{64,32},{80,48},{96,64},{112,80},{1... | collective-permute-start | bytes 1843208 | tf_op jit(solution)/shard_map/ppermute | solution.py:51
  113.7 2.1 copy_dynamic-update-slice_fusion
  115.8 10.8 %collective-permute-done.9 = f32[15,10,1024]{2,0,1:T(8,128)S(1)} collective-permute-done((f32[15,10,1024]{2,0,1:T(8,128)S(1)}, f32[15,10,1024]{2,0,1:T(8,128)S(1)}, u32[]{:S(2)}, u32[]{:S(2)}) %collective-permute-start.9) | collective-permute-done | bytes 614432 | tf_op jit(solution)/shard_map/ppermute | solution.py:51
  128.8 15.0 %gather_fusion.3 = f32[120,10,2048]{2,1,0:T(8,128)} fusion(f32[120,10,2048]{2,1,0:T(8,128)} %maximum_dynamic-update-slice_fusion, s32[1024]{0:T(1024)S(1)} %get-tuple-element.30), kind=kCustom, calls=%fused_computation.1.clone | custom fusion | bytes 19661280 | tf_op jit(solution)/shard_map/jit(_take)/gather | solution.py:99
  143.8 15.0 %gather_fusion.5 = f32[120,10,2048]{2,1,0:T(8,128)} fusion(f32[120,10,2048]{2,1,0:T(8,128)} %maximum_dynamic-update-slice_fusion, s32[1024]{0:T(1024)S(1)} %get-tuple-element.29), kind=kCustom, calls=%fused_computation.3.clone | custom fusion | bytes 19661280 | tf_op jit(solution)/shard_map/jit(_take)/gather | solution.py:100
  158.8 12.8 %broadcast_select_fusion.1 = f32[120,10,2048]{2,1,0:T(8,128)} fusion(f32[120,10,2048]{2,1,0:T(8,128)} %gather_fusion.3, pred[120]{0:T(512)(128)(4,1)S(1)} %compare_and_fusion.1), kind=kLoop, calls=%fused_computation.19 | loop fusion | flops 2457600 | bytes 19660920 | tf_op jit(solution)/shard_map/jit(_take)/select_n | solution.py:99
  171.6 2.9 %copy-done = f32[120,10,2048]{2,1,0:T(8,128)S(1)} copy-done((f32[120,10,2048]{2,1,0:T(8,128)S(1)}, f32[120,10,2048]{2,1,0:T(8,128)}, u32[]{:S(2)}) %copy-start) | copy-done | bytes 9830424
  174.5 6.1 %broadcast_select_fusion = f32[120,10,2048]{2,1,0:T(8,128)} fusion(f32[120,10,2048]{2,1,0:T(8,128)S(1)} %copy-done, pred[120]{0:T(512)(128)(4,1)S(1)} %compare_and_fusion), kind=kLoop, calls=%fused_computation.18 | loop fusion | flops 2457600 | bytes 19660920 | tf_op jit(solution)/shard_map/jit(_take)/select_n | solution.py:100
  180.6 19.0 %fusion = f32[8,15,10,2048]{3,1,0,2:T(8,128)S(1)} fusion(f32[8,15,10,2048]{3,2,1,0:T(8,128)} %bitcast.39, f32[8,15,10,2048]{3,2,1,0:T(8,128)} %bitcast.38, f32[8,15]{1,0:T(8,128)S(1)} %bitcast_select_fusion, f32[8,15]{1,0:T(8,128)S(1)} %select_bitcast_fusion), kind=kLoop, calls=%fused_computation.8 | loop fusion | flops 7372800 | bytes 29492160 | tf_op jit(solution)/shard_map/add | solution.py:101
  199.6 5.5 %fusion.27 = (f32[8,15,8,2047]{3,1,0,2:T(8,128)S(1)}, f32[8,15,8,2047]{3,1,0,2:T(8,128)}) fusion(f32[8,15,10,2048]{3,1,0,2:T(8,128)S(1)} %fusion), kind=kLoop, calls=%fused_computation.95 | loop fusion | bytes 31441920 | tf_op jit(solution)/shard_map/slice | solution.py:23
  205.0 8.7 %fusion.5 = f32[15,8,2048]{2,0,1:T(8,128)S(1)} fusion(f32[8,15,10,2048]{3,1,0,2:T(8,128)S(1)} %fusion, f32[8,15,8,2047]{3,1,0,2:T(8,128)} %get-tuple-element.16, f32[8,15,8,2047]{3,1,0,2:T(8,128)S(1)} %get-tuple-element.15, f32[8,8,2048]{2,0,1:T(8,128)S(1)} %copy.114, f32[8,8,2048]{2,0,1:T(8,128)S(1)} %copy.113, f32[8,8,2048]{2,0,1:T(8,128)S(1)} %copy.112, ...), kind=kLoop, calls=%fused_computation.15 | loop fusion | flops 23347200 | bytes 42394112 | tf_op jit(solution)/shard_map/reduce_sum | solution.py:107
  (85 shorter events, 35.0 us)
Async XLA Ops:
  2.7 23.0 %collective-permute-start = (f32[23,1,2048]{2,0,1:T(8,128)S(1)}, f32[23,1,2048]{2,0,1:T(8,128)S(1)}, u32[]{:S(2)}, u32[]{:S(2)}) collective-permute-start(f32[23,1,2048]{2,0,1:T(8,128)S(1)} %copy.91), channel_id=1, source_target_pairs={{0,1},{1,2},{2,3},{3,4},{4,5},{5,6},{6,7},{7,8},{8,9},{9,10},{10,1... | collective-permute-start | bytes 565256 | tf_op jit(solution)/shard_map/ppermute | solution.py:14
  7.7 18.2 %collective-permute-start.1 = (f32[23,1,2048]{2,0,1:T(8,128)S(1)}, f32[23,1,2048]{2,0,1:T(8,128)S(1)}, u32[]{:S(2)}, u32[]{:S(2)}) collective-permute-start(f32[23,1,2048]{2,0,1:T(8,128)S(1)} %copy.94), channel_id=1, source_target_pairs={{1,0},{2,1},{3,2},{4,3},{5,4},{6,5},{7,6},{8,7},{9,8},{10,9},{11,1... | collective-permute-start | bytes 565256 | tf_op jit(solution)/shard_map/ppermute | solution.py:15
  23.5 13.9 %copy-start.1 = (f32[8,8,2048]{2,1,0:T(8,128)S(1)}, f32[8,8,2048]{2,1,0:T(8,128)}, u32[]{:S(2)}) copy-start(f32[8,8,2048]{2,1,0:T(8,128)} %param.10) | copy-start | bytes 1572868
  25.9 9.3 %copy-start.2 = (f32[23,1,2048]{2,1,0:T(1,128)}, f32[23,1,2048]{2,1,0:T(1,128)S(1)}, u32[]{:S(2)}) copy-start(f32[23,1,2048]{2,1,0:T(1,128)S(1)} %copy.92) | copy-start | bytes 565252
  26.1 9.1 %copy-start.3 = (f32[23,1,2048]{2,1,0:T(1,128)}, f32[23,1,2048]{2,1,0:T(1,128)S(1)}, u32[]{:S(2)}) copy-start(f32[23,1,2048]{2,1,0:T(1,128)S(1)} %copy.96) | copy-start | bytes 565252
  29.6 34.2 %collective-permute-start.2 = (f32[15,10,2048]{2,0,1:T(8,128)}, f32[15,10,2048]{2,0,1:T(8,128)S(1)}, u32[]{:S(2)}, u32[]{:S(2)}) collective-permute-start(f32[15,10,2048]{2,0,1:T(8,128)} %copy.97), channel_id=1, source_target_pairs={{0,32},{16,48},{32,64},{48,80},{64,96},{80,112},{96,0},{112,16},{1... | collective-permute-start | bytes 3686408 | tf_op jit(solution)/shard_map/ppermute | solution.py:51
  30.8 29.5 %collective-permute-start.3 = (f32[15,10,2048]{2,0,1:T(8,128)}, f32[15,10,2048]{2,0,1:T(8,128)}, u32[]{:S(2)}, u32[]{:S(2)}) collective-permute-start(f32[15,10,2048]{2,0,1:T(8,128)} %copy.97), channel_id=1, source_target_pairs={{0,96},{16,112},{32,0},{48,16},{64,32},{80,48},{96,64},{112,80},{1... | collective-permute-start | bytes 3686408 | tf_op jit(solution)/shard_map/ppermute | solution.py:51
  32.2 31.6 %collective-permute-start.6 = (f32[15,10,2048]{2,0,1:T(8,128)}, f32[15,10,2048]{2,0,1:T(8,128)}, u32[]{:S(2)}, u32[]{:S(2)}) collective-permute-start(f32[15,10,2048]{2,0,1:T(8,128)} %copy.97), channel_id=1, source_target_pairs={{0,16},{16,0},{32,48},{48,32},{64,80},{80,64},{96,112},{112,96},{1... | collective-permute-start | bytes 3686408 | tf_op jit(solution)/shard_map/ppermute | solution.py:58
  61.5 16.8 %collective-permute-start.5 = (f32[15,10,1024]{2,0,1:T(8,128)S(1)}, f32[15,10,1024]{2,0,1:T(8,128)S(1)}, u32[]{:S(2)}, u32[]{:S(2)}) collective-permute-start(f32[15,10,1024]{2,0,1:T(8,128)S(1)} %slice.126), channel_id=1, source_target_pairs={{0,96},{16,112},{32,0},{48,16},{64,32},{80,48},{96,64},{112,80},{1... | collective-permute-start | bytes 1843208 | tf_op jit(solution)/shard_map/ppermute | solution.py:51
  63.8 18.0 %collective-permute-start.4 = (f32[15,10,1024]{2,0,1:T(8,128)S(1)}, f32[15,10,1024]{2,0,1:T(8,128)S(1)}, u32[]{:S(2)}, u32[]{:S(2)}) collective-permute-start(f32[15,10,1024]{2,0,1:T(8,128)S(1)} %slice.125), channel_id=1, source_target_pairs={{0,32},{16,48},{32,64},{48,80},{64,96},{80,112},{96,0},{112,16},{1... | collective-permute-start | bytes 1843208 | tf_op jit(solution)/shard_map/ppermute | solution.py:51
  63.9 44.8 %collective-permute-start.7 = (f32[15,10,2048]{2,0,1:T(8,128)}, f32[15,10,2048]{2,0,1:T(8,128)S(1)}, u32[]{:S(2)}, u32[]{:S(2)}) collective-permute-start(f32[15,10,2048]{2,0,1:T(8,128)} %collective-permute-done.6), channel_id=1, source_target_pairs={{0,32},{16,48},{32,64},{48,80},{64,96},{80,112},{96,0},{112,16},{1... | collective-permute-start | bytes 3686408 | tf_op jit(solution)/shard_map/ppermute | solution.py:51
  64.3 44.5 %collective-permute-start.8 = (f32[15,10,2048]{2,0,1:T(8,128)}, f32[15,10,2048]{2,0,1:T(8,128)S(1)}, u32[]{:S(2)}, u32[]{:S(2)}) collective-permute-start(f32[15,10,2048]{2,0,1:T(8,128)} %collective-permute-done.6), channel_id=1, source_target_pairs={{0,96},{16,112},{32,0},{48,16},{64,32},{80,48},{96,64},{112,80},{1... | collective-permute-start | bytes 3686408 | tf_op jit(solution)/shard_map/ppermute | solution.py:51
  108.8 17.8 %collective-permute-start.9 = (f32[15,10,1024]{2,0,1:T(8,128)S(1)}, f32[15,10,1024]{2,0,1:T(8,128)S(1)}, u32[]{:S(2)}, u32[]{:S(2)}) collective-permute-start(f32[15,10,1024]{2,0,1:T(8,128)S(1)} %slice.127), channel_id=1, source_target_pairs={{0,32},{16,48},{32,64},{48,80},{64,96},{80,112},{96,0},{112,16},{1... | collective-permute-start | bytes 1843208 | tf_op jit(solution)/shard_map/ppermute | solution.py:51
  108.9 18.0 %collective-permute-start.10 = (f32[15,10,1024]{2,0,1:T(8,128)S(1)}, f32[15,10,1024]{2,0,1:T(8,128)S(1)}, u32[]{:S(2)}, u32[]{:S(2)}) collective-permute-start(f32[15,10,1024]{2,0,1:T(8,128)S(1)} %slice.128), channel_id=1, source_target_pairs={{0,96},{16,112},{32,0},{48,16},{64,32},{80,48},{96,64},{112,80},{1... | collective-permute-start | bytes 1843208 | tf_op jit(solution)/shard_map/ppermute | solution.py:51
  158.8 15.7 %copy-start = (f32[120,10,2048]{2,1,0:T(8,128)S(1)}, f32[120,10,2048]{2,1,0:T(8,128)}, u32[]{:S(2)}) copy-start(f32[120,10,2048]{2,1,0:T(8,128)} %gather_fusion.5) | copy-start | bytes 29491204

commit v3 on v2

--- a/solution.py
+++ b/solution.py
@@ -1,6 +1,8 @@
 import jax
 import jax.numpy as jnp
 from jax import lax
+from jax.experimental import pallas as pl
+from jax.experimental.pallas import tpu as pltpu
 from jax.sharding import PartitionSpec as P
 
 
@@ -90,21 +92,73 @@
     first = place[first]
     last = place[last]
 
+    weights = jnp.stack([w_first, w_last], axis=-1).transpose(1, 0, 2).reshape(own_modes, 2 * kl_terms)
+    partners = jnp.stack([first, last], axis=-1).transpose(1, 0, 2).reshape(own_modes, 2 * kl_terms)
+    return stencil_apply(every, edge_coefficients(coef), partners, weights)
+
+
+def edge_coefficients(coef):
     a_c = coef[:, 1:-1]
-    c_up = (a_c + coef[:, :-2])[:, None]
-    c_dn = (a_c + coef[:, 2:])[:, None]
-    c_lf = (a_c + shift_cols(a_c, 1))[:, None]
-    c_rt = (a_c + shift_cols(a_c, -1))[:, None]
+    c_up = 0.5 * (a_c + coef[:, :-2])
+    c_dn = 0.5 * (a_c + coef[:, 2:])
+    c_lf = 0.5 * (a_c + shift_cols(a_c, 1))
+    c_rt = 0.5 * (a_c + shift_cols(a_c, -1))
+    total = (c_up + c_dn) + (c_lf + c_rt)
+    column = lax.broadcasted_iota(jnp.int32, a_c.shape, 2)
+    n_lf = jnp.where(column == 0, 0.0, c_lf)
+    n_rt = jnp.where(column == a_c.shape[2] - 1, 0.0, c_rt)
+    return jnp.stack([total, c_up, c_dn, n_lf, n_rt], axis=0)
 
-    g_first = jnp.take(every, first.reshape(-1), axis=0).reshape((kl_terms, own_modes) + every.shape[1:])
-    g_last = jnp.take(every, last.reshape(-1), axis=0).reshape((kl_terms, own_modes) + every.shape[1:])
-    mixed = w_first[:, :, None, None] * g_first + w_last[:, :, None, None] * g_last
-    center = mixed[:, :, 1:-1]
-    result = c_up * (center - mixed[:, :, :-2])
-    result = result + c_dn * (center - mixed[:, :, 2:])
-    result = result + c_lf * (center - shift_cols(center, 1))
-    result = result + c_rt * (center - shift_cols(center, -1))
-    return 0.5 * jnp.sum(result, axis=0)
+
+def stencil_kernel(partners, weights, every, edges, out):
+    slot = pl.program_id(0)
+    kl_terms = edges.shape[1]
+    rows = out.shape[1]
+    cols = out.shape[2]
+    acc = jnp.zeros((rows, cols), jnp.float32)
+    for k in range(kl_terms):
+        j0 = partners[slot, 2 * k]
+        j1 = partners[slot, 2 * k + 1]
+        w0 = weights[slot, 2 * k]
+        w1 = weights[slot, 2 * k + 1]
+
+        def window(offset):
+            return w0 * every[j0, pl.ds(offset, rows), :] + w1 * every[j1, pl.ds(offset, rows), :]
+
+        center = window(1)
+        up = window(0)
+        dn = window(2)
+        lf = pltpu.roll(center, 1, 1)
+        rt = pltpu.roll(center, cols - 1, 1)
+        term = edges[0, k] * center - edges[1, k] * up
+        term = term - edges[2, k] * dn
+        term = term - edges[3, k] * lf
+        term = term - edges[4, k] * rt
+        acc = acc + term
+    out[0] = acc
+
+
+def stencil_apply(every, edges, partners, weights):
+    own_modes = partners.shape[0]
+    rows = edges.shape[2]
+    cols = edges.shape[3]
+    return pl.pallas_call(
+        stencil_kernel,
+        out_shape=jax.ShapeDtypeStruct((own_modes, rows, cols), jnp.float32),
+        grid_spec=pltpu.PrefetchScalarGridSpec(
+            num_scalar_prefetch=1,
+            grid=(own_modes,),
+            in_specs=[
+                pl.BlockSpec(memory_space=pltpu.SMEM),
+                pl.BlockSpec(memory_space=pltpu.VMEM),
+                pl.BlockSpec(memory_space=pltpu.VMEM),
+            ],
+            out_specs=pl.BlockSpec((1, rows, cols), lambda i, p: (i, 0, 0)),
+        ),
+        compiler_params=pltpu.CompilerParams(
+            dimension_semantics=("arbitrary",), vmem_limit_bytes=48 * 1024 * 1024
+        ),
+    )(partners, weights, every, edges)
 
 
 def solution(mesh):

time: 216 us -> 140 us (0.65)
  other arithmetic: 63.5 us -> 12.8 us
  local copies, waits for them, and re-layouts: 68.9 us -> 24.4 us
  Pallas kernels: 0 us -> 15.9 us
    gather x2 -> x0, local copies, waits for them, and re-layouts: 30 us -> none  [the longest x1 15 us: local(): jnp.take(every, last.reshape(-1), axis=0)]
    add x2 -> x0, other arithmetic: 20.2 us -> none  [the longest x1 19 us: local(): w_first[:, :, None, None] * g_first + w_last[:, :, None, None] * g_last]
    select_n x5 -> x1, other arithmetic: 18.9 us -> 0.01 us  [neighbour_table(): w_first = jnp.take_along_axis(local_rows, first[..., None], axis=-1)[..., 0]]
    pallas_call x0 -> x1, Pallas kernels: none -> 15.9 us  [stencil_apply(): pl.pallas_call(stencil_kernel, out_shape=jax.ShapeDtypeStruct((own_modes,...]
    reduce_sum x1 -> x0, other arithmetic: 8.7 us -> none  [local(): return 0.5 * jnp.sum(result, axis=0)]
    slice x3 -> x1, local copies, waits for them, and re-layouts: 5.74 us -> 0.2 us  [shift_cols(): return jnp.concatenate([x[..., 1:], zero], axis=-1)]
    unnamed x14 -> x16, local copies, waits for them, and re-layouts: 17.1 us -> 11.7 us
  transfers between devices with their start and end apart: 11 -> 11, of which waited for: 5 -> 8; matrix products, arithmetic and copies ran while one was open for 18% -> 21% of each run, Pallas kernels for 0% -> 0%
where the time goes in v3:
time: 140 us; the launch traced here: 139 us
  waiting for transfers between devices  63.8 us (46%)
  local copies, waits for them, and re-layouts  24.4 us (17%)
  starting transfers between devices  21.3 us (15%)
  Pallas kernels  15.9 us (11%)
  other arithmetic  12.8 us (9%)
    ppermute x8, waiting for transfers between devices, shifted(): lax.ppermute(x, 'chaos', [(c, (c + step) % count) for c in range(count)])  63.6 us
    pallas_call x1, Pallas kernels, stencil_apply(): pl.pallas_call(stencil_kernel, out_shape=jax.ShapeDtypeStruct((own_modes,...  15.9 us
    unnamed x16, local copies, waits for them, and re-layouts  11.7 us
    ppermute x8, starting transfers between devices, shifted(): lax.ppermute(x, 'chaos', [(c, (c + step) % count) for c in range(count)])  11.6 us
    ppermute x1, starting transfers between devices, extended_2(): before = lax.ppermute(last, axis, up)  4.91 us
    scatter-add x1, other arithmetic, coupling_table(): jnp.zeros((kl_terms * mode_count * mode_count,), jnp.float32).at[flat_index]  4.71 us
    ppermute x1, starting transfers between devices, ring_gather(): partner = lax.ppermute(block, 'chaos', [(c, c ^ 1) for c in range(count)])  2.91 us
  transfers between devices with their start and end apart: 11, of which 8 were waited for; matrix products, arithmetic and copies ran while one was open for 21% of the time, Pallas kernels for 0%

profile of v3, /device:TPU:1, one launch (start us, length us, event | category | flops | bytes accessed | tf_op | source)
XLA Modules:
  0.0 138.7 jit_solution(6800542336561567842)
XLA Ops:
  0.0 1.3 constant_dynamic-update-slice_fusion.1
  3.4 4.9 %collective-permute-start = (f32[23,1,2048]{2,1,0:T(1,128)}, f32[23,1,2048]{2,1,0:T(1,128)S(1)}, u32[]{:S(2)}, u32[]{:S(2)}) collective-permute-start(f32[23,1,2048]{2,1,0:T(1,128)} %get-tuple-element.19), channel_id=1, source_target_pairs={{0,1},{1,2},{2,3},{3,4},{4,5},{5,6},{6,7},{7,8},{8,9},{9,10},{10,1... | collective-permute-start | bytes 565256 | tf_op jit(solution)/shard_map/ppermute | solution.py:16
  8.3 1.9 %collective-permute-start.1 = (f32[23,1,2048]{2,1,0:T(1,128)}, f32[23,1,2048]{2,1,0:T(1,128)S(1)}, u32[]{:S(2)}, u32[]{:S(2)}) collective-permute-start(f32[23,1,2048]{2,1,0:T(1,128)} %get-tuple-element.20), channel_id=1, source_target_pairs={{1,0},{2,1},{3,2},{4,3},{5,4},{6,5},{7,6},{8,7},{9,8},{10,9},{11,1... | collective-permute-start | bytes 565256 | tf_op jit(solution)/shard_map/ppermute | solution.py:17
  10.5 4.7 %scatter_custom_fusion = f32[115200]{0:T(1024)S(1)} fusion(s32[624]{0:T(1024)S(1)} %fusion.19, f32[624]{0:T(1024)S(1)} %fusion.21, f32[]{:T(128)} %constant.105.clone.1), kind=kCustom, calls=%fused_computation.28 | custom fusion | flops 624 | bytes 460804 | tf_op jit(solution)/shard_map/scatter-add | solution.py:35
  18.2 2.1 %gather_fusion.3 = f32[120]{0:T(128)S(1)} fusion(f32[8,15,120]{2,1,0:T(8,128)S(1)} %get-tuple-element.16, s32[120]{0:T(128)S(1)} %reshape.104), kind=kCustom, calls=%fused_computation.1.clone | custom fusion | bytes 2400 | tf_op jit(solution)/shard_map/jit(take_along_axis)/gather | solution.py:46
  20.5 2.1 %gather_fusion.2 = f32[120]{0:T(128)S(1)} fusion(f32[8,15,120]{2,1,0:T(8,128)S(1)} %get-tuple-element.16, s32[120]{0:T(128)S(1)} %reshape.98), kind=kCustom, calls=%fused_computation.clone | custom fusion | bytes 2400 | tf_op jit(solution)/shard_map/jit(take_along_axis)/gather | solution.py:45
  26.4 1.7 %pad_maximum_fusion = (f32[15,10,2048]{2,1,0:T(8,128)S(1)}, f32[120,10,2048]{2,1,0:T(8,128)}) fusion(f32[23,1,2048]{2,1,0:T(1,128)S(1)} %collective-permute-done.1, f32[23,8,2048]{2,1,0:T(8,128)S(1)} %constant_dynamic-update-slice_fusion, f32[23,1,2048]{2,1,0:T(1,128)S(1)} %collective-permute-done), kind=kLoop, calls=%fused_computation.5 | loop fusion | flops 614399 | bytes 5079040 | tf_op jit(solution)/shard_map/concatenate | solution.py:18
  30.1 1.5 %collective-permute-start.3 = (f32[15,10,2048]{2,0,1:T(8,128)S(1)}, f32[15,10,2048]{2,0,1:T(8,128)S(1)}, u32[]{:S(2)}, u32[]{:S(2)}) collective-permute-start(f32[15,10,2048]{2,0,1:T(8,128)S(1)} %copy.33), channel_id=1, source_target_pairs={{0,96},{16,112},{32,0},{48,16},{64,32},{80,48},{96,64},{112,80},{1... | collective-permute-start | bytes 3686408 | tf_op jit(solution)/shard_map/ppermute | solution.py:53
  31.6 2.9 %collective-permute-start.6 = (f32[15,10,2048]{2,0,1:T(8,128)S(1)}, f32[15,10,2048]{2,0,1:T(8,128)S(1)}, u32[]{:S(2)}, u32[]{:S(2)}) collective-permute-start(f32[15,10,2048]{2,0,1:T(8,128)S(1)} %copy.33), channel_id=1, source_target_pairs={{0,16},{16,0},{32,48},{48,32},{64,80},{80,64},{96,112},{112,96},{1... | collective-permute-start | bytes 3686408 | tf_op jit(solution)/shard_map/ppermute | solution.py:60
  35.3 23.3 %collective-permute-done.2 = f32[15,10,2048]{2,0,1:T(8,128)S(1)} collective-permute-done((f32[15,10,2048]{2,0,1:T(8,128)S(1)}, f32[15,10,2048]{2,0,1:T(8,128)S(1)}, u32[]{:S(2)}, u32[]{:S(2)}) %collective-permute-start.2) | collective-permute-done | bytes 1228832 | tf_op jit(solution)/shard_map/ppermute | solution.py:53
  59.4 2.3 %collective-permute-start.5 = (f32[15,10,1024]{2,0,1:T(8,128)S(1)}, f32[15,10,1024]{2,0,1:T(8,128)S(1)}, u32[]{:S(2)}, u32[]{:S(2)}) collective-permute-start(f32[15,10,1024]{2,0,1:T(8,128)S(1)} %slice.103), channel_id=1, source_target_pairs={{0,96},{16,112},{32,0},{48,16},{64,32},{80,48},{96,64},{112,80},{1... | collective-permute-start | bytes 1843208 | tf_op jit(solution)/shard_map/ppermute | solution.py:53
  62.3 2.3 %collective-permute-start.8 = (f32[15,10,2048]{2,0,1:T(8,128)S(1)}, f32[15,10,2048]{2,0,1:T(8,128)S(1)}, u32[]{:S(2)}, u32[]{:S(2)}) collective-permute-start(f32[15,10,2048]{2,0,1:T(8,128)S(1)} %collective-permute-done.6), channel_id=1, source_target_pairs={{0,96},{16,112},{32,0},{48,16},{64,32},{80,48},{96,64},{112,80},{1... | collective-permute-start | bytes 3686408 | tf_op jit(solution)/shard_map/ppermute | solution.py:53
  64.6 2.0 %copy_dynamic-update-slice_fusion.4 = f32[120,10,2048]{2,1,0:T(8,128)} fusion(f32[120,10,2048]{2,1,0:T(8,128)} %get-tuple-element.18, f32[15,10,2048]{2,0,1:T(8,128)S(1)} %collective-permute-done.2), kind=kLoop, calls=%fused_computation.13 | loop fusion | bytes 3194880
  66.6 2.0 %copy_dynamic-update-slice_fusion.3 = f32[120,10,2048]{2,1,0:T(8,128)} fusion(f32[120,10,2048]{2,1,0:T(8,128)} %copy_dynamic-update-slice_fusion.4, f32[15,10,2048]{2,0,1:T(8,128)S(1)} %collective-permute-done.3), kind=kLoop, calls=%fused_computation.12 | loop fusion | bytes 3194880
  68.7 8.0 %collective-permute-done.4 = f32[15,10,1024]{2,0,1:T(8,128)S(1)} collective-permute-done((f32[15,10,1024]{2,0,1:T(8,128)S(1)}, f32[15,10,1024]{2,0,1:T(8,128)S(1)}, u32[]{:S(2)}, u32[]{:S(2)}) %collective-permute-start.4) | collective-permute-done | bytes 614432 | tf_op jit(solution)/shard_map/ppermute | solution.py:53
  77.4 1.4 %maximum_dynamic-update-slice_fusion.1 = f32[120,10,2048]{2,1,0:T(8,128)} fusion(f32[120,10,2048]{2,1,0:T(8,128)} %copy_dynamic-update-slice_fusion.3, f32[15,10,1024]{2,1,0:T(8,128)S(1)} %copy.36, f32[15,10,1024]{2,1,0:T(8,128)S(1)} %copy.35), kind=kLoop, calls=%fused_computation.8 | loop fusion | flops 307200 | bytes 3194880
  78.9 2.1 %copy_dynamic-update-slice_fusion.2 = f32[120,10,2048]{2,1,0:T(8,128)} fusion(f32[120,10,2048]{2,1,0:T(8,128)} %maximum_dynamic-update-slice_fusion.1, f32[15,10,2048]{2,0,1:T(8,128)S(1)} %collective-permute-done.6), kind=kLoop, calls=%fused_computation.11 | loop fusion | bytes 3194880
  81.0 22.0 %collective-permute-done.7 = f32[15,10,2048]{2,0,1:T(8,128)S(1)} collective-permute-done((f32[15,10,2048]{2,0,1:T(8,128)S(1)}, f32[15,10,2048]{2,0,1:T(8,128)S(1)}, u32[]{:S(2)}, u32[]{:S(2)}) %collective-permute-start.7) | collective-permute-done | bytes 1228832 | tf_op jit(solution)/shard_map/ppermute | solution.py:53
  103.3 3.2 %collective-permute-start.10 = (f32[15,10,1024]{2,0,1:T(8,128)S(1)}, f32[15,10,1024]{2,0,1:T(8,128)S(1)}, u32[]{:S(2)}, u32[]{:S(2)}) collective-permute-start(f32[15,10,1024]{2,0,1:T(8,128)S(1)} %slice.105), channel_id=1, source_target_pairs={{0,96},{16,112},{32,0},{48,16},{64,32},{80,48},{96,64},{112,80},{1... | collective-permute-start | bytes 1843208 | tf_op jit(solution)/shard_map/ppermute | solution.py:53
  106.5 2.0 %copy_dynamic-update-slice_fusion.1 = f32[120,10,2048]{2,1,0:T(8,128)} fusion(f32[120,10,2048]{2,1,0:T(8,128)} %copy_dynamic-update-slice_fusion.2, f32[15,10,2048]{2,0,1:T(8,128)S(1)} %collective-permute-done.7), kind=kLoop, calls=%fused_computation.10 | loop fusion | bytes 3194880
  108.5 2.1 %copy_dynamic-update-slice_fusion = f32[120,10,2048]{2,1,0:T(8,128)} fusion(f32[120,10,2048]{2,1,0:T(8,128)} %copy_dynamic-update-slice_fusion.1, f32[15,10,2048]{2,0,1:T(8,128)S(1)} %collective-permute-done.8), kind=kLoop, calls=%fused_computation.9 | loop fusion | bytes 3194880
  110.6 9.8 %collective-permute-done.9 = f32[15,10,1024]{2,0,1:T(8,128)S(1)} collective-permute-done((f32[15,10,1024]{2,0,1:T(8,128)S(1)}, f32[15,10,1024]{2,0,1:T(8,128)S(1)}, u32[]{:S(2)}, u32[]{:S(2)}) %collective-permute-start.9) | collective-permute-done | bytes 614432 | tf_op jit(solution)/shard_map/ppermute | solution.py:53
  121.4 1.4 %maximum_dynamic-update-slice_fusion.every = f32[120,10,2048]{2,1,0:T(8,128)} fusion(f32[120,10,2048]{2,1,0:T(8,128)} %copy_dynamic-update-slice_fusion, f32[15,10,1024]{2,1,0:T(8,128)S(1)} %copy.39, f32[15,10,1024]{2,1,0:T(8,128)S(1)} %copy.38), kind=kLoop, calls=%fused_computation.7 | loop fusion | flops 307200 | bytes 3194880 | tf_op jit(solution)/shard_map/concatenate | solution.py:71
  122.8 15.9 %shard_map.55 = f32[15,8,2048]{2,1,0:T(8,128)} custom-call(s32[15,16]{1,0:T(8,128)S(1)} %copy.45.partners, f32[15,16]{1,0:T(8,128)S(1)} %copy.46.weights, f32[120,10,2048]{2,1,0:T(8,128)} %maximum_dynamic-update-slice_fusion.every, f32[5,8,8,2048]{3,2,1,0:T(8,128)S(1)} %bitcast_dynamic-update-slice_fusion.edges), custom_call_target="tpu_custom_call" | custom-call | tf_op jit(solution)/shard_map/pallas_call | solution.py:145
  (79 shorter events, 15.3 us)
Async XLA Ops:
  0.0 17.9 %copy-start = (f32[8,8,2048]{2,1,0:T(8,128)S(1)}, f32[8,8,2048]{2,1,0:T(8,128)}, u32[]{:S(2)}) copy-start(f32[8,8,2048]{2,1,0:T(8,128)} %param.8) | copy-start | bytes 1572868
  0.0 10.3 %slice-start = ((s32[624,3]{0,1:T(4,128)}), s32[624,2]{0,1:T(2,128)S(1)}, s32[]{:S(2)}) async-start(s32[624,3]{0,1:T(4,128)} %param.9), calls=%async_computation | async-start | bytes 10240 | tf_op jit(solution)/shard_map/slice | solution.py:30
  0.0 10.4 %copy-start.1 = (s32[624,3]{0,1:T(4,128)S(1)}, s32[624,3]{0,1:T(4,128)}, u32[]{:S(2)}) copy-start(s32[624,3]{0,1:T(4,128)} %param.9) | copy-start | bytes 22468
  0.0 10.3 %copy-start.3 = (s32[120]{0:T(128)S(1)}, s32[120]{0:T(128)}, u32[]{:S(2)}) copy-start(s32[120]{0:T(128)} %param.11) | copy-start | bytes 1444
  0.0 10.5 %copy-start.2 = (s32[624,2]{0,1:T(2,128)S(1)}, s32[624,2]{0,1:T(2,128)}, u32[]{:S(2)}) copy-start(s32[624,2]{0,1:T(2,128)} %param.10) | copy-start | bytes 14980
  3.4 23.0 %collective-permute-start = (f32[23,1,2048]{2,1,0:T(1,128)}, f32[23,1,2048]{2,1,0:T(1,128)S(1)}, u32[]{:S(2)}, u32[]{:S(2)}) collective-permute-start(f32[23,1,2048]{2,1,0:T(1,128)} %get-tuple-element.19), channel_id=1, source_target_pairs={{0,1},{1,2},{2,3},{3,4},{4,5},{5,6},{6,7},{7,8},{8,9},{9,10},{10,1... | collective-permute-start | bytes 565256 | tf_op jit(solution)/shard_map/ppermute | solution.py:16
  8.3 18.1 %collective-permute-start.1 = (f32[23,1,2048]{2,1,0:T(1,128)}, f32[23,1,2048]{2,1,0:T(1,128)S(1)}, u32[]{:S(2)}, u32[]{:S(2)}) collective-permute-start(f32[23,1,2048]{2,1,0:T(1,128)} %get-tuple-element.20), channel_id=1, source_target_pairs={{1,0},{2,1},{3,2},{4,3},{5,4},{6,5},{7,6},{8,7},{9,8},{10,9},{11,1... | collective-permute-start | bytes 565256 | tf_op jit(solution)/shard_map/ppermute | solution.py:17
  28.8 29.8 %collective-permute-start.2 = (f32[15,10,2048]{2,0,1:T(8,128)S(1)}, f32[15,10,2048]{2,0,1:T(8,128)S(1)}, u32[]{:S(2)}, u32[]{:S(2)}) collective-permute-start(f32[15,10,2048]{2,0,1:T(8,128)S(1)} %copy.33), channel_id=1, source_target_pairs={{0,32},{16,48},{32,64},{48,80},{64,96},{80,112},{96,0},{112,16},{1... | collective-permute-start | bytes 3686408 | tf_op jit(solution)/shard_map/ppermute | solution.py:53
  30.1 29.2 %collective-permute-start.3 = (f32[15,10,2048]{2,0,1:T(8,128)S(1)}, f32[15,10,2048]{2,0,1:T(8,128)S(1)}, u32[]{:S(2)}, u32[]{:S(2)}) collective-permute-start(f32[15,10,2048]{2,0,1:T(8,128)S(1)} %copy.33), channel_id=1, source_target_pairs={{0,96},{16,112},{32,0},{48,16},{64,32},{80,48},{96,64},{112,80},{1... | collective-permute-start | bytes 3686408 | tf_op jit(solution)/shard_map/ppermute | solution.py:53
  31.6 30.4 %collective-permute-start.6 = (f32[15,10,2048]{2,0,1:T(8,128)S(1)}, f32[15,10,2048]{2,0,1:T(8,128)S(1)}, u32[]{:S(2)}, u32[]{:S(2)}) collective-permute-start(f32[15,10,2048]{2,0,1:T(8,128)S(1)} %copy.33), channel_id=1, source_target_pairs={{0,16},{16,0},{32,48},{48,32},{64,80},{80,64},{96,112},{112,96},{1... | collective-permute-start | bytes 3686408 | tf_op jit(solution)/shard_map/ppermute | solution.py:60
  58.6 18.0 %collective-permute-start.4 = (f32[15,10,1024]{2,0,1:T(8,128)S(1)}, f32[15,10,1024]{2,0,1:T(8,128)S(1)}, u32[]{:S(2)}, u32[]{:S(2)}) collective-permute-start(f32[15,10,1024]{2,0,1:T(8,128)S(1)} %slice.102), channel_id=1, source_target_pairs={{0,32},{16,48},{32,64},{48,80},{64,96},{80,112},{96,0},{112,16},{1... | collective-permute-start | bytes 1843208 | tf_op jit(solution)/shard_map/ppermute | solution.py:53
  59.4 17.7 %collective-permute-start.5 = (f32[15,10,1024]{2,0,1:T(8,128)S(1)}, f32[15,10,1024]{2,0,1:T(8,128)S(1)}, u32[]{:S(2)}, u32[]{:S(2)}) collective-permute-start(f32[15,10,1024]{2,0,1:T(8,128)S(1)} %slice.103), channel_id=1, source_target_pairs={{0,96},{16,112},{32,0},{48,16},{64,32},{80,48},{96,64},{112,80},{1... | collective-permute-start | bytes 1843208 | tf_op jit(solution)/shard_map/ppermute | solution.py:53
  62.0 41.0 %collective-permute-start.7 = (f32[15,10,2048]{2,0,1:T(8,128)S(1)}, f32[15,10,2048]{2,0,1:T(8,128)S(1)}, u32[]{:S(2)}, u32[]{:S(2)}) collective-permute-start(f32[15,10,2048]{2,0,1:T(8,128)S(1)} %collective-permute-done.6), channel_id=1, source_target_pairs={{0,32},{16,48},{32,64},{48,80},{64,96},{80,112},{96,0},{112,16},{1... | collective-permute-start | bytes 3686408 | tf_op jit(solution)/shard_map/ppermute | solution.py:53
  62.3 41.0 %collective-permute-start.8 = (f32[15,10,2048]{2,0,1:T(8,128)S(1)}, f32[15,10,2048]{2,0,1:T(8,128)S(1)}, u32[]{:S(2)}, u32[]{:S(2)}) collective-permute-start(f32[15,10,2048]{2,0,1:T(8,128)S(1)} %collective-permute-done.6), channel_id=1, source_target_pairs={{0,96},{16,112},{32,0},{48,16},{64,32},{80,48},{96,64},{112,80},{1... | collective-permute-start | bytes 3686408 | tf_op jit(solution)/shard_map/ppermute | solution.py:53
  103.0 17.4 %collective-permute-start.9 = (f32[15,10,1024]{2,0,1:T(8,128)S(1)}, f32[15,10,1024]{2,0,1:T(8,128)S(1)}, u32[]{:S(2)}, u32[]{:S(2)}) collective-permute-start(f32[15,10,1024]{2,0,1:T(8,128)S(1)} %slice.104), channel_id=1, source_target_pairs={{0,32},{16,48},{32,64},{48,80},{64,96},{80,112},{96,0},{112,16},{1... | collective-permute-start | bytes 1843208 | tf_op jit(solution)/shard_map/ppermute | solution.py:53
  103.3 17.7 %collective-permute-start.10 = (f32[15,10,1024]{2,0,1:T(8,128)S(1)}, f32[15,10,1024]{2,0,1:T(8,128)S(1)}, u32[]{:S(2)}, u32[]{:S(2)}) collective-permute-start(f32[15,10,1024]{2,0,1:T(8,128)S(1)} %slice.105), channel_id=1, source_target_pairs={{0,96},{16,112},{32,0},{48,16},{64,32},{80,48},{96,64},{112,80},{1... | collective-permute-start | bytes 1843208 | tf_op jit(solution)/shard_map/ppermute | solution.py:53

commit v4 on v3

--- a/solution.py
+++ b/solution.py
@@ -71,30 +71,47 @@
     return jnp.concatenate(pieces, axis=0), jnp.stack(owners).astype(jnp.int32)
 
 
+def space_halo(edge_last, edge_first):
+    count = lax.axis_size("space")
+    up = [(i, i + 1) for i in range(count - 1)]
+    down = [(i + 1, i) for i in range(count - 1)]
+    return lax.ppermute(edge_last, "space", up), lax.ppermute(edge_first, "space", down)
+
+
 def local(modes, kl_fields, triples, ratios, mode_of_slot):
     groups = lax.axis_size("chaos")
     own_modes = modes.shape[0]
     mode_count = own_modes * groups
     kl_terms = kl_fields.shape[0]
+    rows = modes.shape[1]
+    every, order = ring_gather(modes)
+
     first_slot = lax.axis_index("chaos") * own_modes
     coupling = coupling_table(triples, ratios, mode_of_slot, kl_terms, mode_count)
     local_rows = lax.dynamic_slice_in_dim(coupling, first_slot, own_modes, 1)
     first, last, w_first, w_last = neighbour_table(local_rows)
-
-    joined = jnp.concatenate([modes, kl_fields], axis=0)
-    padded = extended_2(joined, (("space", 1),), 1)
-    source = padded[:own_modes]
-    coef = padded[own_modes:]
-    every, order = ring_gather(source)
     owner = jnp.arange(mode_count, dtype=jnp.int32) // own_modes
     position = jnp.argmax(order[None, :] == owner[:, None], axis=1).astype(jnp.int32)
     place = position * own_modes + jnp.arange(mode_count, dtype=jnp.int32) % own_modes
     first = place[first]
     last = place[last]
-
     weights = jnp.stack([w_first, w_last], axis=-1).transpose(1, 0, 2).reshape(own_modes, 2 * kl_terms)
     partners = jnp.stack([first, last], axis=-1).transpose(1, 0, 2).reshape(own_modes, 2 * kl_terms)
-    return stencil_apply(every, edge_coefficients(coef), partners, weights)
+
+    above, below = space_halo(kl_fields[:, rows - 1:], kl_fields[:, :1])
+    coef = jnp.concatenate([above, kl_fields, below], axis=1)
+    edges, c_top, c_bottom = edge_coefficients(coef)
+    applied = stencil_apply(every, edges, partners, weights)
+
+    halo_above, halo_below = space_halo(every[:, rows - 1], every[:, 0])
+    pick_w = weights.reshape(own_modes, kl_terms, 2, 1)
+    mixed_above = jnp.sum(jnp.take(halo_above, partners, axis=0).reshape(own_modes, kl_terms, 2, -1) * pick_w, axis=2)
+    mixed_below = jnp.sum(jnp.take(halo_below, partners, axis=0).reshape(own_modes, kl_terms, 2, -1) * pick_w, axis=2)
+    fix_top = jnp.sum(c_top[None] * mixed_above, axis=1)
+    fix_bottom = jnp.sum(c_bottom[None] * mixed_below, axis=1)
+    applied = applied.at[:, 0].add(-fix_top)
+    applied = applied.at[:, rows - 1].add(-fix_bottom)
+    return applied
 
 
 def edge_coefficients(coef):
@@ -105,9 +122,13 @@
     c_rt = 0.5 * (a_c + shift_cols(a_c, -1))
     total = (c_up + c_dn) + (c_lf + c_rt)
     column = lax.broadcasted_iota(jnp.int32, a_c.shape, 2)
+    row = lax.broadcasted_iota(jnp.int32, a_c.shape, 1)
+    n_up = jnp.where(row == 0, 0.0, c_up)
+    n_dn = jnp.where(row == a_c.shape[1] - 1, 0.0, c_dn)
     n_lf = jnp.where(column == 0, 0.0, c_lf)
     n_rt = jnp.where(column == a_c.shape[2] - 1, 0.0, c_rt)
-    return jnp.stack([total, c_up, c_dn, n_lf, n_rt], axis=0)
+    edges = jnp.stack([total, n_up, n_dn, n_lf, n_rt], axis=0)
+    return edges, c_up[:, 0], c_dn[:, -1]
 
 
 def stencil_kernel(partners, weights, every, edges, out):
@@ -121,13 +142,9 @@
         j1 = partners[slot, 2 * k + 1]
         w0 = weights[slot, 2 * k]
         w1 = weights[slot, 2 * k + 1]
-
-        def window(offset):
-            return w0 * every[j0, pl.ds(offset, rows), :] + w1 * every[j1, pl.ds(offset, rows), :]
-
-        center = window(1)
-        up = window(0)
-        dn = window(2)
+        center = w0 * every[j0] + w1 * every[j1]
+        up = pltpu.roll(center, 1, 0)
+        dn = pltpu.roll(center, rows - 1, 0)
         lf = pltpu.roll(center, 1, 1)
         rt = pltpu.roll(center, cols - 1, 1)
         term = edges[0, k] * center - edges[1, k] * up

time: 140 us -> 159 us (1.14)
  waiting for transfers between devices: 63.8 us -> 33.7 us
  local copies, waits for them, and re-layouts: 24.4 us -> 51.2 us
  other arithmetic: 12.8 us -> 33.8 us
  starting transfers between devices: 21.3 us -> 27.4 us
  Pallas kernels: 15.9 us -> 11.8 us
    ppermute x8, waiting for transfers between devices: 63.6 us -> 33.7 us  [shifted(): lax.ppermute(x, 'chaos', [(c, (c + step) % count) for c in range(count)])]
    slice x2 -> x4, local copies, waits for them, and re-layouts: 1.69 us -> 9.63 us  [the longest x1 7.58 us: local(): halo_above, halo_below = space_halo(every[:, rows - 1], every[:, 0])]
    reduce_sum x0 -> x3, other arithmetic: none -> 7.65 us  [the longest x1 7.05 us: local(): jnp.sum(jnp.take(halo_below, partners, axis=0).reshape(own_modes, kl_term...]
    ppermute x2 -> x4, starting transfers between devices: 6.83 us -> 14.2 us  [the longest x2 10.4 us: space_halo(): lax.ppermute(edge_last, 'space', up)]
    scatter-add x0 -> x2, local copies, waits for them, and re-layouts: none -> 7.03 us  [the longest x1 3.51 us: local(): applied = applied.at[:, 0].add(-fix_top)]
    reshape x0 -> x2, local copies, waits for them, and re-layouts: none -> 5.88 us  [the longest x1 3.43 us: local(): jnp.take(halo_above, partners, axis=0).reshape(own_modes, kl_terms, 2, -1)]
    gather x0 -> x2, local copies, waits for them, and re-layouts: none -> 5.18 us  [the longest x1 2.59 us: local(): jnp.take(halo_above, partners, axis=0).reshape(own_modes, kl_terms, 2, -1)]
    select_n x0 -> x2, other arithmetic: none -> 4.75 us  [local(): jnp.take(halo_above, partners, axis=0).reshape(own_modes, kl_terms, 2, -1)]
  transfers between devices with their start and end apart: 11 -> 13, of which waited for: 8 -> 6; matrix products, arithmetic and copies ran while one was open for 21% -> 29% of each run, Pallas kernels for 0% -> 7%
where the time goes in v4:
time: 159 us; the launch traced here: 158 us
  local copies, waits for them, and re-layouts  51.2 us (32%)
  other arithmetic  33.8 us (21%)
  waiting for transfers between devices  33.7 us (21%)
  starting transfers between devices  27.4 us (17%)
  Pallas kernels  11.8 us (7%)
    ppermute x8, waiting for transfers between devices, shifted(): lax.ppermute(x, 'chaos', [(c, (c + step) % count) for c in range(count)])  33.7 us
    pallas_call x1, Pallas kernels, stencil_apply(): pl.pallas_call(stencil_kernel, out_shape=jax.ShapeDtypeStruct((own_modes,...  11.8 us
    unnamed x30, local copies, waits for them, and re-layouts  11.8 us
    ppermute x2, starting transfers between devices, space_halo(): lax.ppermute(edge_last, 'space', up)  10.4 us
    ppermute x8, starting transfers between devices, shifted(): lax.ppermute(x, 'chaos', [(c, (c + step) % count) for c in range(count)])  10.2 us
    slice x1, local copies, waits for them, and re-layouts, local(): halo_above, halo_below = space_halo(every[:, rows - 1], every[:, 0])  7.58 us
    reduce_sum x1, other arithmetic, local(): jnp.sum(jnp.take(halo_below, partners, axis=0).reshape(own_modes, kl_term...  7.05 us
    select_n x2, other arithmetic, local(): jnp.take(halo_above, partners, axis=0).reshape(own_modes, kl_terms, 2, -1)  4.75 us
  transfers between devices with their start and end apart: 13, of which 6 were waited for; matrix products, arithmetic and copies ran while one was open for 29% of the time, Pallas kernels for 7%

profile of v4, /device:TPU:1, one launch (start us, length us, event | category | flops | bytes accessed | tf_op | source)
XLA Modules:
  0.0 158.4 jit_solution(9541288965986835417)
XLA Ops:
  3.4 3.0 %collective-permute-start.4 = (f32[15,8,2048]{2,1,0:T(8,128)}, f32[15,8,2048]{2,1,0:T(8,128)}, u32[]{:S(2)}, u32[]{:S(2)}) collective-permute-start(f32[15,8,2048]{2,1,0:T(8,128)} %param.13), channel_id=1, source_target_pairs={{0,16},{16,0},{32,48},{48,32},{64,80},{80,64},{96,112},{112,96},{1... | collective-permute-start | bytes 2949128 | tf_op jit(solution)/shard_map/ppermute | solution.py:60
  8.4 4.9 %collective-permute-start.9 = (f32[8,1,2048]{2,1,0:T(1,128)}, f32[8,1,2048]{2,1,0:T(1,128)}, u32[]{:S(2)}, u32[]{:S(2)}) collective-permute-start(f32[8,1,2048]{2,1,0:T(1,128)} %get-tuple-element.46), channel_id=1, source_target_pairs={{0,1},{1,2},{2,3},{3,4},{4,5},{5,6},{6,7},{7,8},{8,9},{9,10},{10,1... | collective-permute-start | bytes 196616 | tf_op jit(solution)/shard_map/ppermute | solution.py:78
  18.9 4.7 %scatter_custom_fusion = f32[115200]{0:T(1024)S(1)} fusion(s32[624]{0:T(1024)S(1)} %fusion.19, f32[624]{0:T(1024)S(1)} %fusion.21, f32[]{:T(128)} %constant.169.clone.1), kind=kCustom, calls=%fused_computation.31 | custom fusion | flops 624 | bytes 460804 | tf_op jit(solution)/shard_map/scatter-add | solution.py:35
  34.6 2.1 %gather_fusion.2 = f32[120]{0:T(128)S(1)} fusion(f32[8,15,120]{2,1,0:T(8,128)S(1)} %get-tuple-element.40, s32[120]{0:T(128)S(1)} %reshape.204), kind=kCustom, calls=%fused_computation.clone | custom fusion | bytes 2400 | tf_op jit(solution)/shard_map/jit(take_along_axis)/gather | solution.py:45
  45.2 2.6 %collective-permute-start.6 = (f32[15,8,2048]{2,1,0:T(8,128)}, f32[15,8,2048]{2,1,0:T(8,128)S(1)}, u32[]{:S(2)}, u32[]{:S(2)}) collective-permute-start(f32[15,8,2048]{2,1,0:T(8,128)} %collective-permute-done.4), channel_id=1, source_target_pairs={{0,96},{16,112},{32,0},{48,16},{64,32},{80,48},{96,64},{112,80},{1... | collective-permute-start | bytes 2949128 | tf_op jit(solution)/shard_map/ppermute | solution.py:53
  48.9 2.3 %constant_dynamic-update-slice_fusion.3 = f32[120,8,2048]{2,1,0:T(8,128)} fusion(f32[120,8,2048]{2,1,0:T(8,128)} %constant_dynamic-update-slice_fusion.4, f32[15,8,2048]{2,1,0:T(8,128)} %collective-permute-done.1), kind=kLoop, calls=%fused_computation.43 | loop fusion | bytes 1966080
  51.1 5.6 %collective-permute-done.3 = f32[15,8,1024]{2,1,0:T(8,128)S(1)} collective-permute-done((f32[15,8,1024]{2,1,0:T(8,128)S(1)}, f32[15,8,1024]{2,1,0:T(8,128)S(1)}, u32[]{:S(2)}, u32[]{:S(2)}) %collective-permute-start.3) | collective-permute-done | bytes 491552 | tf_op jit(solution)/shard_map/ppermute | solution.py:53
  56.8 2.6 %collective-permute-done.2 = f32[15,8,1024]{2,1,0:T(8,128)S(1)} collective-permute-done((f32[15,8,1024]{2,1,0:T(8,128)S(1)}, f32[15,8,1024]{2,1,0:T(8,128)S(1)}, u32[]{:S(2)}, u32[]{:S(2)}) %collective-permute-start.2) | collective-permute-done | bytes 491552 | tf_op jit(solution)/shard_map/ppermute | solution.py:53
  60.4 2.3 %constant_dynamic-update-slice_fusion.2 = f32[120,8,2048]{2,1,0:T(8,128)} fusion(f32[120,8,2048]{2,1,0:T(8,128)} %maximum_dynamic-update-slice_fusion.1, f32[15,8,2048]{2,1,0:T(8,128)} %collective-permute-done.4), kind=kLoop, calls=%fused_computation.42 | loop fusion | bytes 1966080
  62.7 13.5 %collective-permute-done.6 = f32[15,8,2048]{2,1,0:T(8,128)S(1)} collective-permute-done((f32[15,8,2048]{2,1,0:T(8,128)}, f32[15,8,2048]{2,1,0:T(8,128)S(1)}, u32[]{:S(2)}, u32[]{:S(2)}) %collective-permute-start.6) | collective-permute-done | bytes 983072 | tf_op jit(solution)/shard_map/ppermute | solution.py:53
  76.2 2.3 %collective-permute-start.8 = (f32[15,8,1024]{2,1,0:T(8,128)S(1)}, f32[15,8,1024]{2,1,0:T(8,128)S(1)}, u32[]{:S(2)}, u32[]{:S(2)}) collective-permute-start(f32[15,8,1024]{2,1,0:T(8,128)S(1)} %slice.159), channel_id=1, source_target_pairs={{0,96},{16,112},{32,0},{48,16},{64,32},{80,48},{96,64},{112,80},{1... | collective-permute-start | bytes 1474568 | tf_op jit(solution)/shard_map/ppermute | solution.py:53
  81.2 7.8 %collective-permute-done.8 = f32[15,8,1024]{2,1,0:T(8,128)S(1)} collective-permute-done((f32[15,8,1024]{2,1,0:T(8,128)S(1)}, f32[15,8,1024]{2,1,0:T(8,128)S(1)}, u32[]{:S(2)}, u32[]{:S(2)}) %collective-permute-start.8) | collective-permute-done | bytes 491552 | tf_op jit(solution)/shard_map/ppermute | solution.py:53
  88.9 4.0 %collective-permute-done.7 = f32[15,8,1024]{2,1,0:T(8,128)S(1)} collective-permute-done((f32[15,8,1024]{2,1,0:T(8,128)S(1)}, f32[15,8,1024]{2,1,0:T(8,128)S(1)}, u32[]{:S(2)}, u32[]{:S(2)}) %collective-permute-start.7) | collective-permute-done | bytes 491552 | tf_op jit(solution)/shard_map/ppermute | solution.py:53
  93.9 7.6 %fusion.23 = (f32[120,1,2048]{2,1,0:T(1,128)S(1)}, f32[120,1,2048]{2,1,0:T(1,128)S(1)}) fusion(f32[120,8,2048]{2,1,0:T(8,128)} %maximum_dynamic-update-slice_fusion.every), kind=kLoop, calls=%fused_computation.100 | loop fusion | bytes 3932160 | tf_op jit(solution)/shard_map/slice | solution.py:106
  101.9 5.4 %collective-permute-start.11 = (f32[120,2048]{1,0:T(8,128)S(1)}, f32[120,2048]{1,0:T(8,128)S(1)}, u32[]{:S(2)}, u32[]{:S(2)}) collective-permute-start(f32[120,2048]{1,0:T(8,128)S(1)} %bitcast.70), channel_id=1, source_target_pairs={{0,1},{1,2},{2,3},{3,4},{4,5},{5,6},{6,7},{7,8},{8,9},{9,10},{10,1... | collective-permute-start | bytes 2949128 | tf_op jit(solution)/shard_map/ppermute | solution.py:78
  113.3 11.8 %shard_map.55 = f32[15,8,2048]{2,1,0:T(8,128)} custom-call(s32[15,16]{1,0:T(8,128)S(1)} %copy.30.partners, f32[15,16]{1,0:T(8,128)S(1)} %copy.31.weights, f32[120,8,2048]{2,1,0:T(8,128)} %maximum_dynamic-update-slice_fusion.every, f32[5,8,8,2048]{3,2,1,0:T(8,128)S(1)} %bitcast_dynamic-update-slice_fusion.edges), custom_call_target="tpu_custom_call" | custom-call | tf_op jit(solution)/shard_map/pallas_call | solution.py:162
  125.1 2.6 %gather_fusion.4 = f32[240,2048]{1,0:T(8,128)} fusion(f32[120,2048]{1,0:T(8,128)S(1)} %collective-permute-done.11, s32[1024]{0:T(1024)S(1)} %copy-done.5), kind=kCustom, calls=%fused_computation.1.clone | custom fusion | bytes 3933120 | tf_op jit(solution)/shard_map/jit(_take)/gather | solution.py:108
  127.7 2.6 %gather_fusion.5 = f32[240,2048]{1,0:T(8,128)} fusion(f32[120,2048]{1,0:T(8,128)S(1)} %collective-permute-done.12, s32[1024]{0:T(1024)S(1)} %copy-done.5), kind=kCustom, calls=%fused_computation.3.clone | custom fusion | bytes 3933120 | tf_op jit(solution)/shard_map/jit(_take)/gather | solution.py:109
  130.3 4.7 %broadcast_select_fusion.1 = (f32[15,16,2048]{2,1,0:T(8,128)}, f32[15,16,2048]{2,1,0:T(8,128)}) fusion(f32[15,16,2048]{2,1,0:T(8,128)} %bitcast.68, pred[15,16]{1,0:T(8,128)(4,1)S(1)} %copy-done.8, f32[15,16,2048]{2,1,0:T(8,128)} %bitcast.69), kind=kLoop, calls=%fused_computation.14 | loop fusion | flops 983040 | bytes 7864560 | tf_op jit(solution)/shard_map/jit(_take)/select_n | solution.py:108
  135.0 2.5 %reshape.132 = f32[15,8,2,2048]{3,2,1,0:T(2,128)S(1)} reshape(f32[15,16,2048]{2,1,0:T(8,128)} %get-tuple-element.52) | data formatting | bytes 3932160 | tf_op jit(solution)/shard_map/reshape | solution.py:109
  137.5 3.4 %reshape.131 = f32[15,8,2,2048]{3,2,1,0:T(2,128)} reshape(f32[15,16,2048]{2,1,0:T(8,128)} %get-tuple-element.51) | data formatting | bytes 3932160 | tf_op jit(solution)/shard_map/reshape | solution.py:108
  140.9 7.0 %multiply_reduce_fusion = (f32[15,8,2048]{2,1,0:T(8,128)S(1)}, f32[15,8,2048]{2,1,0:T(8,128)S(1)}) fusion(f32[15,8,2,2048]{3,2,1,0:T(2,128)S(1)} %reshape.132, f32[15,8,2]{2,1,0:T(8,128)S(1)} %copy-done.4, f32[15,8,2,2048]{3,2,1,0:T(2,128)} %reshape.131), kind=kLoop, calls=%fused_computation.7 | loop fusion | flops 1474560 | bytes 5899200 | tf_op jit(solution)/shard_map/reduce_sum | solution.py:109
  149.7 3.5 %scatter-add.18 = f32[15,8,2048]{2,1,0:T(8,128)} dynamic-update-slice(f32[15,8,2048]{2,1,0:T(8,128)} %shard_map.55, f32[15,1,2048]{2,1,0:T(1,128)S(1)} %slice_add_fusion.1, s32[]{:T(128)} %constant.160.clone.1, s32[]{:T(128)} %constant.160.clone.1, s32[]{:T(128)} %constant.160.clone.1) | dynamic-update-slice | bytes 245764 | tf_op jit(solution)/shard_map/scatter-add | solution.py:112
  154.9 3.5 %scatter-add.19 = f32[15,8,2048]{2,1,0:T(8,128)} dynamic-update-slice(f32[15,8,2048]{2,1,0:T(8,128)} %scatter-add.18, f32[15,1,2048]{2,1,0:T(1,128)S(1)} %slice_add_fusion, s32[]{:T(128)} %constant.160.clone.1, s32[]{:T(128)} %constant.161.clone.1, s32[]{:T(128)} %constant.160.clone.1) | dynamic-update-slice | bytes 245764 | tf_op jit(solution)/shard_map/scatter-add | solution.py:113
  (118 shorter events, 45.7 us)
Async XLA Ops:
  0.0 26.2 %copy-start.1 = (f32[15,8,2048]{2,1,0:T(8,128)S(1)}, f32[15,8,2048]{2,1,0:T(8,128)}, u32[]{:S(2)}) copy-start(f32[15,8,2048]{2,1,0:T(8,128)} %param.13) | copy-start | bytes 2949124
  0.0 27.2 %copy-start = (f32[8,8,2048]{2,1,0:T(8,128)S(1)}, f32[8,8,2048]{2,1,0:T(8,128)}, u32[]{:S(2)}) copy-start(f32[8,8,2048]{2,1,0:T(8,128)} %param.14) | copy-start | bytes 1572868
  0.0 44.8 %collective-permute-start = (f32[15,8,2048]{2,1,0:T(8,128)}, f32[15,8,2048]{2,1,0:T(8,128)S(1)}, u32[]{:S(2)}, u32[]{:S(2)}) collective-permute-start(f32[15,8,2048]{2,1,0:T(8,128)} %param.13), channel_id=1, source_target_pairs={{0,32},{16,48},{32,64},{48,80},{64,96},{80,112},{96,0},{112,16},{1... | collective-permute-start | bytes 2949128 | tf_op jit(solution)/shard_map/ppermute | solution.py:53
  2.0 40.4 %collective-permute-start.1 = (f32[15,8,2048]{2,1,0:T(8,128)}, f32[15,8,2048]{2,1,0:T(8,128)}, u32[]{:S(2)}, u32[]{:S(2)}) collective-permute-start(f32[15,8,2048]{2,1,0:T(8,128)} %param.13), channel_id=1, source_target_pairs={{0,96},{16,112},{32,0},{48,16},{64,32},{80,48},{96,64},{112,80},{1... | collective-permute-start | bytes 2949128 | tf_op jit(solution)/shard_map/ppermute | solution.py:53
  3.4 41.7 %collective-permute-start.4 = (f32[15,8,2048]{2,1,0:T(8,128)}, f32[15,8,2048]{2,1,0:T(8,128)}, u32[]{:S(2)}, u32[]{:S(2)}) collective-permute-start(f32[15,8,2048]{2,1,0:T(8,128)} %param.13), channel_id=1, source_target_pairs={{0,16},{16,0},{32,48},{48,32},{64,80},{80,64},{96,112},{112,96},{1... | collective-permute-start | bytes 2949128 | tf_op jit(solution)/shard_map/ppermute | solution.py:60
  8.4 30.6 %collective-permute-start.9 = (f32[8,1,2048]{2,1,0:T(1,128)}, f32[8,1,2048]{2,1,0:T(1,128)}, u32[]{:S(2)}, u32[]{:S(2)}) collective-permute-start(f32[8,1,2048]{2,1,0:T(1,128)} %get-tuple-element.46), channel_id=1, source_target_pairs={{0,1},{1,2},{2,3},{3,4},{4,5},{5,6},{6,7},{7,8},{8,9},{9,10},{10,1... | collective-permute-start | bytes 196616 | tf_op jit(solution)/shard_map/ppermute | solution.py:78
  13.3 25.7 %collective-permute-start.10 = (f32[8,1,2048]{2,1,0:T(1,128)}, f32[8,1,2048]{2,1,0:T(1,128)}, u32[]{:S(2)}, u32[]{:S(2)}) collective-permute-start(f32[8,1,2048]{2,1,0:T(1,128)} %get-tuple-element.45), channel_id=1, source_target_pairs={{1,0},{2,1},{3,2},{4,3},{5,4},{6,5},{7,6},{8,7},{9,8},{10,9},{11,1... | collective-permute-start | bytes 196616 | tf_op jit(solution)/shard_map/ppermute | solution.py:78
  24.1 4.6 %copy-start.9 = (s32[120]{0:T(128)S(1)}, s32[120]{0:T(128)}, u32[]{:S(2)}) copy-start(s32[120]{0:T(128)} %and_select_fusion.2) | copy-start | bytes 1444
  43.5 13.3 %collective-permute-start.3 = (f32[15,8,1024]{2,1,0:T(8,128)S(1)}, f32[15,8,1024]{2,1,0:T(8,128)S(1)}, u32[]{:S(2)}, u32[]{:S(2)}) collective-permute-start(f32[15,8,1024]{2,1,0:T(8,128)S(1)} %slice.157), channel_id=1, source_target_pairs={{0,96},{16,112},{32,0},{48,16},{64,32},{80,48},{96,64},{112,80},{1... | collective-permute-start | bytes 1474568 | tf_op jit(solution)/shard_map/ppermute | solution.py:53
  44.9 14.5 %collective-permute-start.2 = (f32[15,8,1024]{2,1,0:T(8,128)S(1)}, f32[15,8,1024]{2,1,0:T(8,128)S(1)}, u32[]{:S(2)}, u32[]{:S(2)}) collective-permute-start(f32[15,8,1024]{2,1,0:T(8,128)S(1)} %slice.156), channel_id=1, source_target_pairs={{0,32},{16,48},{32,64},{48,80},{64,96},{80,112},{96,0},{112,16},{1... | collective-permute-start | bytes 1474568 | tf_op jit(solution)/shard_map/ppermute | solution.py:53
  45.1 33.6 %collective-permute-start.5 = (f32[15,8,2048]{2,1,0:T(8,128)}, f32[15,8,2048]{2,1,0:T(8,128)S(1)}, u32[]{:S(2)}, u32[]{:S(2)}) collective-permute-start(f32[15,8,2048]{2,1,0:T(8,128)} %collective-permute-done.4), channel_id=1, source_target_pairs={{0,32},{16,48},{32,64},{48,80},{64,96},{80,112},{96,0},{112,16},{1... | collective-permute-start | bytes 2949128 | tf_op jit(solution)/shard_map/ppermute | solution.py:53
  45.2 30.9 %collective-permute-start.6 = (f32[15,8,2048]{2,1,0:T(8,128)}, f32[15,8,2048]{2,1,0:T(8,128)S(1)}, u32[]{:S(2)}, u32[]{:S(2)}) collective-permute-start(f32[15,8,2048]{2,1,0:T(8,128)} %collective-permute-done.4), channel_id=1, source_target_pairs={{0,96},{16,112},{32,0},{48,16},{64,32},{80,48},{96,64},{112,80},{1... | collective-permute-start | bytes 2949128 | tf_op jit(solution)/shard_map/ppermute | solution.py:53
  76.2 12.7 %collective-permute-start.8 = (f32[15,8,1024]{2,1,0:T(8,128)S(1)}, f32[15,8,1024]{2,1,0:T(8,128)S(1)}, u32[]{:S(2)}, u32[]{:S(2)}) collective-permute-start(f32[15,8,1024]{2,1,0:T(8,128)S(1)} %slice.159), channel_id=1, source_target_pairs={{0,96},{16,112},{32,0},{48,16},{64,32},{80,48},{96,64},{112,80},{1... | collective-permute-start | bytes 1474568 | tf_op jit(solution)/shard_map/ppermute | solution.py:53
  78.8 14.1 %collective-permute-start.7 = (f32[15,8,1024]{2,1,0:T(8,128)S(1)}, f32[15,8,1024]{2,1,0:T(8,128)S(1)}, u32[]{:S(2)}, u32[]{:S(2)}) collective-permute-start(f32[15,8,1024]{2,1,0:T(8,128)S(1)} %slice.158), channel_id=1, source_target_pairs={{0,32},{16,48},{32,64},{48,80},{64,96},{80,112},{96,0},{112,16},{1... | collective-permute-start | bytes 1474568 | tf_op jit(solution)/shard_map/ppermute | solution.py:53
  101.5 11.5 %copy-start.7 = (pred[2048]{0:T(1024)(128)(4,1)S(1)}, pred[2048]{0:T(1024)(128)(4,1)}, u32[]{:S(2)}) copy-start(pred[2048]{0:T(1024)(128)(4,1)} %iota_compare_fusion.1) | copy-start | bytes 6148
  101.9 11.3 %copy-start.6 = (pred[2048]{0:T(1024)(128)(4,1)S(1)}, pred[2048]{0:T(1024)(128)(4,1)}, u32[]{:S(2)}) copy-start(pred[2048]{0:T(1024)(128)(4,1)} %iota_compare_fusion) | copy-start | bytes 6148
  101.9 23.2 %collective-permute-start.11 = (f32[120,2048]{1,0:T(8,128)S(1)}, f32[120,2048]{1,0:T(8,128)S(1)}, u32[]{:S(2)}, u32[]{:S(2)}) collective-permute-start(f32[120,2048]{1,0:T(8,128)S(1)} %bitcast.70), channel_id=1, source_target_pairs={{0,1},{1,2},{2,3},{3,4},{4,5},{5,6},{6,7},{7,8},{8,9},{9,10},{10,1... | collective-permute-start | bytes 2949128 | tf_op jit(solution)/shard_map/ppermute | solution.py:78
  108.7 19.0 %collective-permute-start.12 = (f32[120,2048]{1,0:T(8,128)}, f32[120,2048]{1,0:T(8,128)S(1)}, u32[]{:S(2)}, u32[]{:S(2)}) collective-permute-start(f32[120,2048]{1,0:T(8,128)} %bitcast.64), channel_id=1, source_target_pairs={{1,0},{2,1},{3,2},{4,3},{5,4},{6,5},{7,6},{8,7},{9,8},{10,9},{11,1... | collective-permute-start | bytes 2949128 | tf_op jit(solution)/shard_map/ppermute | solution.py:78
  113.3 11.8 %copy-start.5 = (s32[1024]{0:T(1024)S(1)}, s32[1024]{0:T(1024)}, u32[]{:S(2)}) copy-start(s32[1024]{0:T(1024)} %pad_clamp_fusion) | copy-start | bytes 12292
  127.7 2.6 %copy-start.8 = (pred[15,16]{1,0:T(8,128)(4,1)S(1)}, pred[15,16]{1,0:T(8,128)(4,1)}, u32[]{:S(2)}) copy-start(pred[15,16]{1,0:T(8,128)(4,1)} %copy.32) | copy-start | bytes 724
  137.5 3.4 %copy-start.4 = (f32[15,8,2]{2,1,0:T(8,128)S(1)}, f32[15,8,2]{2,1,0:T(8,128)}, u32[]{:S(2)}) copy-start(f32[15,8,2]{2,1,0:T(8,128)} %copy.34) | copy-start | bytes 2884
  140.9 7.1 %copy-start.3 = (f32[8,1,2048]{2,0,1:T(8,128)S(1)}, f32[8,1,2048]{2,0,1:T(8,128)}, u32[]{:S(2)}) copy-start(f32[8,1,2048]{2,0,1:T(8,128)} %copy.48) | copy-start | bytes 196612
  140.9 12.2 %copy-start.2 = (f32[8,1,2048]{2,0,1:T(8,128)S(1)}, f32[8,1,2048]{2,0,1:T(8,128)}, u32[]{:S(2)}) copy-start(f32[8,1,2048]{2,0,1:T(8,128)} %copy.47) | copy-start | bytes 196612

commit v5 on v4

--- a/solution.py
+++ b/solution.py
@@ -100,42 +100,37 @@
 
     above, below = space_halo(kl_fields[:, rows - 1:], kl_fields[:, :1])
     coef = jnp.concatenate([above, kl_fields, below], axis=1)
-    edges, c_top, c_bottom = edge_coefficients(coef)
-    applied = stencil_apply(every, edges, partners, weights)
-
-    halo_above, halo_below = space_halo(every[:, rows - 1], every[:, 0])
-    pick_w = weights.reshape(own_modes, kl_terms, 2, 1)
-    mixed_above = jnp.sum(jnp.take(halo_above, partners, axis=0).reshape(own_modes, kl_terms, 2, -1) * pick_w, axis=2)
-    mixed_below = jnp.sum(jnp.take(halo_below, partners, axis=0).reshape(own_modes, kl_terms, 2, -1) * pick_w, axis=2)
-    fix_top = jnp.sum(c_top[None] * mixed_above, axis=1)
-    fix_bottom = jnp.sum(c_bottom[None] * mixed_below, axis=1)
-    applied = applied.at[:, 0].add(-fix_top)
-    applied = applied.at[:, rows - 1].add(-fix_bottom)
-    return applied
-
-
-def edge_coefficients(coef):
-    a_c = coef[:, 1:-1]
-    c_up = 0.5 * (a_c + coef[:, :-2])
-    c_dn = 0.5 * (a_c + coef[:, 2:])
-    c_lf = 0.5 * (a_c + shift_cols(a_c, 1))
-    c_rt = 0.5 * (a_c + shift_cols(a_c, -1))
-    total = (c_up + c_dn) + (c_lf + c_rt)
-    column = lax.broadcasted_iota(jnp.int32, a_c.shape, 2)
-    row = lax.broadcasted_iota(jnp.int32, a_c.shape, 1)
-    n_up = jnp.where(row == 0, 0.0, c_up)
-    n_dn = jnp.where(row == a_c.shape[1] - 1, 0.0, c_dn)
-    n_lf = jnp.where(column == 0, 0.0, c_lf)
-    n_rt = jnp.where(column == a_c.shape[2] - 1, 0.0, c_rt)
-    edges = jnp.stack([total, n_up, n_dn, n_lf, n_rt], axis=0)
-    return edges, c_up[:, 0], c_dn[:, -1]
-
-
-def stencil_kernel(partners, weights, every, edges, out):
+    applied = stencil_apply(every, coef, partners, weights)
+
+    halo_above, halo_below = space_halo(every[:, rows - 1:], every[:, :1])
+    halo = jnp.concatenate([halo_above, halo_below], axis=1)
+    c_rim = 0.5 * jnp.concatenate([coef[:, 1:2] + coef[:, :1], coef[:, rows:rows + 1] + coef[:, rows + 1:]], axis=1)
+    return rim_apply(applied, halo, c_rim, partners, weights)
+
+
+def stencil_kernel(partners, weights, every, coef, out, edges):
     slot = pl.program_id(0)
-    kl_terms = edges.shape[1]
+    kl_terms = coef.shape[0]
     rows = out.shape[1]
     cols = out.shape[2]
+
+    @pl.when(slot == 0)
+    def _():
+        row = lax.broadcasted_iota(jnp.int32, (rows, cols), 0)
+        column = lax.broadcasted_iota(jnp.int32, (rows, cols), 1)
+        zero = jnp.zeros((rows, cols), jnp.float32)
+        for k in range(kl_terms):
+            a_c = coef[k, pl.ds(1, rows), :]
+            c_up = 0.5 * (a_c + coef[k, pl.ds(0, rows), :])
+            c_dn = 0.5 * (a_c + coef[k, pl.ds(2, rows), :])
+            c_lf = 0.5 * (a_c + jnp.where(column == 0, zero, pltpu.roll(a_c, 1, 1)))
+            c_rt = 0.5 * (a_c + jnp.where(column == cols - 1, zero, pltpu.roll(a_c, cols - 1, 1)))
+            edges[0, k] = (c_up + c_dn) + (c_lf + c_rt)
+            edges[1, k] = jnp.where(row == 0, zero, c_up)
+            edges[2, k] = jnp.where(row == rows - 1, zero, c_dn)
+            edges[3, k] = jnp.where(column == 0, zero, c_lf)
+            edges[4, k] = jnp.where(column == cols - 1, zero, c_rt)
+
     acc = jnp.zeros((rows, cols), jnp.float32)
     for k in range(kl_terms):
         j0 = partners[slot, 2 * k]
@@ -155,10 +150,11 @@
     out[0] = acc
 
 
-def stencil_apply(every, edges, partners, weights):
+def stencil_apply(every, coef, partners, weights):
     own_modes = partners.shape[0]
-    rows = edges.shape[2]
-    cols = edges.shape[3]
+    kl_terms = coef.shape[0]
+    rows = every.shape[1]
+    cols = every.shape[2]
     return pl.pallas_call(
         stencil_kernel,
         out_shape=jax.ShapeDtypeStruct((own_modes, rows, cols), jnp.float32),
@@ -171,11 +167,52 @@
                 pl.BlockSpec(memory_space=pltpu.VMEM),
             ],
             out_specs=pl.BlockSpec((1, rows, cols), lambda i, p: (i, 0, 0)),
+            scratch_shapes=[pltpu.VMEM((5, kl_terms, rows, cols), jnp.float32)],
         ),
         compiler_params=pltpu.CompilerParams(
             dimension_semantics=("arbitrary",), vmem_limit_bytes=48 * 1024 * 1024
         ),
-    )(partners, weights, every, edges)
+    )(partners, weights, every, coef)
+
+
+def rim_kernel(partners, weights, halo, c_rim, applied, out):
+    slot = pl.program_id(0)
+    kl_terms = c_rim.shape[0]
+    rows = out.shape[1]
+    cols = out.shape[2]
+    fix = jnp.zeros((2, cols), jnp.float32)
+    for k in range(kl_terms):
+        j0 = partners[slot, 2 * k]
+        j1 = partners[slot, 2 * k + 1]
+        w0 = weights[slot, 2 * k]
+        w1 = weights[slot, 2 * k + 1]
+        fix = fix + c_rim[k] * (w0 * halo[j0] + w1 * halo[j1])
+    row = lax.broadcasted_iota(jnp.int32, (rows, cols), 0)
+    zero = jnp.zeros((rows, cols), jnp.float32)
+    spread = jnp.where(row == 0, jnp.broadcast_to(fix[0:1], (rows, cols)), zero)
+    spread = jnp.where(row == rows - 1, jnp.broadcast_to(fix[1:2], (rows, cols)), spread)
+    out[0] = applied[0] - spread
+
+
+def rim_apply(applied, halo, c_rim, partners, weights):
+    own_modes, rows, cols = applied.shape
+    return pl.pallas_call(
+        rim_kernel,
+        out_shape=jax.ShapeDtypeStruct(applied.shape, jnp.float32),
+        grid_spec=pltpu.PrefetchScalarGridSpec(
+            num_scalar_prefetch=1,
+            grid=(own_modes,),
+            in_specs=[
+                pl.BlockSpec(memory_space=pltpu.SMEM),
+                pl.BlockSpec(memory_space=pltpu.VMEM),
+                pl.BlockSpec(memory_space=pltpu.VMEM),
+                pl.BlockSpec((1, rows, cols), lambda i, p: (i, 0, 0)),
+            ],
+            out_specs=pl.BlockSpec((1, rows, cols), lambda i, p: (i, 0, 0)),
+        ),
+        input_output_aliases={4: 0},
+        compiler_params=pltpu.CompilerParams(dimension_semantics=("arbitrary",)),
+    )(partners, weights, halo, c_rim, applied)
 
 
 def solution(mesh):

time: 159 us -> 122 us (0.77)
  local copies, waits for them, and re-layouts: 51.2 us -> 16.5 us
  other arithmetic: 33.8 us -> 16.9 us
  Pallas kernels: 11.8 us -> 22.9 us
  starting transfers between devices: 27.4 us -> 29.1 us
    pallas_call x0 -> x1, Pallas kernels: none -> 10.2 us  [rim_apply(): pl.pallas_call(rim_kernel, out_shape=jax.ShapeDtypeStruct(applied.shape,...]
    unnamed x30 -> x16, local copies, waits for them, and re-layouts: 11.8 us -> 1.68 us
    reduce_sum x3 -> x0, other arithmetic: 7.65 us -> none  [the longest x1 7.05 us: local(): jnp.sum(jnp.take(halo_below, partners, axis=0).reshape(own_modes, kl_term...]
    scatter-add x2 -> x0, local copies, waits for them, and re-layouts: 7.03 us -> none  [the longest x1 3.51 us: local(): applied = applied.at[:, 0].add(-fix_top)]
    slice x4 -> x1, local copies, waits for them, and re-layouts: 7.88 us -> 1.35 us  [local(): halo_above, halo_below = space_halo(every[:, rows - 1:], every[:, :1])]
    reshape x2 -> x0, local copies, waits for them, and re-layouts: 5.88 us -> none  [the longest x1 3.43 us: local(): jnp.take(halo_above, partners, axis=0).reshape(own_modes, kl_terms, 2, -1)]
    concatenate x0 -> x2, other arithmetic: none -> 5.27 us  [the longest x1 4.26 us: local(): halo = jnp.concatenate([halo_above, halo_below], axis=1)]
    gather x2 -> x0, local copies, waits for them, and re-layouts: 5.18 us -> none  [the longest x1 2.59 us: local(): jnp.take(halo_above, partners, axis=0).reshape(own_modes, kl_terms, 2, -1)]
  transfers between devices with their start and end apart: 13 -> 13, of which waited for: 6 -> 4; matrix products, arithmetic and copies ran while one was open for 29% -> 24% of each run, Pallas kernels for 7% -> 11%
where the time goes in v5:
time: 122 us; the launch traced here: 121 us
  waiting for transfers between devices  35.1 us (29%)
  starting transfers between devices  29.1 us (24%)
  Pallas kernels  22.9 us (19%)
  other arithmetic  16.9 us (14%)
  local copies, waits for them, and re-layouts  16.5 us (14%)
    ppermute x8, waiting for transfers between devices, shifted(): lax.ppermute(x, 'chaos', [(c, (c + step) % count) for c in range(count)])  35.1 us
    pallas_call x1, Pallas kernels, stencil_apply(): pl.pallas_call(stencil_kernel, out_shape=jax.ShapeDtypeStruct((own_modes,...  12.7 us
    ppermute x8, starting transfers between devices, shifted(): lax.ppermute(x, 'chaos', [(c, (c + step) % count) for c in range(count)])  11.8 us
    pallas_call x1, Pallas kernels, rim_apply(): pl.pallas_call(rim_kernel, out_shape=jax.ShapeDtypeStruct(applied.shape,...  10.2 us
    ppermute x2, starting transfers between devices, space_halo(): lax.ppermute(edge_last, 'space', up)  10 us
    scatter-add x1, other arithmetic, coupling_table(): jnp.zeros((kl_terms * mode_count * mode_count,), jnp.float32).at[flat_index]  4.71 us
    concatenate x1, other arithmetic, local(): halo = jnp.concatenate([halo_above, halo_below], axis=1)  4.26 us
    ppermute x2, starting transfers between devices, space_halo(): lax.ppermute(edge_first, 'space', down)  4.09 us
  transfers between devices with their start and end apart: 13, of which 4 were waited for; matrix products, arithmetic and copies ran while one was open for 24% of the time, Pallas kernels for 11%

profile of v5, /device:TPU:1, one launch (start us, length us, event | category | flops | bytes accessed | tf_op | source)
XLA Modules:
  0.0 121.0 jit_solution(15575476258835053478)
XLA Ops:
  0.0 2.0 %collective-permute-start = (f32[15,8,2048]{2,1,0:T(8,128)}, f32[15,8,2048]{2,1,0:T(8,128)S(1)}, u32[]{:S(2)}, u32[]{:S(2)}) collective-permute-start(f32[15,8,2048]{2,1,0:T(8,128)} %param.7), channel_id=1, source_target_pairs={{0,32},{16,48},{32,64},{48,80},{64,96},{80,112},{96,0},{112,16},{1... | collective-permute-start | bytes 2949128 | tf_op jit(solution)/shard_map/ppermute | solution.py:53
  2.0 1.3 %collective-permute-start.1 = (f32[15,8,2048]{2,1,0:T(8,128)}, f32[15,8,2048]{2,1,0:T(8,128)S(1)}, u32[]{:S(2)}, u32[]{:S(2)}) collective-permute-start(f32[15,8,2048]{2,1,0:T(8,128)} %param.7), channel_id=1, source_target_pairs={{0,96},{16,112},{32,0},{48,16},{64,32},{80,48},{96,64},{112,80},{1... | collective-permute-start | bytes 2949128 | tf_op jit(solution)/shard_map/ppermute | solution.py:53
  3.3 3.1 %collective-permute-start.4 = (f32[15,8,2048]{2,1,0:T(8,128)}, f32[15,8,2048]{2,1,0:T(8,128)}, u32[]{:S(2)}, u32[]{:S(2)}) collective-permute-start(f32[15,8,2048]{2,1,0:T(8,128)} %param.7), channel_id=1, source_target_pairs={{0,16},{16,0},{32,48},{48,32},{64,80},{80,64},{96,112},{112,96},{1... | collective-permute-start | bytes 2949128 | tf_op jit(solution)/shard_map/ppermute | solution.py:60
  6.4 2.0 %fusion.20 = (f32[8,1,2048]{2,1,0:T(1,128)}, f32[8,1,2048]{2,1,0:T(1,128)}) fusion(f32[8,8,2048]{2,1,0:T(8,128)} %param.8), kind=kLoop, calls=%fused_computation.72 | loop fusion | bytes 262144 | tf_op jit(solution)/shard_map/slice | solution.py:101
  8.4 4.9 %collective-permute-start.11 = (f32[8,1,2048]{2,1,0:T(1,128)}, f32[8,1,2048]{2,1,0:T(1,128)S(1)}, u32[]{:S(2)}, u32[]{:S(2)}) collective-permute-start(f32[8,1,2048]{2,1,0:T(1,128)} %get-tuple-element.18), channel_id=1, source_target_pairs={{0,1},{1,2},{2,3},{3,4},{4,5},{5,6},{6,7},{7,8},{8,9},{9,10},{10,1... | collective-permute-start | bytes 196616 | tf_op jit(solution)/shard_map/ppermute | solution.py:78
  16.4 4.7 %scatter_custom_fusion = f32[115200]{0:T(1024)S(1)} fusion(s32[624]{0:T(1024)S(1)} %fusion.15, f32[624]{0:T(1024)S(1)} %fusion.17, f32[]{:T(128)} %constant.101.clone.1), kind=kCustom, calls=%fused_computation.10 | custom fusion | flops 624 | bytes 460804 | tf_op jit(solution)/shard_map/scatter-add | solution.py:35
  23.9 2.1 %gather_fusion.3 = f32[120]{0:T(128)S(1)} fusion(f32[8,15,120]{2,1,0:T(8,128)S(1)} %get-tuple-element.13, s32[120]{0:T(128)S(1)} %reshape.104), kind=kCustom, calls=%fused_computation.1.clone | custom fusion | bytes 2400 | tf_op jit(solution)/shard_map/jit(take_along_axis)/gather | solution.py:46
  26.1 2.1 %gather_fusion.2 = f32[120]{0:T(128)S(1)} fusion(f32[8,15,120]{2,1,0:T(8,128)S(1)} %get-tuple-element.13, s32[120]{0:T(128)S(1)} %reshape.98), kind=kCustom, calls=%fused_computation.clone | custom fusion | bytes 2400 | tf_op jit(solution)/shard_map/jit(take_along_axis)/gather | solution.py:45
  29.2 1.2 %gather_fusion = s32[120]{0:T(128)S(1)} fusion(s32[120]{0:T(128)S(1)} %fusion.18, s32[1024]{0:T(1024)S(1)} %get-tuple-element.23), kind=kCustom, calls=%fused_computation.2 | custom fusion | bytes 1440 | tf_op jit(solution)/shard_map/gather | solution.py:96
  30.5 1.2 %gather_fusion.1 = s32[120]{0:T(128)S(1)} fusion(s32[120]{0:T(128)S(1)} %fusion.18, s32[1024]{0:T(1024)S(1)} %get-tuple-element.22), kind=kCustom, calls=%fused_computation.3 | custom fusion | bytes 1440 | tf_op jit(solution)/shard_map/gather | solution.py:97
  32.1 2.7 %collective-permute-start.3 = (f32[15,8,1024]{2,1,0:T(8,128)S(1)}, f32[15,8,1024]{2,1,0:T(8,128)S(1)}, u32[]{:S(2)}, u32[]{:S(2)}) collective-permute-start(f32[15,8,1024]{2,1,0:T(8,128)S(1)} %slice.83), channel_id=1, source_target_pairs={{0,96},{16,112},{32,0},{48,16},{64,32},{80,48},{96,64},{112,80},{1... | collective-permute-start | bytes 1474568 | tf_op jit(solution)/shard_map/ppermute | solution.py:53
  34.8 2.7 %collective-permute-start.6 = (f32[15,8,2048]{2,1,0:T(8,128)}, f32[15,8,2048]{2,1,0:T(8,128)S(1)}, u32[]{:S(2)}, u32[]{:S(2)}) collective-permute-start(f32[15,8,2048]{2,1,0:T(8,128)} %collective-permute-done.4), channel_id=1, source_target_pairs={{0,96},{16,112},{32,0},{48,16},{64,32},{80,48},{96,64},{112,80},{1... | collective-permute-start | bytes 2949128 | tf_op jit(solution)/shard_map/ppermute | solution.py:53
  37.7 8.8 %collective-permute-done.2 = f32[15,8,1024]{2,1,0:T(8,128)S(1)} collective-permute-done((f32[15,8,1024]{2,1,0:T(8,128)S(1)}, f32[15,8,1024]{2,1,0:T(8,128)S(1)}, u32[]{:S(2)}, u32[]{:S(2)}) %collective-permute-start.2) | collective-permute-done | bytes 491552 | tf_op jit(solution)/shard_map/ppermute | solution.py:53
  46.5 2.0 %collective-permute-start.12 = (f32[8,1,2048]{2,1,0:T(1,128)}, f32[8,1,2048]{2,1,0:T(1,128)}, u32[]{:S(2)}, u32[]{:S(2)}) collective-permute-start(f32[8,1,2048]{2,1,0:T(1,128)} %get-tuple-element.19), channel_id=1, source_target_pairs={{1,0},{2,1},{3,2},{4,3},{5,4},{6,5},{7,6},{8,7},{9,8},{10,9},{11,1... | collective-permute-start | bytes 196616 | tf_op jit(solution)/shard_map/ppermute | solution.py:78
  48.6 1.3 %constant_dynamic-update-slice_fusion.2 = f32[120,8,2048]{2,1,0:T(8,128)S(1)} fusion(f32[120,8,2048]{2,1,0:T(8,128)S(1)} %maximum_dynamic-update-slice_fusion.1, f32[15,8,2048]{2,1,0:T(8,128)} %collective-permute-done.4), kind=kLoop, calls=%fused_computation.18 | loop fusion | bytes 1966080
  49.9 15.7 %collective-permute-done.5 = f32[15,8,2048]{2,1,0:T(8,128)S(1)} collective-permute-done((f32[15,8,2048]{2,1,0:T(8,128)}, f32[15,8,2048]{2,1,0:T(8,128)S(1)}, u32[]{:S(2)}, u32[]{:S(2)}) %collective-permute-start.5) | collective-permute-done | bytes 983072 | tf_op jit(solution)/shard_map/ppermute | solution.py:53
  65.8 3.0 %collective-permute-start.8 = (f32[15,8,1024]{2,1,0:T(8,128)S(1)}, f32[15,8,1024]{2,1,0:T(8,128)S(1)}, u32[]{:S(2)}, u32[]{:S(2)}) collective-permute-start(f32[15,8,1024]{2,1,0:T(8,128)S(1)} %slice.85), channel_id=1, source_target_pairs={{0,96},{16,112},{32,0},{48,16},{64,32},{80,48},{96,64},{112,80},{1... | collective-permute-start | bytes 1474568 | tf_op jit(solution)/shard_map/ppermute | solution.py:53
  68.9 10.4 %collective-permute-done.7 = f32[15,8,1024]{2,1,0:T(8,128)S(1)} collective-permute-done((f32[15,8,1024]{2,1,0:T(8,128)S(1)}, f32[15,8,1024]{2,1,0:T(8,128)S(1)}, u32[]{:S(2)}, u32[]{:S(2)}) %collective-permute-start.7) | collective-permute-done | bytes 491552 | tf_op jit(solution)/shard_map/ppermute | solution.py:53
  79.6 1.3 %fusion.19 = (f32[120,1,2048]{2,1,0:T(1,128)S(1)}, f32[120,1,2048]{2,1,0:T(1,128)S(1)}) fusion(f32[120,8,2048]{2,1,0:T(8,128)S(1)} %maximum_dynamic-update-slice_fusion.every), kind=kLoop, calls=%fused_computation.71 | loop fusion | bytes 3932160 | tf_op jit(solution)/shard_map/slice | solution.py:105
  81.0 2.0 %collective-permute-start.10 = (f32[120,1,2048]{2,1,0:T(1,128)S(1)}, f32[120,1,2048]{2,1,0:T(1,128)S(1)}, u32[]{:S(2)}, u32[]{:S(2)}) collective-permute-start(f32[120,1,2048]{2,1,0:T(1,128)S(1)} %get-tuple-element.15), channel_id=1, source_target_pairs={{1,0},{2,1},{3,2},{4,3},{5,4},{6,5},{7,6},{8,7},{9,8},{10,9},{11,1... | collective-permute-start | bytes 2949128 | tf_op jit(solution)/shard_map/ppermute | solution.py:78
  83.0 5.1 %collective-permute-start.9 = (f32[120,1,2048]{2,1,0:T(1,128)S(1)}, f32[120,1,2048]{2,1,0:T(1,128)}, u32[]{:S(2)}, u32[]{:S(2)}) collective-permute-start(f32[120,1,2048]{2,1,0:T(1,128)S(1)} %get-tuple-element.14), channel_id=1, source_target_pairs={{0,1},{1,2},{2,3},{3,4},{4,5},{5,6},{6,7},{7,8},{8,9},{9,10},{10,1... | collective-permute-start | bytes 2949128 | tf_op jit(solution)/shard_map/ppermute | solution.py:78
  93.7 12.7 %shard_map.55.applied = f32[15,8,2048]{2,1,0:T(8,128)} custom-call(s32[15,16]{1,0:T(8,128)S(1)} %copy.21.partners, f32[15,16]{1,0:T(8,128)S(1)} %copy.22.weights, f32[120,8,2048]{2,1,0:T(8,128)} %copy-done.2, f32[8,10,2048]{2,1,0:T(8,128)S(1)} %pad_maximum_fusion.1.coef), custom_call_target="tpu_custom_call" | custom-call | tf_op jit(solution)/shard_map/pallas_call | solution.py:158
  106.5 4.3 %pad_maximum_fusion.halo = f32[120,2,2048]{2,1,0:T(2,128)} fusion(f32[120,1,2048]{2,1,0:T(1,128)S(1)} %collective-permute-done.10, f32[120,1,2048]{2,1,0:T(1,128)} %collective-permute-done.9), kind=kLoop, calls=%fused_computation.5 | loop fusion | flops 491520 | bytes 3932160 | tf_op jit(solution)/shard_map/concatenate | solution.py:106
  110.7 10.2 %shard_map.56 = f32[15,8,2048]{2,1,0:T(8,128)} custom-call(s32[15,16]{1,0:T(8,128)} %copy-done.1, f32[15,16]{1,0:T(8,128)} %copy-done, f32[120,2,2048]{2,1,0:T(2,128)} %pad_maximum_fusion.halo, f32[8,2,2048]{2,1,0:T(2,128)} %maximum_multiply_fusion.c_rim, f32[15,8,2048]{2,1,0:T(8,128)} %shard_map.55.applied), custom_call_target="tpu_custom_call", output_to_operand_aliasing={{}: (4, {})} | custom-call | tf_op jit(solution)/shard_map/pallas_call | solution.py:199
  (75 shorter events, 13.6 us)
Async XLA Ops:
  0.0 31.9 %collective-permute-start = (f32[15,8,2048]{2,1,0:T(8,128)}, f32[15,8,2048]{2,1,0:T(8,128)S(1)}, u32[]{:S(2)}, u32[]{:S(2)}) collective-permute-start(f32[15,8,2048]{2,1,0:T(8,128)} %param.7), channel_id=1, source_target_pairs={{0,32},{16,48},{32,64},{48,80},{64,96},{80,112},{96,0},{112,16},{1... | collective-permute-start | bytes 2949128 | tf_op jit(solution)/shard_map/ppermute | solution.py:53
  2.0 30.0 %collective-permute-start.1 = (f32[15,8,2048]{2,1,0:T(8,128)}, f32[15,8,2048]{2,1,0:T(8,128)S(1)}, u32[]{:S(2)}, u32[]{:S(2)}) collective-permute-start(f32[15,8,2048]{2,1,0:T(8,128)} %param.7), channel_id=1, source_target_pairs={{0,96},{16,112},{32,0},{48,16},{64,32},{80,48},{96,64},{112,80},{1... | collective-permute-start | bytes 2949128 | tf_op jit(solution)/shard_map/ppermute | solution.py:53
  3.3 31.5 %collective-permute-start.4 = (f32[15,8,2048]{2,1,0:T(8,128)}, f32[15,8,2048]{2,1,0:T(8,128)}, u32[]{:S(2)}, u32[]{:S(2)}) collective-permute-start(f32[15,8,2048]{2,1,0:T(8,128)} %param.7), channel_id=1, source_target_pairs={{0,16},{16,0},{32,48},{48,32},{64,80},{80,64},{96,112},{112,96},{1... | collective-permute-start | bytes 2949128 | tf_op jit(solution)/shard_map/ppermute | solution.py:60
  8.4 82.6 %collective-permute-start.11 = (f32[8,1,2048]{2,1,0:T(1,128)}, f32[8,1,2048]{2,1,0:T(1,128)S(1)}, u32[]{:S(2)}, u32[]{:S(2)}) collective-permute-start(f32[8,1,2048]{2,1,0:T(1,128)} %get-tuple-element.18), channel_id=1, source_target_pairs={{0,1},{1,2},{2,3},{3,4},{4,5},{5,6},{6,7},{7,8},{8,9},{9,10},{10,1... | collective-permute-start | bytes 196616 | tf_op jit(solution)/shard_map/ppermute | solution.py:78
  23.9 8.0 %copy-start.4 = (f32[15,8,2048]{2,1,0:T(8,128)S(1)}, f32[15,8,2048]{2,1,0:T(8,128)}, u32[]{:S(2)}) copy-start(f32[15,8,2048]{2,1,0:T(8,128)} %param.7) | copy-start | bytes 2949124
  32.0 14.5 %collective-permute-start.2 = (f32[15,8,1024]{2,1,0:T(8,128)S(1)}, f32[15,8,1024]{2,1,0:T(8,128)S(1)}, u32[]{:S(2)}, u32[]{:S(2)}) collective-permute-start(f32[15,8,1024]{2,1,0:T(8,128)S(1)} %slice.82), channel_id=1, source_target_pairs={{0,32},{16,48},{32,64},{48,80},{64,96},{80,112},{96,0},{112,16},{1... | collective-permute-start | bytes 1474568 | tf_op jit(solution)/shard_map/ppermute | solution.py:53
  32.1 16.4 %collective-permute-start.3 = (f32[15,8,1024]{2,1,0:T(8,128)S(1)}, f32[15,8,1024]{2,1,0:T(8,128)S(1)}, u32[]{:S(2)}, u32[]{:S(2)}) collective-permute-start(f32[15,8,1024]{2,1,0:T(8,128)S(1)} %slice.83), channel_id=1, source_target_pairs={{0,96},{16,112},{32,0},{48,16},{64,32},{80,48},{96,64},{112,80},{1... | collective-permute-start | bytes 1474568 | tf_op jit(solution)/shard_map/ppermute | solution.py:53
  34.8 30.8 %collective-permute-start.5 = (f32[15,8,2048]{2,1,0:T(8,128)}, f32[15,8,2048]{2,1,0:T(8,128)S(1)}, u32[]{:S(2)}, u32[]{:S(2)}) collective-permute-start(f32[15,8,2048]{2,1,0:T(8,128)} %collective-permute-done.4), channel_id=1, source_target_pairs={{0,32},{16,48},{32,64},{48,80},{64,96},{80,112},{96,0},{112,16},{1... | collective-permute-start | bytes 2949128 | tf_op jit(solution)/shard_map/ppermute | solution.py:53
  34.8 30.9 %collective-permute-start.6 = (f32[15,8,2048]{2,1,0:T(8,128)}, f32[15,8,2048]{2,1,0:T(8,128)S(1)}, u32[]{:S(2)}, u32[]{:S(2)}) collective-permute-start(f32[15,8,2048]{2,1,0:T(8,128)} %collective-permute-done.4), channel_id=1, source_target_pairs={{0,96},{16,112},{32,0},{48,16},{64,32},{80,48},{96,64},{112,80},{1... | collective-permute-start | bytes 2949128 | tf_op jit(solution)/shard_map/ppermute | solution.py:53
  46.5 44.5 %copy-start.3 = (f32[8,8,2048]{2,1,0:T(8,128)S(1)}, f32[8,8,2048]{2,1,0:T(8,128)}, u32[]{:S(2)}) copy-start(f32[8,8,2048]{2,1,0:T(8,128)} %param.8) | copy-start | bytes 1572868
  46.5 44.5 %collective-permute-start.12 = (f32[8,1,2048]{2,1,0:T(1,128)}, f32[8,1,2048]{2,1,0:T(1,128)}, u32[]{:S(2)}, u32[]{:S(2)}) collective-permute-start(f32[8,1,2048]{2,1,0:T(1,128)} %get-tuple-element.19), channel_id=1, source_target_pairs={{1,0},{2,1},{3,2},{4,3},{5,4},{6,5},{7,6},{8,7},{9,8},{10,9},{11,1... | collective-permute-start | bytes 196616 | tf_op jit(solution)/shard_map/ppermute | solution.py:78
  65.6 13.7 %collective-permute-start.7 = (f32[15,8,1024]{2,1,0:T(8,128)S(1)}, f32[15,8,1024]{2,1,0:T(8,128)S(1)}, u32[]{:S(2)}, u32[]{:S(2)}) collective-permute-start(f32[15,8,1024]{2,1,0:T(8,128)S(1)} %slice.84), channel_id=1, source_target_pairs={{0,32},{16,48},{32,64},{48,80},{64,96},{80,112},{96,0},{112,16},{1... | collective-permute-start | bytes 1474568 | tf_op jit(solution)/shard_map/ppermute | solution.py:53
  65.8 13.8 %collective-permute-start.8 = (f32[15,8,1024]{2,1,0:T(8,128)S(1)}, f32[15,8,1024]{2,1,0:T(8,128)S(1)}, u32[]{:S(2)}, u32[]{:S(2)}) collective-permute-start(f32[15,8,1024]{2,1,0:T(8,128)S(1)} %slice.85), channel_id=1, source_target_pairs={{0,96},{16,112},{32,0},{48,16},{64,32},{80,48},{96,64},{112,80},{1... | collective-permute-start | bytes 1474568 | tf_op jit(solution)/shard_map/ppermute | solution.py:53
  79.6 9.2 %copy-start.2 = (f32[120,8,2048]{2,1,0:T(8,128)}, f32[120,8,2048]{2,1,0:T(8,128)S(1)}, u32[]{:S(2)}) copy-start(f32[120,8,2048]{2,1,0:T(8,128)S(1)} %maximum_dynamic-update-slice_fusion.every) | copy-start | bytes 23592964
  81.0 25.5 %collective-permute-start.10 = (f32[120,1,2048]{2,1,0:T(1,128)S(1)}, f32[120,1,2048]{2,1,0:T(1,128)S(1)}, u32[]{:S(2)}, u32[]{:S(2)}) collective-permute-start(f32[120,1,2048]{2,1,0:T(1,128)S(1)} %get-tuple-element.15), channel_id=1, source_target_pairs={{1,0},{2,1},{3,2},{4,3},{5,4},{6,5},{7,6},{8,7},{9,8},{10,9},{11,1... | collective-permute-start | bytes 2949128 | tf_op jit(solution)/shard_map/ppermute | solution.py:78
  83.0 23.4 %collective-permute-start.9 = (f32[120,1,2048]{2,1,0:T(1,128)S(1)}, f32[120,1,2048]{2,1,0:T(1,128)}, u32[]{:S(2)}, u32[]{:S(2)}) collective-permute-start(f32[120,1,2048]{2,1,0:T(1,128)S(1)} %get-tuple-element.14), channel_id=1, source_target_pairs={{0,1},{1,2},{2,3},{3,4},{4,5},{5,6},{6,7},{7,8},{8,9},{9,10},{10,1... | collective-permute-start | bytes 2949128 | tf_op jit(solution)/shard_map/ppermute | solution.py:78
  89.6 21.2 %copy-start = (f32[15,16]{1,0:T(8,128)}, f32[15,16]{1,0:T(8,128)S(1)}, u32[]{:S(2)}) copy-start(f32[15,16]{1,0:T(8,128)S(1)} %copy.22.weights) | copy-start | bytes 2884
  90.9 19.8 %copy-start.1 = (s32[15,16]{1,0:T(8,128)}, s32[15,16]{1,0:T(8,128)S(1)}, u32[]{:S(2)}) copy-start(s32[15,16]{1,0:T(8,128)S(1)} %copy.21.partners) | copy-start | bytes 2884

commit v6 on v5

--- a/solution.py
+++ b/solution.py
@@ -53,9 +53,10 @@
     return lax.ppermute(x, "chaos", [(c, (c + step) % count) for c in range(count)])
 
 
-def ring_gather(block):
+def ring_gather(block, tables):
     count = lax.axis_size("chaos")
     me = lax.axis_index("chaos")
+    rows = block.shape[1]
     half = block.shape[-1] // 2
     partner = lax.ppermute(block, "chaos", [(c, c ^ 1) for c in range(count)])
     pieces = []
@@ -63,12 +64,22 @@
     for base, origin in ((block, me), (partner, me ^ 1)):
         from_left = shifted(base, 2)
         from_right = shifted(base, -2)
+        if origin is me:
+            from_left, tables = lax.optimization_barrier((from_left, tables))
         far = jnp.concatenate(
             [shifted(from_left[..., :half], 2), shifted(from_right[..., half:], -2)], axis=-1
         )
         pieces += [base, from_left, from_right, far]
         owners += [origin, (origin - 2) % count, (origin + 2) % count, (origin + 4) % count]
-    return jnp.concatenate(pieces, axis=0), jnp.stack(owners).astype(jnp.int32)
+    above = []
+    below = []
+    for piece in pieces:
+        a, b = space_halo(piece[:, rows - 1:], piece[:, :1])
+        above.append(a)
+        below.append(b)
+    every = jnp.concatenate(pieces, axis=0)
+    halo = jnp.concatenate([jnp.concatenate(above, axis=0), jnp.concatenate(below, axis=0)], axis=1)
+    return every, halo, jnp.stack(owners).astype(jnp.int32), tables
 
 
 def space_halo(edge_last, edge_first):
@@ -84,9 +95,14 @@
     mode_count = own_modes * groups
     kl_terms = kl_fields.shape[0]
     rows = modes.shape[1]
-    every, order = ring_gather(modes)
-
-    first_slot = lax.axis_index("chaos") * own_modes
+    count = lax.axis_size("chaos")
+    me = lax.axis_index("chaos")
+    order = jnp.stack(
+        [me, (me - 2) % count, (me + 2) % count, (me + 4) % count,
+         me ^ 1, ((me ^ 1) - 2) % count, ((me ^ 1) + 2) % count, ((me ^ 1) + 4) % count]
+    ).astype(jnp.int32)
+
+    first_slot = me * own_modes
     coupling = coupling_table(triples, ratios, mode_of_slot, kl_terms, mode_count)
     local_rows = lax.dynamic_slice_in_dim(coupling, first_slot, own_modes, 1)
     first, last, w_first, w_last = neighbour_table(local_rows)
@@ -100,15 +116,14 @@
 
     above, below = space_halo(kl_fields[:, rows - 1:], kl_fields[:, :1])
     coef = jnp.concatenate([above, kl_fields, below], axis=1)
-    applied = stencil_apply(every, coef, partners, weights)
-
-    halo_above, halo_below = space_halo(every[:, rows - 1:], every[:, :1])
-    halo = jnp.concatenate([halo_above, halo_below], axis=1)
     c_rim = 0.5 * jnp.concatenate([coef[:, 1:2] + coef[:, :1], coef[:, rows:rows + 1] + coef[:, rows + 1:]], axis=1)
-    return rim_apply(applied, halo, c_rim, partners, weights)
-
-
-def stencil_kernel(partners, weights, every, coef, out, edges):
+
+    every, halo, _, tables = ring_gather(modes, (partners, weights, coef, c_rim))
+    partners, weights, coef, c_rim = tables
+    return stencil_apply(every, halo, coef, c_rim, partners, weights)
+
+
+def stencil_kernel(partners, weights, every, halo, coef, c_rim, out, edges):
     slot = pl.program_id(0)
     kl_terms = coef.shape[0]
     rows = out.shape[1]
@@ -132,6 +147,7 @@
             edges[4, k] = jnp.where(column == cols - 1, zero, c_rt)
 
     acc = jnp.zeros((rows, cols), jnp.float32)
+    fix = jnp.zeros((2, cols), jnp.float32)
     for k in range(kl_terms):
         j0 = partners[slot, 2 * k]
         j1 = partners[slot, 2 * k + 1]
@@ -147,10 +163,14 @@
         term = term - edges[3, k] * lf
         term = term - edges[4, k] * rt
         acc = acc + term
-    out[0] = acc
-
-
-def stencil_apply(every, coef, partners, weights):
+        fix = fix + c_rim[k] * (w0 * halo[j0] + w1 * halo[j1])
+    row = lax.broadcasted_iota(jnp.int32, (rows, cols), 0)
+    spread = jnp.where(row == 0, jnp.broadcast_to(fix[0:1], (rows, cols)), jnp.zeros((rows, cols), jnp.float32))
+    spread = jnp.where(row == rows - 1, jnp.broadcast_to(fix[1:2], (rows, cols)), spread)
+    out[0] = acc - spread
+
+
+def stencil_apply(every, halo, coef, c_rim, partners, weights):
     own_modes = partners.shape[0]
     kl_terms = coef.shape[0]
     rows = every.shape[1]
@@ -165,6 +185,8 @@
                 pl.BlockSpec(memory_space=pltpu.SMEM),
                 pl.BlockSpec(memory_space=pltpu.VMEM),
                 pl.BlockSpec(memory_space=pltpu.VMEM),
+                pl.BlockSpec(memory_space=pltpu.VMEM),
+                pl.BlockSpec(memory_space=pltpu.VMEM),
             ],
             out_specs=pl.BlockSpec((1, rows, cols), lambda i, p: (i, 0, 0)),
             scratch_shapes=[pltpu.VMEM((5, kl_terms, rows, cols), jnp.float32)],
@@ -172,47 +194,7 @@
         compiler_params=pltpu.CompilerParams(
             dimension_semantics=("arbitrary",), vmem_limit_bytes=48 * 1024 * 1024
         ),
-    )(partners, weights, every, coef)
-
-
-def rim_kernel(partners, weights, halo, c_rim, applied, out):
-    slot = pl.program_id(0)
-    kl_terms = c_rim.shape[0]
-    rows = out.shape[1]
-    cols = out.shape[2]
-    fix = jnp.zeros((2, cols), jnp.float32)
-    for k in range(kl_terms):
-        j0 = partners[slot, 2 * k]
-        j1 = partners[slot, 2 * k + 1]
-        w0 = weights[slot, 2 * k]
-        w1 = weights[slot, 2 * k + 1]
-        fix = fix + c_rim[k] * (w0 * halo[j0] + w1 * halo[j1])
-    row = lax.broadcasted_iota(jnp.int32, (rows, cols), 0)
-    zero = jnp.zeros((rows, cols), jnp.float32)
-    spread = jnp.where(row == 0, jnp.broadcast_to(fix[0:1], (rows, cols)), zero)
-    spread = jnp.where(row == rows - 1, jnp.broadcast_to(fix[1:2], (rows, cols)), spread)
-    out[0] = applied[0] - spread
-
-
-def rim_apply(applied, halo, c_rim, partners, weights):
-    own_modes, rows, cols = applied.shape
-    return pl.pallas_call(
-        rim_kernel,
-        out_shape=jax.ShapeDtypeStruct(applied.shape, jnp.float32),
-        grid_spec=pltpu.PrefetchScalarGridSpec(
-            num_scalar_prefetch=1,
-            grid=(own_modes,),
-            in_specs=[
-                pl.BlockSpec(memory_space=pltpu.SMEM),
-                pl.BlockSpec(memory_space=pltpu.VMEM),
-                pl.BlockSpec(memory_space=pltpu.VMEM),
-                pl.BlockSpec((1, rows, cols), lambda i, p: (i, 0, 0)),
-            ],
-            out_specs=pl.BlockSpec((1, rows, cols), lambda i, p: (i, 0, 0)),
-        ),
-        input_output_aliases={4: 0},
-        compiler_params=pltpu.CompilerParams(dimension_semantics=("arbitrary",)),
-    )(partners, weights, halo, c_rim, applied)
+    )(partners, weights, every, halo, coef, c_rim)
 
 
 def solution(mesh):

time: 122 us -> 155 us (1.27)
  the two profiles are of different devices: /device:TPU:1 before, /device:TPU:97 now
where the time goes in v6:
time: 155 us; the launch traced here: 154 us
  starting transfers between devices  65.4 us (42%)
  local copies, waits for them, and re-layouts  44.1 us (28%)
  waiting for transfers between devices  16.3 us (11%)
  other arithmetic  15.1 us (10%)
  Pallas kernels  12.8 us (8%)
    ppermute x9, starting transfers between devices, space_halo(): lax.ppermute(edge_last, 'space', up)  29.9 us
    ppermute x9, starting transfers between devices, space_halo(): lax.ppermute(edge_first, 'space', down)  21.5 us
    unnamed x26, local copies, waits for them, and re-layouts  20.9 us
    ppermute x9, waiting for transfers between devices, space_halo(): lax.ppermute(edge_first, 'space', down)  16.2 us
    pallas_call x1, Pallas kernels, stencil_apply(): pl.pallas_call(stencil_kernel, out_shape=jax.ShapeDtypeStruct((own_modes,...  12.8 us
    ppermute x8, starting transfers between devices, shifted(): lax.ppermute(x, 'chaos', [(c, (c + step) % count) for c in range(count)])  11 us
    slice x8, local copies, waits for them, and re-layouts, ring_gather(): a, b = space_halo(piece[:, rows - 1:], piece[:, :1])  6.5 us
    scatter-add x1, other arithmetic, coupling_table(): jnp.zeros((kl_terms * mode_count * mode_count,), jnp.float32).at[flat_index]  4.71 us
  transfers between devices with their start and end apart: 27, of which 5 were waited for; matrix products, arithmetic and copies ran while one was open for 36% of the time, Pallas kernels for 0%

profile of v6, /device:TPU:97, one launch (start us, length us, event | category | flops | bytes accessed | tf_op | source)
XLA Modules:
  0.0 154.3 jit_solution(9908046863530225421)
XLA Ops:
  2.7 2.9 %collective-permute-start.6 = (f32[15,8,2048]{2,1,0:T(8,128)}, f32[15,8,2048]{2,1,0:T(8,128)}, u32[]{:S(2)}, u32[]{:S(2)}) collective-permute-start(f32[15,8,2048]{2,1,0:T(8,128)} %param.7), channel_id=1, source_target_pairs={{0,16},{16,0},{32,48},{48,32},{64,80},{80,64},{96,112},{112,96},{1... | collective-permute-start | bytes 2949128 | tf_op jit(solution)/shard_map/ppermute | solution.py:61
  7.6 2.3 %collective-permute-start.1 = (f32[8,1,2048]{2,1,0:T(1,128)}, f32[8,1,2048]{2,1,0:T(1,128)S(1)}, u32[]{:S(2)}, u32[]{:S(2)}) collective-permute-start(f32[8,1,2048]{2,1,0:T(1,128)} %get-tuple-element.42), channel_id=1, source_target_pairs={{0,1},{1,2},{2,3},{3,4},{4,5},{5,6},{6,7},{7,8},{8,9},{9,10},{10,1... | collective-permute-start | bytes 196616 | tf_op jit(solution)/shard_map/ppermute | solution.py:89
  9.9 3.0 %collective-permute-start.2 = (f32[8,1,2048]{2,1,0:T(1,128)}, f32[8,1,2048]{2,1,0:T(1,128)}, u32[]{:S(2)}, u32[]{:S(2)}) collective-permute-start(f32[8,1,2048]{2,1,0:T(1,128)} %get-tuple-element.43), channel_id=1, source_target_pairs={{1,0},{2,1},{3,2},{4,3},{5,4},{6,5},{7,6},{8,7},{9,8},{10,9},{11,1... | collective-permute-start | bytes 196616 | tf_op jit(solution)/shard_map/ppermute | solution.py:89
  16.0 4.7 %scatter_custom_fusion = f32[115200]{0:T(1024)S(1)} fusion(s32[624]{0:T(1024)S(1)} %fusion.15, f32[624]{0:T(1024)S(1)} %fusion.17, f32[]{:T(128)} %constant.101.clone.1), kind=kCustom, calls=%fused_computation.8 | custom fusion | flops 624 | bytes 460804 | tf_op jit(solution)/shard_map/scatter-add | solution.py:35
  23.3 2.3 %constant_dynamic-update-slice_fusion.13 = f32[120,8,2048]{2,1,0:T(8,128)} fusion(f32[15,8,2048]{2,1,0:T(8,128)} %param.7), kind=kLoop, calls=%fused_computation.26 | loop fusion | bytes 1966080
  25.6 2.4 %fusion.26 = (f32[15,1,2048]{2,1,0:T(1,128)}, f32[15,1,2048]{2,1,0:T(1,128)}) fusion(f32[15,8,2048]{2,1,0:T(8,128)} %param.7), kind=kLoop, calls=%fused_computation.100 | loop fusion | bytes 491520 | tf_op jit(solution)/shard_map/slice | solution.py:77
  36.2 4.7 %collective-permute-start.11 = (f32[15,1,2048]{2,1,0:T(1,128)}, f32[15,1,2048]{2,1,0:T(1,128)S(1)}, u32[]{:S(2)}, u32[]{:S(2)}) collective-permute-start(f32[15,1,2048]{2,1,0:T(1,128)} %get-tuple-element.38), channel_id=1, source_target_pairs={{0,1},{1,2},{2,3},{3,4},{4,5},{5,6},{6,7},{7,8},{8,9},{9,10},{10,1... | collective-permute-start | bytes 368648 | tf_op jit(solution)/shard_map/ppermute | solution.py:89
  45.6 3.7 %collective-permute-done.19 = f32[15,1,2048]{2,1,0:T(1,128)S(1)} collective-permute-done((f32[15,1,2048]{2,1,0:T(1,128)}, f32[15,1,2048]{2,1,0:T(1,128)S(1)}, u32[]{:S(2)}, u32[]{:S(2)}) %collective-permute-start.19) | collective-permute-done | bytes 122912 | tf_op jit(solution)/shard_map/ppermute | solution.py:89
  51.7 2.7 %collective-permute-start.5 = (f32[15,8,1024]{2,1,0:T(8,128)}, f32[15,8,1024]{2,1,0:T(8,128)}, u32[]{:S(2)}, u32[]{:S(2)}) collective-permute-start(f32[15,8,1024]{2,1,0:T(8,128)} %slice.138), channel_id=1, source_target_pairs={{0,96},{16,112},{32,0},{48,16},{64,32},{80,48},{96,64},{112,80},{1... | collective-permute-start | bytes 1474568 | tf_op jit(solution)/shard_map/ppermute | solution.py:53
  55.2 2.6 %collective-permute-start.12 = (f32[15,1,2048]{2,1,0:T(1,128)}, f32[15,1,2048]{2,1,0:T(1,128)S(1)}, u32[]{:S(2)}, u32[]{:S(2)}) collective-permute-start(f32[15,1,2048]{2,1,0:T(1,128)} %get-tuple-element.36), channel_id=1, source_target_pairs={{0,1},{1,2},{2,3},{3,4},{4,5},{5,6},{6,7},{7,8},{8,9},{9,10},{10,1... | collective-permute-start | bytes 368648 | tf_op jit(solution)/shard_map/ppermute | solution.py:89
  66.7 2.4 %collective-permute-start.20 = (f32[15,1,2048]{2,1,0:T(1,128)}, f32[15,1,2048]{2,1,0:T(1,128)S(1)}, u32[]{:S(2)}, u32[]{:S(2)}) collective-permute-start(f32[15,1,2048]{2,1,0:T(1,128)} %get-tuple-element.37), channel_id=1, source_target_pairs={{1,0},{2,1},{3,2},{4,3},{5,4},{6,5},{7,6},{8,7},{9,8},{10,9},{11,1... | collective-permute-start | bytes 368648 | tf_op jit(solution)/shard_map/ppermute | solution.py:89
  69.7 3.6 %collective-permute-start.21 = (f32[15,1,2048]{2,1,0:T(1,128)S(1)}, f32[15,1,2048]{2,1,0:T(1,128)S(1)}, u32[]{:S(2)}, u32[]{:S(2)}) collective-permute-start(f32[15,1,2048]{2,1,0:T(1,128)S(1)} %get-tuple-element.35), channel_id=1, source_target_pairs={{1,0},{2,1},{3,2},{4,3},{5,4},{6,5},{7,6},{8,7},{9,8},{10,9},{11,1... | collective-permute-start | bytes 368648 | tf_op jit(solution)/shard_map/ppermute | solution.py:89
  78.7 2.7 %collective-permute-start.8 = (f32[15,8,2048]{2,1,0:T(8,128)}, f32[15,8,2048]{2,1,0:T(8,128)S(1)}, u32[]{:S(2)}, u32[]{:S(2)}) collective-permute-start(f32[15,8,2048]{2,1,0:T(8,128)} %collective-permute-done.6), channel_id=1, source_target_pairs={{0,96},{16,112},{32,0},{48,16},{64,32},{80,48},{96,64},{112,80},{1... | collective-permute-start | bytes 2949128 | tf_op jit(solution)/shard_map/ppermute | solution.py:53
  85.5 6.0 %collective-permute-start.14 = (f32[15,1,2048]{2,1,0:T(1,128)S(1)}, f32[15,1,2048]{2,1,0:T(1,128)S(1)}, u32[]{:S(2)}, u32[]{:S(2)}) collective-permute-start(f32[15,1,2048]{2,1,0:T(1,128)S(1)} %get-tuple-element.32), channel_id=1, source_target_pairs={{0,1},{1,2},{2,3},{3,4},{4,5},{5,6},{6,7},{7,8},{8,9},{9,10},{10,1... | collective-permute-start | bytes 368648 | tf_op jit(solution)/shard_map/ppermute | solution.py:89
  91.5 2.3 %constant_dynamic-update-slice_fusion.8 = f32[120,8,2048]{2,1,0:T(8,128)} fusion(f32[120,8,2048]{2,1,0:T(8,128)} %get-tuple-element.49, f32[15,8,2048]{2,1,0:T(8,128)} %collective-permute-done.6), kind=kLoop, calls=%fused_computation.21 | loop fusion | bytes 1966080
  97.0 5.3 %collective-permute-done.22 = f32[15,1,2048]{2,1,0:T(1,128)S(1)} collective-permute-done((f32[15,1,2048]{2,1,0:T(1,128)S(1)}, f32[15,1,2048]{2,1,0:T(1,128)S(1)}, u32[]{:S(2)}, u32[]{:S(2)}) %collective-permute-start.22) | collective-permute-done | bytes 122912 | tf_op jit(solution)/shard_map/ppermute | solution.py:89
  103.9 2.9 %collective-permute-start.10 = (f32[15,8,1024]{2,1,0:T(8,128)S(1)}, f32[15,8,1024]{2,1,0:T(8,128)S(1)}, u32[]{:S(2)}, u32[]{:S(2)}) collective-permute-start(f32[15,8,1024]{2,1,0:T(8,128)S(1)} %slice.140), channel_id=1, source_target_pairs={{0,96},{16,112},{32,0},{48,16},{64,32},{80,48},{96,64},{112,80},{1... | collective-permute-start | bytes 1474568 | tf_op jit(solution)/shard_map/ppermute | solution.py:53
  106.9 3.4 %collective-permute-start.16 = (f32[15,1,2048]{2,1,0:T(1,128)S(1)}, f32[15,1,2048]{2,1,0:T(1,128)S(1)}, u32[]{:S(2)}, u32[]{:S(2)}) collective-permute-start(f32[15,1,2048]{2,1,0:T(1,128)S(1)} %get-tuple-element.28), channel_id=1, source_target_pairs={{0,1},{1,2},{2,3},{3,4},{4,5},{5,6},{6,7},{7,8},{8,9},{9,10},{10,1... | collective-permute-start | bytes 368648 | tf_op jit(solution)/shard_map/ppermute | solution.py:89
  112.4 2.4 %collective-permute-start.24 = (f32[15,1,2048]{2,1,0:T(1,128)S(1)}, f32[15,1,2048]{2,1,0:T(1,128)S(1)}, u32[]{:S(2)}, u32[]{:S(2)}) collective-permute-start(f32[15,1,2048]{2,1,0:T(1,128)S(1)} %get-tuple-element.29), channel_id=1, source_target_pairs={{1,0},{2,1},{3,2},{4,3},{5,4},{6,5},{7,6},{8,7},{9,8},{10,9},{11,1... | collective-permute-start | bytes 368648 | tf_op jit(solution)/shard_map/ppermute | solution.py:89
  116.9 2.5 %collective-permute-start.25 = (f32[15,1,2048]{2,1,0:T(1,128)S(1)}, f32[15,1,2048]{2,1,0:T(1,128)S(1)}, u32[]{:S(2)}, u32[]{:S(2)}) collective-permute-start(f32[15,1,2048]{2,1,0:T(1,128)S(1)} %get-tuple-element.27), channel_id=1, source_target_pairs={{1,0},{2,1},{3,2},{4,3},{5,4},{6,5},{7,6},{8,7},{9,8},{10,9},{11,1... | collective-permute-start | bytes 368648 | tf_op jit(solution)/shard_map/ppermute | solution.py:89
  123.4 5.2 %collective-permute-start.18 = (f32[15,1,2048]{2,1,0:T(1,128)S(1)}, f32[15,1,2048]{2,1,0:T(1,128)S(1)}, u32[]{:S(2)}, u32[]{:S(2)}) collective-permute-start(f32[15,1,2048]{2,1,0:T(1,128)S(1)} %get-tuple-element.24), channel_id=1, source_target_pairs={{0,1},{1,2},{2,3},{3,4},{4,5},{5,6},{6,7},{7,8},{8,9},{9,10},{10,1... | collective-permute-start | bytes 368648 | tf_op jit(solution)/shard_map/ppermute | solution.py:89
  131.8 5.7 %collective-permute-done.26 = f32[15,1,2048]{2,1,0:T(1,128)S(1)} collective-permute-done((f32[15,1,2048]{2,1,0:T(1,128)S(1)}, f32[15,1,2048]{2,1,0:T(1,128)S(1)}, u32[]{:S(2)}, u32[]{:S(2)}) %collective-permute-start.26) | collective-permute-done | bytes 122912 | tf_op jit(solution)/shard_map/ppermute | solution.py:89
  138.2 3.3 %pad_maximum_fusion.halo = f32[120,2,2048]{2,1,0:T(2,128)S(1)} fusion(f32[120,1,2048]{2,1,0:T(1,128)} %constant_dynamic-update-slice_fusion.22, f32[120,1,2048]{2,1,0:T(1,128)} %constant_dynamic-update-slice_fusion.14), kind=kLoop, calls=%fused_computation.5 | loop fusion | flops 491520 | bytes 3932160 | tf_op jit(solution)/shard_map/concatenate | solution.py:81
  141.5 12.8 %shard_map.55 = f32[15,8,2048]{2,1,0:T(8,128)} custom-call(s32[15,16]{1,0:T(8,128)S(1)} %copy.16.partners, f32[15,16]{1,0:T(8,128)S(1)} %copy.17.weights, f32[120,8,2048]{2,1,0:T(8,128)} %get-tuple-element.45.every, f32[120,2,2048]{2,1,0:T(2,128)S(1)} %pad_maximum_fusion.halo, f32[8,10,2048]{2,1,0:T(8,128)S(1)} %pad_maximum_fusion.1.coef, ...), custom_call_target="tpu_custom_call" | custom-call | tf_op jit(solution)/shard_map/pallas_call | solution.py:178
  (121 shorter events, 62.0 us)
Async XLA Ops:
  0.0 50.0 %collective-permute-start = (f32[15,8,2048]{2,1,0:T(8,128)}, f32[15,8,2048]{2,1,0:T(8,128)S(1)}, u32[]{:S(2)}, u32[]{:S(2)}) collective-permute-start(f32[15,8,2048]{2,1,0:T(8,128)} %param.7), channel_id=1, source_target_pairs={{0,32},{16,48},{32,64},{48,80},{64,96},{80,112},{96,0},{112,16},{1... | collective-permute-start | bytes 2949128 | tf_op jit(solution)/shard_map/ppermute | solution.py:53
  1.2 49.6 %collective-permute-start.3 = (f32[15,8,2048]{2,1,0:T(8,128)}, f32[15,8,2048]{2,1,0:T(8,128)S(1)}, u32[]{:S(2)}, u32[]{:S(2)}) collective-permute-start(f32[15,8,2048]{2,1,0:T(8,128)} %param.7), channel_id=1, source_target_pairs={{0,96},{16,112},{32,0},{48,16},{64,32},{80,48},{96,64},{112,80},{1... | collective-permute-start | bytes 2949128 | tf_op jit(solution)/shard_map/ppermute | solution.py:53
  2.7 59.0 %collective-permute-start.6 = (f32[15,8,2048]{2,1,0:T(8,128)}, f32[15,8,2048]{2,1,0:T(8,128)}, u32[]{:S(2)}, u32[]{:S(2)}) collective-permute-start(f32[15,8,2048]{2,1,0:T(8,128)} %param.7), channel_id=1, source_target_pairs={{0,16},{16,0},{32,48},{48,32},{64,80},{80,64},{96,112},{112,96},{1... | collective-permute-start | bytes 2949128 | tf_op jit(solution)/shard_map/ppermute | solution.py:61
  7.6 28.5 %collective-permute-start.1 = (f32[8,1,2048]{2,1,0:T(1,128)}, f32[8,1,2048]{2,1,0:T(1,128)S(1)}, u32[]{:S(2)}, u32[]{:S(2)}) collective-permute-start(f32[8,1,2048]{2,1,0:T(1,128)} %get-tuple-element.42), channel_id=1, source_target_pairs={{0,1},{1,2},{2,3},{3,4},{4,5},{5,6},{6,7},{7,8},{8,9},{9,10},{10,1... | collective-permute-start | bytes 196616 | tf_op jit(solution)/shard_map/ppermute | solution.py:89
  9.9 30.9 %collective-permute-start.2 = (f32[8,1,2048]{2,1,0:T(1,128)}, f32[8,1,2048]{2,1,0:T(1,128)}, u32[]{:S(2)}, u32[]{:S(2)}) collective-permute-start(f32[8,1,2048]{2,1,0:T(1,128)} %get-tuple-element.43), channel_id=1, source_target_pairs={{1,0},{2,1},{3,2},{4,3},{5,4},{6,5},{7,6},{8,7},{9,8},{10,9},{11,1... | collective-permute-start | bytes 196616 | tf_op jit(solution)/shard_map/ppermute | solution.py:89
  36.2 8.8 %collective-permute-start.11 = (f32[15,1,2048]{2,1,0:T(1,128)}, f32[15,1,2048]{2,1,0:T(1,128)S(1)}, u32[]{:S(2)}, u32[]{:S(2)}) collective-permute-start(f32[15,1,2048]{2,1,0:T(1,128)} %get-tuple-element.38), channel_id=1, source_target_pairs={{0,1},{1,2},{2,3},{3,4},{4,5},{5,6},{6,7},{7,8},{8,9},{9,10},{10,1... | collective-permute-start | bytes 368648 | tf_op jit(solution)/shard_map/ppermute | solution.py:89
  40.8 8.5 %collective-permute-start.19 = (f32[15,1,2048]{2,1,0:T(1,128)}, f32[15,1,2048]{2,1,0:T(1,128)S(1)}, u32[]{:S(2)}, u32[]{:S(2)}) collective-permute-start(f32[15,1,2048]{2,1,0:T(1,128)} %get-tuple-element.39), channel_id=1, source_target_pairs={{1,0},{2,1},{3,2},{4,3},{5,4},{6,5},{7,6},{8,7},{9,8},{10,9},{11,1... | collective-permute-start | bytes 368648 | tf_op jit(solution)/shard_map/ppermute | solution.py:89
  50.8 27.9 %collective-permute-start.4 = (f32[15,8,1024]{2,1,0:T(8,128)}, f32[15,8,1024]{2,1,0:T(8,128)}, u32[]{:S(2)}, u32[]{:S(2)}) collective-permute-start(f32[15,8,1024]{2,1,0:T(8,128)} %slice.94), channel_id=1, source_target_pairs={{0,32},{16,48},{32,64},{48,80},{64,96},{80,112},{96,0},{112,16},{1... | collective-permute-start | bytes 1474568 | tf_op jit(solution)/shard_map/ppermute | solution.py:53
  51.7 31.6 %collective-permute-start.5 = (f32[15,8,1024]{2,1,0:T(8,128)}, f32[15,8,1024]{2,1,0:T(8,128)}, u32[]{:S(2)}, u32[]{:S(2)}) collective-permute-start(f32[15,8,1024]{2,1,0:T(8,128)} %slice.138), channel_id=1, source_target_pairs={{0,96},{16,112},{32,0},{48,16},{64,32},{80,48},{96,64},{112,80},{1... | collective-permute-start | bytes 1474568 | tf_op jit(solution)/shard_map/ppermute | solution.py:53
  55.2 11.4 %collective-permute-start.12 = (f32[15,1,2048]{2,1,0:T(1,128)}, f32[15,1,2048]{2,1,0:T(1,128)S(1)}, u32[]{:S(2)}, u32[]{:S(2)}) collective-permute-start(f32[15,1,2048]{2,1,0:T(1,128)} %get-tuple-element.36), channel_id=1, source_target_pairs={{0,1},{1,2},{2,3},{3,4},{4,5},{5,6},{6,7},{7,8},{8,9},{9,10},{10,1... | collective-permute-start | bytes 368648 | tf_op jit(solution)/shard_map/ppermute | solution.py:89
  58.6 11.1 %collective-permute-start.13 = (f32[15,1,2048]{2,1,0:T(1,128)}, f32[15,1,2048]{2,1,0:T(1,128)S(1)}, u32[]{:S(2)}, u32[]{:S(2)}) collective-permute-start(f32[15,1,2048]{2,1,0:T(1,128)} %get-tuple-element.34), channel_id=1, source_target_pairs={{0,1},{1,2},{2,3},{3,4},{4,5},{5,6},{6,7},{7,8},{8,9},{9,10},{10,1... | collective-permute-start | bytes 368648 | tf_op jit(solution)/shard_map/ppermute | solution.py:89
  63.5 32.8 %collective-permute-start.15 = (f32[15,1,2048]{2,1,0:T(1,128)S(1)}, f32[15,1,2048]{2,1,0:T(1,128)S(1)}, u32[]{:S(2)}, u32[]{:S(2)}) collective-permute-start(f32[15,1,2048]{2,1,0:T(1,128)S(1)} %get-tuple-element.30), channel_id=1, source_target_pairs={{0,1},{1,2},{2,3},{3,4},{4,5},{5,6},{6,7},{7,8},{8,9},{9,10},{10,1... | collective-permute-start | bytes 368648 | tf_op jit(solution)/shard_map/ppermute | solution.py:89
  66.7 8.5 %collective-permute-start.20 = (f32[15,1,2048]{2,1,0:T(1,128)}, f32[15,1,2048]{2,1,0:T(1,128)S(1)}, u32[]{:S(2)}, u32[]{:S(2)}) collective-permute-start(f32[15,1,2048]{2,1,0:T(1,128)} %get-tuple-element.37), channel_id=1, source_target_pairs={{1,0},{2,1},{3,2},{4,3},{5,4},{6,5},{7,6},{8,7},{9,8},{10,9},{11,1... | collective-permute-start | bytes 368648 | tf_op jit(solution)/shard_map/ppermute | solution.py:89
  75.2 27.8 %collective-permute-start.23 = (f32[15,1,2048]{2,1,0:T(1,128)S(1)}, f32[15,1,2048]{2,1,0:T(1,128)S(1)}, u32[]{:S(2)}, u32[]{:S(2)}) collective-permute-start(f32[15,1,2048]{2,1,0:T(1,128)S(1)} %get-tuple-element.31), channel_id=1, source_target_pairs={{1,0},{2,1},{3,2},{4,3},{5,4},{6,5},{7,6},{8,7},{9,8},{10,9},{11,1... | collective-permute-start | bytes 368648 | tf_op jit(solution)/shard_map/ppermute | solution.py:89
  78.0 25.6 %collective-permute-start.7 = (f32[15,8,2048]{2,1,0:T(8,128)}, f32[15,8,2048]{2,1,0:T(8,128)S(1)}, u32[]{:S(2)}, u32[]{:S(2)}) collective-permute-start(f32[15,8,2048]{2,1,0:T(8,128)} %collective-permute-done.6), channel_id=1, source_target_pairs={{0,32},{16,48},{32,64},{48,80},{64,96},{80,112},{96,0},{112,16},{1... | collective-permute-start | bytes 2949128 | tf_op jit(solution)/shard_map/ppermute | solution.py:53
  78.7 25.1 %collective-permute-start.8 = (f32[15,8,2048]{2,1,0:T(8,128)}, f32[15,8,2048]{2,1,0:T(8,128)S(1)}, u32[]{:S(2)}, u32[]{:S(2)}) collective-permute-start(f32[15,8,2048]{2,1,0:T(8,128)} %collective-permute-done.6), channel_id=1, source_target_pairs={{0,96},{16,112},{32,0},{48,16},{64,32},{80,48},{96,64},{112,80},{1... | collective-permute-start | bytes 2949128 | tf_op jit(solution)/shard_map/ppermute | solution.py:53
  85.5 8.3 %collective-permute-start.14 = (f32[15,1,2048]{2,1,0:T(1,128)S(1)}, f32[15,1,2048]{2,1,0:T(1,128)S(1)}, u32[]{:S(2)}, u32[]{:S(2)}) collective-permute-start(f32[15,1,2048]{2,1,0:T(1,128)S(1)} %get-tuple-element.32), channel_id=1, source_target_pairs={{0,1},{1,2},{2,3},{3,4},{4,5},{5,6},{6,7},{7,8},{8,9},{9,10},{10,1... | collective-permute-start | bytes 368648 | tf_op jit(solution)/shard_map/ppermute | solution.py:89
  93.8 8.6 %collective-permute-start.22 = (f32[15,1,2048]{2,1,0:T(1,128)S(1)}, f32[15,1,2048]{2,1,0:T(1,128)S(1)}, u32[]{:S(2)}, u32[]{:S(2)}) collective-permute-start(f32[15,1,2048]{2,1,0:T(1,128)S(1)} %get-tuple-element.33), channel_id=1, source_target_pairs={{1,0},{2,1},{3,2},{4,3},{5,4},{6,5},{7,6},{8,7},{9,8},{10,9},{11,1... | collective-permute-start | bytes 368648 | tf_op jit(solution)/shard_map/ppermute | solution.py:89
  103.7 17.6 %collective-permute-start.9 = (f32[15,8,1024]{2,1,0:T(8,128)S(1)}, f32[15,8,1024]{2,1,0:T(8,128)S(1)}, u32[]{:S(2)}, u32[]{:S(2)}) collective-permute-start(f32[15,8,1024]{2,1,0:T(8,128)S(1)} %slice.139), channel_id=1, source_target_pairs={{0,32},{16,48},{32,64},{48,80},{64,96},{80,112},{96,0},{112,16},{1... | collective-permute-start | bytes 1474568 | tf_op jit(solution)/shard_map/ppermute | solution.py:53
  103.9 18.5 %collective-permute-start.10 = (f32[15,8,1024]{2,1,0:T(8,128)S(1)}, f32[15,8,1024]{2,1,0:T(8,128)S(1)}, u32[]{:S(2)}, u32[]{:S(2)}) collective-permute-start(f32[15,8,1024]{2,1,0:T(8,128)S(1)} %slice.140), channel_id=1, source_target_pairs={{0,96},{16,112},{32,0},{48,16},{64,32},{80,48},{96,64},{112,80},{1... | collective-permute-start | bytes 1474568 | tf_op jit(solution)/shard_map/ppermute | solution.py:53
  106.9 10.0 %collective-permute-start.16 = (f32[15,1,2048]{2,1,0:T(1,128)S(1)}, f32[15,1,2048]{2,1,0:T(1,128)S(1)}, u32[]{:S(2)}, u32[]{:S(2)}) collective-permute-start(f32[15,1,2048]{2,1,0:T(1,128)S(1)} %get-tuple-element.28), channel_id=1, source_target_pairs={{0,1},{1,2},{2,3},{3,4},{4,5},{5,6},{6,7},{7,8},{8,9},{9,10},{10,1... | collective-permute-start | bytes 368648 | tf_op jit(solution)/shard_map/ppermute | solution.py:89
  110.5 9.6 %collective-permute-start.17 = (f32[15,1,2048]{2,1,0:T(1,128)S(1)}, f32[15,1,2048]{2,1,0:T(1,128)S(1)}, u32[]{:S(2)}, u32[]{:S(2)}) collective-permute-start(f32[15,1,2048]{2,1,0:T(1,128)S(1)} %get-tuple-element.26), channel_id=1, source_target_pairs={{0,1},{1,2},{2,3},{3,4},{4,5},{5,6},{6,7},{7,8},{8,9},{9,10},{10,1... | collective-permute-start | bytes 368648 | tf_op jit(solution)/shard_map/ppermute | solution.py:89
  112.4 8.3 %collective-permute-start.24 = (f32[15,1,2048]{2,1,0:T(1,128)S(1)}, f32[15,1,2048]{2,1,0:T(1,128)S(1)}, u32[]{:S(2)}, u32[]{:S(2)}) collective-permute-start(f32[15,1,2048]{2,1,0:T(1,128)S(1)} %get-tuple-element.29), channel_id=1, source_target_pairs={{1,0},{2,1},{3,2},{4,3},{5,4},{6,5},{7,6},{8,7},{9,8},{10,9},{11,1... | collective-permute-start | bytes 368648 | tf_op jit(solution)/shard_map/ppermute | solution.py:89
  116.9 11.7 %collective-permute-start.25 = (f32[15,1,2048]{2,1,0:T(1,128)S(1)}, f32[15,1,2048]{2,1,0:T(1,128)S(1)}, u32[]{:S(2)}, u32[]{:S(2)}) collective-permute-start(f32[15,1,2048]{2,1,0:T(1,128)S(1)} %get-tuple-element.27), channel_id=1, source_target_pairs={{1,0},{2,1},{3,2},{4,3},{5,4},{6,5},{7,6},{8,7},{9,8},{10,9},{11,1... | collective-permute-start | bytes 368648 | tf_op jit(solution)/shard_map/ppermute | solution.py:89
  (5 other events, 45.7 us)

commit v7 on v6

--- a/solution.py
+++ b/solution.py
@@ -56,7 +56,6 @@
 def ring_gather(block, tables):
     count = lax.axis_size("chaos")
     me = lax.axis_index("chaos")
-    rows = block.shape[1]
     half = block.shape[-1] // 2
     partner = lax.ppermute(block, "chaos", [(c, c ^ 1) for c in range(count)])
     pieces = []
@@ -71,15 +70,7 @@
         )
         pieces += [base, from_left, from_right, far]
         owners += [origin, (origin - 2) % count, (origin + 2) % count, (origin + 4) % count]
-    above = []
-    below = []
-    for piece in pieces:
-        a, b = space_halo(piece[:, rows - 1:], piece[:, :1])
-        above.append(a)
-        below.append(b)
-    every = jnp.concatenate(pieces, axis=0)
-    halo = jnp.concatenate([jnp.concatenate(above, axis=0), jnp.concatenate(below, axis=0)], axis=1)
-    return every, halo, jnp.stack(owners).astype(jnp.int32), tables
+    return jnp.concatenate(pieces, axis=0), tables
 
 
 def space_halo(edge_last, edge_first):
@@ -95,11 +86,10 @@
     mode_count = own_modes * groups
     kl_terms = kl_fields.shape[0]
     rows = modes.shape[1]
-    count = lax.axis_size("chaos")
     me = lax.axis_index("chaos")
     order = jnp.stack(
-        [me, (me - 2) % count, (me + 2) % count, (me + 4) % count,
-         me ^ 1, ((me ^ 1) - 2) % count, ((me ^ 1) + 2) % count, ((me ^ 1) + 4) % count]
+        [me, (me - 2) % groups, (me + 2) % groups, (me + 4) % groups,
+         me ^ 1, ((me ^ 1) - 2) % groups, ((me ^ 1) + 2) % groups, ((me ^ 1) + 4) % groups]
     ).astype(jnp.int32)
 
     first_slot = me * own_modes
@@ -116,14 +106,20 @@
 
     above, below = space_halo(kl_fields[:, rows - 1:], kl_fields[:, :1])
     coef = jnp.concatenate([above, kl_fields, below], axis=1)
-    c_rim = 0.5 * jnp.concatenate([coef[:, 1:2] + coef[:, :1], coef[:, rows:rows + 1] + coef[:, rows + 1:]], axis=1)
-
-    every, halo, _, tables = ring_gather(modes, (partners, weights, coef, c_rim))
-    partners, weights, coef, c_rim = tables
-    return stencil_apply(every, halo, coef, c_rim, partners, weights)
-
-
-def stencil_kernel(partners, weights, every, halo, coef, c_rim, out, edges):
+
+    every, tables = ring_gather(modes, (partners, weights, coef))
+    partners, weights, coef = tables
+    applied, to_prev, to_next = stencil_apply(every, coef, partners, weights)
+
+    from_prev, from_next = space_halo(to_next, to_prev)
+    top = applied[:, :1] - from_prev[:, None]
+    bottom = applied[:, rows - 1:] - from_next[:, None]
+    applied = lax.dynamic_update_slice_in_dim(applied, top, 0, 1)
+    applied = lax.dynamic_update_slice_in_dim(applied, bottom, rows - 1, 1)
+    return applied
+
+
+def stencil_kernel(partners, weights, every, coef, out, to_prev, to_next, edges):
     slot = pl.program_id(0)
     kl_terms = coef.shape[0]
     rows = out.shape[1]
@@ -145,9 +141,10 @@
             edges[2, k] = jnp.where(row == rows - 1, zero, c_dn)
             edges[3, k] = jnp.where(column == 0, zero, c_lf)
             edges[4, k] = jnp.where(column == cols - 1, zero, c_rt)
+            edges[5, k] = jnp.where(row == 0, c_up, jnp.where(row == rows - 1, c_dn, zero))
 
     acc = jnp.zeros((rows, cols), jnp.float32)
-    fix = jnp.zeros((2, cols), jnp.float32)
+    rim = jnp.zeros((rows, cols), jnp.float32)
     for k in range(kl_terms):
         j0 = partners[slot, 2 * k]
         j1 = partners[slot, 2 * k + 1]
@@ -163,21 +160,24 @@
         term = term - edges[3, k] * lf
         term = term - edges[4, k] * rt
         acc = acc + term
-        fix = fix + c_rim[k] * (w0 * halo[j0] + w1 * halo[j1])
-    row = lax.broadcasted_iota(jnp.int32, (rows, cols), 0)
-    spread = jnp.where(row == 0, jnp.broadcast_to(fix[0:1], (rows, cols)), jnp.zeros((rows, cols), jnp.float32))
-    spread = jnp.where(row == rows - 1, jnp.broadcast_to(fix[1:2], (rows, cols)), spread)
-    out[0] = acc - spread
-
-
-def stencil_apply(every, halo, coef, c_rim, partners, weights):
+        rim = rim + edges[5, k] * center
+    out[0] = acc
+    to_prev[pl.ds(slot, 1), :] = rim[0:1]
+    to_next[pl.ds(slot, 1), :] = rim[rows - 1:rows]
+
+
+def stencil_apply(every, coef, partners, weights):
     own_modes = partners.shape[0]
     kl_terms = coef.shape[0]
     rows = every.shape[1]
     cols = every.shape[2]
     return pl.pallas_call(
         stencil_kernel,
-        out_shape=jax.ShapeDtypeStruct((own_modes, rows, cols), jnp.float32),
+        out_shape=(
+            jax.ShapeDtypeStruct((own_modes, rows, cols), jnp.float32),
+            jax.ShapeDtypeStruct((own_modes, cols), jnp.float32),
+            jax.ShapeDtypeStruct((own_modes, cols), jnp.float32),
+        ),
         grid_spec=pltpu.PrefetchScalarGridSpec(
             num_scalar_prefetch=1,
             grid=(own_modes,),
@@ -185,16 +185,18 @@
                 pl.BlockSpec(memory_space=pltpu.SMEM),
                 pl.BlockSpec(memory_space=pltpu.VMEM),
                 pl.BlockSpec(memory_space=pltpu.VMEM),
-                pl.BlockSpec(memory_space=pltpu.VMEM),
-                pl.BlockSpec(memory_space=pltpu.VMEM),
             ],
-            out_specs=pl.BlockSpec((1, rows, cols), lambda i, p: (i, 0, 0)),
-            scratch_shapes=[pltpu.VMEM((5, kl_terms, rows, cols), jnp.float32)],
+            out_specs=(
+                pl.BlockSpec((1, rows, cols), lambda i, p: (i, 0, 0)),
+                pl.BlockSpec(memory_space=pltpu.VMEM),
+                pl.BlockSpec(memory_space=pltpu.VMEM),
+            ),
+            scratch_shapes=[pltpu.VMEM((6, kl_terms, rows, cols), jnp.float32)],
         ),
         compiler_params=pltpu.CompilerParams(
             dimension_semantics=("arbitrary",), vmem_limit_bytes=48 * 1024 * 1024
         ),
-    )(partners, weights, every, halo, coef, c_rim)
+    )(partners, weights, every, coef)
 
 
 def solution(mesh):

time: 155 us -> 128 us (0.83)
  the two profiles are of different devices: /device:TPU:97 before, /device:TPU:1 now
where the time goes in v7:
time: 128 us; the launch traced here: 127 us
  waiting for transfers between devices  35.8 us (28%)
  local copies, waits for them, and re-layouts  31.5 us (25%)
  starting transfers between devices  28.3 us (22%)
  other arithmetic  18.1 us (14%)
  Pallas kernels  12.8 us (10%)
    ppermute x8, waiting for transfers between devices, shifted(): lax.ppermute(x, 'chaos', [(c, (c + step) % count) for c in range(count)])  33.2 us
    pallas_call x1, Pallas kernels, stencil_apply(): pl.pallas_call(stencil_kernel, out_shape=(jax.ShapeDtypeStruct((own_modes...  12.8 us
    ppermute x8, starting transfers between devices, shifted(): lax.ppermute(x, 'chaos', [(c, (c + step) % count) for c in range(count)])  11.9 us
    ppermute x2, starting transfers between devices, space_halo(): lax.ppermute(edge_last, 'space', up)  9.53 us
    unnamed x10, local copies, waits for them, and re-layouts  7.51 us
    scatter-add x1, other arithmetic, coupling_table(): jnp.zeros((kl_terms * mode_count * mode_count,), jnp.float32).at[flat_index]  4.71 us
    ppermute x2, starting transfers between devices, space_halo(): lax.ppermute(edge_first, 'space', down)  3.84 us
    dynamic_update_slice x1, local copies, waits for them, and re-layouts, local(): applied = lax.dynamic_update_slice_in_dim(applied, top, 0, 1)  3.51 us
  transfers between devices with their start and end apart: 13, of which 6 were waited for; matrix products, arithmetic and copies ran while one was open for 33% of the time, Pallas kernels for 0%

profile of v7, /device:TPU:1, one launch (start us, length us, event | category | flops | bytes accessed | tf_op | source)
XLA Modules:
  0.0 127.0 jit_solution(2143424536929181660)
XLA Ops:
  0.0 2.0 %collective-permute-start = (f32[15,8,2048]{2,1,0:T(8,128)}, f32[15,8,2048]{2,1,0:T(8,128)S(1)}, u32[]{:S(2)}, u32[]{:S(2)}) collective-permute-start(f32[15,8,2048]{2,1,0:T(8,128)} %param.7), channel_id=1, source_target_pairs={{0,32},{16,48},{32,64},{48,80},{64,96},{80,112},{96,0},{112,16},{1... | collective-permute-start | bytes 2949128 | tf_op jit(solution)/shard_map/ppermute | solution.py:53
  3.3 3.1 %collective-permute-start.6 = (f32[15,8,2048]{2,1,0:T(8,128)}, f32[15,8,2048]{2,1,0:T(8,128)}, u32[]{:S(2)}, u32[]{:S(2)}) collective-permute-start(f32[15,8,2048]{2,1,0:T(8,128)} %param.7), channel_id=1, source_target_pairs={{0,16},{16,0},{32,48},{48,32},{64,80},{80,64},{96,112},{112,96},{1... | collective-permute-start | bytes 2949128 | tf_op jit(solution)/shard_map/ppermute | solution.py:60
  6.4 1.9 %fusion.19 = (f32[8,1,2048]{2,1,0:T(1,128)}, f32[8,1,2048]{2,1,0:T(1,128)}) fusion(f32[8,8,2048]{2,1,0:T(8,128)} %param.8), kind=kLoop, calls=%fused_computation.69 | loop fusion | bytes 262144 | tf_op jit(solution)/shard_map/slice | solution.py:107
  8.4 4.9 %collective-permute-start.1 = (f32[8,1,2048]{2,1,0:T(1,128)}, f32[8,1,2048]{2,1,0:T(1,128)}, u32[]{:S(2)}, u32[]{:S(2)}) collective-permute-start(f32[8,1,2048]{2,1,0:T(1,128)} %get-tuple-element.30), channel_id=1, source_target_pairs={{0,1},{1,2},{2,3},{3,4},{4,5},{5,6},{6,7},{7,8},{8,9},{9,10},{10,1... | collective-permute-start | bytes 196616 | tf_op jit(solution)/shard_map/ppermute | solution.py:80
  13.3 1.9 %collective-permute-start.2 = (f32[8,1,2048]{2,1,0:T(1,128)}, f32[8,1,2048]{2,1,0:T(1,128)}, u32[]{:S(2)}, u32[]{:S(2)}) collective-permute-start(f32[8,1,2048]{2,1,0:T(1,128)} %get-tuple-element.31), channel_id=1, source_target_pairs={{1,0},{2,1},{3,2},{4,3},{5,4},{6,5},{7,6},{8,7},{9,8},{10,9},{11,1... | collective-permute-start | bytes 196616 | tf_op jit(solution)/shard_map/ppermute | solution.py:80
  18.3 4.7 %scatter_custom_fusion = f32[115200]{0:T(1024)S(1)} fusion(s32[624]{0:T(1024)S(1)} %fusion.15, f32[624]{0:T(1024)S(1)} %fusion.17, f32[]{:T(128)} %constant.101.clone.1), kind=kCustom, calls=%fused_computation.9 | custom fusion | flops 624 | bytes 460804 | tf_op jit(solution)/shard_map/scatter-add | solution.py:35
  28.1 2.1 %gather_fusion.3 = f32[120]{0:T(128)S(1)} fusion(f32[8,15,120]{2,1,0:T(8,128)S(1)} %get-tuple-element.27, s32[120]{0:T(128)S(1)} %reshape.104), kind=kCustom, calls=%fused_computation.1.clone | custom fusion | bytes 2400 | tf_op jit(solution)/shard_map/jit(take_along_axis)/gather | solution.py:46
  31.6 2.1 %gather_fusion.2 = f32[120]{0:T(128)S(1)} fusion(f32[8,15,120]{2,1,0:T(8,128)S(1)} %get-tuple-element.27, s32[120]{0:T(128)S(1)} %reshape.98), kind=kCustom, calls=%fused_computation.clone | custom fusion | bytes 2400 | tf_op jit(solution)/shard_map/jit(take_along_axis)/gather | solution.py:45
  43.6 2.7 %collective-permute-start.5 = (f32[15,8,1024]{2,1,0:T(8,128)}, f32[15,8,1024]{2,1,0:T(8,128)}, u32[]{:S(2)}, u32[]{:S(2)}) collective-permute-start(f32[15,8,1024]{2,1,0:T(8,128)} %slice.80), channel_id=1, source_target_pairs={{0,96},{16,112},{32,0},{48,16},{64,32},{80,48},{96,64},{112,80},{1... | collective-permute-start | bytes 1474568 | tf_op jit(solution)/shard_map/ppermute | solution.py:53
  47.1 2.7 %collective-permute-start.8 = (f32[15,8,2048]{2,1,0:T(8,128)}, f32[15,8,2048]{2,1,0:T(8,128)S(1)}, u32[]{:S(2)}, u32[]{:S(2)}) collective-permute-start(f32[15,8,2048]{2,1,0:T(8,128)} %collective-permute-done.6), channel_id=1, source_target_pairs={{0,96},{16,112},{32,0},{48,16},{64,32},{80,48},{96,64},{112,80},{1... | collective-permute-start | bytes 2949128 | tf_op jit(solution)/shard_map/ppermute | solution.py:53
  51.9 5.3 %collective-permute-done.4 = f32[15,8,1024]{2,1,0:T(8,128)} collective-permute-done((f32[15,8,1024]{2,1,0:T(8,128)S(1)}, f32[15,8,1024]{2,1,0:T(8,128)}, u32[]{:S(2)}, u32[]{:S(2)}) %collective-permute-start.4) | collective-permute-done | bytes 491552 | tf_op jit(solution)/shard_map/ppermute | solution.py:53
  57.6 2.2 %maximum_dynamic-update-slice_fusion.1 = f32[120,8,2048]{2,1,0:T(8,128)} fusion(f32[120,8,2048]{2,1,0:T(8,128)} %constant_dynamic-update-slice_fusion.3, f32[15,8,1024]{2,1,0:T(8,128)} %collective-permute-done.5, f32[15,8,1024]{2,1,0:T(8,128)} %collective-permute-done.4), kind=kLoop, calls=%fused_computation.7 | loop fusion | flops 245760 | bytes 1966080
  59.8 2.3 %constant_dynamic-update-slice_fusion.2 = f32[120,8,2048]{2,1,0:T(8,128)} fusion(f32[120,8,2048]{2,1,0:T(8,128)} %maximum_dynamic-update-slice_fusion.1, f32[15,8,2048]{2,1,0:T(8,128)} %collective-permute-done.6), kind=kLoop, calls=%fused_computation.18 | loop fusion | bytes 1966080
  62.1 15.2 %collective-permute-done.8 = f32[15,8,2048]{2,1,0:T(8,128)S(1)} collective-permute-done((f32[15,8,2048]{2,1,0:T(8,128)}, f32[15,8,2048]{2,1,0:T(8,128)S(1)}, u32[]{:S(2)}, u32[]{:S(2)}) %collective-permute-start.8) | collective-permute-done | bytes 983072 | tf_op jit(solution)/shard_map/ppermute | solution.py:53
  77.3 3.1 %collective-permute-start.10 = (f32[15,8,1024]{2,1,0:T(8,128)S(1)}, f32[15,8,1024]{2,1,0:T(8,128)S(1)}, u32[]{:S(2)}, u32[]{:S(2)}) collective-permute-start(f32[15,8,1024]{2,1,0:T(8,128)S(1)} %slice.82), channel_id=1, source_target_pairs={{0,96},{16,112},{32,0},{48,16},{64,32},{80,48},{96,64},{112,80},{1... | collective-permute-start | bytes 1474568 | tf_op jit(solution)/shard_map/ppermute | solution.py:53
  82.6 8.6 %collective-permute-done.10 = f32[15,8,1024]{2,1,0:T(8,128)S(1)} collective-permute-done((f32[15,8,1024]{2,1,0:T(8,128)S(1)}, f32[15,8,1024]{2,1,0:T(8,128)S(1)}, u32[]{:S(2)}, u32[]{:S(2)}) %collective-permute-start.10) | collective-permute-done | bytes 491552 | tf_op jit(solution)/shard_map/ppermute | solution.py:53
  91.1 3.8 %collective-permute-done.9 = f32[15,8,1024]{2,1,0:T(8,128)S(1)} collective-permute-done((f32[15,8,1024]{2,1,0:T(8,128)S(1)}, f32[15,8,1024]{2,1,0:T(8,128)S(1)}, u32[]{:S(2)}, u32[]{:S(2)}) %collective-permute-start.9) | collective-permute-done | bytes 491552 | tf_op jit(solution)/shard_map/ppermute | solution.py:53
  95.9 12.8 %shard_map.55 = (f32[15,8,2048]{2,1,0:T(8,128)}, f32[15,2048]{1,0:T(8,128)S(1)}, f32[15,2048]{1,0:T(8,128)S(1)}) custom-call(s32[15,16]{1,0:T(8,128)S(1)} %copy.24.partners, f32[15,16]{1,0:T(8,128)S(1)} %copy.25.weights, f32[120,8,2048]{2,1,0:T(8,128)} %maximum_dynamic-update-slice_fusion.every, f32[8,10,2048]{2,1,0:T(8,128)S(1)} %pad_maximum_fusion.coef), custom_call_target="tpu_custom_call" | custom-call | tf_op jit(solution)/shard_map/pallas_call | solution.py:174
  108.8 4.6 %collective-permute-start.11 = (f32[15,2048]{1,0:T(8,128)S(1)}, f32[15,2048]{1,0:T(8,128)S(1)}, u32[]{:S(2)}, u32[]{:S(2)}) collective-permute-start(f32[15,2048]{1,0:T(8,128)S(1)} %get-tuple-element.24), channel_id=1, source_target_pairs={{0,1},{1,2},{2,3},{3,4},{4,5},{5,6},{6,7},{7,8},{8,9},{9,10},{10,1... | collective-permute-start | bytes 368648 | tf_op jit(solution)/shard_map/ppermute | solution.py:80
  113.4 1.9 %collective-permute-start.12 = (f32[15,2048]{1,0:T(8,128)S(1)}, f32[15,2048]{1,0:T(8,128)S(1)}, u32[]{:S(2)}, u32[]{:S(2)}) collective-permute-start(f32[15,2048]{1,0:T(8,128)S(1)} %get-tuple-element.25), channel_id=1, source_target_pairs={{1,0},{2,1},{3,2},{4,3},{5,4},{6,5},{7,6},{8,7},{9,8},{10,9},{11,1... | collective-permute-start | bytes 368648 | tf_op jit(solution)/shard_map/ppermute | solution.py:80
  115.3 1.8 %copy.26 = f32[15,8,2048]{2,0,1:T(8,128)S(1)} copy(f32[15,8,2048]{2,1,0:T(8,128)} %get-tuple-element.23) | data formatting | bytes 1966080 | tf_op jit(solution)/shard_map/pallas_call | solution.py:174
  117.1 2.6 %collective-permute-done.12 = f32[15,2048]{1,0:T(8,128)S(1)} collective-permute-done((f32[15,2048]{1,0:T(8,128)S(1)}, f32[15,2048]{1,0:T(8,128)S(1)}, u32[]{:S(2)}, u32[]{:S(2)}) %collective-permute-start.12) | collective-permute-done | bytes 122912 | tf_op jit(solution)/shard_map/ppermute | solution.py:80
  119.8 3.5 %dynamic_update_slice.6 = f32[15,8,2048]{2,1,0:T(8,128)} dynamic-update-slice(f32[15,8,2048]{2,1,0:T(8,128)} %get-tuple-element.23, f32[15,1,2048]{2,1,0:T(1,128)S(1)} %copy.27, s32[]{:T(128)} %constant.92.clone.1, s32[]{:T(128)} %constant.92.clone.1, s32[]{:T(128)} %constant.92.clone.1) | dynamic-update-slice | bytes 245764 | tf_op jit(solution)/shard_map/dynamic_update_slice | solution.py:117
  123.5 3.5 %dynamic_update_slice.7 = f32[15,8,2048]{2,1,0:T(8,128)} dynamic-update-slice(f32[15,8,2048]{2,1,0:T(8,128)} %dynamic_update_slice.6, f32[15,1,2048]{2,1,0:T(1,128)S(1)} %copy.29, s32[]{:T(128)} %constant.92.clone.1, s32[]{:T(128)} %constant.93.clone.1, s32[]{:T(128)} %constant.92.clone.1) | dynamic-update-slice | bytes 245764 | tf_op jit(solution)/shard_map/dynamic_update_slice | solution.py:118
  (70 shorter events, 27.5 us)
Async XLA Ops:
  0.0 42.6 %collective-permute-start = (f32[15,8,2048]{2,1,0:T(8,128)}, f32[15,8,2048]{2,1,0:T(8,128)S(1)}, u32[]{:S(2)}, u32[]{:S(2)}) collective-permute-start(f32[15,8,2048]{2,1,0:T(8,128)} %param.7), channel_id=1, source_target_pairs={{0,32},{16,48},{32,64},{48,80},{64,96},{80,112},{96,0},{112,16},{1... | collective-permute-start | bytes 2949128 | tf_op jit(solution)/shard_map/ppermute | solution.py:53
  2.0 40.7 %collective-permute-start.3 = (f32[15,8,2048]{2,1,0:T(8,128)}, f32[15,8,2048]{2,1,0:T(8,128)S(1)}, u32[]{:S(2)}, u32[]{:S(2)}) collective-permute-start(f32[15,8,2048]{2,1,0:T(8,128)} %param.7), channel_id=1, source_target_pairs={{0,96},{16,112},{32,0},{48,16},{64,32},{80,48},{96,64},{112,80},{1... | collective-permute-start | bytes 2949128 | tf_op jit(solution)/shard_map/ppermute | solution.py:53
  3.3 43.8 %collective-permute-start.6 = (f32[15,8,2048]{2,1,0:T(8,128)}, f32[15,8,2048]{2,1,0:T(8,128)}, u32[]{:S(2)}, u32[]{:S(2)}) collective-permute-start(f32[15,8,2048]{2,1,0:T(8,128)} %param.7), channel_id=1, source_target_pairs={{0,16},{16,0},{32,48},{48,32},{64,80},{80,64},{96,112},{112,96},{1... | collective-permute-start | bytes 2949128 | tf_op jit(solution)/shard_map/ppermute | solution.py:60
  8.4 33.2 %collective-permute-start.1 = (f32[8,1,2048]{2,1,0:T(1,128)}, f32[8,1,2048]{2,1,0:T(1,128)}, u32[]{:S(2)}, u32[]{:S(2)}) collective-permute-start(f32[8,1,2048]{2,1,0:T(1,128)} %get-tuple-element.30), channel_id=1, source_target_pairs={{0,1},{1,2},{2,3},{3,4},{4,5},{5,6},{6,7},{7,8},{8,9},{9,10},{10,1... | collective-permute-start | bytes 196616 | tf_op jit(solution)/shard_map/ppermute | solution.py:80
  13.3 28.3 %collective-permute-start.2 = (f32[8,1,2048]{2,1,0:T(1,128)}, f32[8,1,2048]{2,1,0:T(1,128)}, u32[]{:S(2)}, u32[]{:S(2)}) collective-permute-start(f32[8,1,2048]{2,1,0:T(1,128)} %get-tuple-element.31), channel_id=1, source_target_pairs={{1,0},{2,1},{3,2},{4,3},{5,4},{6,5},{7,6},{8,7},{9,8},{10,9},{11,1... | collective-permute-start | bytes 196616 | tf_op jit(solution)/shard_map/ppermute | solution.py:80
  28.1 12.4 %copy-start = (f32[15,8,2048]{2,1,0:T(8,128)S(1)}, f32[15,8,2048]{2,1,0:T(8,128)}, u32[]{:S(2)}) copy-start(f32[15,8,2048]{2,1,0:T(8,128)} %param.7) | copy-start | bytes 2949124
  30.1 11.4 %copy-start.1 = (f32[8,8,2048]{2,1,0:T(8,128)S(1)}, f32[8,8,2048]{2,1,0:T(8,128)}, u32[]{:S(2)}) copy-start(f32[8,8,2048]{2,1,0:T(8,128)} %param.8) | copy-start | bytes 1572868
  42.7 14.5 %collective-permute-start.4 = (f32[15,8,1024]{2,1,0:T(8,128)S(1)}, f32[15,8,1024]{2,1,0:T(8,128)}, u32[]{:S(2)}, u32[]{:S(2)}) collective-permute-start(f32[15,8,1024]{2,1,0:T(8,128)S(1)} %slice.50), channel_id=1, source_target_pairs={{0,32},{16,48},{32,64},{48,80},{64,96},{80,112},{96,0},{112,16},{1... | collective-permute-start | bytes 1474568 | tf_op jit(solution)/shard_map/ppermute | solution.py:53
  43.6 14.0 %collective-permute-start.5 = (f32[15,8,1024]{2,1,0:T(8,128)}, f32[15,8,1024]{2,1,0:T(8,128)}, u32[]{:S(2)}, u32[]{:S(2)}) collective-permute-start(f32[15,8,1024]{2,1,0:T(8,128)} %slice.80), channel_id=1, source_target_pairs={{0,96},{16,112},{32,0},{48,16},{64,32},{80,48},{96,64},{112,80},{1... | collective-permute-start | bytes 1474568 | tf_op jit(solution)/shard_map/ppermute | solution.py:53
  47.1 33.2 %collective-permute-start.7 = (f32[15,8,2048]{2,1,0:T(8,128)}, f32[15,8,2048]{2,1,0:T(8,128)S(1)}, u32[]{:S(2)}, u32[]{:S(2)}) collective-permute-start(f32[15,8,2048]{2,1,0:T(8,128)} %collective-permute-done.6), channel_id=1, source_target_pairs={{0,32},{16,48},{32,64},{48,80},{64,96},{80,112},{96,0},{112,16},{1... | collective-permute-start | bytes 2949128 | tf_op jit(solution)/shard_map/ppermute | solution.py:53
  47.1 30.1 %collective-permute-start.8 = (f32[15,8,2048]{2,1,0:T(8,128)}, f32[15,8,2048]{2,1,0:T(8,128)S(1)}, u32[]{:S(2)}, u32[]{:S(2)}) collective-permute-start(f32[15,8,2048]{2,1,0:T(8,128)} %collective-permute-done.6), channel_id=1, source_target_pairs={{0,96},{16,112},{32,0},{48,16},{64,32},{80,48},{96,64},{112,80},{1... | collective-permute-start | bytes 2949128 | tf_op jit(solution)/shard_map/ppermute | solution.py:53
  77.3 13.8 %collective-permute-start.10 = (f32[15,8,1024]{2,1,0:T(8,128)S(1)}, f32[15,8,1024]{2,1,0:T(8,128)S(1)}, u32[]{:S(2)}, u32[]{:S(2)}) collective-permute-start(f32[15,8,1024]{2,1,0:T(8,128)S(1)} %slice.82), channel_id=1, source_target_pairs={{0,96},{16,112},{32,0},{48,16},{64,32},{80,48},{96,64},{112,80},{1... | collective-permute-start | bytes 1474568 | tf_op jit(solution)/shard_map/ppermute | solution.py:53
  80.4 14.5 %collective-permute-start.9 = (f32[15,8,1024]{2,1,0:T(8,128)S(1)}, f32[15,8,1024]{2,1,0:T(8,128)S(1)}, u32[]{:S(2)}, u32[]{:S(2)}) collective-permute-start(f32[15,8,1024]{2,1,0:T(8,128)S(1)} %slice.81), channel_id=1, source_target_pairs={{0,32},{16,48},{32,64},{48,80},{64,96},{80,112},{96,0},{112,16},{1... | collective-permute-start | bytes 1474568 | tf_op jit(solution)/shard_map/ppermute | solution.py:53
  108.8 8.3 %collective-permute-start.11 = (f32[15,2048]{1,0:T(8,128)S(1)}, f32[15,2048]{1,0:T(8,128)S(1)}, u32[]{:S(2)}, u32[]{:S(2)}) collective-permute-start(f32[15,2048]{1,0:T(8,128)S(1)} %get-tuple-element.24), channel_id=1, source_target_pairs={{0,1},{1,2},{2,3},{3,4},{4,5},{5,6},{6,7},{7,8},{8,9},{9,10},{10,1... | collective-permute-start | bytes 368648 | tf_op jit(solution)/shard_map/ppermute | solution.py:80
  113.4 6.3 %collective-permute-start.12 = (f32[15,2048]{1,0:T(8,128)S(1)}, f32[15,2048]{1,0:T(8,128)S(1)}, u32[]{:S(2)}, u32[]{:S(2)}) collective-permute-start(f32[15,2048]{1,0:T(8,128)S(1)} %get-tuple-element.25), channel_id=1, source_target_pairs={{1,0},{2,1},{3,2},{4,3},{5,4},{6,5},{7,6},{8,7},{9,8},{10,9},{11,1... | collective-permute-start | bytes 368648 | tf_op jit(solution)/shard_map/ppermute | solution.py:80

commit v8 on v7

--- a/solution.py
+++ b/solution.py
@@ -63,7 +63,7 @@
     for base, origin in ((block, me), (partner, me ^ 1)):
         from_left = shifted(base, 2)
         from_right = shifted(base, -2)
-        if origin is me:
+        if origin is not me:
             from_left, tables = lax.optimization_barrier((from_left, tables))
         far = jnp.concatenate(
             [shifted(from_left[..., :half], 2), shifted(from_right[..., half:], -2)], axis=-1
@@ -112,11 +112,9 @@
     applied, to_prev, to_next = stencil_apply(every, coef, partners, weights)
 
     from_prev, from_next = space_halo(to_next, to_prev)
-    top = applied[:, :1] - from_prev[:, None]
-    bottom = applied[:, rows - 1:] - from_next[:, None]
-    applied = lax.dynamic_update_slice_in_dim(applied, top, 0, 1)
-    applied = lax.dynamic_update_slice_in_dim(applied, bottom, rows - 1, 1)
-    return applied
+    row = lax.broadcasted_iota(jnp.int32, applied.shape, 1)
+    rim = jnp.where(row == 0, from_prev[:, None], jnp.where(row == rows - 1, from_next[:, None], 0.0))
+    return applied - rim
 
 
 def stencil_kernel(partners, weights, every, coef, out, to_prev, to_next, edges):

time: 128 us -> 114 us (0.89)
  local copies, waits for them, and re-layouts: 31.5 us -> 20.8 us
  Pallas kernels: 12.8 us -> 10.6 us
  other arithmetic: 18.1 us -> 15.9 us
    dynamic_update_slice x2 -> x0, local copies, waits for them, and re-layouts: 7.03 us -> none  [the longest x1 3.51 us: local(): applied = lax.dynamic_update_slice_in_dim(applied, top, 0, 1)]
    pallas_call x1, Pallas kernels: 12.8 us -> 10.6 us  [stencil_apply(): pl.pallas_call(stencil_kernel, out_shape=(jax.ShapeDtypeStruct((own_modes...]
    unnamed x1, other arithmetic: 2.21 us -> 0.09 us
    pallas_call x1 -> x0, local copies, waits for them, and re-layouts: 1.78 us -> none  [stencil_apply(): pl.pallas_call(stencil_kernel, out_shape=(jax.ShapeDtypeStruct((own_modes...]
    ppermute x2, waiting for transfers between devices: 2.57 us -> 4.34 us  [space_halo(): lax.ppermute(edge_first, 'space', down)]
    unnamed x10 -> x18, local copies, waits for them, and re-layouts: 7.51 us -> 7.22 us
  transfers between devices with their start and end apart: 13 -> 13, of which waited for: 6 -> 5; matrix products, arithmetic and copies ran while one was open for 33% -> 29% of each run, Pallas kernels for 0% -> 0%
where the time goes in v8:
time: 114 us; the launch traced here: 113 us
  waiting for transfers between devices  36.9 us (32%)
  starting transfers between devices  28.6 us (25%)
  local copies, waits for them, and re-layouts  20.8 us (18%)
  other arithmetic  15.9 us (14%)
  Pallas kernels  10.6 us (9%)
    ppermute x8, waiting for transfers between devices, shifted(): lax.ppermute(x, 'chaos', [(c, (c + step) % count) for c in range(count)])  32.6 us
    ppermute x8, starting transfers between devices, shifted(): lax.ppermute(x, 'chaos', [(c, (c + step) % count) for c in range(count)])  11 us
    pallas_call x1, Pallas kernels, stencil_apply(): pl.pallas_call(stencil_kernel, out_shape=(jax.ShapeDtypeStruct((own_modes...  10.6 us
    ppermute x2, starting transfers between devices, space_halo(): lax.ppermute(edge_last, 'space', up)  10.1 us
    unnamed x18, local copies, waits for them, and re-layouts  7.22 us
    scatter-add x1, other arithmetic, coupling_table(): jnp.zeros((kl_terms * mode_count * mode_count,), jnp.float32).at[flat_index]  4.71 us
    ppermute x2, waiting for transfers between devices, space_halo(): lax.ppermute(edge_first, 'space', down)  4.34 us
    ppermute x2, starting transfers between devices, space_halo(): lax.ppermute(edge_first, 'space', down)  3.84 us
  transfers between devices with their start and end apart: 13, of which 5 were waited for; matrix products, arithmetic and copies ran while one was open for 29% of the time, Pallas kernels for 0%

profile of v8, /device:TPU:1, one launch (start us, length us, event | category | flops | bytes accessed | tf_op | source)
XLA Modules:
  0.0 113.2 jit_solution(13691307157776151885)
XLA Ops:
  0.0 3.7 %collective-permute-start = (f32[15,8,2048]{2,1,0:T(8,128)}, f32[15,8,2048]{2,1,0:T(8,128)}, u32[]{:S(2)}, u32[]{:S(2)}) collective-permute-start(f32[15,8,2048]{2,1,0:T(8,128)} %param.7), channel_id=1, source_target_pairs={{0,16},{16,0},{32,48},{48,32},{64,80},{80,64},{96,112},{112,96},{1... | collective-permute-start | bytes 2949128 | tf_op jit(solution)/shard_map/ppermute | solution.py:60
  4.9 1.5 %collective-permute-start.5 = (f32[15,8,2048]{2,1,0:T(8,128)}, f32[15,8,2048]{2,1,0:T(8,128)S(1)}, u32[]{:S(2)}, u32[]{:S(2)}) collective-permute-start(f32[15,8,2048]{2,1,0:T(8,128)} %param.7), channel_id=1, source_target_pairs={{0,96},{16,112},{32,0},{48,16},{64,32},{80,48},{96,64},{112,80},{1... | collective-permute-start | bytes 2949128 | tf_op jit(solution)/shard_map/ppermute | solution.py:53
  6.4 2.0 %fusion.19 = (f32[8,1,2048]{2,1,0:T(1,128)}, f32[8,1,2048]{2,1,0:T(1,128)}) fusion(f32[8,8,2048]{2,1,0:T(8,128)} %param.8), kind=kLoop, calls=%fused_computation.70 | loop fusion | bytes 262144 | tf_op jit(solution)/shard_map/slice | solution.py:107
  8.4 4.9 %collective-permute-start.2 = (f32[8,1,2048]{2,1,0:T(1,128)}, f32[8,1,2048]{2,1,0:T(1,128)}, u32[]{:S(2)}, u32[]{:S(2)}) collective-permute-start(f32[8,1,2048]{2,1,0:T(1,128)} %get-tuple-element.28), channel_id=1, source_target_pairs={{0,1},{1,2},{2,3},{3,4},{4,5},{5,6},{6,7},{7,8},{8,9},{9,10},{10,1... | collective-permute-start | bytes 196616 | tf_op jit(solution)/shard_map/ppermute | solution.py:80
  13.3 1.9 %collective-permute-start.3 = (f32[8,1,2048]{2,1,0:T(1,128)}, f32[8,1,2048]{2,1,0:T(1,128)}, u32[]{:S(2)}, u32[]{:S(2)}) collective-permute-start(f32[8,1,2048]{2,1,0:T(1,128)} %get-tuple-element.29), channel_id=1, source_target_pairs={{1,0},{2,1},{3,2},{4,3},{5,4},{6,5},{7,6},{8,7},{9,8},{10,9},{11,1... | collective-permute-start | bytes 196616 | tf_op jit(solution)/shard_map/ppermute | solution.py:80
  18.3 4.7 %scatter_custom_fusion = f32[115200]{0:T(1024)S(1)} fusion(s32[624]{0:T(1024)S(1)} %fusion.15, f32[624]{0:T(1024)S(1)} %fusion.17, f32[]{:T(128)} %constant.103.clone.1), kind=kCustom, calls=%fused_computation.10 | custom fusion | flops 624 | bytes 460804 | tf_op jit(solution)/shard_map/scatter-add | solution.py:35
  28.0 2.1 %gather_fusion.3 = f32[120]{0:T(128)S(1)} fusion(f32[8,15,120]{2,1,0:T(8,128)S(1)} %get-tuple-element.27, s32[120]{0:T(128)S(1)} %reshape.106), kind=kCustom, calls=%fused_computation.1.clone | custom fusion | bytes 2400 | tf_op jit(solution)/shard_map/jit(take_along_axis)/gather | solution.py:46
  31.0 2.1 %gather_fusion.2 = f32[120]{0:T(128)S(1)} fusion(f32[8,15,120]{2,1,0:T(8,128)S(1)} %get-tuple-element.27, s32[120]{0:T(128)S(1)} %reshape.100), kind=kCustom, calls=%fused_computation.clone | custom fusion | bytes 2400 | tf_op jit(solution)/shard_map/jit(take_along_axis)/gather | solution.py:45
  33.2 1.2 %iota_reduce_fusion.2 = (pred[120]{0:T(512)(128)(4,1)}, s32[120]{0:T(128)S(1)}) fusion(s32[120]{0:T(128)} %and_select_fusion.2, s32[8]{0:T(128)S(1)} %stack.50), kind=kLoop, calls=%fused_computation.51 | loop fusion | flops 6840 | bytes 1112 | tf_op jit(solution)/shard_map/local/reduce | solution.py:100
  36.0 1.2 %gather_fusion = s32[120]{0:T(128)S(1)} fusion(s32[120]{0:T(128)S(1)} %fusion.18, s32[1024]{0:T(1024)S(1)} %get-tuple-element.33), kind=kCustom, calls=%fused_computation.2 | custom fusion | bytes 1440 | tf_op jit(solution)/shard_map/gather | solution.py:102
  37.3 1.2 %gather_fusion.1 = s32[120]{0:T(128)S(1)} fusion(s32[120]{0:T(128)S(1)} %fusion.18, s32[1024]{0:T(1024)S(1)} %get-tuple-element.32), kind=kCustom, calls=%fused_computation.3 | custom fusion | bytes 1440 | tf_op jit(solution)/shard_map/gather | solution.py:103
  40.6 2.7 %collective-permute-start.7 = (f32[15,8,1024]{2,1,0:T(8,128)S(1)}, f32[15,8,1024]{2,1,0:T(8,128)S(1)}, u32[]{:S(2)}, u32[]{:S(2)}) collective-permute-start(f32[15,8,1024]{2,1,0:T(8,128)S(1)} %slice.73), channel_id=1, source_target_pairs={{0,96},{16,112},{32,0},{48,16},{64,32},{80,48},{96,64},{112,80},{1... | collective-permute-start | bytes 1474568 | tf_op jit(solution)/shard_map/ppermute | solution.py:53
  43.3 2.7 %collective-permute-start.8 = (f32[15,8,2048]{2,1,0:T(8,128)}, f32[15,8,2048]{2,1,0:T(8,128)S(1)}, u32[]{:S(2)}, u32[]{:S(2)}) collective-permute-start(f32[15,8,2048]{2,1,0:T(8,128)} %collective-permute-done), channel_id=1, source_target_pairs={{0,96},{16,112},{32,0},{48,16},{64,32},{80,48},{96,64},{112,80},{1... | collective-permute-start | bytes 2949128 | tf_op jit(solution)/shard_map/ppermute | solution.py:53
  46.2 8.8 %collective-permute-done.6 = f32[15,8,1024]{2,1,0:T(8,128)S(1)} collective-permute-done((f32[15,8,1024]{2,1,0:T(8,128)S(1)}, f32[15,8,1024]{2,1,0:T(8,128)S(1)}, u32[]{:S(2)}, u32[]{:S(2)}) %collective-permute-start.6) | collective-permute-done | bytes 491552 | tf_op jit(solution)/shard_map/ppermute | solution.py:53
  55.1 1.3 %constant_dynamic-update-slice_fusion.2 = f32[120,8,2048]{2,1,0:T(8,128)S(1)} fusion(f32[120,8,2048]{2,1,0:T(8,128)S(1)} %maximum_dynamic-update-slice_fusion.1, f32[15,8,2048]{2,1,0:T(8,128)} %collective-permute-done), kind=kLoop, calls=%fused_computation.17 | loop fusion | bytes 1966080
  56.4 17.7 %collective-permute-done.1 = f32[15,8,2048]{2,1,0:T(8,128)S(1)} collective-permute-done((f32[15,8,2048]{2,1,0:T(8,128)}, f32[15,8,2048]{2,1,0:T(8,128)S(1)}, u32[]{:S(2)}, u32[]{:S(2)}) %collective-permute-start.1) | collective-permute-done | bytes 983072 | tf_op jit(solution)/shard_map/ppermute | solution.py:53
  75.4 2.8 %collective-permute-start.10 = (f32[15,8,1024]{2,1,0:T(8,128)S(1)}, f32[15,8,1024]{2,1,0:T(8,128)S(1)}, u32[]{:S(2)}, u32[]{:S(2)}) collective-permute-start(f32[15,8,1024]{2,1,0:T(8,128)S(1)} %slice.74), channel_id=1, source_target_pairs={{0,96},{16,112},{32,0},{48,16},{64,32},{80,48},{96,64},{112,80},{1... | collective-permute-start | bytes 1474568 | tf_op jit(solution)/shard_map/ppermute | solution.py:53
  78.4 2.3 %constant_dynamic-update-slice_fusion.1 = f32[120,8,2048]{2,1,0:T(8,128)} fusion(f32[120,8,2048]{2,1,0:T(8,128)} %copy-done, f32[15,8,2048]{2,1,0:T(8,128)} %copy-done.1), kind=kLoop, calls=%fused_computation.16 | loop fusion | bytes 1966080
  80.6 2.3 %constant_dynamic-update-slice_fusion = f32[120,8,2048]{2,1,0:T(8,128)} fusion(f32[120,8,2048]{2,1,0:T(8,128)} %constant_dynamic-update-slice_fusion.1, f32[15,8,2048]{2,1,0:T(8,128)} %copy-done.2), kind=kLoop, calls=%fused_computation.15 | loop fusion | bytes 1966080
  82.9 4.9 %collective-permute-done.9 = f32[15,8,1024]{2,1,0:T(8,128)S(1)} collective-permute-done((f32[15,8,1024]{2,1,0:T(8,128)S(1)}, f32[15,8,1024]{2,1,0:T(8,128)S(1)}, u32[]{:S(2)}, u32[]{:S(2)}) %collective-permute-start.9) | collective-permute-done | bytes 491552 | tf_op jit(solution)/shard_map/ppermute | solution.py:53
  90.0 10.6 %shard_map.55 = (f32[15,8,2048]{2,1,0:T(8,128)S(1)}, f32[15,2048]{1,0:T(8,128)S(1)}, f32[15,2048]{1,0:T(8,128)S(1)}) custom-call(s32[15,16]{1,0:T(8,128)S(1)} %copy.16.partners, f32[15,16]{1,0:T(8,128)S(1)} %copy.17.weights, f32[120,8,2048]{2,1,0:T(8,128)} %maximum_dynamic-update-slice_fusion.every, f32[8,10,2048]{2,1,0:T(8,128)S(1)} %pad_maximum_fusion.coef), custom_call_target="tpu_custom_call" | custom-call | tf_op jit(solution)/shard_map/pallas_call | solution.py:172
  100.5 5.2 %collective-permute-start.11 = (f32[15,2048]{1,0:T(8,128)S(1)}, f32[15,2048]{1,0:T(8,128)S(1)}, u32[]{:S(2)}, u32[]{:S(2)}) collective-permute-start(f32[15,2048]{1,0:T(8,128)S(1)} %get-tuple-element.24), channel_id=1, source_target_pairs={{0,1},{1,2},{2,3},{3,4},{4,5},{5,6},{6,7},{7,8},{8,9},{9,10},{10,1... | collective-permute-start | bytes 368648 | tf_op jit(solution)/shard_map/ppermute | solution.py:80
  105.7 1.9 %collective-permute-start.12 = (f32[15,2048]{1,0:T(8,128)S(1)}, f32[15,2048]{1,0:T(8,128)S(1)}, u32[]{:S(2)}, u32[]{:S(2)}) collective-permute-start(f32[15,2048]{1,0:T(8,128)S(1)} %get-tuple-element.25), channel_id=1, source_target_pairs={{1,0},{2,1},{3,2},{4,3},{5,4},{6,5},{7,6},{8,7},{9,8},{10,9},{11,1... | collective-permute-start | bytes 368648 | tf_op jit(solution)/shard_map/ppermute | solution.py:80
  107.6 4.3 %collective-permute-done.12 = f32[15,2048]{1,0:T(8,128)S(1)} collective-permute-done((f32[15,2048]{1,0:T(8,128)S(1)}, f32[15,2048]{1,0:T(8,128)S(1)}, u32[]{:S(2)}, u32[]{:S(2)}) %collective-permute-start.12) | collective-permute-done | bytes 122912 | tf_op jit(solution)/shard_map/ppermute | solution.py:80
  (74 shorter events, 18.9 us)
Async XLA Ops:
  0.0 43.3 %collective-permute-start = (f32[15,8,2048]{2,1,0:T(8,128)}, f32[15,8,2048]{2,1,0:T(8,128)}, u32[]{:S(2)}, u32[]{:S(2)}) collective-permute-start(f32[15,8,2048]{2,1,0:T(8,128)} %param.7), channel_id=1, source_target_pairs={{0,16},{16,0},{32,48},{48,32},{64,80},{80,64},{96,112},{112,96},{1... | collective-permute-start | bytes 2949128 | tf_op jit(solution)/shard_map/ppermute | solution.py:60
  3.7 36.7 %collective-permute-start.4 = (f32[15,8,2048]{2,1,0:T(8,128)}, f32[15,8,2048]{2,1,0:T(8,128)S(1)}, u32[]{:S(2)}, u32[]{:S(2)}) collective-permute-start(f32[15,8,2048]{2,1,0:T(8,128)} %param.7), channel_id=1, source_target_pairs={{0,32},{16,48},{32,64},{48,80},{64,96},{80,112},{96,0},{112,16},{1... | collective-permute-start | bytes 2949128 | tf_op jit(solution)/shard_map/ppermute | solution.py:53
  4.9 35.6 %collective-permute-start.5 = (f32[15,8,2048]{2,1,0:T(8,128)}, f32[15,8,2048]{2,1,0:T(8,128)S(1)}, u32[]{:S(2)}, u32[]{:S(2)}) collective-permute-start(f32[15,8,2048]{2,1,0:T(8,128)} %param.7), channel_id=1, source_target_pairs={{0,96},{16,112},{32,0},{48,16},{64,32},{80,48},{96,64},{112,80},{1... | collective-permute-start | bytes 2949128 | tf_op jit(solution)/shard_map/ppermute | solution.py:53
  8.4 31.0 %collective-permute-start.2 = (f32[8,1,2048]{2,1,0:T(1,128)}, f32[8,1,2048]{2,1,0:T(1,128)}, u32[]{:S(2)}, u32[]{:S(2)}) collective-permute-start(f32[8,1,2048]{2,1,0:T(1,128)} %get-tuple-element.28), channel_id=1, source_target_pairs={{0,1},{1,2},{2,3},{3,4},{4,5},{5,6},{6,7},{7,8},{8,9},{9,10},{10,1... | collective-permute-start | bytes 196616 | tf_op jit(solution)/shard_map/ppermute | solution.py:80
  13.3 26.0 %collective-permute-start.3 = (f32[8,1,2048]{2,1,0:T(1,128)}, f32[8,1,2048]{2,1,0:T(1,128)}, u32[]{:S(2)}, u32[]{:S(2)}) collective-permute-start(f32[8,1,2048]{2,1,0:T(1,128)} %get-tuple-element.29), channel_id=1, source_target_pairs={{1,0},{2,1},{3,2},{4,3},{5,4},{6,5},{7,6},{8,7},{9,8},{10,9},{11,1... | collective-permute-start | bytes 196616 | tf_op jit(solution)/shard_map/ppermute | solution.py:80
  28.0 10.6 %copy-start.3 = (f32[15,8,2048]{2,1,0:T(8,128)S(1)}, f32[15,8,2048]{2,1,0:T(8,128)}, u32[]{:S(2)}) copy-start(f32[15,8,2048]{2,1,0:T(8,128)} %param.7) | copy-start | bytes 2949124
  30.1 9.3 %copy-start.4 = (f32[8,8,2048]{2,1,0:T(8,128)S(1)}, f32[8,8,2048]{2,1,0:T(8,128)}, u32[]{:S(2)}) copy-start(f32[8,8,2048]{2,1,0:T(8,128)} %param.8) | copy-start | bytes 1572868
  40.4 37.8 %copy-start.5 = (s32[15,8,2]{0,2,1:T(2,128)S(1)}, s32[15,8,2]{0,2,1:T(2,128)}, u32[]{:S(2)}) copy-start(s32[15,8,2]{0,2,1:T(2,128)} %copy.14) | copy-start | bytes 2884
  40.5 14.5 %collective-permute-start.6 = (f32[15,8,1024]{2,1,0:T(8,128)S(1)}, f32[15,8,1024]{2,1,0:T(8,128)S(1)}, u32[]{:S(2)}, u32[]{:S(2)}) collective-permute-start(f32[15,8,1024]{2,1,0:T(8,128)S(1)} %slice.72), channel_id=1, source_target_pairs={{0,32},{16,48},{32,64},{48,80},{64,96},{80,112},{96,0},{112,16},{1... | collective-permute-start | bytes 1474568 | tf_op jit(solution)/shard_map/ppermute | solution.py:53
  40.6 14.4 %collective-permute-start.7 = (f32[15,8,1024]{2,1,0:T(8,128)S(1)}, f32[15,8,1024]{2,1,0:T(8,128)S(1)}, u32[]{:S(2)}, u32[]{:S(2)}) collective-permute-start(f32[15,8,1024]{2,1,0:T(8,128)S(1)} %slice.73), channel_id=1, source_target_pairs={{0,96},{16,112},{32,0},{48,16},{64,32},{80,48},{96,64},{112,80},{1... | collective-permute-start | bytes 1474568 | tf_op jit(solution)/shard_map/ppermute | solution.py:53
  43.3 30.7 %collective-permute-start.1 = (f32[15,8,2048]{2,1,0:T(8,128)}, f32[15,8,2048]{2,1,0:T(8,128)S(1)}, u32[]{:S(2)}, u32[]{:S(2)}) collective-permute-start(f32[15,8,2048]{2,1,0:T(8,128)} %collective-permute-done), channel_id=1, source_target_pairs={{0,32},{16,48},{32,64},{48,80},{64,96},{80,112},{96,0},{112,16},{1... | collective-permute-start | bytes 2949128 | tf_op jit(solution)/shard_map/ppermute | solution.py:53
  43.3 30.8 %collective-permute-start.8 = (f32[15,8,2048]{2,1,0:T(8,128)}, f32[15,8,2048]{2,1,0:T(8,128)S(1)}, u32[]{:S(2)}, u32[]{:S(2)}) collective-permute-start(f32[15,8,2048]{2,1,0:T(8,128)} %collective-permute-done), channel_id=1, source_target_pairs={{0,96},{16,112},{32,0},{48,16},{64,32},{80,48},{96,64},{112,80},{1... | collective-permute-start | bytes 2949128 | tf_op jit(solution)/shard_map/ppermute | solution.py:53
  56.4 17.9 %copy-start = (f32[120,8,2048]{2,1,0:T(8,128)}, f32[120,8,2048]{2,1,0:T(8,128)S(1)}, u32[]{:S(2)}) copy-start(f32[120,8,2048]{2,1,0:T(8,128)S(1)} %constant_dynamic-update-slice_fusion.2) | copy-start | bytes 23592964
  74.1 0.9 copy-start.1
  74.1 13.7 %collective-permute-start.9 = (f32[15,8,1024]{2,1,0:T(8,128)S(1)}, f32[15,8,1024]{2,1,0:T(8,128)S(1)}, u32[]{:S(2)}, u32[]{:S(2)}) collective-permute-start(f32[15,8,1024]{2,1,0:T(8,128)S(1)} %slice.46), channel_id=1, source_target_pairs={{0,32},{16,48},{32,64},{48,80},{64,96},{80,112},{96,0},{112,16},{1... | collective-permute-start | bytes 1474568 | tf_op jit(solution)/shard_map/ppermute | solution.py:53
  74.2 1.2 %copy-start.2 = (f32[15,8,2048]{2,1,0:T(8,128)}, f32[15,8,2048]{2,1,0:T(8,128)S(1)}, u32[]{:S(2)}) copy-start(f32[15,8,2048]{2,1,0:T(8,128)S(1)} %collective-permute-done.8) | copy-start | bytes 2949124
  75.4 13.5 %collective-permute-start.10 = (f32[15,8,1024]{2,1,0:T(8,128)S(1)}, f32[15,8,1024]{2,1,0:T(8,128)S(1)}, u32[]{:S(2)}, u32[]{:S(2)}) collective-permute-start(f32[15,8,1024]{2,1,0:T(8,128)S(1)} %slice.74), channel_id=1, source_target_pairs={{0,96},{16,112},{32,0},{48,16},{64,32},{80,48},{96,64},{112,80},{1... | collective-permute-start | bytes 1474568 | tf_op jit(solution)/shard_map/ppermute | solution.py:53
  100.5 7.1 %collective-permute-start.11 = (f32[15,2048]{1,0:T(8,128)S(1)}, f32[15,2048]{1,0:T(8,128)S(1)}, u32[]{:S(2)}, u32[]{:S(2)}) collective-permute-start(f32[15,2048]{1,0:T(8,128)S(1)} %get-tuple-element.24), channel_id=1, source_target_pairs={{0,1},{1,2},{2,3},{3,4},{4,5},{5,6},{6,7},{7,8},{8,9},{9,10},{10,1... | collective-permute-start | bytes 368648 | tf_op jit(solution)/shard_map/ppermute | solution.py:80
  105.7 6.3 %collective-permute-start.12 = (f32[15,2048]{1,0:T(8,128)S(1)}, f32[15,2048]{1,0:T(8,128)S(1)}, u32[]{:S(2)}, u32[]{:S(2)}) collective-permute-start(f32[15,2048]{1,0:T(8,128)S(1)} %get-tuple-element.25), channel_id=1, source_target_pairs={{1,0},{2,1},{3,2},{4,3},{5,4},{6,5},{7,6},{8,7},{9,8},{10,9},{11,1... | collective-permute-start | bytes 368648 | tf_op jit(solution)/shard_map/ppermute | solution.py:80

commit v9 on v8

--- a/solution.py
+++ b/solution.py
@@ -57,12 +57,17 @@
     count = lax.axis_size("chaos")
     me = lax.axis_index("chaos")
     half = block.shape[-1] // 2
+    own_left = shifted(block, 2)
+    own_right = shifted(block, -2)
     partner = lax.ppermute(block, "chaos", [(c, c ^ 1) for c in range(count)])
     pieces = []
     owners = []
     for base, origin in ((block, me), (partner, me ^ 1)):
-        from_left = shifted(base, 2)
-        from_right = shifted(base, -2)
+        if origin is me:
+            from_left, from_right = own_left, own_right
+        else:
+            from_left = shifted(base, 2)
+            from_right = shifted(base, -2)
         if origin is not me:
             from_left, tables = lax.optimization_barrier((from_left, tables))
         far = jnp.concatenate(
@@ -109,7 +114,8 @@
 
     every, tables = ring_gather(modes, (partners, weights, coef))
     partners, weights, coef = tables
-    applied, to_prev, to_next = stencil_apply(every, coef, partners, weights)
+    to_prev, to_next = rim_apply(every, coef, partners, weights)
+    applied = stencil_apply(every, coef, partners, weights)
 
     from_prev, from_next = space_halo(to_next, to_prev)
     row = lax.broadcasted_iota(jnp.int32, applied.shape, 1)
@@ -117,7 +123,7 @@
     return applied - rim
 
 
-def stencil_kernel(partners, weights, every, coef, out, to_prev, to_next, edges):
+def stencil_kernel(partners, weights, every, coef, out, edges):
     slot = pl.program_id(0)
     kl_terms = coef.shape[0]
     rows = out.shape[1]
@@ -139,10 +145,8 @@
             edges[2, k] = jnp.where(row == rows - 1, zero, c_dn)
             edges[3, k] = jnp.where(column == 0, zero, c_lf)
             edges[4, k] = jnp.where(column == cols - 1, zero, c_rt)
-            edges[5, k] = jnp.where(row == 0, c_up, jnp.where(row == rows - 1, c_dn, zero))
 
     acc = jnp.zeros((rows, cols), jnp.float32)
-    rim = jnp.zeros((rows, cols), jnp.float32)
     for k in range(kl_terms):
         j0 = partners[slot, 2 * k]
         j1 = partners[slot, 2 * k + 1]
@@ -158,10 +162,7 @@
         term = term - edges[3, k] * lf
         term = term - edges[4, k] * rt
         acc = acc + term
-        rim = rim + edges[5, k] * center
     out[0] = acc
-    to_prev[pl.ds(slot, 1), :] = rim[0:1]
-    to_next[pl.ds(slot, 1), :] = rim[rows - 1:rows]
 
 
 def stencil_apply(every, coef, partners, weights):
@@ -171,11 +172,7 @@
     cols = every.shape[2]
     return pl.pallas_call(
         stencil_kernel,
-        out_shape=(
-            jax.ShapeDtypeStruct((own_modes, rows, cols), jnp.float32),
-            jax.ShapeDtypeStruct((own_modes, cols), jnp.float32),
-            jax.ShapeDtypeStruct((own_modes, cols), jnp.float32),
-        ),
+        out_shape=jax.ShapeDtypeStruct((own_modes, rows, cols), jnp.float32),
         grid_spec=pltpu.PrefetchScalarGridSpec(
             num_scalar_prefetch=1,
             grid=(own_modes,),
@@ -184,16 +181,55 @@
                 pl.BlockSpec(memory_space=pltpu.VMEM),
                 pl.BlockSpec(memory_space=pltpu.VMEM),
             ],
-            out_specs=(
-                pl.BlockSpec((1, rows, cols), lambda i, p: (i, 0, 0)),
-                pl.BlockSpec(memory_space=pltpu.VMEM),
-                pl.BlockSpec(memory_space=pltpu.VMEM),
-            ),
-            scratch_shapes=[pltpu.VMEM((6, kl_terms, rows, cols), jnp.float32)],
+            out_specs=pl.BlockSpec((1, rows, cols), lambda i, p: (i, 0, 0)),
+            scratch_shapes=[pltpu.VMEM((5, kl_terms, rows, cols), jnp.float32)],
         ),
         compiler_params=pltpu.CompilerParams(
             dimension_semantics=("arbitrary",), vmem_limit_bytes=48 * 1024 * 1024
         ),
+    )(partners, weights, every, coef)
+
+
+def rim_kernel(partners, weights, every, coef, to_prev, to_next):
+    own_modes, cols = to_prev.shape
+    kl_terms = coef.shape[0]
+    rows = every.shape[1]
+
+    def one_slot(slot, carry):
+        first = jnp.zeros((1, cols), jnp.float32)
+        last = jnp.zeros((1, cols), jnp.float32)
+        for k in range(kl_terms):
+            j0 = partners[slot, 2 * k]
+            j1 = partners[slot, 2 * k + 1]
+            w0 = weights[slot, 2 * k]
+            w1 = weights[slot, 2 * k + 1]
+            c_first = 0.5 * (coef[k, pl.ds(1, 1), :] + coef[k, pl.ds(0, 1), :])
+            c_last = 0.5 * (coef[k, pl.ds(rows, 1), :] + coef[k, pl.ds(rows + 1, 1), :])
+            first = first + c_first * (w0 * every[j0, pl.ds(0, 1), :] + w1 * every[j1, pl.ds(0, 1), :])
+            last = last + c_last * (w0 * every[j0, pl.ds(rows - 1, 1), :] + w1 * every[j1, pl.ds(rows - 1, 1), :])
+        to_prev[pl.ds(slot, 1), :] = first
+        to_next[pl.ds(slot, 1), :] = last
+        return carry
+
+    lax.fori_loop(0, own_modes, one_slot, 0)
+
+
+def rim_apply(every, coef, partners, weights):
+    own_modes = partners.shape[0]
+    cols = every.shape[2]
+    return pl.pallas_call(
+        rim_kernel,
+        out_shape=(
+            jax.ShapeDtypeStruct((own_modes, cols), jnp.float32),
+            jax.ShapeDtypeStruct((own_modes, cols), jnp.float32),
+        ),
+        grid_spec=pltpu.PrefetchScalarGridSpec(
+            num_scalar_prefetch=1,
+            grid=(),
+            in_specs=[pl.BlockSpec(memory_space=pltpu.SMEM)] + [pl.BlockSpec(memory_space=pltpu.VMEM)] * 2,
+            out_specs=(pl.BlockSpec(memory_space=pltpu.VMEM), pl.BlockSpec(memory_space=pltpu.VMEM)),
+        ),
+        compiler_params=pltpu.CompilerParams(vmem_limit_bytes=48 * 1024 * 1024),
     )(partners, weights, every, coef)
 
 

time: 114 us -> 115 us (level)
  Pallas kernels: 10.6 us -> 15.7 us
  waiting for transfers between devices: 36.9 us -> 32.6 us
    pallas_call x1 -> x2, Pallas kernels: 10.6 us -> 15.7 us  [the longest x1 10.4 us: stencil_apply(): pl.pallas_call(stencil_kernel, out_shape=jax.ShapeDtypeStruct((own_modes,...]
    ppermute x2, waiting for transfers between devices: 4.34 us -> 0.01 us  [space_halo(): lax.ppermute(edge_first, 'space', down)]
  transfers between devices with their start and end apart: 13 -> 13, of which waited for: 5 -> 4; matrix products, arithmetic and copies ran while one was open for 29% -> 29% of each run, Pallas kernels for 0% -> 9%
where the time goes in v9:
time: 115 us; the launch traced here: 114 us
  waiting for transfers between devices  32.6 us (28%)
  starting transfers between devices  28.6 us (25%)
  local copies, waits for them, and re-layouts  20.8 us (18%)
  other arithmetic  15.8 us (14%)
  Pallas kernels  15.7 us (14%)
    ppermute x8, waiting for transfers between devices, shifted(): lax.ppermute(x, 'chaos', [(c, (c + step) % count) for c in range(count)])  32.6 us
    ppermute x8, starting transfers between devices, shifted(): lax.ppermute(x, 'chaos', [(c, (c + step) % count) for c in range(count)])  11 us
    pallas_call x1, Pallas kernels, stencil_apply(): pl.pallas_call(stencil_kernel, out_shape=jax.ShapeDtypeStruct((own_modes,...  10.4 us
    ppermute x2, starting transfers between devices, space_halo(): lax.ppermute(edge_last, 'space', up)  10.1 us
    unnamed x18, local copies, waits for them, and re-layouts  7.22 us
    pallas_call x1, Pallas kernels, rim_apply(): pl.pallas_call(rim_kernel, out_shape=(jax.ShapeDtypeStruct((own_modes, co...  5.37 us
    scatter-add x1, other arithmetic, coupling_table(): jnp.zeros((kl_terms * mode_count * mode_count,), jnp.float32).at[flat_index]  4.71 us
    ppermute x2, starting transfers between devices, space_halo(): lax.ppermute(edge_first, 'space', down)  3.84 us
  transfers between devices with their start and end apart: 13, of which 4 were waited for; matrix products, arithmetic and copies ran while one was open for 29% of the time, Pallas kernels for 9%

profile of v9, /device:TPU:1, one launch (start us, length us, event | category | flops | bytes accessed | tf_op | source)
XLA Modules:
  0.0 114.0 jit_solution(1016582025309215330)
XLA Ops:
  0.0 3.7 %collective-permute-start = (f32[15,8,2048]{2,1,0:T(8,128)}, f32[15,8,2048]{2,1,0:T(8,128)}, u32[]{:S(2)}, u32[]{:S(2)}) collective-permute-start(f32[15,8,2048]{2,1,0:T(8,128)} %param.7), channel_id=1, source_target_pairs={{0,16},{16,0},{32,48},{48,32},{64,80},{80,64},{96,112},{112,96},{1... | collective-permute-start | bytes 2949128 | tf_op jit(solution)/shard_map/ppermute | solution.py:62
  4.9 1.5 %collective-permute-start.5 = (f32[15,8,2048]{2,1,0:T(8,128)}, f32[15,8,2048]{2,1,0:T(8,128)S(1)}, u32[]{:S(2)}, u32[]{:S(2)}) collective-permute-start(f32[15,8,2048]{2,1,0:T(8,128)} %param.7), channel_id=1, source_target_pairs={{0,96},{16,112},{32,0},{48,16},{64,32},{80,48},{96,64},{112,80},{1... | collective-permute-start | bytes 2949128 | tf_op jit(solution)/shard_map/ppermute | solution.py:53
  6.4 2.0 %fusion.19 = (f32[8,1,2048]{2,1,0:T(1,128)}, f32[8,1,2048]{2,1,0:T(1,128)}) fusion(f32[8,8,2048]{2,1,0:T(8,128)} %param.8), kind=kLoop, calls=%fused_computation.70 | loop fusion | bytes 262144 | tf_op jit(solution)/shard_map/slice | solution.py:112
  8.4 4.9 %collective-permute-start.2 = (f32[8,1,2048]{2,1,0:T(1,128)}, f32[8,1,2048]{2,1,0:T(1,128)}, u32[]{:S(2)}, u32[]{:S(2)}) collective-permute-start(f32[8,1,2048]{2,1,0:T(1,128)} %get-tuple-element.26), channel_id=1, source_target_pairs={{0,1},{1,2},{2,3},{3,4},{4,5},{5,6},{6,7},{7,8},{8,9},{9,10},{10,1... | collective-permute-start | bytes 196616 | tf_op jit(solution)/shard_map/ppermute | solution.py:85
  13.3 1.9 %collective-permute-start.3 = (f32[8,1,2048]{2,1,0:T(1,128)}, f32[8,1,2048]{2,1,0:T(1,128)}, u32[]{:S(2)}, u32[]{:S(2)}) collective-permute-start(f32[8,1,2048]{2,1,0:T(1,128)} %get-tuple-element.27), channel_id=1, source_target_pairs={{1,0},{2,1},{3,2},{4,3},{5,4},{6,5},{7,6},{8,7},{9,8},{10,9},{11,1... | collective-permute-start | bytes 196616 | tf_op jit(solution)/shard_map/ppermute | solution.py:85
  18.3 4.7 %scatter_custom_fusion = f32[115200]{0:T(1024)S(1)} fusion(s32[624]{0:T(1024)S(1)} %fusion.15, f32[624]{0:T(1024)S(1)} %fusion.17, f32[]{:T(128)} %constant.103.clone.1), kind=kCustom, calls=%fused_computation.10 | custom fusion | flops 624 | bytes 460804 | tf_op jit(solution)/shard_map/scatter-add | solution.py:35
  28.0 2.1 %gather_fusion.3 = f32[120]{0:T(128)S(1)} fusion(f32[8,15,120]{2,1,0:T(8,128)S(1)} %get-tuple-element.25, s32[120]{0:T(128)S(1)} %reshape.106), kind=kCustom, calls=%fused_computation.1.clone | custom fusion | bytes 2400 | tf_op jit(solution)/shard_map/jit(take_along_axis)/gather | solution.py:46
  31.0 2.1 %gather_fusion.2 = f32[120]{0:T(128)S(1)} fusion(f32[8,15,120]{2,1,0:T(8,128)S(1)} %get-tuple-element.25, s32[120]{0:T(128)S(1)} %reshape.100), kind=kCustom, calls=%fused_computation.clone | custom fusion | bytes 2400 | tf_op jit(solution)/shard_map/jit(take_along_axis)/gather | solution.py:45
  33.2 1.2 %iota_reduce_fusion.2 = (pred[120]{0:T(512)(128)(4,1)}, s32[120]{0:T(128)S(1)}) fusion(s32[120]{0:T(128)} %and_select_fusion.2, s32[8]{0:T(128)S(1)} %stack.50), kind=kLoop, calls=%fused_computation.51 | loop fusion | flops 6840 | bytes 1112 | tf_op jit(solution)/shard_map/local/reduce | solution.py:105
  36.0 1.2 %gather_fusion = s32[120]{0:T(128)S(1)} fusion(s32[120]{0:T(128)S(1)} %fusion.18, s32[1024]{0:T(1024)S(1)} %get-tuple-element.31), kind=kCustom, calls=%fused_computation.2 | custom fusion | bytes 1440 | tf_op jit(solution)/shard_map/gather | solution.py:107
  37.3 1.2 %gather_fusion.1 = s32[120]{0:T(128)S(1)} fusion(s32[120]{0:T(128)S(1)} %fusion.18, s32[1024]{0:T(1024)S(1)} %get-tuple-element.30), kind=kCustom, calls=%fused_computation.3 | custom fusion | bytes 1440 | tf_op jit(solution)/shard_map/gather | solution.py:108
  40.6 2.7 %collective-permute-start.7 = (f32[15,8,1024]{2,1,0:T(8,128)S(1)}, f32[15,8,1024]{2,1,0:T(8,128)S(1)}, u32[]{:S(2)}, u32[]{:S(2)}) collective-permute-start(f32[15,8,1024]{2,1,0:T(8,128)S(1)} %slice.73), channel_id=1, source_target_pairs={{0,96},{16,112},{32,0},{48,16},{64,32},{80,48},{96,64},{112,80},{1... | collective-permute-start | bytes 1474568 | tf_op jit(solution)/shard_map/ppermute | solution.py:53
  43.3 2.7 %collective-permute-start.8 = (f32[15,8,2048]{2,1,0:T(8,128)}, f32[15,8,2048]{2,1,0:T(8,128)S(1)}, u32[]{:S(2)}, u32[]{:S(2)}) collective-permute-start(f32[15,8,2048]{2,1,0:T(8,128)} %collective-permute-done), channel_id=1, source_target_pairs={{0,96},{16,112},{32,0},{48,16},{64,32},{80,48},{96,64},{112,80},{1... | collective-permute-start | bytes 2949128 | tf_op jit(solution)/shard_map/ppermute | solution.py:53
  46.2 8.8 %collective-permute-done.6 = f32[15,8,1024]{2,1,0:T(8,128)S(1)} collective-permute-done((f32[15,8,1024]{2,1,0:T(8,128)S(1)}, f32[15,8,1024]{2,1,0:T(8,128)S(1)}, u32[]{:S(2)}, u32[]{:S(2)}) %collective-permute-start.6) | collective-permute-done | bytes 491552 | tf_op jit(solution)/shard_map/ppermute | solution.py:53
  55.1 1.3 %constant_dynamic-update-slice_fusion.2 = f32[120,8,2048]{2,1,0:T(8,128)S(1)} fusion(f32[120,8,2048]{2,1,0:T(8,128)S(1)} %maximum_dynamic-update-slice_fusion.1, f32[15,8,2048]{2,1,0:T(8,128)} %collective-permute-done), kind=kLoop, calls=%fused_computation.17 | loop fusion | bytes 1966080
  56.4 17.7 %collective-permute-done.1 = f32[15,8,2048]{2,1,0:T(8,128)S(1)} collective-permute-done((f32[15,8,2048]{2,1,0:T(8,128)}, f32[15,8,2048]{2,1,0:T(8,128)S(1)}, u32[]{:S(2)}, u32[]{:S(2)}) %collective-permute-start.1) | collective-permute-done | bytes 983072 | tf_op jit(solution)/shard_map/ppermute | solution.py:53
  75.4 2.8 %collective-permute-start.10 = (f32[15,8,1024]{2,1,0:T(8,128)S(1)}, f32[15,8,1024]{2,1,0:T(8,128)S(1)}, u32[]{:S(2)}, u32[]{:S(2)}) collective-permute-start(f32[15,8,1024]{2,1,0:T(8,128)S(1)} %slice.74), channel_id=1, source_target_pairs={{0,96},{16,112},{32,0},{48,16},{64,32},{80,48},{96,64},{112,80},{1... | collective-permute-start | bytes 1474568 | tf_op jit(solution)/shard_map/ppermute | solution.py:53
  78.4 2.3 %constant_dynamic-update-slice_fusion.1 = f32[120,8,2048]{2,1,0:T(8,128)} fusion(f32[120,8,2048]{2,1,0:T(8,128)} %copy-done, f32[15,8,2048]{2,1,0:T(8,128)} %copy-done.1), kind=kLoop, calls=%fused_computation.16 | loop fusion | bytes 1966080
  80.6 2.3 %constant_dynamic-update-slice_fusion = f32[120,8,2048]{2,1,0:T(8,128)} fusion(f32[120,8,2048]{2,1,0:T(8,128)} %constant_dynamic-update-slice_fusion.1, f32[15,8,2048]{2,1,0:T(8,128)} %copy-done.2), kind=kLoop, calls=%fused_computation.15 | loop fusion | bytes 1966080
  82.9 4.9 %collective-permute-done.9 = f32[15,8,1024]{2,1,0:T(8,128)S(1)} collective-permute-done((f32[15,8,1024]{2,1,0:T(8,128)S(1)}, f32[15,8,1024]{2,1,0:T(8,128)S(1)}, u32[]{:S(2)}, u32[]{:S(2)}) %collective-permute-start.9) | collective-permute-done | bytes 491552 | tf_op jit(solution)/shard_map/ppermute | solution.py:53
  90.0 5.4 %shard_map.56 = (f32[15,2048]{1,0:T(8,128)S(1)}, f32[15,2048]{1,0:T(8,128)S(1)}) custom-call(s32[15,16]{1,0:T(8,128)S(1)} %copy.18.partners, f32[15,16]{1,0:T(8,128)S(1)} %copy.19.weights, f32[120,8,2048]{2,1,0:T(8,128)} %maximum_dynamic-update-slice_fusion.every, f32[8,10,2048]{2,1,0:T(8,128)S(1)} %pad_maximum_fusion.coef), custom_call_target="tpu_custom_call" | custom-call | tf_op jit(solution)/shard_map/pallas_call | solution.py:220
  95.3 5.2 %collective-permute-start.11 = (f32[15,2048]{1,0:T(8,128)S(1)}, f32[15,2048]{1,0:T(8,128)S(1)}, u32[]{:S(2)}, u32[]{:S(2)}) collective-permute-start(f32[15,2048]{1,0:T(8,128)S(1)} %get-tuple-element.22), channel_id=1, source_target_pairs={{0,1},{1,2},{2,3},{3,4},{4,5},{5,6},{6,7},{7,8},{8,9},{9,10},{10,1... | collective-permute-start | bytes 368648 | tf_op jit(solution)/shard_map/ppermute | solution.py:85
  100.5 1.9 %collective-permute-start.12 = (f32[15,2048]{1,0:T(8,128)S(1)}, f32[15,2048]{1,0:T(8,128)S(1)}, u32[]{:S(2)}, u32[]{:S(2)}) collective-permute-start(f32[15,2048]{1,0:T(8,128)S(1)} %get-tuple-element.23), channel_id=1, source_target_pairs={{1,0},{2,1},{3,2},{4,3},{5,4},{6,5},{7,6},{8,7},{9,8},{10,9},{11,1... | collective-permute-start | bytes 368648 | tf_op jit(solution)/shard_map/ppermute | solution.py:85
  102.4 10.4 %shard_map.55 = f32[15,8,2048]{2,1,0:T(8,128)S(1)} custom-call(s32[15,16]{1,0:T(8,128)S(1)} %copy.18.partners, f32[15,16]{1,0:T(8,128)S(1)} %copy.19.weights, f32[120,8,2048]{2,1,0:T(8,128)} %maximum_dynamic-update-slice_fusion.every, f32[8,10,2048]{2,1,0:T(8,128)S(1)} %pad_maximum_fusion.coef), custom_call_target="tpu_custom_call" | custom-call | tf_op jit(solution)/shard_map/pallas_call | solution.py:173
  (75 shorter events, 18.9 us)
Async XLA Ops:
  0.0 43.3 %collective-permute-start = (f32[15,8,2048]{2,1,0:T(8,128)}, f32[15,8,2048]{2,1,0:T(8,128)}, u32[]{:S(2)}, u32[]{:S(2)}) collective-permute-start(f32[15,8,2048]{2,1,0:T(8,128)} %param.7), channel_id=1, source_target_pairs={{0,16},{16,0},{32,48},{48,32},{64,80},{80,64},{96,112},{112,96},{1... | collective-permute-start | bytes 2949128 | tf_op jit(solution)/shard_map/ppermute | solution.py:62
  3.7 36.7 %collective-permute-start.4 = (f32[15,8,2048]{2,1,0:T(8,128)}, f32[15,8,2048]{2,1,0:T(8,128)S(1)}, u32[]{:S(2)}, u32[]{:S(2)}) collective-permute-start(f32[15,8,2048]{2,1,0:T(8,128)} %param.7), channel_id=1, source_target_pairs={{0,32},{16,48},{32,64},{48,80},{64,96},{80,112},{96,0},{112,16},{1... | collective-permute-start | bytes 2949128 | tf_op jit(solution)/shard_map/ppermute | solution.py:53
  4.9 35.6 %collective-permute-start.5 = (f32[15,8,2048]{2,1,0:T(8,128)}, f32[15,8,2048]{2,1,0:T(8,128)S(1)}, u32[]{:S(2)}, u32[]{:S(2)}) collective-permute-start(f32[15,8,2048]{2,1,0:T(8,128)} %param.7), channel_id=1, source_target_pairs={{0,96},{16,112},{32,0},{48,16},{64,32},{80,48},{96,64},{112,80},{1... | collective-permute-start | bytes 2949128 | tf_op jit(solution)/shard_map/ppermute | solution.py:53
  8.4 31.0 %collective-permute-start.2 = (f32[8,1,2048]{2,1,0:T(1,128)}, f32[8,1,2048]{2,1,0:T(1,128)}, u32[]{:S(2)}, u32[]{:S(2)}) collective-permute-start(f32[8,1,2048]{2,1,0:T(1,128)} %get-tuple-element.26), channel_id=1, source_target_pairs={{0,1},{1,2},{2,3},{3,4},{4,5},{5,6},{6,7},{7,8},{8,9},{9,10},{10,1... | collective-permute-start | bytes 196616 | tf_op jit(solution)/shard_map/ppermute | solution.py:85
  13.3 26.0 %collective-permute-start.3 = (f32[8,1,2048]{2,1,0:T(1,128)}, f32[8,1,2048]{2,1,0:T(1,128)}, u32[]{:S(2)}, u32[]{:S(2)}) collective-permute-start(f32[8,1,2048]{2,1,0:T(1,128)} %get-tuple-element.27), channel_id=1, source_target_pairs={{1,0},{2,1},{3,2},{4,3},{5,4},{6,5},{7,6},{8,7},{9,8},{10,9},{11,1... | collective-permute-start | bytes 196616 | tf_op jit(solution)/shard_map/ppermute | solution.py:85
  28.0 10.6 %copy-start.3 = (f32[15,8,2048]{2,1,0:T(8,128)S(1)}, f32[15,8,2048]{2,1,0:T(8,128)}, u32[]{:S(2)}) copy-start(f32[15,8,2048]{2,1,0:T(8,128)} %param.7) | copy-start | bytes 2949124
  30.1 9.3 %copy-start.4 = (f32[8,8,2048]{2,1,0:T(8,128)S(1)}, f32[8,8,2048]{2,1,0:T(8,128)}, u32[]{:S(2)}) copy-start(f32[8,8,2048]{2,1,0:T(8,128)} %param.8) | copy-start | bytes 1572868
  40.4 37.8 %copy-start.5 = (s32[15,8,2]{0,2,1:T(2,128)S(1)}, s32[15,8,2]{0,2,1:T(2,128)}, u32[]{:S(2)}) copy-start(s32[15,8,2]{0,2,1:T(2,128)} %copy.16) | copy-start | bytes 2884
  40.5 14.5 %collective-permute-start.6 = (f32[15,8,1024]{2,1,0:T(8,128)S(1)}, f32[15,8,1024]{2,1,0:T(8,128)S(1)}, u32[]{:S(2)}, u32[]{:S(2)}) collective-permute-start(f32[15,8,1024]{2,1,0:T(8,128)S(1)} %slice.72), channel_id=1, source_target_pairs={{0,32},{16,48},{32,64},{48,80},{64,96},{80,112},{96,0},{112,16},{1... | collective-permute-start | bytes 1474568 | tf_op jit(solution)/shard_map/ppermute | solution.py:53
  40.6 14.4 %collective-permute-start.7 = (f32[15,8,1024]{2,1,0:T(8,128)S(1)}, f32[15,8,1024]{2,1,0:T(8,128)S(1)}, u32[]{:S(2)}, u32[]{:S(2)}) collective-permute-start(f32[15,8,1024]{2,1,0:T(8,128)S(1)} %slice.73), channel_id=1, source_target_pairs={{0,96},{16,112},{32,0},{48,16},{64,32},{80,48},{96,64},{112,80},{1... | collective-permute-start | bytes 1474568 | tf_op jit(solution)/shard_map/ppermute | solution.py:53
  43.3 30.7 %collective-permute-start.1 = (f32[15,8,2048]{2,1,0:T(8,128)}, f32[15,8,2048]{2,1,0:T(8,128)S(1)}, u32[]{:S(2)}, u32[]{:S(2)}) collective-permute-start(f32[15,8,2048]{2,1,0:T(8,128)} %collective-permute-done), channel_id=1, source_target_pairs={{0,32},{16,48},{32,64},{48,80},{64,96},{80,112},{96,0},{112,16},{1... | collective-permute-start | bytes 2949128 | tf_op jit(solution)/shard_map/ppermute | solution.py:53
  43.3 30.8 %collective-permute-start.8 = (f32[15,8,2048]{2,1,0:T(8,128)}, f32[15,8,2048]{2,1,0:T(8,128)S(1)}, u32[]{:S(2)}, u32[]{:S(2)}) collective-permute-start(f32[15,8,2048]{2,1,0:T(8,128)} %collective-permute-done), channel_id=1, source_target_pairs={{0,96},{16,112},{32,0},{48,16},{64,32},{80,48},{96,64},{112,80},{1... | collective-permute-start | bytes 2949128 | tf_op jit(solution)/shard_map/ppermute | solution.py:53
  56.4 17.9 %copy-start = (f32[120,8,2048]{2,1,0:T(8,128)}, f32[120,8,2048]{2,1,0:T(8,128)S(1)}, u32[]{:S(2)}) copy-start(f32[120,8,2048]{2,1,0:T(8,128)S(1)} %constant_dynamic-update-slice_fusion.2) | copy-start | bytes 23592964
  74.1 0.9 copy-start.1
  74.1 13.7 %collective-permute-start.9 = (f32[15,8,1024]{2,1,0:T(8,128)S(1)}, f32[15,8,1024]{2,1,0:T(8,128)S(1)}, u32[]{:S(2)}, u32[]{:S(2)}) collective-permute-start(f32[15,8,1024]{2,1,0:T(8,128)S(1)} %slice.46), channel_id=1, source_target_pairs={{0,32},{16,48},{32,64},{48,80},{64,96},{80,112},{96,0},{112,16},{1... | collective-permute-start | bytes 1474568 | tf_op jit(solution)/shard_map/ppermute | solution.py:53
  74.2 1.2 %copy-start.2 = (f32[15,8,2048]{2,1,0:T(8,128)}, f32[15,8,2048]{2,1,0:T(8,128)S(1)}, u32[]{:S(2)}) copy-start(f32[15,8,2048]{2,1,0:T(8,128)S(1)} %collective-permute-done.8) | copy-start | bytes 2949124
  75.4 13.5 %collective-permute-start.10 = (f32[15,8,1024]{2,1,0:T(8,128)S(1)}, f32[15,8,1024]{2,1,0:T(8,128)S(1)}, u32[]{:S(2)}, u32[]{:S(2)}) collective-permute-start(f32[15,8,1024]{2,1,0:T(8,128)S(1)} %slice.74), channel_id=1, source_target_pairs={{0,96},{16,112},{32,0},{48,16},{64,32},{80,48},{96,64},{112,80},{1... | collective-permute-start | bytes 1474568 | tf_op jit(solution)/shard_map/ppermute | solution.py:53
  95.3 17.5 %collective-permute-start.11 = (f32[15,2048]{1,0:T(8,128)S(1)}, f32[15,2048]{1,0:T(8,128)S(1)}, u32[]{:S(2)}, u32[]{:S(2)}) collective-permute-start(f32[15,2048]{1,0:T(8,128)S(1)} %get-tuple-element.22), channel_id=1, source_target_pairs={{0,1},{1,2},{2,3},{3,4},{4,5},{5,6},{6,7},{7,8},{8,9},{9,10},{10,1... | collective-permute-start | bytes 368648 | tf_op jit(solution)/shard_map/ppermute | solution.py:85
  100.5 12.3 %collective-permute-start.12 = (f32[15,2048]{1,0:T(8,128)S(1)}, f32[15,2048]{1,0:T(8,128)S(1)}, u32[]{:S(2)}, u32[]{:S(2)}) collective-permute-start(f32[15,2048]{1,0:T(8,128)S(1)} %get-tuple-element.23), channel_id=1, source_target_pairs={{1,0},{2,1},{3,2},{4,3},{5,4},{6,5},{7,6},{8,7},{9,8},{10,9},{11,1... | collective-permute-start | bytes 368648 | tf_op jit(solution)/shard_map/ppermute | solution.py:85

commit v10 on v8

--- a/solution.py
+++ b/solution.py
@@ -6,46 +6,11 @@
 from jax.sharding import PartitionSpec as P
 
 
-def extended_2(x, sides, width):
-    for axis, dim in sides:
-        count, length = (lax.axis_size(axis), x.shape[dim])
-        up = [(i, (i + 1) % count) for i in range(count - 1)]
-        down = [(j, i) for i, j in up]
-        last = lax.slice_in_dim(x, length - width, length, axis=dim)
-        first = lax.slice_in_dim(x, 0, width, axis=dim)
-        before = lax.ppermute(last, axis, up)
-        after = lax.ppermute(first, axis, down)
-        x = jnp.concatenate([before, x, after], axis=dim)
-    return x
-
-
 def shift_cols(x, direction):
     zero = jnp.zeros_like(x[..., :1])
     if direction > 0:
         return jnp.concatenate([zero, x[..., :-1]], axis=-1)
     return jnp.concatenate([x[..., 1:], zero], axis=-1)
-
-
-def coupling_table(triples, ratios, mode_of_slot, kl_terms, mode_count):
-    matches = triples[:, :2, None] == mode_of_slot[None, None, :]
-    slot_pairs = jnp.sum(jnp.where(matches, jnp.arange(mode_count, dtype=jnp.int32), 0), axis=2)
-    weights = ratios[:, 0].astype(jnp.float32) / ratios[:, 1].astype(jnp.float32)
-    flat_index = (triples[:, 2] * mode_count + slot_pairs[:, 0]) * mode_count + slot_pairs[:, 1]
-    coupling = (
-        jnp.zeros((kl_terms * mode_count * mode_count,), jnp.float32).at[flat_index].add(weights)
-    )
-    return coupling.reshape(kl_terms, mode_count, mode_count)
-
-
-def neighbour_table(local_rows):
-    mode_count = local_rows.shape[-1]
-    present = local_rows > 0
-    first = jnp.argmax(present, axis=-1).astype(jnp.int32)
-    last = (mode_count - 1 - jnp.argmax(present[..., ::-1], axis=-1)).astype(jnp.int32)
-    w_first = jnp.take_along_axis(local_rows, first[..., None], axis=-1)[..., 0]
-    w_last = jnp.take_along_axis(local_rows, last[..., None], axis=-1)[..., 0]
-    w_last = jnp.where(last == first, jnp.zeros_like(w_last), w_last)
-    return first, last, w_first, w_last
 
 
 def shifted(x, step):
@@ -92,17 +57,25 @@
          me ^ 1, ((me ^ 1) - 2) % groups, ((me ^ 1) + 2) % groups, ((me ^ 1) + 4) % groups]
     ).astype(jnp.int32)
 
-    first_slot = me * own_modes
-    coupling = coupling_table(triples, ratios, mode_of_slot, kl_terms, mode_count)
-    local_rows = lax.dynamic_slice_in_dim(coupling, first_slot, own_modes, 1)
-    first, last, w_first, w_last = neighbour_table(local_rows)
-    owner = jnp.arange(mode_count, dtype=jnp.int32) // own_modes
-    position = jnp.argmax(order[None, :] == owner[:, None], axis=1).astype(jnp.int32)
-    place = position * own_modes + jnp.arange(mode_count, dtype=jnp.int32) % own_modes
-    first = place[first]
-    last = place[last]
-    weights = jnp.stack([w_first, w_last], axis=-1).transpose(1, 0, 2).reshape(own_modes, 2 * kl_terms)
-    partners = jnp.stack([first, last], axis=-1).transpose(1, 0, 2).reshape(own_modes, 2 * kl_terms)
+    slot_ids = jnp.arange(mode_count, dtype=jnp.int32)
+    slot_of_mode = jnp.sum(jnp.where(mode_of_slot[None, :] == slot_ids[:, None], slot_ids[None, :], 0), axis=1)
+    position = jnp.argmax(order[None, :] == (slot_ids // own_modes)[:, None], axis=1).astype(jnp.int32)
+    place = position * own_modes + slot_ids % own_modes
+    local_modes = lax.dynamic_slice_in_dim(mode_of_slot, me * own_modes, own_modes)
+    row_count = triples.shape[0]
+    hit = (triples[None, None, :, 0] == local_modes[:, None, None]) & (
+        triples[None, None, :, 2] == jnp.arange(kl_terms, dtype=jnp.int32)[None, :, None]
+    )
+    found = jnp.any(hit, axis=-1)
+    t0 = jnp.argmax(hit, axis=-1).astype(jnp.int32)
+    t1 = (row_count - 1 - jnp.argmax(hit[..., ::-1], axis=-1)).astype(jnp.int32)
+    row_weight = ratios[:, 0].astype(jnp.float32) / ratios[:, 1].astype(jnp.float32)
+    w_first = jnp.where(found, row_weight[t0], 0.0)
+    w_last = jnp.where(found & (t1 != t0), row_weight[t1], 0.0)
+    first = place[slot_of_mode[triples[t0, 1]]]
+    last = place[slot_of_mode[triples[t1, 1]]]
+    weights = jnp.stack([w_first, w_last], axis=-1).reshape(own_modes, 2 * kl_terms)
+    partners = jnp.stack([first, last], axis=-1).reshape(own_modes, 2 * kl_terms)
 
     above, below = space_halo(kl_fields[:, rows - 1:], kl_fields[:, :1])
     coef = jnp.concatenate([above, kl_fields, below], axis=1)

time: 114 us -> 111 us (0.974)
  local copies, waits for them, and re-layouts: 20.8 us -> 28.1 us
  other arithmetic: 15.9 us -> 9.65 us
  waiting for transfers between devices: 36.9 us -> 33.1 us
    scatter-add x1 -> x0, other arithmetic: 4.71 us -> none  [coupling_table(): jnp.zeros((kl_terms * mode_count * mode_count,), jnp.float32).at[flat_index]]
    unnamed x18 -> x17, local copies, waits for them, and re-layouts: 7.22 us -> 11.7 us
    ppermute x8, waiting for transfers between devices: 32.6 us -> 28.7 us  [shifted(): lax.ppermute(x, 'chaos', [(c, (c + step) % count) for c in range(count)])]
    gather x8 -> x14, local copies, waits for them, and re-layouts: 7.61 us -> 11.4 us  [the longest x5 4.66 us: local(): last = place[slot_of_mode[triples[t1, 1]]]]
    select_n x5 -> x8, other arithmetic: 2.46 us -> 0.06 us  [the longest x3 0.02 us: local(): first = place[slot_of_mode[triples[t0, 1]]]]
    broadcast_in_dim x2, local copies, waits for them, and re-layouts: 1.5 us -> 0.16 us  [the longest x1 0.08 us: local(): first = place[slot_of_mode[triples[t0, 1]]]]
    another operation x4 -> x5, other arithmetic: 3.08 us -> 3.28 us  [the longest x2 2.59 us: local(): t0 = jnp.argmax(hit, axis=-1).astype(jnp.int32)]
  transfers between devices with their start and end apart: 13 -> 13, of which waited for: 5 -> 5; matrix products, arithmetic and copies ran while one was open for 29% -> 31% of each run, Pallas kernels for 0% -> 0%
where the time goes in v10:
time: 111 us; the launch traced here: 110 us
  waiting for transfers between devices  33.1 us (30%)
  starting transfers between devices  28.6 us (26%)
  local copies, waits for them, and re-layouts  28.1 us (25%)
  Pallas kernels  10.6 us (10%)
  other arithmetic  9.65 us (9%)
    ppermute x8, waiting for transfers between devices, shifted(): lax.ppermute(x, 'chaos', [(c, (c + step) % count) for c in range(count)])  28.7 us
    unnamed x17, local copies, waits for them, and re-layouts  11.7 us
    ppermute x8, starting transfers between devices, shifted(): lax.ppermute(x, 'chaos', [(c, (c + step) % count) for c in range(count)])  11 us
    pallas_call x1, Pallas kernels, stencil_apply(): pl.pallas_call(stencil_kernel, out_shape=(jax.ShapeDtypeStruct((own_modes...  10.6 us
    ppermute x2, starting transfers between devices, space_halo(): lax.ppermute(edge_last, 'space', up)  10.1 us
    gather x5, local copies, waits for them, and re-layouts, local(): last = place[slot_of_mode[triples[t1, 1]]]  4.66 us
    gather x5, local copies, waits for them, and re-layouts, local(): first = place[slot_of_mode[triples[t0, 1]]]  4.65 us
    ppermute x2, waiting for transfers between devices, space_halo(): lax.ppermute(edge_first, 'space', down)  4.34 us
  transfers between devices with their start and end apart: 13, of which 5 were waited for; matrix products, arithmetic and copies ran while one was open for 31% of the time, Pallas kernels for 0%

profile of v10, /device:TPU:1, one launch (start us, length us, event | category | flops | bytes accessed | tf_op | source)
XLA Modules:
  0.0 110.5 jit_solution(3912854076736857462)
XLA Ops:
  0.0 3.7 %collective-permute-start = (f32[15,8,2048]{2,1,0:T(8,128)}, f32[15,8,2048]{2,1,0:T(8,128)}, u32[]{:S(2)}, u32[]{:S(2)}) collective-permute-start(f32[15,8,2048]{2,1,0:T(8,128)} %param.5), channel_id=1, source_target_pairs={{0,16},{16,0},{32,48},{48,32},{64,80},{80,64},{96,112},{112,96},{1... | collective-permute-start | bytes 2949128 | tf_op jit(solution)/shard_map/ppermute | solution.py:25
  4.9 1.5 %collective-permute-start.5 = (f32[15,8,2048]{2,1,0:T(8,128)}, f32[15,8,2048]{2,1,0:T(8,128)S(1)}, u32[]{:S(2)}, u32[]{:S(2)}) collective-permute-start(f32[15,8,2048]{2,1,0:T(8,128)} %param.5), channel_id=1, source_target_pairs={{0,96},{16,112},{32,0},{48,16},{64,32},{80,48},{96,64},{112,80},{1... | collective-permute-start | bytes 2949128 | tf_op jit(solution)/shard_map/ppermute | solution.py:18
  6.4 2.0 %fusion.2 = (f32[8,1,2048]{2,1,0:T(1,128)}, f32[8,1,2048]{2,1,0:T(1,128)}) fusion(f32[8,8,2048]{2,1,0:T(8,128)} %param.6), kind=kLoop, calls=%fused_computation.57 | loop fusion | bytes 262144 | tf_op jit(solution)/shard_map/slice | solution.py:80
  8.4 4.9 %collective-permute-start.2 = (f32[8,1,2048]{2,1,0:T(1,128)}, f32[8,1,2048]{2,1,0:T(1,128)}, u32[]{:S(2)}, u32[]{:S(2)}) collective-permute-start(f32[8,1,2048]{2,1,0:T(1,128)} %get-tuple-element.27), channel_id=1, source_target_pairs={{0,1},{1,2},{2,3},{3,4},{4,5},{5,6},{6,7},{7,8},{8,9},{9,10},{10,1... | collective-permute-start | bytes 196616 | tf_op jit(solution)/shard_map/ppermute | solution.py:45
  13.3 1.9 %collective-permute-start.3 = (f32[8,1,2048]{2,1,0:T(1,128)}, f32[8,1,2048]{2,1,0:T(1,128)}, u32[]{:S(2)}, u32[]{:S(2)}) collective-permute-start(f32[8,1,2048]{2,1,0:T(1,128)} %get-tuple-element.28), channel_id=1, source_target_pairs={{1,0},{2,1},{3,2},{4,3},{5,4},{6,5},{7,6},{8,7},{9,8},{10,9},{11,1... | collective-permute-start | bytes 196616 | tf_op jit(solution)/shard_map/ppermute | solution.py:45
  19.8 1.4 %iota_reduce_fusion = (pred[15,8]{1,0:T(8,128)(4,1)}, s32[15,8]{1,0:T(8,128)S(1)}) fusion(pred[15,8,640]{2,1,0:T(8,128)(4,1)S(1)} %reverse), kind=kLoop, calls=%fused_computation.12 | loop fusion | flops 523320 | bytes 75480 | tf_op jit(solution)/shard_map/local/reduce | solution.py:70
  24.6 2.0 %gather_fusion.3 = s32[120]{0:T(128)S(1)} fusion(s32[624,3]{0,1:T(4,128)S(1)} %copy-done, s32[120]{0:T(128)S(1)} %reshape.174), kind=kCustom, calls=%fused_computation.3 | custom fusion | bytes 1920 | tf_op jit(solution)/shard_map/gather | solution.py:76
  26.9 1.2 %gather_fusion.4 = s32[120]{0:T(128)S(1)} fusion(s32[120]{0:T(128)S(1)} %select_reduce_fusion, s32[1024]{0:T(1024)S(1)} %pad_clamp_fusion.3), kind=kCustom, calls=%fused_computation.4 | custom fusion | bytes 1440 | tf_op jit(solution)/shard_map/gather | solution.py:76
  28.3 2.0 %gather_fusion = s32[120]{0:T(128)S(1)} fusion(s32[624,3]{0,1:T(4,128)S(1)} %copy-done, s32[120]{0:T(128)S(1)} %reshape.152), kind=kCustom, calls=%fused_computation | custom fusion | bytes 1920 | tf_op jit(solution)/shard_map/gather | solution.py:75
  30.5 1.2 %gather_fusion.1 = s32[120]{0:T(128)S(1)} fusion(s32[120]{0:T(128)S(1)} %select_reduce_fusion, s32[1024]{0:T(1024)S(1)} %pad_clamp_fusion.5), kind=kCustom, calls=%fused_computation.1 | custom fusion | bytes 1440 | tf_op jit(solution)/shard_map/gather | solution.py:75
  34.2 1.2 %gather_fusion.5 = s32[120]{0:T(128)S(1)} fusion(s32[120]{0:T(128)S(1)} %fusion.1, s32[1024]{0:T(1024)S(1)} %get-tuple-element.39), kind=kCustom, calls=%fused_computation.5 | custom fusion | bytes 1440 | tf_op jit(solution)/shard_map/gather | solution.py:76
  37.9 2.7 %collective-permute-start.7 = (f32[15,8,1024]{2,1,0:T(8,128)S(1)}, f32[15,8,1024]{2,1,0:T(8,128)S(1)}, u32[]{:S(2)}, u32[]{:S(2)}) collective-permute-start(f32[15,8,1024]{2,1,0:T(8,128)S(1)} %slice.57), channel_id=1, source_target_pairs={{0,96},{16,112},{32,0},{48,16},{64,32},{80,48},{96,64},{112,80},{1... | collective-permute-start | bytes 1474568 | tf_op jit(solution)/shard_map/ppermute | solution.py:18
  40.7 2.7 %collective-permute-start.8 = (f32[15,8,2048]{2,1,0:T(8,128)}, f32[15,8,2048]{2,1,0:T(8,128)S(1)}, u32[]{:S(2)}, u32[]{:S(2)}) collective-permute-start(f32[15,8,2048]{2,1,0:T(8,128)} %collective-permute-done), channel_id=1, source_target_pairs={{0,96},{16,112},{32,0},{48,16},{64,32},{80,48},{96,64},{112,80},{1... | collective-permute-start | bytes 2949128 | tf_op jit(solution)/shard_map/ppermute | solution.py:18
  45.5 6.8 %collective-permute-done.6 = f32[15,8,1024]{2,1,0:T(8,128)S(1)} collective-permute-done((f32[15,8,1024]{2,1,0:T(8,128)S(1)}, f32[15,8,1024]{2,1,0:T(8,128)S(1)}, u32[]{:S(2)}, u32[]{:S(2)}) %collective-permute-start.6) | collective-permute-done | bytes 491552 | tf_op jit(solution)/shard_map/ppermute | solution.py:18
  53.3 2.3 %constant_dynamic-update-slice_fusion.2 = f32[120,8,2048]{2,1,0:T(8,128)} fusion(f32[120,8,2048]{2,1,0:T(8,128)} %maximum_dynamic-update-slice_fusion.1, f32[15,8,2048]{2,1,0:T(8,128)} %collective-permute-done), kind=kLoop, calls=%fused_computation.29 | loop fusion | bytes 1966080
  55.6 15.8 %collective-permute-done.1 = f32[15,8,2048]{2,1,0:T(8,128)S(1)} collective-permute-done((f32[15,8,2048]{2,1,0:T(8,128)}, f32[15,8,2048]{2,1,0:T(8,128)S(1)}, u32[]{:S(2)}, u32[]{:S(2)}) %collective-permute-start.1) | collective-permute-done | bytes 983072 | tf_op jit(solution)/shard_map/ppermute | solution.py:18
  72.8 2.8 %collective-permute-start.10 = (f32[15,8,1024]{2,1,0:T(8,128)S(1)}, f32[15,8,1024]{2,1,0:T(8,128)S(1)}, u32[]{:S(2)}, u32[]{:S(2)}) collective-permute-start(f32[15,8,1024]{2,1,0:T(8,128)S(1)} %slice.58), channel_id=1, source_target_pairs={{0,96},{16,112},{32,0},{48,16},{64,32},{80,48},{96,64},{112,80},{1... | collective-permute-start | bytes 1474568 | tf_op jit(solution)/shard_map/ppermute | solution.py:18
  75.7 2.3 %constant_dynamic-update-slice_fusion.1 = f32[120,8,2048]{2,1,0:T(8,128)} fusion(f32[120,8,2048]{2,1,0:T(8,128)} %constant_dynamic-update-slice_fusion.2, f32[15,8,2048]{2,1,0:T(8,128)} %copy-done.1), kind=kLoop, calls=%fused_computation.28 | loop fusion | bytes 1966080
  77.9 2.3 %constant_dynamic-update-slice_fusion = f32[120,8,2048]{2,1,0:T(8,128)} fusion(f32[120,8,2048]{2,1,0:T(8,128)} %constant_dynamic-update-slice_fusion.1, f32[15,8,2048]{2,1,0:T(8,128)} %copy-done.2), kind=kLoop, calls=%fused_computation.27 | loop fusion | bytes 1966080
  80.2 4.9 %collective-permute-done.9 = f32[15,8,1024]{2,1,0:T(8,128)S(1)} collective-permute-done((f32[15,8,1024]{2,1,0:T(8,128)S(1)}, f32[15,8,1024]{2,1,0:T(8,128)S(1)}, u32[]{:S(2)}, u32[]{:S(2)}) %collective-permute-start.9) | collective-permute-done | bytes 491552 | tf_op jit(solution)/shard_map/ppermute | solution.py:18
  87.3 10.6 %shard_map.55 = (f32[15,8,2048]{2,1,0:T(8,128)S(1)}, f32[15,2048]{1,0:T(8,128)S(1)}, f32[15,2048]{1,0:T(8,128)S(1)}) custom-call(s32[15,16]{1,0:T(8,128)S(1)} %copy.20.partners, f32[15,16]{1,0:T(8,128)S(1)} %copy.21.weights, f32[120,8,2048]{2,1,0:T(8,128)} %maximum_dynamic-update-slice_fusion.every, f32[8,10,2048]{2,1,0:T(8,128)S(1)} %pad_maximum_fusion.coef), custom_call_target="tpu_custom_call" | custom-call | tf_op jit(solution)/shard_map/pallas_call | solution.py:145
  97.9 5.2 %collective-permute-start.11 = (f32[15,2048]{1,0:T(8,128)S(1)}, f32[15,2048]{1,0:T(8,128)S(1)}, u32[]{:S(2)}, u32[]{:S(2)}) collective-permute-start(f32[15,2048]{1,0:T(8,128)S(1)} %get-tuple-element.23), channel_id=1, source_target_pairs={{0,1},{1,2},{2,3},{3,4},{4,5},{5,6},{6,7},{7,8},{8,9},{9,10},{10,1... | collective-permute-start | bytes 368648 | tf_op jit(solution)/shard_map/ppermute | solution.py:45
  103.0 1.9 %collective-permute-start.12 = (f32[15,2048]{1,0:T(8,128)S(1)}, f32[15,2048]{1,0:T(8,128)S(1)}, u32[]{:S(2)}, u32[]{:S(2)}) collective-permute-start(f32[15,2048]{1,0:T(8,128)S(1)} %get-tuple-element.24), channel_id=1, source_target_pairs={{1,0},{2,1},{3,2},{4,3},{5,4},{6,5},{7,6},{8,7},{9,8},{10,9},{11,1... | collective-permute-start | bytes 368648 | tf_op jit(solution)/shard_map/ppermute | solution.py:45
  105.0 4.3 %collective-permute-done.12 = f32[15,2048]{1,0:T(8,128)S(1)} collective-permute-done((f32[15,2048]{1,0:T(8,128)S(1)}, f32[15,2048]{1,0:T(8,128)S(1)}, u32[]{:S(2)}, u32[]{:S(2)}) %collective-permute-start.12) | collective-permute-done | bytes 122912 | tf_op jit(solution)/shard_map/ppermute | solution.py:45
  (86 shorter events, 22.5 us)
Async XLA Ops:
  0.0 40.7 %collective-permute-start = (f32[15,8,2048]{2,1,0:T(8,128)}, f32[15,8,2048]{2,1,0:T(8,128)}, u32[]{:S(2)}, u32[]{:S(2)}) collective-permute-start(f32[15,8,2048]{2,1,0:T(8,128)} %param.5), channel_id=1, source_target_pairs={{0,16},{16,0},{32,48},{48,32},{64,80},{80,64},{96,112},{112,96},{1... | collective-permute-start | bytes 2949128 | tf_op jit(solution)/shard_map/ppermute | solution.py:25
  3.7 34.0 %collective-permute-start.4 = (f32[15,8,2048]{2,1,0:T(8,128)}, f32[15,8,2048]{2,1,0:T(8,128)S(1)}, u32[]{:S(2)}, u32[]{:S(2)}) collective-permute-start(f32[15,8,2048]{2,1,0:T(8,128)} %param.5), channel_id=1, source_target_pairs={{0,32},{16,48},{32,64},{48,80},{64,96},{80,112},{96,0},{112,16},{1... | collective-permute-start | bytes 2949128 | tf_op jit(solution)/shard_map/ppermute | solution.py:18
  4.9 32.9 %collective-permute-start.5 = (f32[15,8,2048]{2,1,0:T(8,128)}, f32[15,8,2048]{2,1,0:T(8,128)S(1)}, u32[]{:S(2)}, u32[]{:S(2)}) collective-permute-start(f32[15,8,2048]{2,1,0:T(8,128)} %param.5), channel_id=1, source_target_pairs={{0,96},{16,112},{32,0},{48,16},{64,32},{80,48},{96,64},{112,80},{1... | collective-permute-start | bytes 2949128 | tf_op jit(solution)/shard_map/ppermute | solution.py:18
  8.4 28.3 %collective-permute-start.2 = (f32[8,1,2048]{2,1,0:T(1,128)}, f32[8,1,2048]{2,1,0:T(1,128)}, u32[]{:S(2)}, u32[]{:S(2)}) collective-permute-start(f32[8,1,2048]{2,1,0:T(1,128)} %get-tuple-element.27), channel_id=1, source_target_pairs={{0,1},{1,2},{2,3},{3,4},{4,5},{5,6},{6,7},{7,8},{8,9},{9,10},{10,1... | collective-permute-start | bytes 196616 | tf_op jit(solution)/shard_map/ppermute | solution.py:45
  13.3 23.4 %collective-permute-start.3 = (f32[8,1,2048]{2,1,0:T(1,128)}, f32[8,1,2048]{2,1,0:T(1,128)}, u32[]{:S(2)}, u32[]{:S(2)}) collective-permute-start(f32[8,1,2048]{2,1,0:T(1,128)} %get-tuple-element.28), channel_id=1, source_target_pairs={{1,0},{2,1},{3,2},{4,3},{5,4},{6,5},{7,6},{8,7},{9,8},{10,9},{11,1... | collective-permute-start | bytes 196616 | tf_op jit(solution)/shard_map/ppermute | solution.py:45
  22.2 2.4 %copy-start = (s32[624,3]{0,1:T(4,128)S(1)}, s32[624,3]{0,1:T(4,128)}, u32[]{:S(2)}) copy-start(s32[624,3]{0,1:T(4,128)} %param.7) | copy-start | bytes 22468
  32.9 2.7 %copy-start.3 = (f32[15,8,2048]{2,1,0:T(8,128)S(1)}, f32[15,8,2048]{2,1,0:T(8,128)}, u32[]{:S(2)}) copy-start(f32[15,8,2048]{2,1,0:T(8,128)} %param.5) | copy-start | bytes 2949124
  32.9 3.8 %copy-start.4 = (f32[8,8,2048]{2,1,0:T(8,128)S(1)}, f32[8,8,2048]{2,1,0:T(8,128)}, u32[]{:S(2)}) copy-start(f32[8,8,2048]{2,1,0:T(8,128)} %param.6) | copy-start | bytes 1572868
  37.8 14.5 %collective-permute-start.6 = (f32[15,8,1024]{2,1,0:T(8,128)S(1)}, f32[15,8,1024]{2,1,0:T(8,128)S(1)}, u32[]{:S(2)}, u32[]{:S(2)}) collective-permute-start(f32[15,8,1024]{2,1,0:T(8,128)S(1)} %slice.56), channel_id=1, source_target_pairs={{0,32},{16,48},{32,64},{48,80},{64,96},{80,112},{96,0},{112,16},{1... | collective-permute-start | bytes 1474568 | tf_op jit(solution)/shard_map/ppermute | solution.py:18
  37.9 14.4 %collective-permute-start.7 = (f32[15,8,1024]{2,1,0:T(8,128)S(1)}, f32[15,8,1024]{2,1,0:T(8,128)S(1)}, u32[]{:S(2)}, u32[]{:S(2)}) collective-permute-start(f32[15,8,1024]{2,1,0:T(8,128)S(1)} %slice.57), channel_id=1, source_target_pairs={{0,96},{16,112},{32,0},{48,16},{64,32},{80,48},{96,64},{112,80},{1... | collective-permute-start | bytes 1474568 | tf_op jit(solution)/shard_map/ppermute | solution.py:18
  40.7 30.7 %collective-permute-start.1 = (f32[15,8,2048]{2,1,0:T(8,128)}, f32[15,8,2048]{2,1,0:T(8,128)S(1)}, u32[]{:S(2)}, u32[]{:S(2)}) collective-permute-start(f32[15,8,2048]{2,1,0:T(8,128)} %collective-permute-done), channel_id=1, source_target_pairs={{0,32},{16,48},{32,64},{48,80},{64,96},{80,112},{96,0},{112,16},{1... | collective-permute-start | bytes 2949128 | tf_op jit(solution)/shard_map/ppermute | solution.py:18
  40.7 30.8 %collective-permute-start.8 = (f32[15,8,2048]{2,1,0:T(8,128)}, f32[15,8,2048]{2,1,0:T(8,128)S(1)}, u32[]{:S(2)}, u32[]{:S(2)}) collective-permute-start(f32[15,8,2048]{2,1,0:T(8,128)} %collective-permute-done), channel_id=1, source_target_pairs={{0,96},{16,112},{32,0},{48,16},{64,32},{80,48},{96,64},{112,80},{1... | collective-permute-start | bytes 2949128 | tf_op jit(solution)/shard_map/ppermute | solution.py:18
  71.4 0.9 copy-start.1
  71.4 13.7 %collective-permute-start.9 = (f32[15,8,1024]{2,1,0:T(8,128)S(1)}, f32[15,8,1024]{2,1,0:T(8,128)S(1)}, u32[]{:S(2)}, u32[]{:S(2)}) collective-permute-start(f32[15,8,1024]{2,1,0:T(8,128)S(1)} %slice.38), channel_id=1, source_target_pairs={{0,32},{16,48},{32,64},{48,80},{64,96},{80,112},{96,0},{112,16},{1... | collective-permute-start | bytes 1474568 | tf_op jit(solution)/shard_map/ppermute | solution.py:18
  71.5 1.2 %copy-start.2 = (f32[15,8,2048]{2,1,0:T(8,128)}, f32[15,8,2048]{2,1,0:T(8,128)S(1)}, u32[]{:S(2)}) copy-start(f32[15,8,2048]{2,1,0:T(8,128)S(1)} %collective-permute-done.8) | copy-start | bytes 2949124
  72.8 13.5 %collective-permute-start.10 = (f32[15,8,1024]{2,1,0:T(8,128)S(1)}, f32[15,8,1024]{2,1,0:T(8,128)S(1)}, u32[]{:S(2)}, u32[]{:S(2)}) collective-permute-start(f32[15,8,1024]{2,1,0:T(8,128)S(1)} %slice.58), channel_id=1, source_target_pairs={{0,96},{16,112},{32,0},{48,16},{64,32},{80,48},{96,64},{112,80},{1... | collective-permute-start | bytes 1474568 | tf_op jit(solution)/shard_map/ppermute | solution.py:18
  97.9 7.1 %collective-permute-start.11 = (f32[15,2048]{1,0:T(8,128)S(1)}, f32[15,2048]{1,0:T(8,128)S(1)}, u32[]{:S(2)}, u32[]{:S(2)}) collective-permute-start(f32[15,2048]{1,0:T(8,128)S(1)} %get-tuple-element.23), channel_id=1, source_target_pairs={{0,1},{1,2},{2,3},{3,4},{4,5},{5,6},{6,7},{7,8},{8,9},{9,10},{10,1... | collective-permute-start | bytes 368648 | tf_op jit(solution)/shard_map/ppermute | solution.py:45
  103.0 6.3 %collective-permute-start.12 = (f32[15,2048]{1,0:T(8,128)S(1)}, f32[15,2048]{1,0:T(8,128)S(1)}, u32[]{:S(2)}, u32[]{:S(2)}) collective-permute-start(f32[15,2048]{1,0:T(8,128)S(1)} %get-tuple-element.24), channel_id=1, source_target_pairs={{1,0},{2,1},{3,2},{4,3},{5,4},{6,5},{7,6},{8,7},{9,8},{10,9},{11,1... | collective-permute-start | bytes 368648 | tf_op jit(solution)/shard_map/ppermute | solution.py:45

commit v11 on v10

--- a/solution.py
+++ b/solution.py
@@ -59,21 +59,25 @@
 
     slot_ids = jnp.arange(mode_count, dtype=jnp.int32)
     slot_of_mode = jnp.sum(jnp.where(mode_of_slot[None, :] == slot_ids[:, None], slot_ids[None, :], 0), axis=1)
-    position = jnp.argmax(order[None, :] == (slot_ids // own_modes)[:, None], axis=1).astype(jnp.int32)
-    place = position * own_modes + slot_ids % own_modes
+    owner_at = jnp.argmax(order[None, :] == jnp.arange(groups, dtype=jnp.int32)[:, None], axis=1).astype(jnp.int32)
+    place_of_mode = owner_at[slot_of_mode // own_modes] * own_modes + slot_of_mode % own_modes
+    partner_place = jnp.sum(
+        jnp.where(triples[:, 1:2] == slot_ids[None, :], place_of_mode[None, :], 0), axis=1
+    )
+    row_weight = ratios[:, 0].astype(jnp.float32) / ratios[:, 1].astype(jnp.float32)
     local_modes = lax.dynamic_slice_in_dim(mode_of_slot, me * own_modes, own_modes)
     row_count = triples.shape[0]
     hit = (triples[None, None, :, 0] == local_modes[:, None, None]) & (
         triples[None, None, :, 2] == jnp.arange(kl_terms, dtype=jnp.int32)[None, :, None]
     )
-    found = jnp.any(hit, axis=-1)
+    row_ids = jnp.arange(row_count, dtype=jnp.int32)
     t0 = jnp.argmax(hit, axis=-1).astype(jnp.int32)
-    t1 = (row_count - 1 - jnp.argmax(hit[..., ::-1], axis=-1)).astype(jnp.int32)
-    row_weight = ratios[:, 0].astype(jnp.float32) / ratios[:, 1].astype(jnp.float32)
-    w_first = jnp.where(found, row_weight[t0], 0.0)
-    w_last = jnp.where(found & (t1 != t0), row_weight[t1], 0.0)
-    first = place[slot_of_mode[triples[t0, 1]]]
-    last = place[slot_of_mode[triples[t1, 1]]]
+    is_first = hit & (row_ids == t0[..., None])
+    is_other = hit & (row_ids != t0[..., None])
+    w_first = jnp.sum(jnp.where(is_first, row_weight, 0.0), axis=-1)
+    w_last = jnp.sum(jnp.where(is_other, row_weight, 0.0), axis=-1)
+    first = jnp.sum(jnp.where(is_first, partner_place, 0), axis=-1)
+    last = jnp.sum(jnp.where(is_other, partner_place, 0), axis=-1)
     weights = jnp.stack([w_first, w_last], axis=-1).reshape(own_modes, 2 * kl_terms)
     partners = jnp.stack([first, last], axis=-1).reshape(own_modes, 2 * kl_terms)
 

time: 111 us -> 103 us (0.928)
  local copies, waits for them, and re-layouts: 28.1 us -> 12.7 us
  waiting for transfers between devices: 33.1 us -> 37.7 us
  other arithmetic: 9.65 us -> 13.2 us
    gather x14 -> x1, local copies, waits for them, and re-layouts: 11.4 us -> 0.7 us  [local(): owner_at[slot_of_mode // own_modes] * own_modes + slot_of_mode % own_modes]
    add x1, other arithmetic: 0.01 us -> 5 us  [local(): owner_at[slot_of_mode // own_modes] * own_modes + slot_of_mode % own_modes]
    ppermute x8, waiting for transfers between devices: 28.7 us -> 33.4 us  [shifted(): lax.ppermute(x, 'chaos', [(c, (c + step) % count) for c in range(count)])]
    unnamed x17 -> x12, local copies, waits for them, and re-layouts: 11.7 us -> 8.4 us
    another operation x2 -> x1, other arithmetic: 2.59 us -> 1.2 us  [local(): t0 = jnp.argmax(hit, axis=-1).astype(jnp.int32)]
  transfers between devices with their start and end apart: 13 -> 13, of which waited for: 5 -> 5; matrix products, arithmetic and copies ran while one was open for 31% -> 22% of each run, Pallas kernels for 0% -> 0%
where the time goes in v11:
time: 103 us; the launch traced here: 102 us
  waiting for transfers between devices  37.7 us (37%)
  starting transfers between devices  27.8 us (27%)
  other arithmetic  13.2 us (13%)
  local copies, waits for them, and re-layouts  12.7 us (12%)
  Pallas kernels  10.6 us (10%)
    ppermute x8, waiting for transfers between devices, shifted(): lax.ppermute(x, 'chaos', [(c, (c + step) % count) for c in range(count)])  33.4 us
    ppermute x8, starting transfers between devices, shifted(): lax.ppermute(x, 'chaos', [(c, (c + step) % count) for c in range(count)])  10.7 us
    pallas_call x1, Pallas kernels, stencil_apply(): pl.pallas_call(stencil_kernel, out_shape=(jax.ShapeDtypeStruct((own_modes...  10.6 us
    ppermute x2, starting transfers between devices, space_halo(): lax.ppermute(edge_last, 'space', up)  9.57 us
    unnamed x12, local copies, waits for them, and re-layouts  8.4 us
    add x1, other arithmetic, local(): owner_at[slot_of_mode // own_modes] * own_modes + slot_of_mode % own_modes  5 us
    ppermute x2, waiting for transfers between devices, space_halo(): lax.ppermute(edge_first, 'space', down)  4.34 us
    ppermute x2, starting transfers between devices, space_halo(): lax.ppermute(edge_first, 'space', down)  3.84 us
  transfers between devices with their start and end apart: 13, of which 5 were waited for; matrix products, arithmetic and copies ran while one was open for 22% of the time, Pallas kernels for 0%

profile of v11, /device:TPU:1, one launch (start us, length us, event | category | flops | bytes accessed | tf_op | source)
XLA Modules:
  0.0 102.3 jit_solution(12268625244168039317)
XLA Ops:
  0.0 3.7 %collective-permute-start = (f32[15,8,2048]{2,1,0:T(8,128)}, f32[15,8,2048]{2,1,0:T(8,128)}, u32[]{:S(2)}, u32[]{:S(2)}) collective-permute-start(f32[15,8,2048]{2,1,0:T(8,128)} %param.5), channel_id=1, source_target_pairs={{0,16},{16,0},{32,48},{48,32},{64,80},{80,64},{96,112},{112,96},{1... | collective-permute-start | bytes 2949128 | tf_op jit(solution)/shard_map/ppermute | solution.py:25
  3.7 1.2 %collective-permute-start.4 = (f32[15,8,2048]{2,1,0:T(8,128)}, f32[15,8,2048]{2,1,0:T(8,128)S(1)}, u32[]{:S(2)}, u32[]{:S(2)}) collective-permute-start(f32[15,8,2048]{2,1,0:T(8,128)} %param.5), channel_id=1, source_target_pairs={{0,32},{16,48},{32,64},{48,80},{64,96},{80,112},{96,0},{112,16},{1... | collective-permute-start | bytes 2949128 | tf_op jit(solution)/shard_map/ppermute | solution.py:18
  4.9 1.5 %collective-permute-start.5 = (f32[15,8,2048]{2,1,0:T(8,128)}, f32[15,8,2048]{2,1,0:T(8,128)S(1)}, u32[]{:S(2)}, u32[]{:S(2)}) collective-permute-start(f32[15,8,2048]{2,1,0:T(8,128)} %param.5), channel_id=1, source_target_pairs={{0,96},{16,112},{32,0},{48,16},{64,32},{80,48},{96,64},{112,80},{1... | collective-permute-start | bytes 2949128 | tf_op jit(solution)/shard_map/ppermute | solution.py:18
  6.4 1.3 %fusion.4 = (f32[8,1,2048]{2,1,0:T(1,128)S(1)}, f32[8,1,2048]{2,1,0:T(1,128)S(1)}) fusion(f32[8,8,2048]{2,1,0:T(8,128)} %param.6), kind=kLoop, calls=%fused_computation.49 | loop fusion | bytes 262144 | tf_op jit(solution)/shard_map/slice | solution.py:84
  7.7 4.9 %collective-permute-start.2 = (f32[8,1,2048]{2,1,0:T(1,128)S(1)}, f32[8,1,2048]{2,1,0:T(1,128)S(1)}, u32[]{:S(2)}, u32[]{:S(2)}) collective-permute-start(f32[8,1,2048]{2,1,0:T(1,128)S(1)} %get-tuple-element.30), channel_id=1, source_target_pairs={{0,1},{1,2},{2,3},{3,4},{4,5},{5,6},{6,7},{7,8},{8,9},{9,10},{10,1... | collective-permute-start | bytes 196616 | tf_op jit(solution)/shard_map/ppermute | solution.py:45
  12.7 1.9 %collective-permute-start.3 = (f32[8,1,2048]{2,1,0:T(1,128)S(1)}, f32[8,1,2048]{2,1,0:T(1,128)S(1)}, u32[]{:S(2)}, u32[]{:S(2)}) collective-permute-start(f32[8,1,2048]{2,1,0:T(1,128)S(1)} %get-tuple-element.31), channel_id=1, source_target_pairs={{1,0},{2,1},{3,2},{4,3},{5,4},{6,5},{7,6},{8,7},{9,8},{10,9},{11,1... | collective-permute-start | bytes 196616 | tf_op jit(solution)/shard_map/ppermute | solution.py:45
  18.6 5.0 %fusion.1 = s32[120]{0:T(128)S(1)} fusion(s32[120]{0:T(128)S(1)} %select_reduce_fusion.5, s32[]{:T(128)} %bitcast.12, s32[]{:T(128)} %bitcast.13, s32[]{:T(128)} %bitcast.14, s32[]{:T(128)} %bitcast.15, s32[]{:T(128)} %bitcast.16, s32[]{:T(128)} %bitcast.18, s32[]{:T(128)} %bitcast.17, s32[]{:T(128)} %bitcast.11), kind=kLoop, calls=%fused_computation.44 | loop fusion | flops 3720 | bytes 992 | tf_op jit(solution)/shard_map/add | solution.py:63
  23.8 1.2 %and_reduce_fusion = (pred[15,8]{1,0:T(8,128)(4,1)}, s32[15,8]{1,0:T(8,128)S(1)}) fusion(pred[8,624]{1,0:T(8,128)(4,1)S(1)} %iota_compare_fusion.4, pred[15,624]{1,0:T(8,128)(4,1)S(1)} %broadcast_compare_fusion), kind=kLoop, calls=%fused_computation.6 | loop fusion | flops 598200 | bytes 14952 | tf_op jit(solution)/shard_map/local/reduce | solution.py:74
  27.1 1.3 %constant_dynamic-update-slice_fusion.5 = f32[120,8,2048]{2,1,0:T(8,128)S(1)} fusion(f32[15,8,2048]{2,1,0:T(8,128)} %param.5), kind=kLoop, calls=%fused_computation.24 | loop fusion | bytes 1966080
  28.4 1.2 %pad_maximum_fusion.coef = f32[8,10,2048]{2,1,0:T(8,128)S(1)} fusion(f32[8,1,2048]{2,1,0:T(1,128)S(1)} %collective-permute-done.3, f32[8,8,2048]{2,1,0:T(8,128)} %param.6, f32[8,1,2048]{2,1,0:T(1,128)S(1)} %collective-permute-done.2), kind=kLoop, calls=%fused_computation | loop fusion | flops 327680 | bytes 1310720 | tf_op jit(solution)/shard_map/concatenate | solution.py:85
  29.8 2.7 %collective-permute-start.7 = (f32[15,8,1024]{2,1,0:T(8,128)S(1)}, f32[15,8,1024]{2,1,0:T(8,128)S(1)}, u32[]{:S(2)}, u32[]{:S(2)}) collective-permute-start(f32[15,8,1024]{2,1,0:T(8,128)S(1)} %slice.54), channel_id=1, source_target_pairs={{0,96},{16,112},{32,0},{48,16},{64,32},{80,48},{96,64},{112,80},{1... | collective-permute-start | bytes 1474568 | tf_op jit(solution)/shard_map/ppermute | solution.py:18
  32.5 2.7 %collective-permute-start.8 = (f32[15,8,2048]{2,1,0:T(8,128)}, f32[15,8,2048]{2,1,0:T(8,128)S(1)}, u32[]{:S(2)}, u32[]{:S(2)}) collective-permute-start(f32[15,8,2048]{2,1,0:T(8,128)} %collective-permute-done), channel_id=1, source_target_pairs={{0,96},{16,112},{32,0},{48,16},{64,32},{80,48},{96,64},{112,80},{1... | collective-permute-start | bytes 2949128 | tf_op jit(solution)/shard_map/ppermute | solution.py:18
  35.4 8.6 %collective-permute-done.6 = f32[15,8,1024]{2,1,0:T(8,128)S(1)} collective-permute-done((f32[15,8,1024]{2,1,0:T(8,128)S(1)}, f32[15,8,1024]{2,1,0:T(8,128)S(1)}, u32[]{:S(2)}, u32[]{:S(2)}) %collective-permute-start.6) | collective-permute-done | bytes 491552 | tf_op jit(solution)/shard_map/ppermute | solution.py:18
  44.1 1.3 %constant_dynamic-update-slice_fusion.2 = f32[120,8,2048]{2,1,0:T(8,128)S(1)} fusion(f32[120,8,2048]{2,1,0:T(8,128)S(1)} %maximum_dynamic-update-slice_fusion.1, f32[15,8,2048]{2,1,0:T(8,128)} %collective-permute-done), kind=kLoop, calls=%fused_computation.21 | loop fusion | bytes 1966080
  45.4 19.7 %collective-permute-done.1 = f32[15,8,2048]{2,1,0:T(8,128)S(1)} collective-permute-done((f32[15,8,2048]{2,1,0:T(8,128)}, f32[15,8,2048]{2,1,0:T(8,128)S(1)}, u32[]{:S(2)}, u32[]{:S(2)}) %collective-permute-start.1) | collective-permute-done | bytes 983072 | tf_op jit(solution)/shard_map/ppermute | solution.py:18
  66.5 2.5 %collective-permute-start.10 = (f32[15,8,1024]{2,1,0:T(8,128)S(1)}, f32[15,8,1024]{2,1,0:T(8,128)S(1)}, u32[]{:S(2)}, u32[]{:S(2)}) collective-permute-start(f32[15,8,1024]{2,1,0:T(8,128)S(1)} %slice.55), channel_id=1, source_target_pairs={{0,96},{16,112},{32,0},{48,16},{64,32},{80,48},{96,64},{112,80},{1... | collective-permute-start | bytes 1474568 | tf_op jit(solution)/shard_map/ppermute | solution.py:18
  69.1 2.3 %constant_dynamic-update-slice_fusion.1 = f32[120,8,2048]{2,1,0:T(8,128)} fusion(f32[120,8,2048]{2,1,0:T(8,128)} %copy-done, f32[15,8,2048]{2,1,0:T(8,128)} %copy-done.1), kind=kLoop, calls=%fused_computation.20 | loop fusion | bytes 1966080
  71.4 2.3 %constant_dynamic-update-slice_fusion = f32[120,8,2048]{2,1,0:T(8,128)} fusion(f32[120,8,2048]{2,1,0:T(8,128)} %constant_dynamic-update-slice_fusion.1, f32[15,8,2048]{2,1,0:T(8,128)} %copy-done.2), kind=kLoop, calls=%fused_computation.19 | loop fusion | bytes 1966080
  73.6 5.0 %collective-permute-done.9 = f32[15,8,1024]{2,1,0:T(8,128)S(1)} collective-permute-done((f32[15,8,1024]{2,1,0:T(8,128)S(1)}, f32[15,8,1024]{2,1,0:T(8,128)S(1)}, u32[]{:S(2)}, u32[]{:S(2)}) %collective-permute-start.9) | collective-permute-done | bytes 491552 | tf_op jit(solution)/shard_map/ppermute | solution.py:18
  79.7 10.6 %shard_map.55 = (f32[15,8,2048]{2,1,0:T(8,128)S(1)}, f32[15,2048]{1,0:T(8,128)S(1)}, f32[15,2048]{1,0:T(8,128)S(1)}) custom-call(s32[15,16]{1,0:T(8,128)S(1)} %copy.18.partners, f32[15,16]{1,0:T(8,128)S(1)} %copy.19.weights, f32[120,8,2048]{2,1,0:T(8,128)} %maximum_dynamic-update-slice_fusion.every, f32[8,10,2048]{2,1,0:T(8,128)S(1)} %pad_maximum_fusion.coef), custom_call_target="tpu_custom_call" | custom-call | tf_op jit(solution)/shard_map/pallas_call | solution.py:149
  90.3 4.6 %collective-permute-start.11 = (f32[15,2048]{1,0:T(8,128)S(1)}, f32[15,2048]{1,0:T(8,128)S(1)}, u32[]{:S(2)}, u32[]{:S(2)}) collective-permute-start(f32[15,2048]{1,0:T(8,128)S(1)} %get-tuple-element.21), channel_id=1, source_target_pairs={{0,1},{1,2},{2,3},{3,4},{4,5},{5,6},{6,7},{7,8},{8,9},{9,10},{10,1... | collective-permute-start | bytes 368648 | tf_op jit(solution)/shard_map/ppermute | solution.py:45
  94.9 1.9 %collective-permute-start.12 = (f32[15,2048]{1,0:T(8,128)S(1)}, f32[15,2048]{1,0:T(8,128)S(1)}, u32[]{:S(2)}, u32[]{:S(2)}) collective-permute-start(f32[15,2048]{1,0:T(8,128)S(1)} %get-tuple-element.22), channel_id=1, source_target_pairs={{1,0},{2,1},{3,2},{4,3},{5,4},{6,5},{7,6},{8,7},{9,8},{10,9},{11,1... | collective-permute-start | bytes 368648 | tf_op jit(solution)/shard_map/ppermute | solution.py:45
  96.8 4.3 %collective-permute-done.12 = f32[15,2048]{1,0:T(8,128)S(1)} collective-permute-done((f32[15,2048]{1,0:T(8,128)S(1)}, f32[15,2048]{1,0:T(8,128)S(1)}, u32[]{:S(2)}, u32[]{:S(2)}) %collective-permute-start.12) | collective-permute-done | bytes 122912 | tf_op jit(solution)/shard_map/ppermute | solution.py:45
  101.2 1.2 %select_subtract_fusion = f32[15,8,2048]{2,1,0:T(8,128)} fusion(f32[15,8,2048]{2,1,0:T(8,128)S(1)} %get-tuple-element.20, f32[15,2048]{1,0:T(8,128)S(1)} %collective-permute-done.12, f32[15,2048]{1,0:T(8,128)S(1)} %collective-permute-done.11, pred[8]{0:T(512)(128)(4,1)S(1)} %get-tuple-element.40, pred[8]{0:T(512)(128)(4,1)S(1)} %get-tuple-element.41), kind=kLoop, calls=%fused_computation.3 | loop fusion | flops 737280 | bytes 2211856 | tf_op jit(solution)/shard_map/sub | solution.py:94
  (49 shorter events, 9.1 us)
Async XLA Ops:
  0.0 32.5 %collective-permute-start = (f32[15,8,2048]{2,1,0:T(8,128)}, f32[15,8,2048]{2,1,0:T(8,128)}, u32[]{:S(2)}, u32[]{:S(2)}) collective-permute-start(f32[15,8,2048]{2,1,0:T(8,128)} %param.5), channel_id=1, source_target_pairs={{0,16},{16,0},{32,48},{48,32},{64,80},{80,64},{96,112},{112,96},{1... | collective-permute-start | bytes 2949128 | tf_op jit(solution)/shard_map/ppermute | solution.py:25
  3.7 25.9 %collective-permute-start.4 = (f32[15,8,2048]{2,1,0:T(8,128)}, f32[15,8,2048]{2,1,0:T(8,128)S(1)}, u32[]{:S(2)}, u32[]{:S(2)}) collective-permute-start(f32[15,8,2048]{2,1,0:T(8,128)} %param.5), channel_id=1, source_target_pairs={{0,32},{16,48},{32,64},{48,80},{64,96},{80,112},{96,0},{112,16},{1... | collective-permute-start | bytes 2949128 | tf_op jit(solution)/shard_map/ppermute | solution.py:18
  4.9 24.8 %collective-permute-start.5 = (f32[15,8,2048]{2,1,0:T(8,128)}, f32[15,8,2048]{2,1,0:T(8,128)S(1)}, u32[]{:S(2)}, u32[]{:S(2)}) collective-permute-start(f32[15,8,2048]{2,1,0:T(8,128)} %param.5), channel_id=1, source_target_pairs={{0,96},{16,112},{32,0},{48,16},{64,32},{80,48},{96,64},{112,80},{1... | collective-permute-start | bytes 2949128 | tf_op jit(solution)/shard_map/ppermute | solution.py:18
  7.7 20.6 %collective-permute-start.2 = (f32[8,1,2048]{2,1,0:T(1,128)S(1)}, f32[8,1,2048]{2,1,0:T(1,128)S(1)}, u32[]{:S(2)}, u32[]{:S(2)}) collective-permute-start(f32[8,1,2048]{2,1,0:T(1,128)S(1)} %get-tuple-element.30), channel_id=1, source_target_pairs={{0,1},{1,2},{2,3},{3,4},{4,5},{5,6},{6,7},{7,8},{8,9},{9,10},{10,1... | collective-permute-start | bytes 196616 | tf_op jit(solution)/shard_map/ppermute | solution.py:45
  12.7 15.7 %collective-permute-start.3 = (f32[8,1,2048]{2,1,0:T(1,128)S(1)}, f32[8,1,2048]{2,1,0:T(1,128)S(1)}, u32[]{:S(2)}, u32[]{:S(2)}) collective-permute-start(f32[8,1,2048]{2,1,0:T(1,128)S(1)} %get-tuple-element.31), channel_id=1, source_target_pairs={{1,0},{2,1},{3,2},{4,3},{5,4},{6,5},{7,6},{8,7},{9,8},{10,9},{11,1... | collective-permute-start | bytes 196616 | tf_op jit(solution)/shard_map/ppermute | solution.py:45
  29.7 14.4 %collective-permute-start.6 = (f32[15,8,1024]{2,1,0:T(8,128)S(1)}, f32[15,8,1024]{2,1,0:T(8,128)S(1)}, u32[]{:S(2)}, u32[]{:S(2)}) collective-permute-start(f32[15,8,1024]{2,1,0:T(8,128)S(1)} %slice.53), channel_id=1, source_target_pairs={{0,32},{16,48},{32,64},{48,80},{64,96},{80,112},{96,0},{112,16},{1... | collective-permute-start | bytes 1474568 | tf_op jit(solution)/shard_map/ppermute | solution.py:18
  29.8 14.2 %collective-permute-start.7 = (f32[15,8,1024]{2,1,0:T(8,128)S(1)}, f32[15,8,1024]{2,1,0:T(8,128)S(1)}, u32[]{:S(2)}, u32[]{:S(2)}) collective-permute-start(f32[15,8,1024]{2,1,0:T(8,128)S(1)} %slice.54), channel_id=1, source_target_pairs={{0,96},{16,112},{32,0},{48,16},{64,32},{80,48},{96,64},{112,80},{1... | collective-permute-start | bytes 1474568 | tf_op jit(solution)/shard_map/ppermute | solution.py:18
  32.5 32.6 %collective-permute-start.1 = (f32[15,8,2048]{2,1,0:T(8,128)}, f32[15,8,2048]{2,1,0:T(8,128)S(1)}, u32[]{:S(2)}, u32[]{:S(2)}) collective-permute-start(f32[15,8,2048]{2,1,0:T(8,128)} %collective-permute-done), channel_id=1, source_target_pairs={{0,32},{16,48},{32,64},{48,80},{64,96},{80,112},{96,0},{112,16},{1... | collective-permute-start | bytes 2949128 | tf_op jit(solution)/shard_map/ppermute | solution.py:18
  32.5 32.7 %collective-permute-start.8 = (f32[15,8,2048]{2,1,0:T(8,128)}, f32[15,8,2048]{2,1,0:T(8,128)S(1)}, u32[]{:S(2)}, u32[]{:S(2)}) collective-permute-start(f32[15,8,2048]{2,1,0:T(8,128)} %collective-permute-done), channel_id=1, source_target_pairs={{0,96},{16,112},{32,0},{48,16},{64,32},{80,48},{96,64},{112,80},{1... | collective-permute-start | bytes 2949128 | tf_op jit(solution)/shard_map/ppermute | solution.py:18
  45.4 19.9 %copy-start = (f32[120,8,2048]{2,1,0:T(8,128)}, f32[120,8,2048]{2,1,0:T(8,128)S(1)}, u32[]{:S(2)}) copy-start(f32[120,8,2048]{2,1,0:T(8,128)S(1)} %constant_dynamic-update-slice_fusion.2) | copy-start | bytes 23592964
  65.1 0.9 copy-start.1
  65.1 13.5 %collective-permute-start.9 = (f32[15,8,1024]{2,1,0:T(8,128)S(1)}, f32[15,8,1024]{2,1,0:T(8,128)S(1)}, u32[]{:S(2)}, u32[]{:S(2)}) collective-permute-start(f32[15,8,1024]{2,1,0:T(8,128)S(1)} %slice.42), channel_id=1, source_target_pairs={{0,32},{16,48},{32,64},{48,80},{64,96},{80,112},{96,0},{112,16},{1... | collective-permute-start | bytes 1474568 | tf_op jit(solution)/shard_map/ppermute | solution.py:18
  65.2 1.2 %copy-start.2 = (f32[15,8,2048]{2,1,0:T(8,128)}, f32[15,8,2048]{2,1,0:T(8,128)S(1)}, u32[]{:S(2)}) copy-start(f32[15,8,2048]{2,1,0:T(8,128)S(1)} %collective-permute-done.8) | copy-start | bytes 2949124
  66.5 12.2 %collective-permute-start.10 = (f32[15,8,1024]{2,1,0:T(8,128)S(1)}, f32[15,8,1024]{2,1,0:T(8,128)S(1)}, u32[]{:S(2)}, u32[]{:S(2)}) collective-permute-start(f32[15,8,1024]{2,1,0:T(8,128)S(1)} %slice.55), channel_id=1, source_target_pairs={{0,96},{16,112},{32,0},{48,16},{64,32},{80,48},{96,64},{112,80},{1... | collective-permute-start | bytes 1474568 | tf_op jit(solution)/shard_map/ppermute | solution.py:18
  90.3 6.6 %collective-permute-start.11 = (f32[15,2048]{1,0:T(8,128)S(1)}, f32[15,2048]{1,0:T(8,128)S(1)}, u32[]{:S(2)}, u32[]{:S(2)}) collective-permute-start(f32[15,2048]{1,0:T(8,128)S(1)} %get-tuple-element.21), channel_id=1, source_target_pairs={{0,1},{1,2},{2,3},{3,4},{4,5},{5,6},{6,7},{7,8},{8,9},{9,10},{10,1... | collective-permute-start | bytes 368648 | tf_op jit(solution)/shard_map/ppermute | solution.py:45
  94.9 6.3 %collective-permute-start.12 = (f32[15,2048]{1,0:T(8,128)S(1)}, f32[15,2048]{1,0:T(8,128)S(1)}, u32[]{:S(2)}, u32[]{:S(2)}) collective-permute-start(f32[15,2048]{1,0:T(8,128)S(1)} %get-tuple-element.22), channel_id=1, source_target_pairs={{1,0},{2,1},{3,2},{4,3},{5,4},{6,5},{7,6},{8,7},{9,8},{10,9},{11,1... | collective-permute-start | bytes 368648 | tf_op jit(solution)/shard_map/ppermute | solution.py:45

commit v12 on v11

--- a/solution.py
+++ b/solution.py
@@ -35,7 +35,7 @@
         )
         pieces += [base, from_left, from_right, far]
         owners += [origin, (origin - 2) % count, (origin + 2) % count, (origin + 4) % count]
-    return jnp.concatenate(pieces, axis=0), tables
+    return pieces, tables
 
 
 def space_halo(edge_last, edge_first):
@@ -84,9 +84,29 @@
     above, below = space_halo(kl_fields[:, rows - 1:], kl_fields[:, :1])
     coef = jnp.concatenate([above, kl_fields, below], axis=1)
 
-    every, tables = ring_gather(modes, (partners, weights, coef))
-    partners, weights, coef = tables
-    applied, to_prev, to_next = stencil_apply(every, coef, partners, weights)
+    early = (groups - 1) * own_modes
+    late_a = partners >= early
+    partners_a = jnp.where(late_a, 0, partners)
+    weights_a = jnp.where(late_a, 0.0, weights)
+    partners_b = jnp.where(late_a, partners - early, 0)
+    weights_b = jnp.where(late_a, weights, 0.0)
+    pair_b = weights_b.reshape(own_modes * kl_terms, 2)
+    active = jnp.any(pair_b != 0.0, axis=1)
+    rank = jnp.cumsum(active.astype(jnp.int32)) - 1
+    pair_ids = jnp.arange(own_modes * kl_terms, dtype=jnp.int32)
+    pick = active[None, :] & (rank[None, :] == pair_ids[:, None])
+    b_pair = jnp.sum(jnp.where(pick, pair_ids[None, :], 0), axis=1)
+    b_count = jnp.sum(active.astype(jnp.int32)).reshape(1)
+    b_index = jnp.sum(jnp.where(pick[:, :, None], partners_b.reshape(-1, 2)[None], 0), axis=1)
+    b_weight = jnp.sum(jnp.where(pick[:, :, None], pair_b[None], 0.0), axis=1)
+
+    pieces, tables = ring_gather(modes, (partners_a, weights_a, coef, b_pair, b_count, b_index, b_weight))
+    partners_a, weights_a, coef, b_pair, b_count, b_index, b_weight = tables
+    every = jnp.concatenate(pieces[:-1], axis=0)
+    applied, to_prev, to_next = stencil_apply(every, coef, partners_a, weights_a)
+    applied, to_prev, to_next = late_apply(
+        pieces[-1], coef, b_count, b_pair, b_index, b_weight, applied, to_prev, to_next
+    )
 
     from_prev, from_next = space_halo(to_next, to_prev)
     row = lax.broadcasted_iota(jnp.int32, applied.shape, 1)
@@ -174,6 +194,71 @@
     )(partners, weights, every, coef)
 
 
+def late_kernel(count, pair, index, weight, last, coef, applied, prev_in, next_in, out, to_prev, to_next, edges):
+    kl_terms = coef.shape[0]
+    rows = out.shape[1]
+    cols = out.shape[2]
+    row = lax.broadcasted_iota(jnp.int32, (rows, cols), 0)
+    column = lax.broadcasted_iota(jnp.int32, (rows, cols), 1)
+    zero = jnp.zeros((rows, cols), jnp.float32)
+    for k in range(kl_terms):
+        a_c = coef[k, pl.ds(1, rows), :]
+        c_up = 0.5 * (a_c + coef[k, pl.ds(0, rows), :])
+        c_dn = 0.5 * (a_c + coef[k, pl.ds(2, rows), :])
+        c_lf = 0.5 * (a_c + jnp.where(column == 0, zero, pltpu.roll(a_c, 1, 1)))
+        c_rt = 0.5 * (a_c + jnp.where(column == cols - 1, zero, pltpu.roll(a_c, cols - 1, 1)))
+        edges[0, k] = (c_up + c_dn) + (c_lf + c_rt)
+        edges[1, k] = jnp.where(row == 0, zero, c_up)
+        edges[2, k] = jnp.where(row == rows - 1, zero, c_dn)
+        edges[3, k] = jnp.where(column == 0, zero, c_lf)
+        edges[4, k] = jnp.where(column == cols - 1, zero, c_rt)
+        edges[5, k] = jnp.where(row == 0, c_up, jnp.where(row == rows - 1, c_dn, zero))
+    out[...] = applied[...]
+    to_prev[...] = prev_in[...]
+    to_next[...] = next_in[...]
+
+    def one_pair(r, carry):
+        q = pair[r]
+        slot = q // kl_terms
+        k = q % kl_terms
+        center = weight[r, 0] * last[index[r, 0]] + weight[r, 1] * last[index[r, 1]]
+        up = pltpu.roll(center, 1, 0)
+        dn = pltpu.roll(center, rows - 1, 0)
+        lf = pltpu.roll(center, 1, 1)
+        rt = pltpu.roll(center, cols - 1, 1)
+        term = edges[0, k] * center - edges[1, k] * up
+        term = term - edges[2, k] * dn
+        term = term - edges[3, k] * lf
+        term = term - edges[4, k] * rt
+        out[slot] = out[slot] + term
+        rim = edges[5, k] * center
+        to_prev[pl.ds(slot, 1), :] = to_prev[pl.ds(slot, 1), :] + rim[0:1]
+        to_next[pl.ds(slot, 1), :] = to_next[pl.ds(slot, 1), :] + rim[rows - 1:rows]
+        return carry
+
+    lax.fori_loop(0, count[0], one_pair, 0)
+
+
+def late_apply(last, coef, count, pair, index, weight, applied, to_prev, to_next):
+    own_modes, rows, cols = applied.shape
+    kl_terms = coef.shape[0]
+    smem = pl.BlockSpec(memory_space=pltpu.SMEM)
+    vmem = pl.BlockSpec(memory_space=pltpu.VMEM)
+    return pl.pallas_call(
+        late_kernel,
+        out_shape=(
+            jax.ShapeDtypeStruct(applied.shape, jnp.float32),
+            jax.ShapeDtypeStruct(to_prev.shape, jnp.float32),
+            jax.ShapeDtypeStruct(to_next.shape, jnp.float32),
+        ),
+        in_specs=[smem, smem, smem, smem, vmem, vmem, vmem, vmem, vmem],
+        out_specs=(vmem, vmem, vmem),
+        scratch_shapes=[pltpu.VMEM((6, kl_terms, rows, cols), jnp.float32)],
+        input_output_aliases={6: 0, 7: 1, 8: 2},
+        compiler_params=pltpu.CompilerParams(vmem_limit_bytes=48 * 1024 * 1024),
+    )(count, pair, index, weight, last, coef, applied, to_prev, to_next)
+
+
 def solution(mesh):
     return jax.shard_map(
         local,

time: 103 us -> 108 us (1.049)
  Pallas kernels: 10.6 us -> 15.9 us
  waiting for transfers between devices: 37.7 us -> 34.1 us
  other arithmetic: 13.2 us -> 15 us
  local copies, waits for them, and re-layouts: 12.7 us -> 13.8 us
    pallas_call x0 -> x1, Pallas kernels: none -> 5.67 us  [late_apply(): pl.pallas_call(late_kernel, out_shape=(jax.ShapeDtypeStruct(applied.shape...]
    gather x0 -> x2, other arithmetic: none -> 4.54 us  [local(): owner_at[slot_of_mode // own_modes] * own_modes + slot_of_mode % own_modes]
    add x1, other arithmetic: 5 us -> 0.7 us  [local(): owner_at[slot_of_mode // own_modes] * own_modes + slot_of_mode % own_modes]
    ppermute x8, waiting for transfers between devices: 33.4 us -> 29.8 us  [shifted(): lax.ppermute(x, 'chaos', [(c, (c + step) % count) for c in range(count)])]
    unnamed x12 -> x11, local copies, waits for them, and re-layouts: 8.4 us -> 6.04 us
    concatenate x0 -> x1, local copies, waits for them, and re-layouts: none -> 2.26 us  [local(): every = jnp.concatenate(pieces[:-1], axis=0)]
    ppermute x8, starting transfers between devices: 10.7 us -> 9.5 us  [shifted(): lax.ppermute(x, 'chaos', [(c, (c + step) % count) for c in range(count)])]
  transfers between devices with their start and end apart: 13 -> 13, of which waited for: 5 -> 4; matrix products, arithmetic and copies ran while one was open for 22% -> 24% of each run, Pallas kernels for 0% -> 10%
where the time goes in v12:
time: 108 us; the launch traced here: 107 us
  waiting for transfers between devices  34.1 us (32%)
  starting transfers between devices  27.7 us (26%)
  Pallas kernels  15.9 us (15%)
  other arithmetic  15 us (14%)
  local copies, waits for them, and re-layouts  13.8 us (13%)
    ppermute x8, waiting for transfers between devices, shifted(): lax.ppermute(x, 'chaos', [(c, (c + step) % count) for c in range(count)])  29.8 us
    ppermute x2, starting transfers between devices, space_halo(): lax.ppermute(edge_last, 'space', up)  10.6 us
    pallas_call x1, Pallas kernels, stencil_apply(): pl.pallas_call(stencil_kernel, out_shape=(jax.ShapeDtypeStruct((own_modes...  10.3 us
    ppermute x8, starting transfers between devices, shifted(): lax.ppermute(x, 'chaos', [(c, (c + step) % count) for c in range(count)])  9.5 us
    unnamed x11, local copies, waits for them, and re-layouts  6.04 us
    pallas_call x1, Pallas kernels, late_apply(): pl.pallas_call(late_kernel, out_shape=(jax.ShapeDtypeStruct(applied.shape...  5.67 us
    gather x2, other arithmetic, local(): owner_at[slot_of_mode // own_modes] * own_modes + slot_of_mode % own_modes  4.54 us
    ppermute x2, waiting for transfers between devices, space_halo(): lax.ppermute(edge_first, 'space', down)  4.34 us
  transfers between devices with their start and end apart: 13, of which 4 were waited for; matrix products, arithmetic and copies ran while one was open for 24% of the time, Pallas kernels for 10%

profile of v12, /device:TPU:1, one launch (start us, length us, event | category | flops | bytes accessed | tf_op | source)
XLA Modules:
  0.0 107.1 jit_solution(2149000181137965645)
XLA Ops:
  0.0 3.7 %collective-permute-start = (f32[15,8,2048]{2,1,0:T(8,128)}, f32[15,8,2048]{2,1,0:T(8,128)}, u32[]{:S(2)}, u32[]{:S(2)}) collective-permute-start(f32[15,8,2048]{2,1,0:T(8,128)} %param.5), channel_id=1, source_target_pairs={{0,16},{16,0},{32,48},{48,32},{64,80},{80,64},{96,112},{112,96},{1... | collective-permute-start | bytes 2949128 | tf_op jit(solution)/shard_map/ppermute | solution.py:25
  3.7 1.2 %collective-permute-start.7 = (f32[15,8,2048]{2,1,0:T(8,128)}, f32[15,8,2048]{2,1,0:T(8,128)S(1)}, u32[]{:S(2)}, u32[]{:S(2)}) collective-permute-start(f32[15,8,2048]{2,1,0:T(8,128)} %param.5), channel_id=1, source_target_pairs={{0,32},{16,48},{32,64},{48,80},{64,96},{80,112},{96,0},{112,16},{1... | collective-permute-start | bytes 2949128 | tf_op jit(solution)/shard_map/ppermute | solution.py:18
  4.9 1.5 %collective-permute-start.8 = (f32[15,8,2048]{2,1,0:T(8,128)}, f32[15,8,2048]{2,1,0:T(8,128)S(1)}, u32[]{:S(2)}, u32[]{:S(2)}) collective-permute-start(f32[15,8,2048]{2,1,0:T(8,128)} %param.5), channel_id=1, source_target_pairs={{0,96},{16,112},{32,0},{48,16},{64,32},{80,48},{96,64},{112,80},{1... | collective-permute-start | bytes 2949128 | tf_op jit(solution)/shard_map/ppermute | solution.py:18
  6.4 1.3 %fusion.4 = (f32[8,1,2048]{2,1,0:T(1,128)S(1)}, f32[8,1,2048]{2,1,0:T(1,128)S(1)}) fusion(f32[8,8,2048]{2,1,0:T(8,128)} %param.6), kind=kLoop, calls=%fused_computation.60 | loop fusion | bytes 262144 | tf_op jit(solution)/shard_map/slice | solution.py:84
  7.7 4.9 %collective-permute-start.2 = (f32[8,1,2048]{2,1,0:T(1,128)S(1)}, f32[8,1,2048]{2,1,0:T(1,128)S(1)}, u32[]{:S(2)}, u32[]{:S(2)}) collective-permute-start(f32[8,1,2048]{2,1,0:T(1,128)S(1)} %get-tuple-element.44), channel_id=1, source_target_pairs={{0,1},{1,2},{2,3},{3,4},{4,5},{5,6},{6,7},{7,8},{8,9},{9,10},{10,1... | collective-permute-start | bytes 196616 | tf_op jit(solution)/shard_map/ppermute | solution.py:45
  12.7 1.9 %collective-permute-start.3 = (f32[8,1,2048]{2,1,0:T(1,128)S(1)}, f32[8,1,2048]{2,1,0:T(1,128)S(1)}, u32[]{:S(2)}, u32[]{:S(2)}) collective-permute-start(f32[8,1,2048]{2,1,0:T(1,128)S(1)} %get-tuple-element.45), channel_id=1, source_target_pairs={{1,0},{2,1},{3,2},{4,3},{5,4},{6,5},{7,6},{8,7},{9,8},{10,9},{11,1... | collective-permute-start | bytes 196616 | tf_op jit(solution)/shard_map/ppermute | solution.py:45
  19.0 4.4 %select_reduce_fusion.7 = s32[120]{0:T(128)S(1)} fusion(pred[120,1]{1,0:T(8,128)(4,1)S(1)} %copy.54, s32[120,1]{1,0:T(8,128)S(1)} %copy.53, s32[]{:T(128)} %bitcast.11, s32[]{:T(128)} %bitcast.12, s32[]{:T(128)} %bitcast.13, s32[]{:T(128)} %bitcast.14, s32[]{:T(128)} %bitcast.15, s32[]{:T(128)} %bitcast.17, s32[]{:T(128)} %bitcast.16), kind=kLoop, calls=%fused_computation.19 | loop fusion | flops 2040 | bytes 1108 | tf_op jit(solution)/shard_map/gather | solution.py:63
  29.3 1.3 %constant_dynamic-update-slice_fusion.5 = f32[105,8,2048]{2,1,0:T(8,128)S(1)} fusion(f32[15,8,2048]{2,1,0:T(8,128)} %param.5), kind=kLoop, calls=%fused_computation.34 | loop fusion | bytes 1966080
  31.2 1.2 %pad_maximum_fusion.coef = f32[8,10,2048]{2,1,0:T(8,128)S(1)} fusion(f32[8,1,2048]{2,1,0:T(1,128)S(1)} %collective-permute-done.3, f32[8,8,2048]{2,1,0:T(8,128)} %param.6, f32[8,1,2048]{2,1,0:T(1,128)S(1)} %collective-permute-done.2), kind=kLoop, calls=%fused_computation | loop fusion | flops 327680 | bytes 1310720 | tf_op jit(solution)/shard_map/concatenate | solution.py:85
  32.5 1.3 %collective-permute-start.10 = (f32[15,8,1024]{2,1,0:T(8,128)S(1)}, f32[15,8,1024]{2,1,0:T(8,128)S(1)}, u32[]{:S(2)}, u32[]{:S(2)}) collective-permute-start(f32[15,8,1024]{2,1,0:T(8,128)S(1)} %slice.55), channel_id=1, source_target_pairs={{0,96},{16,112},{32,0},{48,16},{64,32},{80,48},{96,64},{112,80},{1... | collective-permute-start | bytes 1474568 | tf_op jit(solution)/shard_map/ppermute | solution.py:18
  34.3 2.6 %collective-permute-start.5 = (f32[15,8,2048]{2,1,0:T(8,128)}, f32[15,8,2048]{2,1,0:T(8,128)S(1)}, u32[]{:S(2)}, u32[]{:S(2)}) collective-permute-start(f32[15,8,2048]{2,1,0:T(8,128)} %collective-permute-done), channel_id=1, source_target_pairs={{0,96},{16,112},{32,0},{48,16},{64,32},{80,48},{96,64},{112,80},{1... | collective-permute-start | bytes 2949128 | tf_op jit(solution)/shard_map/ppermute | solution.py:18
  37.0 8.8 %collective-permute-done.10 = f32[15,8,1024]{2,1,0:T(8,128)S(1)} collective-permute-done((f32[15,8,1024]{2,1,0:T(8,128)S(1)}, f32[15,8,1024]{2,1,0:T(8,128)S(1)}, u32[]{:S(2)}, u32[]{:S(2)}) %collective-permute-start.10) | collective-permute-done | bytes 491552 | tf_op jit(solution)/shard_map/ppermute | solution.py:18
  45.8 2.6 %collective-permute-done.9 = f32[15,8,1024]{2,1,0:T(8,128)S(1)} collective-permute-done((f32[15,8,1024]{2,1,0:T(8,128)S(1)}, f32[15,8,1024]{2,1,0:T(8,128)S(1)}, u32[]{:S(2)}, u32[]{:S(2)}) %collective-permute-start.9) | collective-permute-done | bytes 491552 | tf_op jit(solution)/shard_map/ppermute | solution.py:18
  48.5 1.3 %constant_dynamic-update-slice_fusion.2 = f32[105,8,2048]{2,1,0:T(8,128)S(1)} fusion(f32[105,8,2048]{2,1,0:T(8,128)S(1)} %maximum_dynamic-update-slice_fusion, f32[15,8,2048]{2,1,0:T(8,128)} %collective-permute-done), kind=kLoop, calls=%fused_computation.31 | loop fusion | bytes 1966080
  49.8 18.4 %collective-permute-done.1 = f32[15,8,2048]{2,1,0:T(8,128)S(1)} collective-permute-done((f32[15,8,2048]{2,1,0:T(8,128)}, f32[15,8,2048]{2,1,0:T(8,128)S(1)}, u32[]{:S(2)}, u32[]{:S(2)}) %collective-permute-start.1) | collective-permute-done | bytes 983072 | tf_op jit(solution)/shard_map/ppermute | solution.py:18
  69.5 2.5 %collective-permute-start.6 = (f32[15,8,1024]{2,1,0:T(8,128)S(1)}, f32[15,8,1024]{2,1,0:T(8,128)}, u32[]{:S(2)}, u32[]{:S(2)}) collective-permute-start(f32[15,8,1024]{2,1,0:T(8,128)S(1)} %slice.53), channel_id=1, source_target_pairs={{0,96},{16,112},{32,0},{48,16},{64,32},{80,48},{96,64},{112,80},{1... | collective-permute-start | bytes 1474568 | tf_op jit(solution)/shard_map/ppermute | solution.py:18
  72.2 2.3 %constant_dynamic-update-slice_fusion.1 = f32[105,8,2048]{2,1,0:T(8,128)} fusion(f32[105,8,2048]{2,1,0:T(8,128)} %copy-done, f32[15,8,2048]{2,1,0:T(8,128)} %copy-done.1), kind=kLoop, calls=%fused_computation.30 | loop fusion | bytes 1966080
  74.4 2.3 %constant_dynamic-update-slice_fusion.every = f32[105,8,2048]{2,1,0:T(8,128)} fusion(f32[105,8,2048]{2,1,0:T(8,128)} %constant_dynamic-update-slice_fusion.1, f32[15,8,2048]{2,1,0:T(8,128)} %copy-done.2), kind=kLoop, calls=%fused_computation.29 | loop fusion | bytes 1966080 | tf_op jit(solution)/shard_map/concatenate | solution.py:105
  76.7 10.3 %shard_map.55 = (f32[15,8,2048]{2,1,0:T(8,128)S(1)}, f32[15,2048]{1,0:T(8,128)S(1)}, f32[15,2048]{1,0:T(8,128)S(1)}) custom-call(s32[15,16]{1,0:T(8,128)S(1)} %compare_select_fusion.2.partners, f32[15,16]{1,0:T(8,128)S(1)} %compare_select_fusion.1.weights, f32[105,8,2048]{2,1,0:T(8,128)} %constant_dynamic-update-slice_fusion.every, ...), custom_call_target="tpu_custom_call" | custom-call | tf_op jit(solution)/shard_map/pallas_call | solution.py:169
  87.0 1.3 %pad_maximum_fusion.1.last = f32[15,8,2048]{2,1,0:T(8,128)S(1)} fusion(f32[15,8,1024]{2,1,0:T(8,128)} %collective-permute-done.6, f32[15,8,1024]{2,1,0:T(8,128)} %collective-permute-done.4), kind=kLoop, calls=%fused_computation.1 | loop fusion | flops 245760 | bytes 1966080 | tf_op jit(solution)/shard_map/concatenate | solution.py:33
  88.3 5.7 %shard_map.56 = (f32[15,8,2048]{2,1,0:T(8,128)S(1)}, f32[15,2048]{1,0:T(8,128)S(1)}, f32[15,2048]{1,0:T(8,128)S(1)}) custom-call(s32[1]{0:T(128)} %bitcast.24.count, s32[120]{0:T(128)S(1)} %select_reduce_fusion.8.pair, s32[120,2]{1,0:T(8,128)S(1)} %copy.68.index, ...), custom_call_target="tpu_custom_call", output_to_operand_aliasing={{0}: (6, {}), {1}: (7, {}), {2}: (8, {})} | custom-call | tf_op jit(solution)/shard_map/pallas_call | solution.py:247
  93.9 5.7 %collective-permute-start.11 = (f32[15,2048]{1,0:T(8,128)S(1)}, f32[15,2048]{1,0:T(8,128)S(1)}, u32[]{:S(2)}, u32[]{:S(2)}) collective-permute-start(f32[15,2048]{1,0:T(8,128)S(1)} %get-tuple-element.35), channel_id=1, source_target_pairs={{0,1},{1,2},{2,3},{3,4},{4,5},{5,6},{6,7},{7,8},{8,9},{9,10},{10,1... | collective-permute-start | bytes 368648 | tf_op jit(solution)/shard_map/ppermute | solution.py:45
  99.6 1.9 %collective-permute-start.12 = (f32[15,2048]{1,0:T(8,128)S(1)}, f32[15,2048]{1,0:T(8,128)S(1)}, u32[]{:S(2)}, u32[]{:S(2)}) collective-permute-start(f32[15,2048]{1,0:T(8,128)S(1)} %get-tuple-element.36), channel_id=1, source_target_pairs={{1,0},{2,1},{3,2},{4,3},{5,4},{6,5},{7,6},{8,7},{9,8},{10,9},{11,1... | collective-permute-start | bytes 368648 | tf_op jit(solution)/shard_map/ppermute | solution.py:45
  101.6 4.3 %collective-permute-done.12 = f32[15,2048]{1,0:T(8,128)S(1)} collective-permute-done((f32[15,2048]{1,0:T(8,128)S(1)}, f32[15,2048]{1,0:T(8,128)S(1)}, u32[]{:S(2)}, u32[]{:S(2)}) %collective-permute-start.12) | collective-permute-done | bytes 122912 | tf_op jit(solution)/shard_map/ppermute | solution.py:45
  (79 shorter events, 13.9 us)
Async XLA Ops:
  0.0 34.2 %collective-permute-start = (f32[15,8,2048]{2,1,0:T(8,128)}, f32[15,8,2048]{2,1,0:T(8,128)}, u32[]{:S(2)}, u32[]{:S(2)}) collective-permute-start(f32[15,8,2048]{2,1,0:T(8,128)} %param.5), channel_id=1, source_target_pairs={{0,16},{16,0},{32,48},{48,32},{64,80},{80,64},{96,112},{112,96},{1... | collective-permute-start | bytes 2949128 | tf_op jit(solution)/shard_map/ppermute | solution.py:25
  3.7 30.1 %collective-permute-start.7 = (f32[15,8,2048]{2,1,0:T(8,128)}, f32[15,8,2048]{2,1,0:T(8,128)S(1)}, u32[]{:S(2)}, u32[]{:S(2)}) collective-permute-start(f32[15,8,2048]{2,1,0:T(8,128)} %param.5), channel_id=1, source_target_pairs={{0,32},{16,48},{32,64},{48,80},{64,96},{80,112},{96,0},{112,16},{1... | collective-permute-start | bytes 2949128 | tf_op jit(solution)/shard_map/ppermute | solution.py:18
  4.9 27.5 %collective-permute-start.8 = (f32[15,8,2048]{2,1,0:T(8,128)}, f32[15,8,2048]{2,1,0:T(8,128)S(1)}, u32[]{:S(2)}, u32[]{:S(2)}) collective-permute-start(f32[15,8,2048]{2,1,0:T(8,128)} %param.5), channel_id=1, source_target_pairs={{0,96},{16,112},{32,0},{48,16},{64,32},{80,48},{96,64},{112,80},{1... | collective-permute-start | bytes 2949128 | tf_op jit(solution)/shard_map/ppermute | solution.py:18
  7.7 23.5 %collective-permute-start.2 = (f32[8,1,2048]{2,1,0:T(1,128)S(1)}, f32[8,1,2048]{2,1,0:T(1,128)S(1)}, u32[]{:S(2)}, u32[]{:S(2)}) collective-permute-start(f32[8,1,2048]{2,1,0:T(1,128)S(1)} %get-tuple-element.44), channel_id=1, source_target_pairs={{0,1},{1,2},{2,3},{3,4},{4,5},{5,6},{6,7},{7,8},{8,9},{9,10},{10,1... | collective-permute-start | bytes 196616 | tf_op jit(solution)/shard_map/ppermute | solution.py:45
  12.7 18.6 %collective-permute-start.3 = (f32[8,1,2048]{2,1,0:T(1,128)S(1)}, f32[8,1,2048]{2,1,0:T(1,128)S(1)}, u32[]{:S(2)}, u32[]{:S(2)}) collective-permute-start(f32[8,1,2048]{2,1,0:T(1,128)S(1)} %get-tuple-element.45), channel_id=1, source_target_pairs={{1,0},{2,1},{3,2},{4,3},{5,4},{6,5},{7,6},{8,7},{9,8},{10,9},{11,1... | collective-permute-start | bytes 196616 | tf_op jit(solution)/shard_map/ppermute | solution.py:45
  32.5 13.3 %collective-permute-start.10 = (f32[15,8,1024]{2,1,0:T(8,128)S(1)}, f32[15,8,1024]{2,1,0:T(8,128)S(1)}, u32[]{:S(2)}, u32[]{:S(2)}) collective-permute-start(f32[15,8,1024]{2,1,0:T(8,128)S(1)} %slice.55), channel_id=1, source_target_pairs={{0,96},{16,112},{32,0},{48,16},{64,32},{80,48},{96,64},{112,80},{1... | collective-permute-start | bytes 1474568 | tf_op jit(solution)/shard_map/ppermute | solution.py:18
  33.9 14.5 %collective-permute-start.9 = (f32[15,8,1024]{2,1,0:T(8,128)S(1)}, f32[15,8,1024]{2,1,0:T(8,128)S(1)}, u32[]{:S(2)}, u32[]{:S(2)}) collective-permute-start(f32[15,8,1024]{2,1,0:T(8,128)S(1)} %slice.54), channel_id=1, source_target_pairs={{0,32},{16,48},{32,64},{48,80},{64,96},{80,112},{96,0},{112,16},{1... | collective-permute-start | bytes 1474568 | tf_op jit(solution)/shard_map/ppermute | solution.py:18
  34.2 34.0 %collective-permute-start.1 = (f32[15,8,2048]{2,1,0:T(8,128)}, f32[15,8,2048]{2,1,0:T(8,128)S(1)}, u32[]{:S(2)}, u32[]{:S(2)}) collective-permute-start(f32[15,8,2048]{2,1,0:T(8,128)} %collective-permute-done), channel_id=1, source_target_pairs={{0,32},{16,48},{32,64},{48,80},{64,96},{80,112},{96,0},{112,16},{1... | collective-permute-start | bytes 2949128 | tf_op jit(solution)/shard_map/ppermute | solution.py:18
  34.3 34.1 %collective-permute-start.5 = (f32[15,8,2048]{2,1,0:T(8,128)}, f32[15,8,2048]{2,1,0:T(8,128)S(1)}, u32[]{:S(2)}, u32[]{:S(2)}) collective-permute-start(f32[15,8,2048]{2,1,0:T(8,128)} %collective-permute-done), channel_id=1, source_target_pairs={{0,96},{16,112},{32,0},{48,16},{64,32},{80,48},{96,64},{112,80},{1... | collective-permute-start | bytes 2949128 | tf_op jit(solution)/shard_map/ppermute | solution.py:18
  49.8 18.6 %copy-start = (f32[105,8,2048]{2,1,0:T(8,128)}, f32[105,8,2048]{2,1,0:T(8,128)S(1)}, u32[]{:S(2)}) copy-start(f32[105,8,2048]{2,1,0:T(8,128)S(1)} %constant_dynamic-update-slice_fusion.2) | copy-start | bytes 20643844
  68.2 0.9 copy-start.1
  68.2 18.7 %collective-permute-start.4 = (f32[15,8,1024]{2,1,0:T(8,128)S(1)}, f32[15,8,1024]{2,1,0:T(8,128)}, u32[]{:S(2)}, u32[]{:S(2)}) collective-permute-start(f32[15,8,1024]{2,1,0:T(8,128)S(1)} %slice.40), channel_id=1, source_target_pairs={{0,32},{16,48},{32,64},{48,80},{64,96},{80,112},{96,0},{112,16},{1... | collective-permute-start | bytes 1474568 | tf_op jit(solution)/shard_map/ppermute | solution.py:18
  68.3 1.1 %copy-start.2 = (f32[15,8,2048]{2,1,0:T(8,128)}, f32[15,8,2048]{2,1,0:T(8,128)S(1)}, u32[]{:S(2)}) copy-start(f32[15,8,2048]{2,1,0:T(8,128)S(1)} %collective-permute-done.5) | copy-start | bytes 2949124
  69.5 17.5 %collective-permute-start.6 = (f32[15,8,1024]{2,1,0:T(8,128)S(1)}, f32[15,8,1024]{2,1,0:T(8,128)}, u32[]{:S(2)}, u32[]{:S(2)}) collective-permute-start(f32[15,8,1024]{2,1,0:T(8,128)S(1)} %slice.53), channel_id=1, source_target_pairs={{0,96},{16,112},{32,0},{48,16},{64,32},{80,48},{96,64},{112,80},{1... | collective-permute-start | bytes 1474568 | tf_op jit(solution)/shard_map/ppermute | solution.py:18
  93.9 7.6 %collective-permute-start.11 = (f32[15,2048]{1,0:T(8,128)S(1)}, f32[15,2048]{1,0:T(8,128)S(1)}, u32[]{:S(2)}, u32[]{:S(2)}) collective-permute-start(f32[15,2048]{1,0:T(8,128)S(1)} %get-tuple-element.35), channel_id=1, source_target_pairs={{0,1},{1,2},{2,3},{3,4},{4,5},{5,6},{6,7},{7,8},{8,9},{9,10},{10,1... | collective-permute-start | bytes 368648 | tf_op jit(solution)/shard_map/ppermute | solution.py:45
  99.6 6.3 %collective-permute-start.12 = (f32[15,2048]{1,0:T(8,128)S(1)}, f32[15,2048]{1,0:T(8,128)S(1)}, u32[]{:S(2)}, u32[]{:S(2)}) collective-permute-start(f32[15,2048]{1,0:T(8,128)S(1)} %get-tuple-element.36), channel_id=1, source_target_pairs={{1,0},{2,1},{3,2},{4,3},{5,4},{6,5},{7,6},{8,7},{9,8},{10,9},{11,1... | collective-permute-start | bytes 368648 | tf_op jit(solution)/shard_map/ppermute | solution.py:45

commit v13 on v11

--- a/solution.py
+++ b/solution.py
@@ -118,6 +118,20 @@
             edges[4, k] = jnp.where(column == cols - 1, zero, c_rt)
             edges[5, k] = jnp.where(row == 0, c_up, jnp.where(row == rows - 1, c_dn, zero))
 
+    group = out.shape[0]
+
+    def one_slot(s, carry):
+        slot = pl.program_id(0) * group + s
+        acc, rim = stencil_slot(partners, weights, every, edges, slot, kl_terms, rows, cols)
+        out[s] = acc
+        to_prev[pl.ds(slot, 1), :] = rim[0:1]
+        to_next[pl.ds(slot, 1), :] = rim[rows - 1:rows]
+        return carry
+
+    lax.fori_loop(0, group, one_slot, 0)
+
+
+def stencil_slot(partners, weights, every, edges, slot, kl_terms, rows, cols):
     acc = jnp.zeros((rows, cols), jnp.float32)
     rim = jnp.zeros((rows, cols), jnp.float32)
     for k in range(kl_terms):
@@ -136,13 +150,12 @@
         term = term - edges[4, k] * rt
         acc = acc + term
         rim = rim + edges[5, k] * center
-    out[0] = acc
-    to_prev[pl.ds(slot, 1), :] = rim[0:1]
-    to_next[pl.ds(slot, 1), :] = rim[rows - 1:rows]
+    return acc, rim
 
 
 def stencil_apply(every, coef, partners, weights):
     own_modes = partners.shape[0]
+    group = next(g for g in (5, 3, 1) if own_modes % g == 0)
     kl_terms = coef.shape[0]
     rows = every.shape[1]
     cols = every.shape[2]
@@ -155,14 +168,14 @@
         ),
         grid_spec=pltpu.PrefetchScalarGridSpec(
             num_scalar_prefetch=1,
-            grid=(own_modes,),
+            grid=(own_modes // group,),
             in_specs=[
                 pl.BlockSpec(memory_space=pltpu.SMEM),
                 pl.BlockSpec(memory_space=pltpu.VMEM),
                 pl.BlockSpec(memory_space=pltpu.VMEM),
             ],
             out_specs=(
-                pl.BlockSpec((1, rows, cols), lambda i, p: (i, 0, 0)),
+                pl.BlockSpec((group, rows, cols), lambda i, p: (i, 0, 0)),
                 pl.BlockSpec(memory_space=pltpu.VMEM),
                 pl.BlockSpec(memory_space=pltpu.VMEM),
             ),

time: 103 us -> 103 us (level)
  no operation moved by 1% of the time
where the time goes in v13:
time: 103 us; the launch traced here: 102 us
  waiting for transfers between devices  37.7 us (37%)
  starting transfers between devices  27.8 us (27%)
  other arithmetic  13.2 us (13%)
  local copies, waits for them, and re-layouts  12.7 us (12%)
  Pallas kernels  10.3 us (10%)
    ppermute x8, waiting for transfers between devices, shifted(): lax.ppermute(x, 'chaos', [(c, (c + step) % count) for c in range(count)])  33.4 us
    ppermute x8, starting transfers between devices, shifted(): lax.ppermute(x, 'chaos', [(c, (c + step) % count) for c in range(count)])  10.7 us
    pallas_call x1, Pallas kernels, stencil_apply(): pl.pallas_call(stencil_kernel, out_shape=(jax.ShapeDtypeStruct((own_modes...  10.3 us
    ppermute x2, starting transfers between devices, space_halo(): lax.ppermute(edge_last, 'space', up)  9.57 us
    unnamed x12, local copies, waits for them, and re-layouts  8.4 us
    add x1, other arithmetic, local(): owner_at[slot_of_mode // own_modes] * own_modes + slot_of_mode % own_modes  5 us
    ppermute x2, waiting for transfers between devices, space_halo(): lax.ppermute(edge_first, 'space', down)  4.34 us
    ppermute x2, starting transfers between devices, space_halo(): lax.ppermute(edge_first, 'space', down)  3.84 us
  transfers between devices with their start and end apart: 13, of which 5 were waited for; matrix products, arithmetic and copies ran while one was open for 22% of the time, Pallas kernels for 0%

profile of v13, /device:TPU:1, one launch (start us, length us, event | category | flops | bytes accessed | tf_op | source)
XLA Modules:
  0.0 102.1 jit_solution(6351627816100316353)
XLA Ops:
  0.0 3.7 %collective-permute-start = (f32[15,8,2048]{2,1,0:T(8,128)}, f32[15,8,2048]{2,1,0:T(8,128)}, u32[]{:S(2)}, u32[]{:S(2)}) collective-permute-start(f32[15,8,2048]{2,1,0:T(8,128)} %param.5), channel_id=1, source_target_pairs={{0,16},{16,0},{32,48},{48,32},{64,80},{80,64},{96,112},{112,96},{1... | collective-permute-start | bytes 2949128 | tf_op jit(solution)/shard_map/ppermute | solution.py:25
  3.7 1.2 %collective-permute-start.4 = (f32[15,8,2048]{2,1,0:T(8,128)}, f32[15,8,2048]{2,1,0:T(8,128)S(1)}, u32[]{:S(2)}, u32[]{:S(2)}) collective-permute-start(f32[15,8,2048]{2,1,0:T(8,128)} %param.5), channel_id=1, source_target_pairs={{0,32},{16,48},{32,64},{48,80},{64,96},{80,112},{96,0},{112,16},{1... | collective-permute-start | bytes 2949128 | tf_op jit(solution)/shard_map/ppermute | solution.py:18
  4.9 1.5 %collective-permute-start.5 = (f32[15,8,2048]{2,1,0:T(8,128)}, f32[15,8,2048]{2,1,0:T(8,128)S(1)}, u32[]{:S(2)}, u32[]{:S(2)}) collective-permute-start(f32[15,8,2048]{2,1,0:T(8,128)} %param.5), channel_id=1, source_target_pairs={{0,96},{16,112},{32,0},{48,16},{64,32},{80,48},{96,64},{112,80},{1... | collective-permute-start | bytes 2949128 | tf_op jit(solution)/shard_map/ppermute | solution.py:18
  6.4 1.3 %fusion.4 = (f32[8,1,2048]{2,1,0:T(1,128)S(1)}, f32[8,1,2048]{2,1,0:T(1,128)S(1)}) fusion(f32[8,8,2048]{2,1,0:T(8,128)} %param.6), kind=kLoop, calls=%fused_computation.49 | loop fusion | bytes 262144 | tf_op jit(solution)/shard_map/slice | solution.py:84
  7.7 4.9 %collective-permute-start.2 = (f32[8,1,2048]{2,1,0:T(1,128)S(1)}, f32[8,1,2048]{2,1,0:T(1,128)S(1)}, u32[]{:S(2)}, u32[]{:S(2)}) collective-permute-start(f32[8,1,2048]{2,1,0:T(1,128)S(1)} %get-tuple-element.30), channel_id=1, source_target_pairs={{0,1},{1,2},{2,3},{3,4},{4,5},{5,6},{6,7},{7,8},{8,9},{9,10},{10,1... | collective-permute-start | bytes 196616 | tf_op jit(solution)/shard_map/ppermute | solution.py:45
  12.7 1.9 %collective-permute-start.3 = (f32[8,1,2048]{2,1,0:T(1,128)S(1)}, f32[8,1,2048]{2,1,0:T(1,128)S(1)}, u32[]{:S(2)}, u32[]{:S(2)}) collective-permute-start(f32[8,1,2048]{2,1,0:T(1,128)S(1)} %get-tuple-element.31), channel_id=1, source_target_pairs={{1,0},{2,1},{3,2},{4,3},{5,4},{6,5},{7,6},{8,7},{9,8},{10,9},{11,1... | collective-permute-start | bytes 196616 | tf_op jit(solution)/shard_map/ppermute | solution.py:45
  18.6 5.0 %fusion.1 = s32[120]{0:T(128)S(1)} fusion(s32[120]{0:T(128)S(1)} %select_reduce_fusion.5, s32[]{:T(128)} %bitcast.12, s32[]{:T(128)} %bitcast.13, s32[]{:T(128)} %bitcast.14, s32[]{:T(128)} %bitcast.15, s32[]{:T(128)} %bitcast.16, s32[]{:T(128)} %bitcast.18, s32[]{:T(128)} %bitcast.17, s32[]{:T(128)} %bitcast.11), kind=kLoop, calls=%fused_computation.44 | loop fusion | flops 3720 | bytes 992 | tf_op jit(solution)/shard_map/add | solution.py:63
  23.8 1.2 %and_reduce_fusion = (pred[15,8]{1,0:T(8,128)(4,1)}, s32[15,8]{1,0:T(8,128)S(1)}) fusion(pred[8,624]{1,0:T(8,128)(4,1)S(1)} %iota_compare_fusion.4, pred[15,624]{1,0:T(8,128)(4,1)S(1)} %broadcast_compare_fusion), kind=kLoop, calls=%fused_computation.6 | loop fusion | flops 598200 | bytes 14952 | tf_op jit(solution)/shard_map/local/reduce | solution.py:74
  27.1 1.3 %constant_dynamic-update-slice_fusion.5 = f32[120,8,2048]{2,1,0:T(8,128)S(1)} fusion(f32[15,8,2048]{2,1,0:T(8,128)} %param.5), kind=kLoop, calls=%fused_computation.24 | loop fusion | bytes 1966080
  28.4 1.2 %pad_maximum_fusion.coef = f32[8,10,2048]{2,1,0:T(8,128)S(1)} fusion(f32[8,1,2048]{2,1,0:T(1,128)S(1)} %collective-permute-done.3, f32[8,8,2048]{2,1,0:T(8,128)} %param.6, f32[8,1,2048]{2,1,0:T(1,128)S(1)} %collective-permute-done.2), kind=kLoop, calls=%fused_computation | loop fusion | flops 327680 | bytes 1310720 | tf_op jit(solution)/shard_map/concatenate | solution.py:85
  29.8 2.7 %collective-permute-start.7 = (f32[15,8,1024]{2,1,0:T(8,128)S(1)}, f32[15,8,1024]{2,1,0:T(8,128)S(1)}, u32[]{:S(2)}, u32[]{:S(2)}) collective-permute-start(f32[15,8,1024]{2,1,0:T(8,128)S(1)} %slice.54), channel_id=1, source_target_pairs={{0,96},{16,112},{32,0},{48,16},{64,32},{80,48},{96,64},{112,80},{1... | collective-permute-start | bytes 1474568 | tf_op jit(solution)/shard_map/ppermute | solution.py:18
  32.5 2.7 %collective-permute-start.8 = (f32[15,8,2048]{2,1,0:T(8,128)}, f32[15,8,2048]{2,1,0:T(8,128)S(1)}, u32[]{:S(2)}, u32[]{:S(2)}) collective-permute-start(f32[15,8,2048]{2,1,0:T(8,128)} %collective-permute-done), channel_id=1, source_target_pairs={{0,96},{16,112},{32,0},{48,16},{64,32},{80,48},{96,64},{112,80},{1... | collective-permute-start | bytes 2949128 | tf_op jit(solution)/shard_map/ppermute | solution.py:18
  35.4 8.6 %collective-permute-done.6 = f32[15,8,1024]{2,1,0:T(8,128)S(1)} collective-permute-done((f32[15,8,1024]{2,1,0:T(8,128)S(1)}, f32[15,8,1024]{2,1,0:T(8,128)S(1)}, u32[]{:S(2)}, u32[]{:S(2)}) %collective-permute-start.6) | collective-permute-done | bytes 491552 | tf_op jit(solution)/shard_map/ppermute | solution.py:18
  44.1 1.3 %constant_dynamic-update-slice_fusion.2 = f32[120,8,2048]{2,1,0:T(8,128)S(1)} fusion(f32[120,8,2048]{2,1,0:T(8,128)S(1)} %maximum_dynamic-update-slice_fusion.1, f32[15,8,2048]{2,1,0:T(8,128)} %collective-permute-done), kind=kLoop, calls=%fused_computation.21 | loop fusion | bytes 1966080
  45.4 19.7 %collective-permute-done.1 = f32[15,8,2048]{2,1,0:T(8,128)S(1)} collective-permute-done((f32[15,8,2048]{2,1,0:T(8,128)}, f32[15,8,2048]{2,1,0:T(8,128)S(1)}, u32[]{:S(2)}, u32[]{:S(2)}) %collective-permute-start.1) | collective-permute-done | bytes 983072 | tf_op jit(solution)/shard_map/ppermute | solution.py:18
  66.5 2.5 %collective-permute-start.10 = (f32[15,8,1024]{2,1,0:T(8,128)S(1)}, f32[15,8,1024]{2,1,0:T(8,128)S(1)}, u32[]{:S(2)}, u32[]{:S(2)}) collective-permute-start(f32[15,8,1024]{2,1,0:T(8,128)S(1)} %slice.55), channel_id=1, source_target_pairs={{0,96},{16,112},{32,0},{48,16},{64,32},{80,48},{96,64},{112,80},{1... | collective-permute-start | bytes 1474568 | tf_op jit(solution)/shard_map/ppermute | solution.py:18
  69.1 2.3 %constant_dynamic-update-slice_fusion.1 = f32[120,8,2048]{2,1,0:T(8,128)} fusion(f32[120,8,2048]{2,1,0:T(8,128)} %copy-done, f32[15,8,2048]{2,1,0:T(8,128)} %copy-done.1), kind=kLoop, calls=%fused_computation.20 | loop fusion | bytes 1966080
  71.4 2.3 %constant_dynamic-update-slice_fusion = f32[120,8,2048]{2,1,0:T(8,128)} fusion(f32[120,8,2048]{2,1,0:T(8,128)} %constant_dynamic-update-slice_fusion.1, f32[15,8,2048]{2,1,0:T(8,128)} %copy-done.2), kind=kLoop, calls=%fused_computation.19 | loop fusion | bytes 1966080
  73.6 5.0 %collective-permute-done.9 = f32[15,8,1024]{2,1,0:T(8,128)S(1)} collective-permute-done((f32[15,8,1024]{2,1,0:T(8,128)S(1)}, f32[15,8,1024]{2,1,0:T(8,128)S(1)}, u32[]{:S(2)}, u32[]{:S(2)}) %collective-permute-start.9) | collective-permute-done | bytes 491552 | tf_op jit(solution)/shard_map/ppermute | solution.py:18
  79.7 10.3 %shard_map.55 = (f32[15,8,2048]{2,1,0:T(8,128)S(1)}, f32[15,2048]{1,0:T(8,128)S(1)}, f32[15,2048]{1,0:T(8,128)S(1)}) custom-call(s32[15,16]{1,0:T(8,128)S(1)} %copy.18.partners, f32[15,16]{1,0:T(8,128)S(1)} %copy.19.weights, f32[120,8,2048]{2,1,0:T(8,128)} %maximum_dynamic-update-slice_fusion.every, f32[8,10,2048]{2,1,0:T(8,128)S(1)} %pad_maximum_fusion.coef), custom_call_target="tpu_custom_call" | custom-call | tf_op jit(solution)/shard_map/pallas_call | solution.py:162
  90.0 4.6 %collective-permute-start.11 = (f32[15,2048]{1,0:T(8,128)S(1)}, f32[15,2048]{1,0:T(8,128)S(1)}, u32[]{:S(2)}, u32[]{:S(2)}) collective-permute-start(f32[15,2048]{1,0:T(8,128)S(1)} %get-tuple-element.21), channel_id=1, source_target_pairs={{0,1},{1,2},{2,3},{3,4},{4,5},{5,6},{6,7},{7,8},{8,9},{9,10},{10,1... | collective-permute-start | bytes 368648 | tf_op jit(solution)/shard_map/ppermute | solution.py:45
  94.7 1.9 %collective-permute-start.12 = (f32[15,2048]{1,0:T(8,128)S(1)}, f32[15,2048]{1,0:T(8,128)S(1)}, u32[]{:S(2)}, u32[]{:S(2)}) collective-permute-start(f32[15,2048]{1,0:T(8,128)S(1)} %get-tuple-element.22), channel_id=1, source_target_pairs={{1,0},{2,1},{3,2},{4,3},{5,4},{6,5},{7,6},{8,7},{9,8},{10,9},{11,1... | collective-permute-start | bytes 368648 | tf_op jit(solution)/shard_map/ppermute | solution.py:45
  96.6 4.3 %collective-permute-done.12 = f32[15,2048]{1,0:T(8,128)S(1)} collective-permute-done((f32[15,2048]{1,0:T(8,128)S(1)}, f32[15,2048]{1,0:T(8,128)S(1)}, u32[]{:S(2)}, u32[]{:S(2)}) %collective-permute-start.12) | collective-permute-done | bytes 122912 | tf_op jit(solution)/shard_map/ppermute | solution.py:45
  101.0 1.2 %select_subtract_fusion = f32[15,8,2048]{2,1,0:T(8,128)} fusion(f32[15,8,2048]{2,1,0:T(8,128)S(1)} %get-tuple-element.20, f32[15,2048]{1,0:T(8,128)S(1)} %collective-permute-done.12, f32[15,2048]{1,0:T(8,128)S(1)} %collective-permute-done.11, pred[8]{0:T(512)(128)(4,1)S(1)} %get-tuple-element.40, pred[8]{0:T(512)(128)(4,1)S(1)} %get-tuple-element.41), kind=kLoop, calls=%fused_computation.3 | loop fusion | flops 737280 | bytes 2211856 | tf_op jit(solution)/shard_map/sub | solution.py:94
  (49 shorter events, 9.1 us)
Async XLA Ops:
  0.0 32.5 %collective-permute-start = (f32[15,8,2048]{2,1,0:T(8,128)}, f32[15,8,2048]{2,1,0:T(8,128)}, u32[]{:S(2)}, u32[]{:S(2)}) collective-permute-start(f32[15,8,2048]{2,1,0:T(8,128)} %param.5), channel_id=1, source_target_pairs={{0,16},{16,0},{32,48},{48,32},{64,80},{80,64},{96,112},{112,96},{1... | collective-permute-start | bytes 2949128 | tf_op jit(solution)/shard_map/ppermute | solution.py:25
  3.7 25.9 %collective-permute-start.4 = (f32[15,8,2048]{2,1,0:T(8,128)}, f32[15,8,2048]{2,1,0:T(8,128)S(1)}, u32[]{:S(2)}, u32[]{:S(2)}) collective-permute-start(f32[15,8,2048]{2,1,0:T(8,128)} %param.5), channel_id=1, source_target_pairs={{0,32},{16,48},{32,64},{48,80},{64,96},{80,112},{96,0},{112,16},{1... | collective-permute-start | bytes 2949128 | tf_op jit(solution)/shard_map/ppermute | solution.py:18
  4.9 24.8 %collective-permute-start.5 = (f32[15,8,2048]{2,1,0:T(8,128)}, f32[15,8,2048]{2,1,0:T(8,128)S(1)}, u32[]{:S(2)}, u32[]{:S(2)}) collective-permute-start(f32[15,8,2048]{2,1,0:T(8,128)} %param.5), channel_id=1, source_target_pairs={{0,96},{16,112},{32,0},{48,16},{64,32},{80,48},{96,64},{112,80},{1... | collective-permute-start | bytes 2949128 | tf_op jit(solution)/shard_map/ppermute | solution.py:18
  7.7 20.6 %collective-permute-start.2 = (f32[8,1,2048]{2,1,0:T(1,128)S(1)}, f32[8,1,2048]{2,1,0:T(1,128)S(1)}, u32[]{:S(2)}, u32[]{:S(2)}) collective-permute-start(f32[8,1,2048]{2,1,0:T(1,128)S(1)} %get-tuple-element.30), channel_id=1, source_target_pairs={{0,1},{1,2},{2,3},{3,4},{4,5},{5,6},{6,7},{7,8},{8,9},{9,10},{10,1... | collective-permute-start | bytes 196616 | tf_op jit(solution)/shard_map/ppermute | solution.py:45
  12.7 15.7 %collective-permute-start.3 = (f32[8,1,2048]{2,1,0:T(1,128)S(1)}, f32[8,1,2048]{2,1,0:T(1,128)S(1)}, u32[]{:S(2)}, u32[]{:S(2)}) collective-permute-start(f32[8,1,2048]{2,1,0:T(1,128)S(1)} %get-tuple-element.31), channel_id=1, source_target_pairs={{1,0},{2,1},{3,2},{4,3},{5,4},{6,5},{7,6},{8,7},{9,8},{10,9},{11,1... | collective-permute-start | bytes 196616 | tf_op jit(solution)/shard_map/ppermute | solution.py:45
  29.7 14.4 %collective-permute-start.6 = (f32[15,8,1024]{2,1,0:T(8,128)S(1)}, f32[15,8,1024]{2,1,0:T(8,128)S(1)}, u32[]{:S(2)}, u32[]{:S(2)}) collective-permute-start(f32[15,8,1024]{2,1,0:T(8,128)S(1)} %slice.53), channel_id=1, source_target_pairs={{0,32},{16,48},{32,64},{48,80},{64,96},{80,112},{96,0},{112,16},{1... | collective-permute-start | bytes 1474568 | tf_op jit(solution)/shard_map/ppermute | solution.py:18
  29.8 14.2 %collective-permute-start.7 = (f32[15,8,1024]{2,1,0:T(8,128)S(1)}, f32[15,8,1024]{2,1,0:T(8,128)S(1)}, u32[]{:S(2)}, u32[]{:S(2)}) collective-permute-start(f32[15,8,1024]{2,1,0:T(8,128)S(1)} %slice.54), channel_id=1, source_target_pairs={{0,96},{16,112},{32,0},{48,16},{64,32},{80,48},{96,64},{112,80},{1... | collective-permute-start | bytes 1474568 | tf_op jit(solution)/shard_map/ppermute | solution.py:18
  32.5 32.6 %collective-permute-start.1 = (f32[15,8,2048]{2,1,0:T(8,128)}, f32[15,8,2048]{2,1,0:T(8,128)S(1)}, u32[]{:S(2)}, u32[]{:S(2)}) collective-permute-start(f32[15,8,2048]{2,1,0:T(8,128)} %collective-permute-done), channel_id=1, source_target_pairs={{0,32},{16,48},{32,64},{48,80},{64,96},{80,112},{96,0},{112,16},{1... | collective-permute-start | bytes 2949128 | tf_op jit(solution)/shard_map/ppermute | solution.py:18
  32.5 32.7 %collective-permute-start.8 = (f32[15,8,2048]{2,1,0:T(8,128)}, f32[15,8,2048]{2,1,0:T(8,128)S(1)}, u32[]{:S(2)}, u32[]{:S(2)}) collective-permute-start(f32[15,8,2048]{2,1,0:T(8,128)} %collective-permute-done), channel_id=1, source_target_pairs={{0,96},{16,112},{32,0},{48,16},{64,32},{80,48},{96,64},{112,80},{1... | collective-permute-start | bytes 2949128 | tf_op jit(solution)/shard_map/ppermute | solution.py:18
  45.4 19.9 %copy-start = (f32[120,8,2048]{2,1,0:T(8,128)}, f32[120,8,2048]{2,1,0:T(8,128)S(1)}, u32[]{:S(2)}) copy-start(f32[120,8,2048]{2,1,0:T(8,128)S(1)} %constant_dynamic-update-slice_fusion.2) | copy-start | bytes 23592964
  65.1 0.9 copy-start.1
  65.1 13.5 %collective-permute-start.9 = (f32[15,8,1024]{2,1,0:T(8,128)S(1)}, f32[15,8,1024]{2,1,0:T(8,128)S(1)}, u32[]{:S(2)}, u32[]{:S(2)}) collective-permute-start(f32[15,8,1024]{2,1,0:T(8,128)S(1)} %slice.42), channel_id=1, source_target_pairs={{0,32},{16,48},{32,64},{48,80},{64,96},{80,112},{96,0},{112,16},{1... | collective-permute-start | bytes 1474568 | tf_op jit(solution)/shard_map/ppermute | solution.py:18
  65.2 1.2 %copy-start.2 = (f32[15,8,2048]{2,1,0:T(8,128)}, f32[15,8,2048]{2,1,0:T(8,128)S(1)}, u32[]{:S(2)}) copy-start(f32[15,8,2048]{2,1,0:T(8,128)S(1)} %collective-permute-done.8) | copy-start | bytes 2949124
  66.5 12.2 %collective-permute-start.10 = (f32[15,8,1024]{2,1,0:T(8,128)S(1)}, f32[15,8,1024]{2,1,0:T(8,128)S(1)}, u32[]{:S(2)}, u32[]{:S(2)}) collective-permute-start(f32[15,8,1024]{2,1,0:T(8,128)S(1)} %slice.55), channel_id=1, source_target_pairs={{0,96},{16,112},{32,0},{48,16},{64,32},{80,48},{96,64},{112,80},{1... | collective-permute-start | bytes 1474568 | tf_op jit(solution)/shard_map/ppermute | solution.py:18
  90.0 6.6 %collective-permute-start.11 = (f32[15,2048]{1,0:T(8,128)S(1)}, f32[15,2048]{1,0:T(8,128)S(1)}, u32[]{:S(2)}, u32[]{:S(2)}) collective-permute-start(f32[15,2048]{1,0:T(8,128)S(1)} %get-tuple-element.21), channel_id=1, source_target_pairs={{0,1},{1,2},{2,3},{3,4},{4,5},{5,6},{6,7},{7,8},{8,9},{9,10},{10,1... | collective-permute-start | bytes 368648 | tf_op jit(solution)/shard_map/ppermute | solution.py:45
  94.7 6.3 %collective-permute-start.12 = (f32[15,2048]{1,0:T(8,128)S(1)}, f32[15,2048]{1,0:T(8,128)S(1)}, u32[]{:S(2)}, u32[]{:S(2)}) collective-permute-start(f32[15,2048]{1,0:T(8,128)S(1)} %get-tuple-element.22), channel_id=1, source_target_pairs={{1,0},{2,1},{3,2},{4,3},{5,4},{6,5},{7,6},{8,7},{9,8},{10,9},{11,1... | collective-permute-start | bytes 368648 | tf_op jit(solution)/shard_map/ppermute | solution.py:45

commit v14 on v11

--- a/solution.py
+++ b/solution.py
@@ -4,13 +4,6 @@
 from jax.experimental import pallas as pl
 from jax.experimental.pallas import tpu as pltpu
 from jax.sharding import PartitionSpec as P
-
-
-def shift_cols(x, direction):
-    zero = jnp.zeros_like(x[..., :1])
-    if direction > 0:
-        return jnp.concatenate([zero, x[..., :-1]], axis=-1)
-    return jnp.concatenate([x[..., 1:], zero], axis=-1)
 
 
 def shifted(x, step):
@@ -22,19 +15,20 @@
     count = lax.axis_size("chaos")
     me = lax.axis_index("chaos")
     half = block.shape[-1] // 2
+    own_left = shifted(block, 2)
+    own_right = shifted(block, -2)
     partner = lax.ppermute(block, "chaos", [(c, c ^ 1) for c in range(count)])
     pieces = []
-    owners = []
     for base, origin in ((block, me), (partner, me ^ 1)):
-        from_left = shifted(base, 2)
-        from_right = shifted(base, -2)
-        if origin is not me:
-            from_left, tables = lax.optimization_barrier((from_left, tables))
+        if origin is me:
+            from_left, from_right = own_left, own_right
+        else:
+            from_left = shifted(base, 2)
+            from_right = shifted(base, -2)
         far = jnp.concatenate(
             [shifted(from_left[..., :half], 2), shifted(from_right[..., half:], -2)], axis=-1
         )
         pieces += [base, from_left, from_right, far]
-        owners += [origin, (origin - 2) % count, (origin + 2) % count, (origin + 4) % count]
     return jnp.concatenate(pieces, axis=0), tables
 
 

time: 103 us -> 104 us (level)
    ppermute x2, starting transfers between devices: 9.57 us -> 7.85 us  [space_halo(): lax.ppermute(edge_last, 'space', up)]
    ppermute x2, starting transfers between devices: 3.84 us -> 5.34 us  [space_halo(): lax.ppermute(edge_first, 'space', down)]
    ppermute x8, starting transfers between devices: 10.7 us -> 11.9 us  [shifted(): lax.ppermute(x, 'chaos', [(c, (c + step) % count) for c in range(count)])]
    unnamed x12 -> x6, local copies, waits for them, and re-layouts: 8.4 us -> 7.57 us
  transfers between devices with their start and end apart: 13 -> 13, of which waited for: 5 -> 4; matrix products, arithmetic and copies ran while one was open for 22% -> 23% of each run, Pallas kernels for 0% -> 0%
where the time goes in v14:
time: 104 us; the launch traced here: 103 us
  waiting for transfers between devices  38 us (37%)
  starting transfers between devices  28.2 us (27%)
  other arithmetic  14.2 us (14%)
  local copies, waits for them, and re-layouts  11.9 us (11%)
  Pallas kernels  10.6 us (10%)
    ppermute x8, waiting for transfers between devices, shifted(): lax.ppermute(x, 'chaos', [(c, (c + step) % count) for c in range(count)])  33.6 us
    ppermute x8, starting transfers between devices, shifted(): lax.ppermute(x, 'chaos', [(c, (c + step) % count) for c in range(count)])  11.9 us
    pallas_call x1, Pallas kernels, stencil_apply(): pl.pallas_call(stencil_kernel, out_shape=(jax.ShapeDtypeStruct((own_modes...  10.6 us
    ppermute x2, starting transfers between devices, space_halo(): lax.ppermute(edge_last, 'space', up)  7.85 us
    unnamed x6, local copies, waits for them, and re-layouts  7.57 us
    ppermute x2, starting transfers between devices, space_halo(): lax.ppermute(edge_first, 'space', down)  5.34 us
    add x1, other arithmetic, local(): owner_at[slot_of_mode // own_modes] * own_modes + slot_of_mode % own_modes  5 us
    ppermute x2, waiting for transfers between devices, space_halo(): lax.ppermute(edge_first, 'space', down)  4.34 us
  transfers between devices with their start and end apart: 13, of which 4 were waited for; matrix products, arithmetic and copies ran while one was open for 23% of the time, Pallas kernels for 0%

profile of v14, /device:TPU:1, one launch (start us, length us, event | category | flops | bytes accessed | tf_op | source)
XLA Modules:
  0.0 103.0 jit_solution(15154392232491282720)
XLA Ops:
  0.0 2.0 %collective-permute-start = (f32[15,8,2048]{2,1,0:T(8,128)}, f32[15,8,2048]{2,1,0:T(8,128)S(1)}, u32[]{:S(2)}, u32[]{:S(2)}) collective-permute-start(f32[15,8,2048]{2,1,0:T(8,128)} %param.5), channel_id=1, source_target_pairs={{0,32},{16,48},{32,64},{48,80},{64,96},{80,112},{96,0},{112,16},{1... | collective-permute-start | bytes 2949128 | tf_op jit(solution)/shard_map/ppermute | solution.py:11
  2.0 1.3 %collective-permute-start.1 = (f32[15,8,2048]{2,1,0:T(8,128)}, f32[15,8,2048]{2,1,0:T(8,128)S(1)}, u32[]{:S(2)}, u32[]{:S(2)}) collective-permute-start(f32[15,8,2048]{2,1,0:T(8,128)} %param.5), channel_id=1, source_target_pairs={{0,96},{16,112},{32,0},{48,16},{64,32},{80,48},{96,64},{112,80},{1... | collective-permute-start | bytes 2949128 | tf_op jit(solution)/shard_map/ppermute | solution.py:11
  3.3 3.1 %collective-permute-start.4 = (f32[15,8,2048]{2,1,0:T(8,128)}, f32[15,8,2048]{2,1,0:T(8,128)S(1)}, u32[]{:S(2)}, u32[]{:S(2)}) collective-permute-start(f32[15,8,2048]{2,1,0:T(8,128)} %param.5), channel_id=1, source_target_pairs={{0,16},{16,0},{32,48},{48,32},{64,80},{80,64},{96,112},{112,96},{1... | collective-permute-start | bytes 2949128 | tf_op jit(solution)/shard_map/ppermute | solution.py:20
  6.4 1.3 %fusion.4 = (f32[8,1,2048]{2,1,0:T(1,128)S(1)}, f32[8,1,2048]{2,1,0:T(1,128)S(1)}) fusion(f32[8,8,2048]{2,1,0:T(8,128)} %param.6), kind=kLoop, calls=%fused_computation.49 | loop fusion | bytes 262144 | tf_op jit(solution)/shard_map/slice | solution.py:78
  7.7 3.4 %collective-permute-start.10 = (f32[8,1,2048]{2,1,0:T(1,128)S(1)}, f32[8,1,2048]{2,1,0:T(1,128)S(1)}, u32[]{:S(2)}, u32[]{:S(2)}) collective-permute-start(f32[8,1,2048]{2,1,0:T(1,128)S(1)} %get-tuple-element.23), channel_id=1, source_target_pairs={{1,0},{2,1},{3,2},{4,3},{5,4},{6,5},{7,6},{8,7},{9,8},{10,9},{11,1... | collective-permute-start | bytes 196616 | tf_op jit(solution)/shard_map/ppermute | solution.py:39
  11.1 3.4 %collective-permute-start.9 = (f32[8,1,2048]{2,1,0:T(1,128)S(1)}, f32[8,1,2048]{2,1,0:T(1,128)S(1)}, u32[]{:S(2)}, u32[]{:S(2)}) collective-permute-start(f32[8,1,2048]{2,1,0:T(1,128)S(1)} %get-tuple-element.22), channel_id=1, source_target_pairs={{0,1},{1,2},{2,3},{3,4},{4,5},{5,6},{6,7},{7,8},{8,9},{9,10},{10,1... | collective-permute-start | bytes 196616 | tf_op jit(solution)/shard_map/ppermute | solution.py:39
  18.6 5.0 %fusion.1 = s32[120]{0:T(128)S(1)} fusion(s32[120]{0:T(128)S(1)} %select_reduce_fusion.5, s32[]{:T(128)} %bitcast.12, s32[]{:T(128)} %bitcast.13, s32[]{:T(128)} %bitcast.14, s32[]{:T(128)} %bitcast.15, s32[]{:T(128)} %bitcast.16, s32[]{:T(128)} %bitcast.18, s32[]{:T(128)} %bitcast.17, s32[]{:T(128)} %bitcast.11), kind=kLoop, calls=%fused_computation.44 | loop fusion | flops 3720 | bytes 992 | tf_op jit(solution)/shard_map/add | solution.py:57
  23.7 1.2 %and_reduce_fusion = (pred[15,8]{1,0:T(8,128)(4,1)}, s32[15,8]{1,0:T(8,128)S(1)}) fusion(pred[8,624]{1,0:T(8,128)(4,1)S(1)} %iota_compare_fusion.4, pred[15,624]{1,0:T(8,128)(4,1)S(1)} %broadcast_compare_fusion), kind=kLoop, calls=%fused_computation.6 | loop fusion | flops 598200 | bytes 14952 | tf_op jit(solution)/shard_map/local/reduce | solution.py:68
  27.1 2.2 %constant_dynamic-update-slice_fusion.5 = f32[120,8,2048]{2,1,0:T(8,128)} fusion(f32[15,8,2048]{2,1,0:T(8,128)} %param.5), kind=kLoop, calls=%fused_computation.24 | loop fusion | bytes 1966080
  29.5 1.2 %pad_maximum_fusion.coef = f32[8,10,2048]{2,1,0:T(8,128)S(1)} fusion(f32[8,1,2048]{2,1,0:T(1,128)S(1)} %collective-permute-done.10, f32[8,8,2048]{2,1,0:T(8,128)} %param.6, f32[8,1,2048]{2,1,0:T(1,128)S(1)} %collective-permute-done.9), kind=kLoop, calls=%fused_computation | loop fusion | flops 327680 | bytes 1310720 | tf_op jit(solution)/shard_map/concatenate | solution.py:79
  30.9 2.7 %collective-permute-start.3 = (f32[15,8,1024]{2,1,0:T(8,128)S(1)}, f32[15,8,1024]{2,1,0:T(8,128)S(1)}, u32[]{:S(2)}, u32[]{:S(2)}) collective-permute-start(f32[15,8,1024]{2,1,0:T(8,128)S(1)} %slice.54), channel_id=1, source_target_pairs={{0,96},{16,112},{32,0},{48,16},{64,32},{80,48},{96,64},{112,80},{1... | collective-permute-start | bytes 1474568 | tf_op jit(solution)/shard_map/ppermute | solution.py:11
  33.6 2.7 %collective-permute-start.6 = (f32[15,8,2048]{2,1,0:T(8,128)S(1)}, f32[15,8,2048]{2,1,0:T(8,128)S(1)}, u32[]{:S(2)}, u32[]{:S(2)}) collective-permute-start(f32[15,8,2048]{2,1,0:T(8,128)S(1)} %collective-permute-done.4), channel_id=1, source_target_pairs={{0,96},{16,112},{32,0},{48,16},{64,32},{80,48},{96,64},{112,80},{1... | collective-permute-start | bytes 2949128 | tf_op jit(solution)/shard_map/ppermute | solution.py:11
  36.3 1.1 %constant_dynamic-update-slice_fusion.4 = f32[120,8,2048]{2,1,0:T(8,128)} fusion(f32[120,8,2048]{2,1,0:T(8,128)} %constant_dynamic-update-slice_fusion.5, f32[15,8,2048]{2,1,0:T(8,128)S(1)} %collective-permute-done), kind=kLoop, calls=%fused_computation.23 | loop fusion | bytes 1966080
  38.4 6.8 %collective-permute-done.2 = f32[15,8,1024]{2,1,0:T(8,128)S(1)} collective-permute-done((f32[15,8,1024]{2,1,0:T(8,128)S(1)}, f32[15,8,1024]{2,1,0:T(8,128)S(1)}, u32[]{:S(2)}, u32[]{:S(2)}) %collective-permute-start.2) | collective-permute-done | bytes 491552 | tf_op jit(solution)/shard_map/ppermute | solution.py:11
  47.4 18.1 %collective-permute-done.5 = f32[15,8,2048]{2,1,0:T(8,128)S(1)} collective-permute-done((f32[15,8,2048]{2,1,0:T(8,128)S(1)}, f32[15,8,2048]{2,1,0:T(8,128)S(1)}, u32[]{:S(2)}, u32[]{:S(2)}) %collective-permute-start.5) | collective-permute-done | bytes 983072 | tf_op jit(solution)/shard_map/ppermute | solution.py:11
  65.7 3.0 %collective-permute-start.8 = (f32[15,8,1024]{2,1,0:T(8,128)S(1)}, f32[15,8,1024]{2,1,0:T(8,128)S(1)}, u32[]{:S(2)}, u32[]{:S(2)}) collective-permute-start(f32[15,8,1024]{2,1,0:T(8,128)S(1)} %slice.56), channel_id=1, source_target_pairs={{0,96},{16,112},{32,0},{48,16},{64,32},{80,48},{96,64},{112,80},{1... | collective-permute-start | bytes 1474568 | tf_op jit(solution)/shard_map/ppermute | solution.py:11
  68.7 1.1 %constant_dynamic-update-slice_fusion.1 = f32[120,8,2048]{2,1,0:T(8,128)} fusion(f32[120,8,2048]{2,1,0:T(8,128)} %constant_dynamic-update-slice_fusion.2, f32[15,8,2048]{2,1,0:T(8,128)S(1)} %collective-permute-done.5), kind=kLoop, calls=%fused_computation.20 | loop fusion | bytes 1966080
  69.8 1.1 %constant_dynamic-update-slice_fusion = f32[120,8,2048]{2,1,0:T(8,128)} fusion(f32[120,8,2048]{2,1,0:T(8,128)} %constant_dynamic-update-slice_fusion.1, f32[15,8,2048]{2,1,0:T(8,128)S(1)} %collective-permute-done.6), kind=kLoop, calls=%fused_computation.19 | loop fusion | bytes 1966080
  70.8 8.7 %collective-permute-done.7 = f32[15,8,1024]{2,1,0:T(8,128)S(1)} collective-permute-done((f32[15,8,1024]{2,1,0:T(8,128)S(1)}, f32[15,8,1024]{2,1,0:T(8,128)S(1)}, u32[]{:S(2)}, u32[]{:S(2)}) %collective-permute-start.7) | collective-permute-done | bytes 491552 | tf_op jit(solution)/shard_map/ppermute | solution.py:11
  80.5 10.6 %shard_map.55 = (f32[15,8,2048]{2,1,0:T(8,128)S(1)}, f32[15,2048]{1,0:T(8,128)S(1)}, f32[15,2048]{1,0:T(8,128)S(1)}) custom-call(s32[15,16]{1,0:T(8,128)S(1)} %copy.18.partners, f32[15,16]{1,0:T(8,128)S(1)} %copy.19.weights, f32[120,8,2048]{2,1,0:T(8,128)} %maximum_dynamic-update-slice_fusion.every, f32[8,10,2048]{2,1,0:T(8,128)S(1)} %pad_maximum_fusion.coef), custom_call_target="tpu_custom_call" | custom-call | tf_op jit(solution)/shard_map/pallas_call | solution.py:143
  91.1 4.4 %collective-permute-start.11 = (f32[15,2048]{1,0:T(8,128)S(1)}, f32[15,2048]{1,0:T(8,128)S(1)}, u32[]{:S(2)}, u32[]{:S(2)}) collective-permute-start(f32[15,2048]{1,0:T(8,128)S(1)} %get-tuple-element.13), channel_id=1, source_target_pairs={{0,1},{1,2},{2,3},{3,4},{4,5},{5,6},{6,7},{7,8},{8,9},{9,10},{10,1... | collective-permute-start | bytes 368648 | tf_op jit(solution)/shard_map/ppermute | solution.py:39
  95.5 1.9 %collective-permute-start.12 = (f32[15,2048]{1,0:T(8,128)S(1)}, f32[15,2048]{1,0:T(8,128)S(1)}, u32[]{:S(2)}, u32[]{:S(2)}) collective-permute-start(f32[15,2048]{1,0:T(8,128)S(1)} %get-tuple-element.14), channel_id=1, source_target_pairs={{1,0},{2,1},{3,2},{4,3},{5,4},{6,5},{7,6},{8,7},{9,8},{10,9},{11,1... | collective-permute-start | bytes 368648 | tf_op jit(solution)/shard_map/ppermute | solution.py:39
  97.4 4.3 %collective-permute-done.12 = f32[15,2048]{1,0:T(8,128)S(1)} collective-permute-done((f32[15,2048]{1,0:T(8,128)S(1)}, f32[15,2048]{1,0:T(8,128)S(1)}, u32[]{:S(2)}, u32[]{:S(2)}) %collective-permute-start.12) | collective-permute-done | bytes 122912 | tf_op jit(solution)/shard_map/ppermute | solution.py:39
  101.8 1.2 %select_subtract_fusion = f32[15,8,2048]{2,1,0:T(8,128)} fusion(f32[15,8,2048]{2,1,0:T(8,128)S(1)} %get-tuple-element.12, f32[15,2048]{1,0:T(8,128)S(1)} %collective-permute-done.12, f32[15,2048]{1,0:T(8,128)S(1)} %collective-permute-done.11, pred[8]{0:T(512)(128)(4,1)S(1)} %get-tuple-element.32, pred[8]{0:T(512)(128)(4,1)S(1)} %get-tuple-element.33), kind=kLoop, calls=%fused_computation.3 | loop fusion | flops 737280 | bytes 2211856 | tf_op jit(solution)/shard_map/sub | solution.py:88
  (43 shorter events, 10.8 us)
Async XLA Ops:
  0.0 30.7 %collective-permute-start = (f32[15,8,2048]{2,1,0:T(8,128)}, f32[15,8,2048]{2,1,0:T(8,128)S(1)}, u32[]{:S(2)}, u32[]{:S(2)}) collective-permute-start(f32[15,8,2048]{2,1,0:T(8,128)} %param.5), channel_id=1, source_target_pairs={{0,32},{16,48},{32,64},{48,80},{64,96},{80,112},{96,0},{112,16},{1... | collective-permute-start | bytes 2949128 | tf_op jit(solution)/shard_map/ppermute | solution.py:11
  2.0 28.8 %collective-permute-start.1 = (f32[15,8,2048]{2,1,0:T(8,128)}, f32[15,8,2048]{2,1,0:T(8,128)S(1)}, u32[]{:S(2)}, u32[]{:S(2)}) collective-permute-start(f32[15,8,2048]{2,1,0:T(8,128)} %param.5), channel_id=1, source_target_pairs={{0,96},{16,112},{32,0},{48,16},{64,32},{80,48},{96,64},{112,80},{1... | collective-permute-start | bytes 2949128 | tf_op jit(solution)/shard_map/ppermute | solution.py:11
  3.3 30.3 %collective-permute-start.4 = (f32[15,8,2048]{2,1,0:T(8,128)}, f32[15,8,2048]{2,1,0:T(8,128)S(1)}, u32[]{:S(2)}, u32[]{:S(2)}) collective-permute-start(f32[15,8,2048]{2,1,0:T(8,128)} %param.5), channel_id=1, source_target_pairs={{0,16},{16,0},{32,48},{48,32},{64,80},{80,64},{96,112},{112,96},{1... | collective-permute-start | bytes 2949128 | tf_op jit(solution)/shard_map/ppermute | solution.py:20
  7.7 21.8 %collective-permute-start.10 = (f32[8,1,2048]{2,1,0:T(1,128)S(1)}, f32[8,1,2048]{2,1,0:T(1,128)S(1)}, u32[]{:S(2)}, u32[]{:S(2)}) collective-permute-start(f32[8,1,2048]{2,1,0:T(1,128)S(1)} %get-tuple-element.23), channel_id=1, source_target_pairs={{1,0},{2,1},{3,2},{4,3},{5,4},{6,5},{7,6},{8,7},{9,8},{10,9},{11,1... | collective-permute-start | bytes 196616 | tf_op jit(solution)/shard_map/ppermute | solution.py:39
  11.1 18.3 %collective-permute-start.9 = (f32[8,1,2048]{2,1,0:T(1,128)S(1)}, f32[8,1,2048]{2,1,0:T(1,128)S(1)}, u32[]{:S(2)}, u32[]{:S(2)}) collective-permute-start(f32[8,1,2048]{2,1,0:T(1,128)S(1)} %get-tuple-element.22), channel_id=1, source_target_pairs={{0,1},{1,2},{2,3},{3,4},{4,5},{5,6},{6,7},{7,8},{8,9},{9,10},{10,1... | collective-permute-start | bytes 196616 | tf_op jit(solution)/shard_map/ppermute | solution.py:39
  30.8 14.5 %collective-permute-start.2 = (f32[15,8,1024]{2,1,0:T(8,128)S(1)}, f32[15,8,1024]{2,1,0:T(8,128)S(1)}, u32[]{:S(2)}, u32[]{:S(2)}) collective-permute-start(f32[15,8,1024]{2,1,0:T(8,128)S(1)} %slice.53), channel_id=1, source_target_pairs={{0,32},{16,48},{32,64},{48,80},{64,96},{80,112},{96,0},{112,16},{1... | collective-permute-start | bytes 1474568 | tf_op jit(solution)/shard_map/ppermute | solution.py:11
  30.9 14.4 %collective-permute-start.3 = (f32[15,8,1024]{2,1,0:T(8,128)S(1)}, f32[15,8,1024]{2,1,0:T(8,128)S(1)}, u32[]{:S(2)}, u32[]{:S(2)}) collective-permute-start(f32[15,8,1024]{2,1,0:T(8,128)S(1)} %slice.54), channel_id=1, source_target_pairs={{0,96},{16,112},{32,0},{48,16},{64,32},{80,48},{96,64},{112,80},{1... | collective-permute-start | bytes 1474568 | tf_op jit(solution)/shard_map/ppermute | solution.py:11
  33.6 31.9 %collective-permute-start.5 = (f32[15,8,2048]{2,1,0:T(8,128)S(1)}, f32[15,8,2048]{2,1,0:T(8,128)S(1)}, u32[]{:S(2)}, u32[]{:S(2)}) collective-permute-start(f32[15,8,2048]{2,1,0:T(8,128)S(1)} %collective-permute-done.4), channel_id=1, source_target_pairs={{0,32},{16,48},{32,64},{48,80},{64,96},{80,112},{96,0},{112,16},{1... | collective-permute-start | bytes 2949128 | tf_op jit(solution)/shard_map/ppermute | solution.py:11
  33.6 32.0 %collective-permute-start.6 = (f32[15,8,2048]{2,1,0:T(8,128)S(1)}, f32[15,8,2048]{2,1,0:T(8,128)S(1)}, u32[]{:S(2)}, u32[]{:S(2)}) collective-permute-start(f32[15,8,2048]{2,1,0:T(8,128)S(1)} %collective-permute-done.4), channel_id=1, source_target_pairs={{0,96},{16,112},{32,0},{48,16},{64,32},{80,48},{96,64},{112,80},{1... | collective-permute-start | bytes 2949128 | tf_op jit(solution)/shard_map/ppermute | solution.py:11
  65.5 13.9 %collective-permute-start.7 = (f32[15,8,1024]{2,1,0:T(8,128)S(1)}, f32[15,8,1024]{2,1,0:T(8,128)S(1)}, u32[]{:S(2)}, u32[]{:S(2)}) collective-permute-start(f32[15,8,1024]{2,1,0:T(8,128)S(1)} %slice.55), channel_id=1, source_target_pairs={{0,32},{16,48},{32,64},{48,80},{64,96},{80,112},{96,0},{112,16},{1... | collective-permute-start | bytes 1474568 | tf_op jit(solution)/shard_map/ppermute | solution.py:11
  65.7 13.8 %collective-permute-start.8 = (f32[15,8,1024]{2,1,0:T(8,128)S(1)}, f32[15,8,1024]{2,1,0:T(8,128)S(1)}, u32[]{:S(2)}, u32[]{:S(2)}) collective-permute-start(f32[15,8,1024]{2,1,0:T(8,128)S(1)} %slice.56), channel_id=1, source_target_pairs={{0,96},{16,112},{32,0},{48,16},{64,32},{80,48},{96,64},{112,80},{1... | collective-permute-start | bytes 1474568 | tf_op jit(solution)/shard_map/ppermute | solution.py:11
  91.1 6.4 %collective-permute-start.11 = (f32[15,2048]{1,0:T(8,128)S(1)}, f32[15,2048]{1,0:T(8,128)S(1)}, u32[]{:S(2)}, u32[]{:S(2)}) collective-permute-start(f32[15,2048]{1,0:T(8,128)S(1)} %get-tuple-element.13), channel_id=1, source_target_pairs={{0,1},{1,2},{2,3},{3,4},{4,5},{5,6},{6,7},{7,8},{8,9},{9,10},{10,1... | collective-permute-start | bytes 368648 | tf_op jit(solution)/shard_map/ppermute | solution.py:39
  95.5 6.3 %collective-permute-start.12 = (f32[15,2048]{1,0:T(8,128)S(1)}, f32[15,2048]{1,0:T(8,128)S(1)}, u32[]{:S(2)}, u32[]{:S(2)}) collective-permute-start(f32[15,2048]{1,0:T(8,128)S(1)} %get-tuple-element.14), channel_id=1, source_target_pairs={{1,0},{2,1},{3,2},{4,3},{5,4},{6,5},{7,6},{8,7},{9,8},{10,9},{11,1... | collective-permute-start | bytes 368648 | tf_op jit(solution)/shard_map/ppermute | solution.py:39
